TPU v7x, 32 devices: a whole 2x2x4 slice. The times are simulated.
32 devices in a mesh: clips: 2 (over x), rows: 16 (over z, y, core).
Axes of the slice: x: 2, y: 2, z: 4, core: 2. Of those that a mesh axis runs over, the one named last changes fastest.
Arguments:
- frames: bfloat16 [2, 32, 128, 384], P('clips', 'rows'), parts along dimension 0, may hold values from -48 to 48
- norm_attn: float32 [384], replicated, may hold values from 0.25 to 1.75
- w_query: bfloat16 [384, 384], replicated, may hold values from -12 to 12
- w_key: bfloat16 [384, 384], replicated, may hold values from -12 to 12
- w_value: bfloat16 [384, 384], replicated, may hold values from -2 to 2
- w_out: bfloat16 [384, 384], replicated, may hold values from -9 to 9
- cache_one: bfloat16 [4, 32, 128, 384], P('clips', 'rows'), parts along dimension 0, may hold values from -6 to 6
- norm_conv: float32 [384], replicated, may hold values from 0.25 to 1.75
- conv_weight: bfloat16 [3, 3, 3, 384, 384], replicated, may hold values from -0.109375 to 0.109375
- w_up: bfloat16 [3, 3, 384, 192], replicated, may hold values from -0.109375 to 0.109375
Outputs:
- upsampled: bfloat16 [2, 64, 49152], P('clips', 'rows'), parts along dimension 0
There are 2 independent parts, one for each index of `clips`. A program takes and returns all parts, laid end to end along the dimension named above; an argument that names none is the same for every part. Nothing has to cross between parts.
All inputs are finite; a program needn't handle non-finite values.
Results may differ from a plain program's by a relative error of at most 0.013.
Values may be sent and summed in bfloat16 or wider, within the bound.
No kernel may reach another device: no remote copies, remote signals or barrier semaphores. Data moves between devices by JAX's collectives and lax.ppermute only.
A program may use at most 128 MiB of HBM per device.

v0:
```python
import jax
import jax.numpy as jnp
from jax import lax
from jax.sharding import PartitionSpec as P

EPS = 1e-06


def padded_2(array, sides, width):
    for axis, dim in sides:
        size, length = (lax.axis_size(axis), array.shape[dim])
        up = [(i, (i + 1) % size) for i in range(size - 1)]
        down = [(j, i) for i, j in up]
        last = lax.slice_in_dim(array, length - width, length, axis=dim)
        first = lax.slice_in_dim(array, 0, width, axis=dim)
        before = lax.ppermute(last, axis, up)
        after = lax.ppermute(first, axis, down)
        array = jnp.concatenate([before, array, after], axis=dim)
    return array


def rms_gain(values, gain):
    return values * lax.rsqrt(jnp.mean(values * values, axis=-1, keepdims=True) + EPS) * gain


def project(inputs, weight):
    return jnp.einsum("fqc,cd->fqd", inputs, weight, preferred_element_type=jnp.float32).astype(
        jnp.bfloat16
    )


def conv_core(padded, weight, frames_out, rows_out, cols_out):
    chans = padded.shape[-1]
    outs = weight.shape[-1]
    wide = jnp.concatenate(
        [padded[:, :, shift : shift + cols_out, :] for shift in range(3)], axis=-1
    )
    total = jnp.zeros((frames_out * rows_out * cols_out, outs), jnp.float32)
    for tstep in range(weight.shape[0]):
        for rstep in range(3):
            part = wide[tstep : tstep + frames_out, rstep : rstep + rows_out].reshape(-1, 3 * chans)
            total = total + jnp.dot(
                part,
                weight[tstep, rstep].reshape(3 * chans, outs),
                preferred_element_type=jnp.float32,
            )
    return total


def attend_block(carry, queries, keys, values, scale):
    running, denom, accum = carry
    scores = jnp.einsum("fqc,fkc->fqk", queries, keys, preferred_element_type=jnp.float32) * scale
    newtop = jnp.maximum(running, jnp.max(scores, axis=-1))
    expo = jnp.exp(scores - newtop[..., None])
    denom = jnp.sum(expo, axis=-1)
    accum = jnp.einsum(
        "fqk,fkc->fqc", expo.astype(jnp.bfloat16), values, preferred_element_type=jnp.float32
    )
    return (newtop, denom, accum)


def body(
    frames, norm_attn, w_query, w_key, w_value, w_out, cache_one, norm_conv, conv_weight, w_up
):
    nframes, nrows, ncols, chans = frames.shape
    scale = chans ** (-0.5)
    flat = frames.reshape(nframes, nrows * ncols, chans)
    normed = rms_gain(flat.astype(jnp.float32), norm_attn).astype(jnp.bfloat16)
    queries = project(normed, w_query)
    start_carry = (
        jnp.full((nframes, nrows * ncols), -1e30, jnp.float32),
        jnp.zeros((nframes, nrows * ncols), jnp.float32),
        jnp.zeros((nframes, nrows * ncols, chans), jnp.float32),
    )
    keys = project(normed, w_key).reshape(nframes, nrows, ncols, chans)
    values = project(normed, w_value).reshape(nframes, nrows, ncols, chans)
    keys_in = lax.all_gather(keys, "rows", axis=1, tiled=True).reshape(nframes, -1, chans)
    values_in = lax.all_gather(values, "rows", axis=1, tiled=True).reshape(nframes, -1, chans)
    carry = attend_block(start_carry, queries, keys_in, values_in, scale)
    attended = (carry[2] / carry[1][..., None]).astype(jnp.bfloat16)
    mixed = (
        flat.astype(jnp.float32)
        + jnp.einsum("fqc,cd->fqd", attended, w_out, preferred_element_type=jnp.float32)
    ).astype(jnp.bfloat16)
    activ = (
        jax.nn.silu(rms_gain(mixed.astype(jnp.float32), norm_conv))
        .astype(jnp.bfloat16)
        .reshape(nframes, nrows, ncols, chans)
    )
    stack = jnp.concatenate([cache_one, activ], axis=0)
    haloed = padded_2(stack, (("rows", 1),), 1)
    padded = jnp.pad(haloed, ((0, 0), (0, 0), (1, 1), (0, 0)))
    conv_out = (
        conv_core(padded, conv_weight, nframes, nrows, ncols)
        .astype(jnp.bfloat16)
        .reshape(nframes, nrows, ncols, chans)
    )
    extended = padded_2(conv_out, (("rows", 1),), 1)
    doubled = jnp.repeat(jnp.repeat(extended, 2, axis=1), 2, axis=2)[:, 1 : 2 * nrows + 3]
    padded_up = jnp.pad(doubled, ((0, 0), (0, 0), (1, 1), (0, 0)))
    result = conv_core(padded_up, w_up[None], nframes, 2 * nrows, 2 * ncols)
    return result.astype(jnp.bfloat16).reshape(nframes, 2 * nrows, 2 * ncols * w_up.shape[-1])


def solution(mesh):
    placed = (
        P("clips", "rows", None, None),
        P(),
        P(),
        P(),
        P(),
        P(),
        P("clips", "rows", None, None),
        P(),
        P(),
        P(),
    )
    return jax.shard_map(
        body, mesh=mesh, in_specs=placed, out_specs=P("clips", "rows", None), check_vma=False
    )
```

profile of v0, /device:TPU:5, one launch (start us, length us, event | category | flops | bytes accessed | tf_op | source)
XLA Modules:
  0.0 151.7 jit_solution(1694360441257205537)
XLA Ops:
  6.5 1.1 multiply_reduce_fusion.1
  7.6 1.0 fusion.29
  8.7 1.9 %convolution_convert_fusion.1 = bf16[256,384]{1,0:T(8,128)(2,1)} fusion(bf16[256,384]{1,0:T(8,128)(2,1)S(1)} %fusion.29, bf16[384,384]{1,0:T(8,128)(2,1)} %param.13), kind=kOutput, calls=%fused_computation.30 | convolution fusion | flops 75595776 | bytes 688128 | tf_op jit(solution)/shard_map/fqc,cd->fqd/dot_general | solution.py:27
  10.7 1.9 %convolution_convert_fusion = bf16[256,384]{1,0:T(8,128)(2,1)} fusion(bf16[256,384]{1,0:T(8,128)(2,1)S(1)} %fusion.29, bf16[384,384]{1,0:T(8,128)(2,1)} %param.14), kind=kOutput, calls=%fused_computation.29 | convolution fusion | flops 75595776 | bytes 688128 | tf_op jit(solution)/shard_map/fqc,cd->fqd/dot_general | solution.py:27
  12.6 44.3 %all-gather.3.cloned.1.call-done = bf16[1,32,128,384]{3,2,0,1:T(8,128)(2,1)} async-done(((bf16[1,2,128,384]{3,2,0,1:T(8,128)(2,1)}), bf16[1,32,128,384]{3,2,0,1:T(8,128)(2,1)}) %all-gather.3.cloned.1.call-update) | async-done | bytes 3145744 | tf_op jit(solution)/shard_map/all_gather | solution.py:77
  56.9 5.3 %fusion.38 = (f32[256]{0:T(256)S(1)}, f32[256,4096]{1,0:T(8,128)}) fusion(bf16[4096,384]{1,0:T(8,128)(2,1)} %bitcast.108, bf16[256,384]{1,0:T(8,128)(2,1)S(1)} %fusion.29, bf16[384,384]{1,0:T(8,128)(2,1)S(1)} %copy-done), kind=kOutput, calls=%fused_computation.59 | convolution fusion | flops 882999040 | bytes 7832576 | tf_op jit(solution)/shard_map/fqc,fkc->fqk/dot_general | solution.py:52
  62.3 3.0 %fusion = f32[256]{0:T(256)S(1)} fusion(f32[256,4096]{1,0:T(8,128)} %get-tuple-element.38, f32[256]{0:T(256)S(1)} %broadcast_maximum_fusion), kind=kLoop, calls=%fused_computation.4 | loop fusion | flops 2096896 | bytes 4196352 | tf_op jit(solution)/shard_map/reduce_sum | solution.py:55
  65.2 37.8 %all-gather.5.cloned.1.call-done = bf16[1,32,128,384]{3,2,0,1:T(8,128)(2,1)} async-done(((bf16[1,2,128,384]{3,2,0,1:T(8,128)(2,1)}), bf16[1,32,128,384]{3,2,0,1:T(8,128)(2,1)}) %all-gather.5.cloned.1.call-update) | async-done | bytes 3145744 | tf_op jit(solution)/shard_map/all_gather | solution.py:78
  103.0 4.8 %multiply_reduce_fusion = (f32[256]{0:T(256)S(1)}, f32[256,384]{1,0:T(8,128)S(1)}) fusion(bf16[384,384]{1,0:T(8,128)(2,1)S(1)} %copy-done.9, bf16[4096,384]{1,0:T(8,128)(2,1)} %bitcast.130, f32[256,4096]{1,0:T(8,128)} %get-tuple-element.38, f32[256]{0:T(256)S(1)} %broadcast_maximum_fusion, f32[256]{0:T(256)S(1)} %fusion, bf16[256,384]{1,0:T(8,128)(2,1)S(1)} %bitcast.127), kind=kOutput, calls=%fused_computation.45 | convolution fusion | flops 883687168 | bytes 8227840 | tf_op jit(solution)/shard_map/fqc,cd->fqd/dot_general | solution.py:83
  107.9 0.2 multiply_convert_fusion
  108.2 4.1 %collective-permute-start = (bf16[3,1,128,384]{3,2,1,0:T(8,128)(2,1)S(1)}, bf16[3,1,128,384]{3,2,1,0:T(8,128)(2,1)S(1)}, u32[]{:S(2)}, u32[]{:S(2)}) collective-permute-start(bf16[3,1,128,384]{3,2,1,0:T(8,128)(2,1)S(1)} %get-tuple-element.33), channel_id=1, source_target_pairs={{0,1},{1,2},{2,3},{3,4},{4,5},{5,6},{6,7},{7,8},{8,9},{9,10},{10,1... | collective-permute-start | bytes 884744 | tf_op jit(solution)/shard_map/ppermute | solution.py:16
  112.3 1.9 %collective-permute-start.1 = (bf16[3,1,128,384]{3,2,1,0:T(8,128)(2,1)S(1)}, bf16[3,1,128,384]{3,2,1,0:T(8,128)(2,1)S(1)}, u32[]{:S(2)}, u32[]{:S(2)}) collective-permute-start(bf16[3,1,128,384]{3,2,1,0:T(8,128)(2,1)S(1)} %get-tuple-element.34), channel_id=1, source_target_pairs={{1,0},{2,1},{3,2},{4,3},{5,4},{6,5},{7,6},{8,7},{9,8},{10,9},{11,1... | collective-permute-start | bytes 884744 | tf_op jit(solution)/shard_map/ppermute | solution.py:17
  114.2 3.9 %fusion.32 = (bf16[1,1,3,384,384]{4,3,2,1,0:T(8,128)(2,1)S(1)}, bf16[1,1,3,384,384]{4,3,2,1,0:T(8,128)(2,1)S(1)}, bf16[1,1,3,384,384]{4,3,2,1,0:T(8,128)(2,1)S(1...) fusion(bf16[3,3,3,384,384]{4,3,2,1,0:T(8,128)(2,1)} %param.18), kind=kLoop, calls=%fused_computation.53 | loop fusion | bytes 15925248 | tf_op jit(solution)/shard_map/slice | solution.py:44
  118.2 3.1 %collective-permute-done.1 = bf16[3,1,128,384]{3,2,1,0:T(8,128)(2,1)S(1)} collective-permute-done((bf16[3,1,128,384]{3,2,1,0:T(8,128)(2,1)S(1)}, bf16[3,1,128,384]{3,2,1,0:T(8,128)(2,1)S(1)}, u32[]{:S(2)}, u32[]{:S(2)}) %collective-permute-start.1) | collective-permute-done | bytes 294944 | tf_op jit(solution)/shard_map/ppermute | solution.py:17
  121.2 0.3 select_maximum_fusion
  121.6 0.5 fusion.36
  122.1 0.5 pad_maximum_fusion
  122.7 0.7 fusion.34
  123.4 0.5 fusion.41
  123.9 0.5 fusion.42
  124.4 0.5 fusion.43
  124.8 0.5 fusion.44
  125.3 0.5 fusion.45
  125.8 0.5 fusion.46
  126.3 0.5 fusion.47
  126.8 0.5 fusion.48
  127.3 0.6 fusion.17
  127.9 1.9 %collective-permute-start.2 = (bf16[1,1,128,384]{3,2,1,0:T(8,128)(2,1)S(1)}, bf16[1,1,128,384]{3,2,1,0:T(8,128)(2,1)S(1)}, u32[]{:S(2)}, u32[]{:S(2)}) collective-permute-start(bf16[1,1,128,384]{3,2,1,0:T(8,128)(2,1)S(1)} %get-tuple-element.35), channel_id=1, source_target_pairs={{0,1},{1,2},{2,3},{3,4},{4,5},{5,6},{6,7},{7,8},{8,9},{9,10},{10,1... | collective-permute-start | bytes 294920 | tf_op jit(solution)/shard_map/ppermute | solution.py:16
  129.9 2.6 %collective-permute-start.3 = (bf16[1,1,128,384]{3,2,1,0:T(8,128)(2,1)S(1)}, bf16[1,1,128,384]{3,2,1,0:T(8,128)(2,1)S(1)}, u32[]{:S(2)}, u32[]{:S(2)}) collective-permute-start(bf16[1,1,128,384]{3,2,1,0:T(8,128)(2,1)S(1)} %get-tuple-element.36), channel_id=1, source_target_pairs={{1,0},{2,1},{3,2},{4,3},{5,4},{6,5},{7,6},{8,7},{9,8},{10,9},{11,1... | collective-permute-start | bytes 294920 | tf_op jit(solution)/shard_map/ppermute | solution.py:17
  132.5 0.1 fusion.35
  132.6 0.4 copy.17
  133.0 0.8 copy.21
  133.8 0.4 copy.18
  134.2 0.8 copy.22
  135.0 0.4 copy.19
  135.4 0.8 copy.23
  136.3 0.4 collective-permute-done.3
  136.8 0.8 broadcast_in_dim.25
  137.6 0.6 broadcast_in_dim.26
  138.3 0.1 slice.149
  138.4 0.5 pad_slice_fusion.1
  139.0 0.4 pad_maximum_fusion.1
  139.3 0.9 fusion.33
  140.3 0.9 fusion.49
  141.4 0.9 convolution_add_fusion.1
  142.4 0.9 fusion.9
  143.3 0.2 copy.20
  143.5 1.3 reshape.221
  (33 shorter events, 0.6 us)
Async XLA Ops:
  6.5 50.4 %copy-start = (bf16[384,384]{1,0:T(8,128)(2,1)S(1)}, bf16[384,384]{1,0:T(8,128)(2,1)}, u32[]{:S(2)}) copy-start(bf16[384,384]{1,0:T(8,128)(2,1)} %param.12) | copy-start | bytes 884740
  6.5 50.4 %all-gather.3.cloned.1.call-start = ((), (), s32[]{:S(2)}) async-start(), calls=%async_computation | async-start | bytes 3342336 | tf_op jit(solution)/shard_map/all_gather | solution.py:77
  10.6 92.4 %all-gather.5.cloned.1.call-start = ((), (), s32[]{:S(2)}) async-start(), calls=%async_computation.1 | async-start | bytes 3342336 | tf_op jit(solution)/shard_map/all_gather | solution.py:78
  62.2 40.8 %copy-start.7 = (bf16[1,2,128,384]{3,2,1,0:T(8,128)(2,1)S(1)}, bf16[1,2,128,384]{3,2,1,0:T(8,128)(2,1)}, u32[]{:S(2)}) copy-start(bf16[1,2,128,384]{3,2,1,0:T(8,128)(2,1)} %param.10) | copy-start | bytes 589828
  62.2 40.8 %copy-start.9 = (bf16[384,384]{1,0:T(8,128)(2,1)S(1)}, bf16[384,384]{1,0:T(8,128)(2,1)}, u32[]{:S(2)}) copy-start(bf16[384,384]{1,0:T(8,128)(2,1)} %param.15) | copy-start | bytes 884740
  103.0 4.8 %copy-start.8 = (f32[384]{0:T(512)S(1)}, f32[384]{0:T(512)}, u32[]{:S(2)}) copy-start(f32[384]{0:T(512)} %param.17) | copy-start | bytes 4612
  103.0 5.0 %copy-start.2 = (bf16[2,2,128,384]{3,2,1,0:T(8,128)(2,1)S(1)}, bf16[2,2,128,384]{3,2,1,0:T(8,128)(2,1)}, u32[]{:S(2)}) copy-start(bf16[2,2,128,384]{3,2,1,0:T(8,128)(2,1)} %param.16) | copy-start | bytes 1179652
  108.2 10.0 %collective-permute-start = (bf16[3,1,128,384]{3,2,1,0:T(8,128)(2,1)S(1)}, bf16[3,1,128,384]{3,2,1,0:T(8,128)(2,1)S(1)}, u32[]{:S(2)}, u32[]{:S(2)}) collective-permute-start(bf16[3,1,128,384]{3,2,1,0:T(8,128)(2,1)S(1)} %get-tuple-element.33), channel_id=1, source_target_pairs={{0,1},{1,2},{2,3},{3,4},{4,5},{5,6},{6,7},{7,8},{8,9},{9,10},{10,1... | collective-permute-start | bytes 884744 | tf_op jit(solution)/shard_map/ppermute | solution.py:16
  112.3 8.9 %collective-permute-start.1 = (bf16[3,1,128,384]{3,2,1,0:T(8,128)(2,1)S(1)}, bf16[3,1,128,384]{3,2,1,0:T(8,128)(2,1)S(1)}, u32[]{:S(2)}, u32[]{:S(2)}) collective-permute-start(bf16[3,1,128,384]{3,2,1,0:T(8,128)(2,1)S(1)} %get-tuple-element.34), channel_id=1, source_target_pairs={{1,0},{2,1},{3,2},{4,3},{5,4},{6,5},{7,6},{8,7},{9,8},{10,9},{11,1... | collective-permute-start | bytes 884744 | tf_op jit(solution)/shard_map/ppermute | solution.py:17
  127.2 5.2 %copy-start.6 = (bf16[3,3,384,192]{2,3,1,0:T(8,128)(2,1)S(1)}, bf16[3,3,384,192]{2,3,1,0:T(8,128)(2,1)}, u32[]{:S(2)}) copy-start(bf16[3,3,384,192]{2,3,1,0:T(8,128)(2,1)} %param.19) | copy-start | bytes 3981316
  127.9 8.3 %collective-permute-start.2 = (bf16[1,1,128,384]{3,2,1,0:T(8,128)(2,1)S(1)}, bf16[1,1,128,384]{3,2,1,0:T(8,128)(2,1)S(1)}, u32[]{:S(2)}, u32[]{:S(2)}) collective-permute-start(bf16[1,1,128,384]{3,2,1,0:T(8,128)(2,1)S(1)} %get-tuple-element.35), channel_id=1, source_target_pairs={{0,1},{1,2},{2,3},{3,4},{4,5},{5,6},{6,7},{7,8},{8,9},{9,10},{10,1... | collective-permute-start | bytes 294920 | tf_op jit(solution)/shard_map/ppermute | solution.py:16
  129.9 6.8 %collective-permute-start.3 = (bf16[1,1,128,384]{3,2,1,0:T(8,128)(2,1)S(1)}, bf16[1,1,128,384]{3,2,1,0:T(8,128)(2,1)S(1)}, u32[]{:S(2)}, u32[]{:S(2)}) collective-permute-start(bf16[1,1,128,384]{3,2,1,0:T(8,128)(2,1)S(1)} %get-tuple-element.36), channel_id=1, source_target_pairs={{1,0},{2,1},{3,2},{4,3},{5,4},{6,5},{7,6},{8,7},{9,8},{10,9},{11,1... | collective-permute-start | bytes 294920 | tf_op jit(solution)/shard_map/ppermute | solution.py:17
  139.3 1.0 copy-start.4
  140.3 1.0 copy-start.3
  141.4 1.0 copy-start.5
  142.4 2.5 %copy-start.1 = (bf16[384,384]{1,0:T(8,128)(2,1)S(1)}, bf16[384,384]{1,0:T(8,128)(2,1)}, u32[]{:S(2)}) copy-start(bf16[384,384]{1,0:T(8,128)(2,1)} %param.12) | copy-start | bytes 884740
Sparse Core Ops, SparseCore 0:
  10.8 46.1 all-gather.2
  59.2 43.7 all-gather.4
where the time goes:
time: 152 us
  waiting for transfers between devices  85.7 us (56%)
  matrix products  21.2 us (14%)
  local copies, waits for them, and re-layouts  13.9 us (9%)
  between operations  13.7 us (9%)
  starting transfers between devices  10.6 us (7%)
  other arithmetic  6.63 us (4%)
    all_gather x1, waiting for transfers between devices, body(): lax.all_gather(keys, 'rows', axis=1, tiled=True).reshape(nframes, -1, chans)  44.3 us
    all_gather x1, waiting for transfers between devices, body(): lax.all_gather(values, 'rows', axis=1, tiled=True)  37.8 us
    dot_general x12, matrix products, conv_core(): jnp.dot(part, weight[tstep, rstep].reshape(3 * chans, outs), preferred_el...  7.22 us
    ppermute x2, starting transfers between devices, padded_2(): before = lax.ppermute(last, axis, up)  6.06 us
    dot_general x1, matrix products, attend_block(): jnp.einsum('fqc,fkc->fqk', queries, keys, preferred_element_type=jnp.floa...  5.32 us
    slice x5, local copies, waits for them, and re-layouts, conv_core(): weight[tstep, rstep].reshape(3 * chans, outs)  5.2 us
    dot_general x1, matrix products, body(): jnp.einsum('fqc,cd->fqd', attended, w_out, preferred_element_type=jnp.flo...  4.82 us
    ppermute x2, starting transfers between devices, padded_2(): after = lax.ppermute(first, axis, down)  4.51 us
  transfers between devices with their start and end apart: 6, of which 4 were waited for; matrix products, arithmetic and copies ran while one was open for 12% of the time, Pallas kernels for 0%

commit v1 on v0

v1 whole, which is shorter than its diff:
```python
import jax
import jax.numpy as jnp
from jax import lax
from jax.sharding import PartitionSpec as P

EPS = 1e-06


def padded_2(array, sides, width):
    for axis, dim in sides:
        size, length = (lax.axis_size(axis), array.shape[dim])
        up = [(i, (i + 1) % size) for i in range(size - 1)]
        down = [(j, i) for i, j in up]
        last = lax.slice_in_dim(array, length - width, length, axis=dim)
        first = lax.slice_in_dim(array, 0, width, axis=dim)
        before = lax.ppermute(last, axis, up)
        after = lax.ppermute(first, axis, down)
        array = jnp.concatenate([before, array, after], axis=dim)
    return array


def rms_gain(values, gain):
    return values * lax.rsqrt(jnp.mean(values * values, axis=-1, keepdims=True) + EPS) * gain


def project(inputs, weight):
    return jnp.einsum("fqc,cd->fqd", inputs, weight, preferred_element_type=jnp.float32).astype(
        jnp.bfloat16
    )


def conv_rows(haloed, weight):
    total = None
    for tstep in range(weight.shape[0]):
        part = lax.conv_general_dilated(
            haloed[tstep : tstep + 1],
            weight[tstep],
            window_strides=(1, 1),
            padding=((0, 0), (1, 1)),
            dimension_numbers=("NHWC", "HWIO", "NHWC"),
            preferred_element_type=jnp.float32,
        )
        total = part if total is None else total + part
    return total


def upsample_conv(extended, w_up):
    nf, rp, ncols, chans = extended.shape
    nrows = rp - 2
    outs = w_up.shape[-1]
    padded = jnp.pad(extended, ((0, 0), (0, 0), (1, 1), (0, 0)))
    taps = jnp.einsum(
        "frwc,ijco->frwijo", padded, w_up, preferred_element_type=jnp.float32
    )
    phases_a = []
    for a in range(2):
        phases_b = []
        for b in range(2):
            acc = None
            for dr in range(3):
                ro = (a + dr + 1) // 2
                for dc in range(3):
                    co = (b + dc + 1) // 2
                    term = taps[:, ro : ro + nrows, co : co + ncols, dr, dc, :]
                    acc = term if acc is None else acc + term
            phases_b.append(acc)
        phases_a.append(jnp.stack(phases_b, axis=3))
    result = jnp.stack(phases_a, axis=2)
    return result.astype(jnp.bfloat16).reshape(nf, 2 * nrows, 2 * ncols * outs)


def body(
    frames, norm_attn, w_query, w_key, w_value, w_out, cache_one, norm_conv, conv_weight, w_up
):
    nframes, nrows, ncols, chans = frames.shape
    scale = chans ** (-0.5)

    cache_haloed = padded_2(cache_one, (("rows", 1),), 1)
    cache_part = conv_rows(cache_haloed, conv_weight[:2])

    flat = frames.reshape(nframes, nrows * ncols, chans)
    normed = rms_gain(flat.astype(jnp.float32), norm_attn).astype(jnp.bfloat16)
    normed_all = lax.all_gather(
        normed.reshape(nframes, nrows, ncols, chans), "rows", axis=1, tiled=True
    ).reshape(nframes, -1, chans)
    queries = project(normed, w_query)
    keys = project(normed_all, w_key)
    values = project(normed_all, w_value)
    scores = jnp.einsum("fqc,fkc->fqk", queries, keys, preferred_element_type=jnp.float32) * scale
    top = jnp.max(scores, axis=-1, keepdims=True)
    expo = jnp.exp(scores - top)
    denom = jnp.sum(expo, axis=-1, keepdims=True)
    numer = jnp.einsum(
        "fqk,fkc->fqc", expo.astype(jnp.bfloat16), values, preferred_element_type=jnp.float32
    )
    attended = (numer / denom).astype(jnp.bfloat16)
    mixed = (
        flat.astype(jnp.float32)
        + jnp.einsum("fqc,cd->fqd", attended, w_out, preferred_element_type=jnp.float32)
    ).astype(jnp.bfloat16)
    activ = (
        jax.nn.silu(rms_gain(mixed.astype(jnp.float32), norm_conv))
        .astype(jnp.bfloat16)
        .reshape(nframes, nrows, ncols, chans)
    )
    activ_haloed = padded_2(activ, (("rows", 1),), 1)
    conv_out = (cache_part + conv_rows(activ_haloed, conv_weight[2:])).astype(jnp.bfloat16)
    extended = padded_2(conv_out, (("rows", 1),), 1)
    return upsample_conv(extended, w_up)


def solution(mesh):
    placed = (
        P("clips", "rows", None, None),
        P(),
        P(),
        P(),
        P(),
        P(),
        P("clips", "rows", None, None),
        P(),
        P(),
        P(),
    )
    return jax.shard_map(
        body, mesh=mesh, in_specs=placed, out_specs=P("clips", "rows", None), check_vma=False
    )
```

time: 152 us -> 110 us (0.72)
  waiting for transfers between devices: 85.7 us -> 41.2 us
  local copies, waits for them, and re-layouts: 13.9 us -> 6.49 us
  starting transfers between devices: 10.6 us -> 16.6 us
  other arithmetic: 6.63 us -> 9.6 us
    all_gather x2 -> x1, waiting for transfers between devices: 82.1 us -> 31 us  [body(): lax.all_gather(normed.reshape(nframes, nrows, ncols, chans), 'rows', axis...]
    ppermute x2 -> x3, waiting for transfers between devices: 3.51 us -> 10.2 us  [padded_2(): after = lax.ppermute(first, axis, down)]
    slice x10 -> x4, local copies, waits for them, and re-layouts: 8.05 us -> 1.51 us  [the longest x1 1.11 us: padded_2(): first = lax.slice_in_dim(array, 0, width, axis=dim)]
    conv_general_dilated x0 -> x3, matrix products: none -> 5.32 us  [conv_rows(): lax.conv_general_dilated(haloed[tstep:tstep + 1], weight[tstep], window_s...]
    dot_general x1, matrix products: 4.82 us -> 0.38 us  [body(): jnp.einsum('fqc,cd->fqd', attended, w_out, preferred_element_type=jnp.flo...]
    ppermute x2 -> x3, starting transfers between devices: 6.06 us -> 10.3 us  [padded_2(): before = lax.ppermute(last, axis, up)]
    dot_general x2 -> x1, matrix products: 3.83 us -> 1.23 us  [project(): jnp.einsum('fqc,cd->fqd', inputs, weight, preferred_element_type=jnp.floa...]
    dot_general x13 -> x3, matrix products: 12.5 us -> 14.9 us  [the longest x1 7.05 us: body(): jnp.einsum('fqc,fkc->fqk', queries, keys, preferred_element_type=jnp.floa...]
  transfers between devices with their start and end apart: 6 -> 7, of which waited for: 4 -> 4; matrix products, arithmetic and copies ran while one was open for 12% -> 9% of each run, Pallas kernels for 0% -> 0%
where the time goes in v1:
time: 110 us
  waiting for transfers between devices  41.2 us (37%)
  matrix products  21.8 us (20%)
  starting transfers between devices  16.6 us (15%)
  between operations  13.9 us (13%)
  other arithmetic  9.6 us (9%)
  local copies, waits for them, and re-layouts  6.49 us (6%)
    all_gather x1, waiting for transfers between devices, body(): lax.all_gather(normed.reshape(nframes, nrows, ncols, chans), 'rows', axis...  31 us
    ppermute x3, starting transfers between devices, padded_2(): before = lax.ppermute(last, axis, up)  10.3 us
    ppermute x3, waiting for transfers between devices, padded_2(): after = lax.ppermute(first, axis, down)  10.2 us
    dot_general x1, matrix products, body(): jnp.einsum('fqc,fkc->fqk', queries, keys, preferred_element_type=jnp.floa...  7.05 us
    dot_general x1, matrix products, body(): jnp.einsum('fqk,fkc->fqc', expo.astype(jnp.bfloat16), values, preferred_e...  6.36 us
    ppermute x3, starting transfers between devices, padded_2(): after = lax.ppermute(first, axis, down)  6.31 us
    conv_general_dilated x3, matrix products, conv_rows(): lax.conv_general_dilated(haloed[tstep:tstep + 1], weight[tstep], window_s...  5.32 us
    reduce_sum x1, other arithmetic, body(): denom = jnp.sum(expo, axis=-1, keepdims=True)  2.89 us
  transfers between devices with their start and end apart: 7, of which 4 were waited for; matrix products, arithmetic and copies ran while one was open for 9% of the time, Pallas kernels for 0%

profile of v1, /device:TPU:5, one launch (start us, length us, event | category | flops | bytes accessed | tf_op | source)
XLA Modules:
  0.0 109.6 jit_solution(9928257195442375067)
XLA Ops:
  6.5 1.1 %multiply_reduce_fusion.1 = f32[2,128]{1,0:T(2,128)S(1)} fusion(bf16[1,2,128,384]{3,2,1,0:T(8,128)(2,1)} %param.10), kind=kLoop, calls=%fused_computation.74 | loop fusion | flops 294656 | bytes 197632 | tf_op jit(solution)/shard_map/reduce_sum | solution.py:23
  7.7 1.7 %multiply_convert_fusion.1 = bf16[1,2,128,384]{3,2,0,1:T(8,128)(2,1)} fusion(bf16[1,2,128,384]{3,2,1,0:T(8,128)(2,1)} %param.10, f32[384]{0:T(512)} %param.11, f32[2,128]{1,0:T(2,128)S(1)} %get-tuple-element.15), kind=kLoop, calls=%fused_computation.73 | loop fusion | flops 393216 | bytes 395776 | tf_op jit(solution)/shard_map/convert_element_type | solution.py:82
  9.4 0.0 all-gather.2.cloned.1.call-update
  9.5 1.1 %fusion.137 = (bf16[2,1,128,384]{3,2,1,0:T(8,128)(2,1)S(1)}, bf16[2,1,128,384]{3,2,1,0:T(8,128)(2,1)S(1)}) fusion(bf16[2,2,128,384]{3,2,1,0:T(8,128)(2,1)} %param.16), kind=kLoop, calls=%fused_computation.167 | loop fusion | bytes 786432 | tf_op jit(solution)/shard_map/slice | solution.py:15
  10.6 3.7 %collective-permute-start = (bf16[2,1,128,384]{3,2,1,0:T(8,128)(2,1)S(1)}, bf16[2,1,128,384]{3,2,1,0:T(8,128)(2,1)S(1)}, u32[]{:S(2)}, u32[]{:S(2)}) collective-permute-start(bf16[2,1,128,384]{3,2,1,0:T(8,128)(2,1)S(1)} %get-tuple-element.10), channel_id=1, source_target_pairs={{0,1},{1,2},{2,3},{3,4},{4,5},{5,6},{6,7},{7,8},{8,9},{9,10},{10,1... | collective-permute-start | bytes 589832 | tf_op jit(solution)/shard_map/ppermute | solution.py:16
  14.3 1.9 %collective-permute-start.1 = (bf16[2,1,128,384]{3,2,1,0:T(8,128)(2,1)S(1)}, bf16[2,1,128,384]{3,2,1,0:T(8,128)(2,1)S(1)}, u32[]{:S(2)}, u32[]{:S(2)}) collective-permute-start(bf16[2,1,128,384]{3,2,1,0:T(8,128)(2,1)S(1)} %get-tuple-element.9), channel_id=1, source_target_pairs={{1,0},{2,1},{3,2},{4,3},{5,4},{6,5},{7,6},{8,7},{9,8},{10,9},{11,1... | collective-permute-start | bytes 589832 | tf_op jit(solution)/shard_map/ppermute | solution.py:17
  16.2 1.0 fusion.78
  17.3 1.2 %convolution_convert_fusion.2 = bf16[256,384]{1,0:T(8,128)(2,1)S(1)} fusion(bf16[256,384]{1,0:T(8,128)(2,1)S(1)} %fusion.78, bf16[384,384]{1,0:T(8,128)(2,1)} %param.12), kind=kOutput, calls=%fused_computation.22 | convolution fusion | flops 75595776 | bytes 688128 | tf_op jit(solution)/shard_map/fqc,cd->fqd/dot_general | solution.py:27
  18.5 1.0 bitcast_convert_fusion
  19.5 1.1 constant_dynamic-update-slice_fusion.1
  20.6 3.5 %collective-permute-done.1 = bf16[2,1,128,384]{3,2,1,0:T(8,128)(2,1)S(1)} collective-permute-done((bf16[2,1,128,384]{3,2,1,0:T(8,128)(2,1)S(1)}, bf16[2,1,128,384]{3,2,1,0:T(8,128)(2,1)S(1)}, u32[]{:S(2)}, u32[]{:S(2)}) %collective-permute-start.1) | collective-permute-done | bytes 196640 | tf_op jit(solution)/shard_map/ppermute | solution.py:17
  24.2 0.1 slice_bitcast_fusion.1
  24.3 0.3 copy.146
  24.6 0.2 pad.7.clone
  24.7 0.1 copy.82
  24.8 31.0 %all-gather.2.cloned.1.call-done = bf16[1,32,128,384]{3,2,0,1:T(8,128)(2,1)} async-done(((bf16[1,2,128,384]{3,2,0,1:T(8,128)(2,1)}), bf16[1,32,128,384]{3,2,0,1:T(8,128)(2,1)}) %all-gather.2.cloned.1.call-update) | async-done | bytes 3145744 | tf_op jit(solution)/shard_map/all_gather | solution.py:83
  55.8 7.0 %fusion.140 = (f32[256]{0:T(256)S(1)}, f32[256,4096]{1,0:T(8,128)}) fusion(bf16[256,384]{1,0:T(8,128)(2,1)S(1)} %convolution_convert_fusion.2, bf16[4096,384]{1,0:T(8,128)(2,1)} %bitcast.358, bf16[384,384]{1,0:T(8,128)(2,1)S(1)} %copy-done.3), kind=kOutput, calls=%fused_computation.170 | convolution fusion | flops 2016935680 | bytes 7832576 | tf_op jit(solution)/shard_map/fqc,fkc->fqk/dot_general | solution.py:89
  62.9 2.9 %fusion = f32[256]{0:T(256)S(1)} fusion(f32[256,4096]{1,0:T(8,128)} %get-tuple-element.18, f32[256]{0:T(256)S(1)} %get-tuple-element.17), kind=kLoop, calls=%fused_computation.4 | loop fusion | flops 2096896 | bytes 4196352 | tf_op jit(solution)/shard_map/reduce_sum | solution.py:92
  65.8 6.4 %fusion.38 = bf16[256,384]{1,0:T(8,128)(2,1)S(1)} fusion(f32[256,4096]{1,0:T(8,128)} %get-tuple-element.18, f32[256]{0:T(256)S(1)} %get-tuple-element.17, bf16[4096,384]{1,0:T(8,128)(2,1)} %bitcast.359, bf16[384,384]{1,0:T(8,128)(2,1)} %param.14, f32[256]{0:T(256)S(1)} %fusion), kind=kOutput, calls=%fused_computation.32 | convolution fusion | flops 2017132544 | bytes 7833600 | tf_op jit(solution)/shard_map/fqk,fkc->fqc/dot_general | solution.py:93
  72.2 0.4 multiply_reduce_fusion
  72.6 0.2 multiply_convert_fusion
  72.8 0.2 copy.84
  73.0 0.3 fusion.139
  73.3 4.3 %collective-permute-start.2 = (bf16[1,1,128,384]{3,1,2,0:T(2,128)(2,1)S(1)}, bf16[1,1,128,384]{3,1,2,0:T(2,128)(2,1)S(1)}, u32[]{:S(2)}, u32[]{:S(2)}) collective-permute-start(bf16[1,1,128,384]{3,1,2,0:T(2,128)(2,1)S(1)} %get-tuple-element.13), channel_id=1, source_target_pairs={{0,1},{1,2},{2,3},{3,4},{4,5},{5,6},{6,7},{7,8},{8,9},{9,10},{10,1... | collective-permute-start | bytes 294920 | tf_op jit(solution)/shard_map/ppermute | solution.py:16
  77.5 2.4 %collective-permute-start.3 = (bf16[1,1,128,384]{3,1,2,0:T(2,128)(2,1)S(1)}, bf16[1,1,128,384]{3,1,2,0:T(2,128)(2,1)S(1)}, u32[]{:S(2)}, u32[]{:S(2)}) collective-permute-start(bf16[1,1,128,384]{3,1,2,0:T(2,128)(2,1)S(1)} %get-tuple-element.14), channel_id=1, source_target_pairs={{1,0},{2,1},{3,2},{4,3},{5,4},{6,5},{7,6},{8,7},{9,8},{10,9},{11,1... | collective-permute-start | bytes 294920 | tf_op jit(solution)/shard_map/ppermute | solution.py:17
  79.9 2.9 %fusion.29 = f32[2,8,17,384]{3,1,2,0:T(8,128)S(1)} fusion(bf16[3,3,3,384,384]{4,3,2,1,0:T(8,128)(2,1)} %param.18, bf16[4,1,7,2,384]{4,2,3,0,1:T(8,128)(2,1)S(1)} %slice.169, bf16[4,1,8,17,384]{4,2,3,0,1:T(8,128)(2,1)S(1)} %copy.82, pred[8,17]{0,1:T(8,128)(4,1)S(1)} %copy-done.4), kind=kOutput, calls=%fused_computation.29 | convolution fusion | flops 723449856 | bytes 3532936 | tf_op jit(solution)/shard_map/conv_general_dilated | solution.py:35
  82.9 0.3 copy.145
  83.2 0.2 pad.5.clone
  83.3 0.1 copy.79
  83.4 2.3 %collective-permute-done.3 = bf16[1,1,128,384]{3,1,2,0:T(2,128)(2,1)S(1)} collective-permute-done((bf16[1,1,128,384]{3,1,2,0:T(2,128)(2,1)S(1)}, bf16[1,1,128,384]{3,1,2,0:T(2,128)(2,1)S(1)}, u32[]{:S(2)}, u32[]{:S(2)}) %collective-permute-start.3) | collective-permute-done | bytes 98336 | tf_op jit(solution)/shard_map/ppermute | solution.py:17
  85.7 0.7 maximum_bitcast_fusion
  86.4 0.2 pad.9
  86.5 0.1 copy.88
  86.6 1.2 %fusion.32 = f32[2,8,17,384]{3,1,2,0:T(8,128)S(1)} fusion(bf16[3,3,3,384,384]{4,3,2,1,0:T(8,128)(2,1)S(1)} %bitcast.357, bf16[4,1,7,2,384]{4,2,3,0,1:T(8,128)(2,1)S(1)} %slice.172, bf16[4,1,8,17,384]{4,2,3,0,1:T(8,128)(2,1)S(1)} %copy.88, pred[8,17]{0,1:T(8,128)(4,1)S(1)} %copy-done.4), kind=kOutput, calls=%fused_computation.30 | convolution fusion | flops 723449856 | bytes 3542016 | tf_op jit(solution)/shard_map/conv_general_dilated | solution.py:35
  87.8 1.2 %fusion.26 = bf16[2,8,17,384]{3,1,2,0:T(8,128)(2,1)S(1)} fusion(f32[2,8,17,384]{3,1,2,0:T(8,128)S(1)} %fusion.32, f32[2,8,17,384]{3,1,2,0:T(8,128)S(1)} %fusion.29, bf16[3,3,3,384,384]{4,3,2,1,0:T(8,128)(2,1)S(1)} %bitcast.357, bf16[4,1,7,2,384]{4,2,3,0,1:T(8,128)(2,1)S(1)} %slice.167, bf16[4,1,8,17,384]{4,2,3,0,1:T(8,128)(2,1)S(1)} %copy.79, ...), kind=kOutput, calls=%fused_computation.28 | convolution fusion | flops 723763200 | bytes 4168704 | tf_op jit(solution)/shard_map/conv_general_dilated | solution.py:35
  89.2 2.3 %collective-permute-start.4 = (bf16[1,1,128,384]{3,2,1,0:T(8,128)(2,1)S(1)}, bf16[1,1,128,384]{3,2,1,0:T(8,128)(2,1)S(1)}, u32[]{:S(2)}, u32[]{:S(2)}) collective-permute-start(bf16[1,1,128,384]{3,2,1,0:T(8,128)(2,1)S(1)} %slice.174), channel_id=1, source_target_pairs={{0,1},{1,2},{2,3},{3,4},{4,5},{5,6},{6,7},{7,8},{8,9},{9,10},{10,1... | collective-permute-start | bytes 294920 | tf_op jit(solution)/shard_map/ppermute | solution.py:16
  91.6 2.0 %collective-permute-start.5 = (bf16[1,1,128,384]{3,2,1,0:T(8,128)(2,1)S(1)}, bf16[1,1,128,384]{3,2,1,0:T(8,128)(2,1)S(1)}, u32[]{:S(2)}, u32[]{:S(2)}) collective-permute-start(bf16[1,1,128,384]{3,2,1,0:T(8,128)(2,1)S(1)} %slice.177), channel_id=1, source_target_pairs={{1,0},{2,1},{3,2},{4,3},{5,4},{6,5},{7,6},{8,7},{9,8},{10,9},{11,1... | collective-permute-start | bytes 294920 | tf_op jit(solution)/shard_map/ppermute | solution.py:17
  93.6 0.2 copy.90
  93.8 0.1 slice.175
  94.0 4.4 %collective-permute-done.5 = bf16[1,1,128,384]{3,2,1,0:T(8,128)(2,1)S(1)} collective-permute-done((bf16[1,1,128,384]{3,2,1,0:T(8,128)(2,1)S(1)}, bf16[1,1,128,384]{3,2,1,0:T(8,128)(2,1)S(1)}, u32[]{:S(2)}, u32[]{:S(2)}) %collective-permute-start.5) | collective-permute-done | bytes 98336 | tf_op jit(solution)/shard_map/ppermute | solution.py:17
  98.4 1.5 %convolution_bitcast_fusion = f32[1,4,130,3,3,192]{5,2,4,3,1,0:T(8,128)S(1)} fusion(bf16[3,3,384,192]{2,3,1,0:T(8,128)(2,1)S(1)} %copy-done, bf16[1,1,128,384]{3,2,1,0:T(8,128)(2,1)S(1)} %collective-permute-done.5, bf16[1,2,128,384]{3,2,1,0:T(8,128)(2,1)S(1)} %bitcast.354, bf16[1,1,128,384]{3,2,1,0:T(8,128)(2,1)S(1)} %collective-permute-done.4), kind=kOutput, calls=%fused_computation.15 | convolution fusion | flops 692490240 | bytes 5314560 | tf_op jit(solution)/shard_map/frwc,ijco->frwijo/dot_general | solution.py:52
  99.9 0.4 fusion.119
  100.3 0.2 fusion.121
  100.5 0.2 fusion.122
  100.7 0.1 maximum_bitcast_fusion.1
  100.8 0.1 pad_maximum_fusion
  100.9 0.5 copy.118
  101.5 1.3 %convert_element_type.88 = bf16[1,4,49152]{2,1,0:T(4,128)(2,1)} reshape(bf16[1,2,2,128,2,192]{5,4,3,2,1,0:T(2,128)(2,1)S(1)} %copy.118) | data formatting | bytes 786432 | tf_op jit(solution)/shard_map/convert_element_type | solution.py:69
  (34 shorter events, 0.4 us)
Async XLA Ops:
  6.5 91.9 %copy-start = (bf16[3,3,384,192]{2,3,1,0:T(8,128)(2,1)S(1)}, bf16[3,3,384,192]{2,3,1,0:T(8,128)(2,1)}, u32[]{:S(2)}) copy-start(bf16[3,3,384,192]{2,3,1,0:T(8,128)(2,1)} %param.19) | copy-start | bytes 3981316
  6.5 49.3 %all-gather.2.cloned.1.call-start = ((), (), s32[]{:S(2)}) async-start(), calls=%async_computation | async-start | bytes 3342336 | tf_op jit(solution)/shard_map/all_gather | solution.py:83
  9.4 46.4 %copy-start.3 = (bf16[384,384]{1,0:T(8,128)(2,1)S(1)}, bf16[384,384]{1,0:T(8,128)(2,1)}, u32[]{:S(2)}) copy-start(bf16[384,384]{1,0:T(8,128)(2,1)} %param.13) | copy-start | bytes 884740
  10.6 8.9 %collective-permute-start = (bf16[2,1,128,384]{3,2,1,0:T(8,128)(2,1)S(1)}, bf16[2,1,128,384]{3,2,1,0:T(8,128)(2,1)S(1)}, u32[]{:S(2)}, u32[]{:S(2)}) collective-permute-start(bf16[2,1,128,384]{3,2,1,0:T(8,128)(2,1)S(1)} %get-tuple-element.10), channel_id=1, source_target_pairs={{0,1},{1,2},{2,3},{3,4},{4,5},{5,6},{6,7},{7,8},{8,9},{9,10},{10,1... | collective-permute-start | bytes 589832 | tf_op jit(solution)/shard_map/ppermute | solution.py:16
  14.3 9.8 %collective-permute-start.1 = (bf16[2,1,128,384]{3,2,1,0:T(8,128)(2,1)S(1)}, bf16[2,1,128,384]{3,2,1,0:T(8,128)(2,1)S(1)}, u32[]{:S(2)}, u32[]{:S(2)}) collective-permute-start(bf16[2,1,128,384]{3,2,1,0:T(8,128)(2,1)S(1)} %get-tuple-element.9), channel_id=1, source_target_pairs={{1,0},{2,1},{3,2},{4,3},{5,4},{6,5},{7,6},{8,7},{9,8},{10,9},{11,1... | collective-permute-start | bytes 589832 | tf_op jit(solution)/shard_map/ppermute | solution.py:17
  65.8 6.4 %copy-start.1 = (bf16[384,384]{1,0:T(8,128)(2,1)S(1)}, bf16[384,384]{1,0:T(8,128)(2,1)}, u32[]{:S(2)}) copy-start(bf16[384,384]{1,0:T(8,128)(2,1)} %param.15) | copy-start | bytes 884740
  65.8 6.8 %copy-start.2 = (f32[384]{0:T(512)S(1)}, f32[384]{0:T(512)}, u32[]{:S(2)}) copy-start(f32[384]{0:T(512)} %param.17) | copy-start | bytes 4612
  65.8 14.1 %copy-start.4 = (pred[8,17]{0,1:T(8,128)(4,1)S(1)}, pred[8,17]{0,1:T(8,128)(4,1)}, u32[]{:S(2)}) copy-start(pred[8,17]{0,1:T(8,128)(4,1)} %constant.34) | copy-start | bytes 412
  72.6 14.1 %slice-start = ((s8[7962624]{0:T(1024)(128)(4,1)}), s8[4194304]{0:T(1024)(128)(4,1)S(1)}, s32[]{:S(2)}) async-start(s8[7962624]{0:T(1024)(128)(4,1)} %bitcast.356), calls=%async_computation.1 | async-start | bytes 8388608
  73.3 10.2 %collective-permute-start.2 = (bf16[1,1,128,384]{3,1,2,0:T(2,128)(2,1)S(1)}, bf16[1,1,128,384]{3,1,2,0:T(2,128)(2,1)S(1)}, u32[]{:S(2)}, u32[]{:S(2)}) collective-permute-start(bf16[1,1,128,384]{3,1,2,0:T(2,128)(2,1)S(1)} %get-tuple-element.13), channel_id=1, source_target_pairs={{0,1},{1,2},{2,3},{3,4},{4,5},{5,6},{6,7},{7,8},{8,9},{9,10},{10,1... | collective-permute-start | bytes 294920 | tf_op jit(solution)/shard_map/ppermute | solution.py:16
  77.5 9.1 %slice-start.1 = ((s8[7962624]{0:T(1024)(128)(4,1)}), s8[3768320]{0:T(1024)(128)(4,1)S(1)}, s32[]{:S(2)}) async-start(s8[7962624]{0:T(1024)(128)(4,1)} %bitcast.356), calls=%async_computation.2 | async-start | bytes 7536640
  77.5 8.2 %collective-permute-start.3 = (bf16[1,1,128,384]{3,1,2,0:T(2,128)(2,1)S(1)}, bf16[1,1,128,384]{3,1,2,0:T(2,128)(2,1)S(1)}, u32[]{:S(2)}, u32[]{:S(2)}) collective-permute-start(bf16[1,1,128,384]{3,1,2,0:T(2,128)(2,1)S(1)} %get-tuple-element.14), channel_id=1, source_target_pairs={{1,0},{2,1},{3,2},{4,3},{5,4},{6,5},{7,6},{8,7},{9,8},{10,9},{11,1... | collective-permute-start | bytes 294920 | tf_op jit(solution)/shard_map/ppermute | solution.py:17
  89.2 4.8 %collective-permute-start.4 = (bf16[1,1,128,384]{3,2,1,0:T(8,128)(2,1)S(1)}, bf16[1,1,128,384]{3,2,1,0:T(8,128)(2,1)S(1)}, u32[]{:S(2)}, u32[]{:S(2)}) collective-permute-start(bf16[1,1,128,384]{3,2,1,0:T(8,128)(2,1)S(1)} %slice.174), channel_id=1, source_target_pairs={{0,1},{1,2},{2,3},{3,4},{4,5},{5,6},{6,7},{7,8},{8,9},{9,10},{10,1... | collective-permute-start | bytes 294920 | tf_op jit(solution)/shard_map/ppermute | solution.py:16
  91.6 6.8 %collective-permute-start.5 = (bf16[1,1,128,384]{3,2,1,0:T(8,128)(2,1)S(1)}, bf16[1,1,128,384]{3,2,1,0:T(8,128)(2,1)S(1)}, u32[]{:S(2)}, u32[]{:S(2)}) collective-permute-start(bf16[1,1,128,384]{3,2,1,0:T(8,128)(2,1)S(1)} %slice.177), channel_id=1, source_target_pairs={{1,0},{2,1},{3,2},{4,3},{5,4},{6,5},{7,6},{8,7},{9,8},{10,9},{11,1... | collective-permute-start | bytes 294920 | tf_op jit(solution)/shard_map/ppermute | solution.py:17
Sparse Core Ops, SparseCore 0:
  9.6 46.1 all-gather.1

commit v2 on v1

--- a/solution.py
+++ b/solution.py
@@ -4,6 +4,9 @@
 from jax.sharding import PartitionSpec as P
 
 EPS = 1e-06
+
+
+ROWS = ("chip", "core")
 
 
 def padded_2(array, sides, width):
@@ -75,14 +78,13 @@
     nframes, nrows, ncols, chans = frames.shape
     scale = chans ** (-0.5)
 
-    cache_haloed = padded_2(cache_one, (("rows", 1),), 1)
+    cache_haloed = padded_2(cache_one, ((ROWS, 1),), 1)
     cache_part = conv_rows(cache_haloed, conv_weight[:2])
 
     flat = frames.reshape(nframes, nrows * ncols, chans)
     normed = rms_gain(flat.astype(jnp.float32), norm_attn).astype(jnp.bfloat16)
-    normed_all = lax.all_gather(
-        normed.reshape(nframes, nrows, ncols, chans), "rows", axis=1, tiled=True
-    ).reshape(nframes, -1, chans)
+    by_chip = lax.all_gather(normed, "chip", axis=1, tiled=True)
+    normed_all = lax.all_gather(by_chip, "core", axis=1, tiled=True)
     queries = project(normed, w_query)
     keys = project(normed_all, w_key)
     values = project(normed_all, w_value)
@@ -103,25 +105,27 @@
         .astype(jnp.bfloat16)
         .reshape(nframes, nrows, ncols, chans)
     )
-    activ_haloed = padded_2(activ, (("rows", 1),), 1)
+    activ_haloed = padded_2(activ, ((ROWS, 1),), 1)
     conv_out = (cache_part + conv_rows(activ_haloed, conv_weight[2:])).astype(jnp.bfloat16)
-    extended = padded_2(conv_out, (("rows", 1),), 1)
+    extended = padded_2(conv_out, ((ROWS, 1),), 1)
     return upsample_conv(extended, w_up)
 
 
 def solution(mesh):
+    clips, rows = mesh.devices.shape
+    mesh = jax.sharding.Mesh(mesh.devices.reshape(clips, rows // 2, 2), ("clips",) + ROWS)
     placed = (
-        P("clips", "rows", None, None),
+        P("clips", ROWS, None, None),
         P(),
         P(),
         P(),
         P(),
         P(),
-        P("clips", "rows", None, None),
+        P("clips", ROWS, None, None),
         P(),
         P(),
         P(),
     )
     return jax.shard_map(
-        body, mesh=mesh, in_specs=placed, out_specs=P("clips", "rows", None), check_vma=False
+        body, mesh=mesh, in_specs=placed, out_specs=P("clips", ROWS, None), check_vma=False
     )

time: 110 us -> 121 us (1.10)
  waiting for transfers between devices: 41.2 us -> 53.8 us
    all_gather x1 -> x2, waiting for transfers between devices: 31 us -> 43.6 us  [the longest x1 43.6 us: body(): by_chip = lax.all_gather(normed, 'chip', axis=1, tiled=True)]
  transfers between devices with their start and end apart: 7 -> 8, of which waited for: 4 -> 4; matrix products, arithmetic and copies ran while one was open for 9% -> 7% of each run, Pallas kernels for 0% -> 0%
where the time goes in v2:
time: 121 us
  waiting for transfers between devices  53.8 us (44%)
  matrix products  21.9 us (18%)
  starting transfers between devices  16.9 us (14%)
  between operations  13.9 us (11%)
  other arithmetic  8.73 us (7%)
  local copies, waits for them, and re-layouts  5.49 us (5%)
    all_gather x1, waiting for transfers between devices, body(): by_chip = lax.all_gather(normed, 'chip', axis=1, tiled=True)  43.6 us
    ppermute x3, starting transfers between devices, padded_2(): before = lax.ppermute(last, axis, up)  10.6 us
    ppermute x3, waiting for transfers between devices, padded_2(): after = lax.ppermute(first, axis, down)  10.2 us
    dot_general x1, matrix products, body(): jnp.einsum('fqc,fkc->fqk', queries, keys, preferred_element_type=jnp.floa...  7.03 us
    dot_general x1, matrix products, body(): jnp.einsum('fqk,fkc->fqc', expo.astype(jnp.bfloat16), values, preferred_e...  6.39 us
    ppermute x3, starting transfers between devices, padded_2(): after = lax.ppermute(first, axis, down)  6.32 us
    conv_general_dilated x3, matrix products, conv_rows(): lax.conv_general_dilated(haloed[tstep:tstep + 1], weight[tstep], window_s...  5.32 us
    reduce_sum x1, other arithmetic, body(): denom = jnp.sum(expo, axis=-1, keepdims=True)  2.94 us
  transfers between devices with their start and end apart: 8, of which 4 were waited for; matrix products, arithmetic and copies ran while one was open for 7% of the time, Pallas kernels for 0%

profile of v2, /device:TPU:5, one launch (start us, length us, event | category | flops | bytes accessed | tf_op | source)
XLA Modules:
  0.0 120.7 jit_solution(1440930561166299125)
XLA Ops:
  6.5 1.2 multiply_reduce_fusion.1
  7.7 1.7 %fusion.84 = bf16[1,256,384]{2,1,0:T(8,128)(2,1)} fusion(bf16[1,2,128,384]{3,2,1,0:T(8,128)(2,1)} %param.10, f32[384]{0:T(512)} %param.11, f32[256]{0:T(256)S(1)} %rsqrt_bitcast_fusion), kind=kLoop, calls=%fused_computation.72 | loop fusion | flops 393216 | bytes 395776 | tf_op jit(solution)/shard_map/convert_element_type | solution.py:85
  9.5 0.0 all-gather.5.cloned.1.call-start
  9.5 43.6 %all-gather.3.cloned.1.call-done = bf16[1,2048,384]{2,1,0:T(8,128)(2,1)} async-done(((bf16[1,256,384]{2,1,0:T(8,128)(2,1)}), bf16[1,2048,384]{2,1,0:T(8,128)(2,1)}) %all-gather.3.cloned.1.call-update) | async-done | bytes 1572880 | tf_op jit(solution)/shard_map/all_gather | solution.py:86
  53.1 1.1 fusion.144
  54.2 5.6 %collective-permute-start = (bf16[2,1,128,384]{3,2,1,0:T(8,128)(2,1)S(1)}, bf16[2,1,128,384]{3,2,1,0:T(8,128)(2,1)S(1)}, u32[]{:S(2)}, u32[]{:S(2)}) collective-permute-start(bf16[2,1,128,384]{3,2,1,0:T(8,128)(2,1)S(1)} %get-tuple-element.10), channel_id=1, source_target_pairs={{0,1},{1,2},{2,3},{3,4},{4,5},{5,6},{6,7},{7,8},{8,9},{9,10},{10,1... | collective-permute-start | bytes 589832 | tf_op jit(solution)/shard_map/ppermute | solution.py:19
  59.8 1.9 %collective-permute-start.1 = (bf16[2,1,128,384]{3,2,1,0:T(8,128)(2,1)S(1)}, bf16[2,1,128,384]{3,2,1,0:T(8,128)(2,1)S(1)}, u32[]{:S(2)}, u32[]{:S(2)}) collective-permute-start(bf16[2,1,128,384]{3,2,1,0:T(8,128)(2,1)S(1)} %get-tuple-element.9), channel_id=1, source_target_pairs={{1,0},{2,1},{3,2},{4,3},{5,4},{6,5},{7,6},{8,7},{9,8},{10,9},{11,1... | collective-permute-start | bytes 589832 | tf_op jit(solution)/shard_map/ppermute | solution.py:20
  61.7 1.1 fusion.86
  62.8 1.3 %convolution_convert_fusion.2 = bf16[256,384]{1,0:T(8,128)(2,1)S(1)} fusion(bf16[256,384]{1,0:T(8,128)(2,1)S(1)} %fusion.86, bf16[384,384]{1,0:T(8,128)(2,1)} %param.12), kind=kOutput, calls=%fused_computation.24 | convolution fusion | flops 75595776 | bytes 688128 | tf_op jit(solution)/shard_map/fqc,cd->fqd/dot_general | solution.py:30
  64.1 0.1 constant_dynamic-update-slice_fusion.1
  64.2 3.5 %collective-permute-done.1 = bf16[2,1,128,384]{3,2,1,0:T(8,128)(2,1)S(1)} collective-permute-done((bf16[2,1,128,384]{3,2,1,0:T(8,128)(2,1)S(1)}, bf16[2,1,128,384]{3,2,1,0:T(8,128)(2,1)S(1)}, u32[]{:S(2)}, u32[]{:S(2)}) %collective-permute-start.1) | collective-permute-done | bytes 196640 | tf_op jit(solution)/shard_map/ppermute | solution.py:20
  67.7 0.1 slice_bitcast_fusion.1
  67.8 0.3 copy.104
  68.1 0.2 pad.7.clone
  68.3 0.1 copy.41
  68.4 0.0 all-gather.5.cloned.1.call-done
  68.4 7.0 %fusion.147 = (f32[256]{0:T(256)S(1)}, f32[256,4096]{1,0:T(8,128)}) fusion(bf16[256,384]{1,0:T(8,128)(2,1)S(1)} %convolution_convert_fusion.2, bf16[384,384]{1,0:T(8,128)(2,1)S(1)} %copy-done.5, bf16[1,4096,384]{2,1,0:T(8,128)(2,1)} %all-gather.5.cloned.1.call-done), kind=kOutput, calls=%fused_computation.172 | convolution fusion | flops 2016935680 | bytes 7832576 | tf_op jit(solution)/shard_map/fqc,fkc->fqk/dot_general | solution.py:91
  75.4 2.9 %fusion = f32[256]{0:T(256)S(1)} fusion(f32[256,4096]{1,0:T(8,128)} %get-tuple-element.16, f32[256]{0:T(256)S(1)} %get-tuple-element.15), kind=kLoop, calls=%fused_computation.4 | loop fusion | flops 2096896 | bytes 4196352 | tf_op jit(solution)/shard_map/reduce_sum | solution.py:94
  78.4 6.4 %fusion.42 = bf16[256,384]{1,0:T(8,128)(2,1)S(1)} fusion(f32[256,4096]{1,0:T(8,128)} %get-tuple-element.16, f32[256]{0:T(256)S(1)} %get-tuple-element.15, bf16[384,384]{1,0:T(8,128)(2,1)S(1)} %copy-done.6, bf16[1,4096,384]{2,1,0:T(8,128)(2,1)} %all-gather.5.cloned.1.call-done, f32[256]{0:T(256)S(1)} %fusion), kind=kOutput, calls=%fused_computation.34 | convolution fusion | flops 2017132544 | bytes 7833600 | tf_op jit(solution)/shard_map/fqk,fkc->fqc/dot_general | solution.py:95
  84.9 0.4 multiply_reduce_fusion
  85.3 0.2 multiply_convert_fusion
  85.5 0.2 copy.42
  85.7 0.3 fusion.146
  86.0 2.7 %collective-permute-start.2 = (bf16[1,1,128,384]{3,1,2,0:T(2,128)(2,1)S(1)}, bf16[1,1,128,384]{3,1,2,0:T(2,128)(2,1)S(1)}, u32[]{:S(2)}, u32[]{:S(2)}) collective-permute-start(bf16[1,1,128,384]{3,1,2,0:T(2,128)(2,1)S(1)} %get-tuple-element.13), channel_id=1, source_target_pairs={{0,1},{1,2},{2,3},{3,4},{4,5},{5,6},{6,7},{7,8},{8,9},{9,10},{10,1... | collective-permute-start | bytes 294920 | tf_op jit(solution)/shard_map/ppermute | solution.py:19
  88.7 2.4 %collective-permute-start.3 = (bf16[1,1,128,384]{3,1,2,0:T(2,128)(2,1)S(1)}, bf16[1,1,128,384]{3,1,2,0:T(2,128)(2,1)S(1)}, u32[]{:S(2)}, u32[]{:S(2)}) collective-permute-start(bf16[1,1,128,384]{3,1,2,0:T(2,128)(2,1)S(1)} %get-tuple-element.14), channel_id=1, source_target_pairs={{1,0},{2,1},{3,2},{4,3},{5,4},{6,5},{7,6},{8,7},{9,8},{10,9},{11,1... | collective-permute-start | bytes 294920 | tf_op jit(solution)/shard_map/ppermute | solution.py:20
  91.1 2.9 %fusion.33 = f32[2,8,17,384]{3,1,2,0:T(8,128)S(1)} fusion(bf16[3,3,3,384,384]{4,3,2,1,0:T(8,128)(2,1)} %param.18, bf16[4,1,7,2,384]{4,2,3,0,1:T(8,128)(2,1)S(1)} %slice.169, bf16[4,1,8,17,384]{4,2,3,0,1:T(8,128)(2,1)S(1)} %copy.41, pred[8,17]{0,1:T(8,128)(4,1)S(1)} %copy-done.7), kind=kOutput, calls=%fused_computation.31 | convolution fusion | flops 723449856 | bytes 3532936 | tf_op jit(solution)/shard_map/conv_general_dilated | solution.py:38
  94.0 0.3 copy.103
  94.3 0.2 pad.5.clone
  94.5 0.1 copy.38
  94.6 2.3 %collective-permute-done.3 = bf16[1,1,128,384]{3,1,2,0:T(2,128)(2,1)S(1)} collective-permute-done((bf16[1,1,128,384]{3,1,2,0:T(2,128)(2,1)S(1)}, bf16[1,1,128,384]{3,1,2,0:T(2,128)(2,1)S(1)}, u32[]{:S(2)}, u32[]{:S(2)}) %collective-permute-start.3) | collective-permute-done | bytes 98336 | tf_op jit(solution)/shard_map/ppermute | solution.py:20
  96.8 0.7 maximum_bitcast_fusion
  97.5 0.2 pad.9
  97.7 0.1 copy.46
  97.8 1.2 fusion.36
  99.0 1.2 fusion.30
  100.3 2.3 %collective-permute-start.4 = (bf16[1,1,128,384]{3,2,1,0:T(8,128)(2,1)S(1)}, bf16[1,1,128,384]{3,2,1,0:T(8,128)(2,1)S(1)}, u32[]{:S(2)}, u32[]{:S(2)}) collective-permute-start(bf16[1,1,128,384]{3,2,1,0:T(8,128)(2,1)S(1)} %slice.174), channel_id=1, source_target_pairs={{0,1},{1,2},{2,3},{3,4},{4,5},{5,6},{6,7},{7,8},{8,9},{9,10},{10,1... | collective-permute-start | bytes 294920 | tf_op jit(solution)/shard_map/ppermute | solution.py:19
  102.7 2.0 %collective-permute-start.5 = (bf16[1,1,128,384]{3,2,1,0:T(8,128)(2,1)S(1)}, bf16[1,1,128,384]{3,2,1,0:T(8,128)(2,1)S(1)}, u32[]{:S(2)}, u32[]{:S(2)}) collective-permute-start(bf16[1,1,128,384]{3,2,1,0:T(8,128)(2,1)S(1)} %slice.177), channel_id=1, source_target_pairs={{1,0},{2,1},{3,2},{4,3},{5,4},{6,5},{7,6},{8,7},{9,8},{10,9},{11,1... | collective-permute-start | bytes 294920 | tf_op jit(solution)/shard_map/ppermute | solution.py:20
  104.8 0.2 copy.48
  105.0 0.1 slice.175
  105.1 4.4 %collective-permute-done.5 = bf16[1,1,128,384]{3,2,1,0:T(8,128)(2,1)S(1)} collective-permute-done((bf16[1,1,128,384]{3,2,1,0:T(8,128)(2,1)S(1)}, bf16[1,1,128,384]{3,2,1,0:T(8,128)(2,1)S(1)}, u32[]{:S(2)}, u32[]{:S(2)}) %collective-permute-start.5) | collective-permute-done | bytes 98336 | tf_op jit(solution)/shard_map/ppermute | solution.py:20
  109.6 1.5 %convolution_bitcast_fusion = f32[1,4,130,3,3,192]{5,2,4,3,1,0:T(8,128)S(1)} fusion(bf16[3,3,384,192]{2,3,1,0:T(8,128)(2,1)S(1)} %copy-done, bf16[1,1,128,384]{3,2,1,0:T(8,128)(2,1)S(1)} %collective-permute-done.5, bf16[1,2,128,384]{3,2,1,0:T(8,128)(2,1)S(1)} %bitcast.364, bf16[1,1,128,384]{3,2,1,0:T(8,128)(2,1)S(1)} %collective-permute-done.4), kind=kOutput, calls=%fused_computation.17 | convolution fusion | flops 692490240 | bytes 5314560 | tf_op jit(solution)/shard_map/frwc,ijco->frwijo/dot_general | solution.py:55
  111.1 0.4 fusion.127
  111.4 0.2 fusion.129
  111.6 0.2 fusion.130
  111.9 0.1 maximum_bitcast_fusion.1
  112.0 0.1 pad_maximum_fusion
  112.1 0.5 copy.76
  112.6 1.3 %convert_element_type.105 = bf16[1,4,49152]{2,1,0:T(4,128)(2,1)} reshape(bf16[1,2,2,128,2,192]{5,4,3,2,1,0:T(2,128)(2,1)S(1)} %copy.76) | data formatting | bytes 786432 | tf_op jit(solution)/shard_map/convert_element_type | solution.py:72
  (42 shorter events, 0.4 us)
Async XLA Ops:
  6.5 103.0 %copy-start = (bf16[3,3,384,192]{2,3,1,0:T(8,128)(2,1)S(1)}, bf16[3,3,384,192]{2,3,1,0:T(8,128)(2,1)}, u32[]{:S(2)}) copy-start(bf16[3,3,384,192]{2,3,1,0:T(8,128)(2,1)} %param.19) | copy-start | bytes 3981316
  6.5 57.6 %copy-start.2 = (bf16[2,2,128,384]{3,2,1,0:T(8,128)(2,1)S(1)}, bf16[2,2,128,384]{3,2,1,0:T(8,128)(2,1)}, u32[]{:S(2)}) copy-start(bf16[2,2,128,384]{3,2,1,0:T(8,128)(2,1)} %param.16) | copy-start | bytes 1179652
  6.5 46.5 %all-gather.3.cloned.1.call-start = ((), (), s32[]{:S(2)}) async-start(), calls=%async_computation | async-start | bytes 1769472 | tf_op jit(solution)/shard_map/all_gather | solution.py:86
  9.5 58.9 %all-gather.5.cloned.1.call-start = ((), (), s32[]{:S(2)}) async-start(), calls=%async_computation.1 | async-start | bytes 4718592 | tf_op jit(solution)/shard_map/all_gather | solution.py:87
  53.1 15.3 %copy-start.5 = (bf16[384,384]{1,0:T(8,128)(2,1)S(1)}, bf16[384,384]{1,0:T(8,128)(2,1)}, u32[]{:S(2)}) copy-start(bf16[384,384]{1,0:T(8,128)(2,1)} %param.13) | copy-start | bytes 884740
  54.2 9.9 %collective-permute-start = (bf16[2,1,128,384]{3,2,1,0:T(8,128)(2,1)S(1)}, bf16[2,1,128,384]{3,2,1,0:T(8,128)(2,1)S(1)}, u32[]{:S(2)}, u32[]{:S(2)}) collective-permute-start(bf16[2,1,128,384]{3,2,1,0:T(8,128)(2,1)S(1)} %get-tuple-element.10), channel_id=1, source_target_pairs={{0,1},{1,2},{2,3},{3,4},{4,5},{5,6},{6,7},{7,8},{8,9},{9,10},{10,1... | collective-permute-start | bytes 589832 | tf_op jit(solution)/shard_map/ppermute | solution.py:19
  59.8 7.9 %collective-permute-start.1 = (bf16[2,1,128,384]{3,2,1,0:T(8,128)(2,1)S(1)}, bf16[2,1,128,384]{3,2,1,0:T(8,128)(2,1)S(1)}, u32[]{:S(2)}, u32[]{:S(2)}) collective-permute-start(bf16[2,1,128,384]{3,2,1,0:T(8,128)(2,1)S(1)} %get-tuple-element.9), channel_id=1, source_target_pairs={{1,0},{2,1},{3,2},{4,3},{5,4},{6,5},{7,6},{8,7},{9,8},{10,9},{11,1... | collective-permute-start | bytes 589832 | tf_op jit(solution)/shard_map/ppermute | solution.py:20
  75.4 2.9 %copy-start.6 = (bf16[384,384]{1,0:T(8,128)(2,1)S(1)}, bf16[384,384]{1,0:T(8,128)(2,1)}, u32[]{:S(2)}) copy-start(bf16[384,384]{1,0:T(8,128)(2,1)} %param.14) | copy-start | bytes 884740
  78.4 6.5 %copy-start.1 = (bf16[1,2,128,384]{3,2,1,0:T(8,128)(2,1)S(1)}, bf16[1,2,128,384]{3,2,1,0:T(8,128)(2,1)}, u32[]{:S(2)}) copy-start(bf16[1,2,128,384]{3,2,1,0:T(8,128)(2,1)} %param.10) | copy-start | bytes 589828
  78.4 6.4 %copy-start.3 = (bf16[384,384]{1,0:T(8,128)(2,1)S(1)}, bf16[384,384]{1,0:T(8,128)(2,1)}, u32[]{:S(2)}) copy-start(bf16[384,384]{1,0:T(8,128)(2,1)} %param.15) | copy-start | bytes 884740
  78.4 6.8 %copy-start.4 = (f32[384]{0:T(512)S(1)}, f32[384]{0:T(512)}, u32[]{:S(2)}) copy-start(f32[384]{0:T(512)} %param.17) | copy-start | bytes 4612
  78.4 12.6 %copy-start.7 = (pred[8,17]{0,1:T(8,128)(4,1)S(1)}, pred[8,17]{0,1:T(8,128)(4,1)}, u32[]{:S(2)}) copy-start(pred[8,17]{0,1:T(8,128)(4,1)} %constant.34) | copy-start | bytes 412
  85.3 12.5 %slice-start = ((s8[7962624]{0:T(1024)(128)(4,1)}), s8[4194304]{0:T(1024)(128)(4,1)S(1)}, s32[]{:S(2)}) async-start(s8[7962624]{0:T(1024)(128)(4,1)} %bitcast.366), calls=%async_computation.2 | async-start | bytes 8388608
  86.0 8.6 %collective-permute-start.2 = (bf16[1,1,128,384]{3,1,2,0:T(2,128)(2,1)S(1)}, bf16[1,1,128,384]{3,1,2,0:T(2,128)(2,1)S(1)}, u32[]{:S(2)}, u32[]{:S(2)}) collective-permute-start(bf16[1,1,128,384]{3,1,2,0:T(2,128)(2,1)S(1)} %get-tuple-element.13), channel_id=1, source_target_pairs={{0,1},{1,2},{2,3},{3,4},{4,5},{5,6},{6,7},{7,8},{8,9},{9,10},{10,1... | collective-permute-start | bytes 294920 | tf_op jit(solution)/shard_map/ppermute | solution.py:19
  88.7 9.1 %slice-start.1 = ((s8[7962624]{0:T(1024)(128)(4,1)}), s8[3768320]{0:T(1024)(128)(4,1)S(1)}, s32[]{:S(2)}) async-start(s8[7962624]{0:T(1024)(128)(4,1)} %bitcast.366), calls=%async_computation.3 | async-start | bytes 7536640
  88.7 8.2 %collective-permute-start.3 = (bf16[1,1,128,384]{3,1,2,0:T(2,128)(2,1)S(1)}, bf16[1,1,128,384]{3,1,2,0:T(2,128)(2,1)S(1)}, u32[]{:S(2)}, u32[]{:S(2)}) collective-permute-start(bf16[1,1,128,384]{3,1,2,0:T(2,128)(2,1)S(1)} %get-tuple-element.14), channel_id=1, source_target_pairs={{1,0},{2,1},{3,2},{4,3},{5,4},{6,5},{7,6},{8,7},{9,8},{10,9},{11,1... | collective-permute-start | bytes 294920 | tf_op jit(solution)/shard_map/ppermute | solution.py:20
  100.3 4.8 %collective-permute-start.4 = (bf16[1,1,128,384]{3,2,1,0:T(8,128)(2,1)S(1)}, bf16[1,1,128,384]{3,2,1,0:T(8,128)(2,1)S(1)}, u32[]{:S(2)}, u32[]{:S(2)}) collective-permute-start(bf16[1,1,128,384]{3,2,1,0:T(8,128)(2,1)S(1)} %slice.174), channel_id=1, source_target_pairs={{0,1},{1,2},{2,3},{3,4},{4,5},{5,6},{6,7},{7,8},{8,9},{9,10},{10,1... | collective-permute-start | bytes 294920 | tf_op jit(solution)/shard_map/ppermute | solution.py:19
  102.7 6.8 %collective-permute-start.5 = (bf16[1,1,128,384]{3,2,1,0:T(8,128)(2,1)S(1)}, bf16[1,1,128,384]{3,2,1,0:T(8,128)(2,1)S(1)}, u32[]{:S(2)}, u32[]{:S(2)}) collective-permute-start(bf16[1,1,128,384]{3,2,1,0:T(8,128)(2,1)S(1)} %slice.177), channel_id=1, source_target_pairs={{1,0},{2,1},{3,2},{4,3},{5,4},{6,5},{7,6},{8,7},{9,8},{10,9},{11,1... | collective-permute-start | bytes 294920 | tf_op jit(solution)/shard_map/ppermute | solution.py:20
Sparse Core Ops, SparseCore 0:
  9.6 43.4 all-gather.2
  54.6 13.1 all-gather.4

commit v3 on v2

--- a/solution.py
+++ b/solution.py
@@ -83,17 +83,28 @@
 
     flat = frames.reshape(nframes, nrows * ncols, chans)
     normed = rms_gain(flat.astype(jnp.float32), norm_attn).astype(jnp.bfloat16)
-    by_chip = lax.all_gather(normed, "chip", axis=1, tiled=True)
-    normed_all = lax.all_gather(by_chip, "core", axis=1, tiled=True)
     queries = project(normed, w_query)
-    keys = project(normed_all, w_key)
-    values = project(normed_all, w_value)
-    scores = jnp.einsum("fqc,fkc->fqk", queries, keys, preferred_element_type=jnp.float32) * scale
-    top = jnp.max(scores, axis=-1, keepdims=True)
-    expo = jnp.exp(scores - top)
-    denom = jnp.sum(expo, axis=-1, keepdims=True)
-    numer = jnp.einsum(
-        "fqk,fkc->fqc", expo.astype(jnp.bfloat16), values, preferred_element_type=jnp.float32
+    size = lax.axis_size(ROWS)
+    pieces, held, bit = [normed], normed, size // 2
+    while bit >= 1:
+        other = lax.ppermute(held, ROWS, [(i, i ^ bit) for i in range(size)])
+        pieces.append(other)
+        if bit > 1:
+            held = jnp.concatenate([held, other], axis=1)
+        bit //= 2
+    scores, values = [], []
+    for piece in pieces:
+        keys = project(piece, w_key)
+        values.append(project(piece, w_value))
+        scores.append(
+            jnp.einsum("fqc,fkc->fqk", queries, keys, preferred_element_type=jnp.float32) * scale
+        )
+    top = jnp.max(jnp.stack([jnp.max(s, axis=-1) for s in scores], axis=-1), axis=-1)[..., None]
+    expos = [jnp.exp(s - top) for s in scores]
+    denom = sum(jnp.sum(e, axis=-1, keepdims=True) for e in expos)
+    numer = sum(
+        jnp.einsum("fqk,fkc->fqc", e.astype(jnp.bfloat16), v, preferred_element_type=jnp.float32)
+        for e, v in zip(expos, values)
     )
     attended = (numer / denom).astype(jnp.bfloat16)
     mixed = (

time: 121 us -> 107 us (0.88)
  the two profiles are of different devices: /device:TPU:5 before, /device:TPU:24 now
where the time goes in v3:
time: 107 us; the launch traced here: 106 us
  waiting for transfers between devices  40.4 us (38%)
  matrix products  27.1 us (25%)
  starting transfers between devices  20.5 us (19%)
  local copies, waits for them, and re-layouts  9.19 us (9%)
  other arithmetic  8.48 us (8%)
    ppermute x4, waiting for transfers between devices, body(): other = lax.ppermute(held, ROWS, [(i, i ^ bit) for i in range(size)])  33.7 us
    ppermute x3, starting transfers between devices, padded_2(): after = lax.ppermute(first, axis, down)  12.2 us
    dot_general x5, matrix products, body(): jnp.einsum('fqc,fkc->fqk', queries, keys, preferred_element_type=jnp.floa...  10 us
    dot_general x5, matrix products, body(): jnp.einsum('fqk,fkc->fqc', e.astype(jnp.bfloat16), v, preferred_element_t...  9.64 us
    ppermute x3, waiting for transfers between devices, padded_2(): before = lax.ppermute(last, axis, up)  6.71 us
    ppermute x3, starting transfers between devices, padded_2(): before = lax.ppermute(last, axis, up)  6.25 us
    conv_general_dilated x3, matrix products, conv_rows(): lax.conv_general_dilated(haloed[tstep:tstep + 1], weight[tstep], window_s...  5.35 us
    reduce_sum x4, other arithmetic, body(): denom = sum((jnp.sum(e, axis=-1, keepdims=True) for e in expos))  2.77 us
  transfers between devices with their start and end apart: 10, of which 5 were waited for; matrix products, arithmetic and copies ran while one was open for 15% of the time, Pallas kernels for 0%

profile of v3, /device:TPU:24, one launch (start us, length us, event | category | flops | bytes accessed | tf_op | source)
XLA Modules:
  0.0 106.4 jit_solution(2374936530241075642)
XLA Ops:
  0.0 1.2 %multiply_reduce_fusion.1 = f32[2,128]{1,0:T(2,128)S(1)} fusion(bf16[1,2,128,384]{3,2,1,0:T(8,128)(2,1)} %param.10), kind=kLoop, calls=%fused_computation.111 | loop fusion | flops 294656 | bytes 197632 | tf_op jit(solution)/shard_map/reduce_sum | solution.py:26
  1.2 1.0 fusion.100
  2.3 0.4 collective-permute-start.2
  2.7 11.3 %collective-permute-done.2 = bf16[1,256,384]{2,1,0:T(8,128)(2,1)S(1)} collective-permute-done((bf16[1,256,384]{2,1,0:T(8,128)(2,1)S(1)}, bf16[1,256,384]{2,1,0:T(8,128)(2,1)S(1)}, u32[]{:S(2)}, u32[]{:S(2)}) %collective-permute-start.2) | collective-permute-done | bytes 196640 | tf_op jit(solution)/shard_map/ppermute | solution.py:90
  14.1 11.0 %collective-permute-done.3 = bf16[1,512,384]{2,1,0:T(8,128)(2,1)S(1)} collective-permute-done((bf16[1,512,384]{2,1,0:T(8,128)(2,1)S(1)}, bf16[1,512,384]{2,1,0:T(8,128)(2,1)S(1)}, u32[]{:S(2)}, u32[]{:S(2)}) %collective-permute-start.3) | collective-permute-done | bytes 393248 | tf_op jit(solution)/shard_map/ppermute | solution.py:90
  25.2 1.6 %collective-permute-start.4 = (bf16[1,1024,384]{2,1,0:T(8,128)(2,1)S(1)}, bf16[1,1024,384]{2,1,0:T(8,128)(2,1)S(1)}, u32[]{:S(2)}, u32[]{:S(2)}) collective-permute-start(bf16[1,1024,384]{2,1,0:T(8,128)(2,1)S(1)} %pad_maximum_fusion.1), channel_id=1, source_target_pairs={{0,2},{1,3},{2,0},{3,1},{4,6},{5,7},{6,4},{7,5},{8,10},{9,11},{10,... | collective-permute-start | bytes 2359304 | tf_op jit(solution)/shard_map/ppermute | solution.py:90
  26.8 0.8 fusion.174
  27.6 1.9 %collective-permute-start = (bf16[2,1,128,384]{3,2,1,0:T(8,128)(2,1)}, bf16[2,1,128,384]{3,2,1,0:T(8,128)(2,1)}, u32[]{:S(2)}, u32[]{:S(2)}) collective-permute-start(bf16[2,1,128,384]{3,2,1,0:T(8,128)(2,1)} %get-tuple-element.12), channel_id=1, source_target_pairs={{0,1},{1,2},{2,3},{3,4},{4,5},{5,6},{6,7},{7,8},{8,9},{9,10},{10,1... | collective-permute-start | bytes 589832 | tf_op jit(solution)/shard_map/ppermute | solution.py:19
  29.5 4.7 %collective-permute-start.1 = (bf16[2,1,128,384]{3,2,1,0:T(8,128)(2,1)}, bf16[2,1,128,384]{3,2,1,0:T(8,128)(2,1)}, u32[]{:S(2)}, u32[]{:S(2)}) collective-permute-start(bf16[2,1,128,384]{3,2,1,0:T(8,128)(2,1)} %get-tuple-element.11), channel_id=1, source_target_pairs={{1,0},{2,1},{3,2},{4,3},{5,4},{6,5},{7,6},{8,7},{9,8},{10,9},{11,1... | collective-permute-start | bytes 589832 | tf_op jit(solution)/shard_map/ppermute | solution.py:20
  34.4 0.3 convolution_convert_fusion.10
  34.6 11.4 %collective-permute-done.4 = bf16[1,1024,384]{2,1,0:T(8,128)(2,1)S(1)} collective-permute-done((bf16[1,1024,384]{2,1,0:T(8,128)(2,1)S(1)}, bf16[1,1024,384]{2,1,0:T(8,128)(2,1)S(1)}, u32[]{:S(2)}, u32[]{:S(2)}) %collective-permute-start.4) | collective-permute-done | bytes 786464 | tf_op jit(solution)/shard_map/ppermute | solution.py:90
  46.0 1.4 %pad_maximum_fusion = bf16[1,2048,384]{2,1,0:T(8,128)(2,1)} fusion(bf16[1,1024,384]{2,1,0:T(8,128)(2,1)S(1)} %collective-permute-done.4, bf16[1,512,384]{2,1,0:T(8,128)(2,1)S(1)} %collective-permute-done.3, bf16[1,256,384]{2,1,0:T(8,128)(2,1)S(1)} %collective-permute-done.2, bf16[1,256,384]{2,1,0:T(8,128)(2,1)S(1)} %fusion.100), kind=kLoop, calls=%fused_computation.16 | loop fusion | flops 6291456 | bytes 3145728 | tf_op jit(solution)/shard_map/concatenate | solution.py:93
  47.4 0.5 fusion.186
  47.9 0.9 constant_dynamic-update-slice_fusion.2
  49.0 1.0 constant_dynamic-update-slice_fusion
  49.9 0.9 slice_bitcast_fusion.1
  50.8 0.3 copy.104
  51.3 0.8 copy-done.9
  52.1 0.6 slice.169
  52.7 0.5 fusion.187
  53.2 1.5 %fusion.183 = (f32[256]{0:T(256)S(1)}, f32[256,512]{1,0:T(8,128)}) fusion(bf16[256,384]{1,0:T(8,128)(2,1)S(1)} %convolution_convert_fusion.10, bf16[384,384]{1,0:T(8,128)(2,1)S(1)} %copy-done.6, bf16[1,512,384]{2,1,0:T(8,128)(2,1)S(1)} %collective-permute-done.3), kind=kOutput, calls=%fused_computation.220 | convolution fusion | flops 252116736 | bytes 1410048 | tf_op jit(solution)/shard_map/fqc,fkc->fqk/dot_general | solution.py:100
  54.7 3.1 %fusion.180 = (f32[256]{0:T(256)S(1)}, f32[256,1024]{1,0:T(8,128)}) fusion(bf16[256,384]{1,0:T(8,128)(2,1)S(1)} %convolution_convert_fusion.10, bf16[384,384]{1,0:T(8,128)(2,1)S(1)} %copy-done.6, bf16[1,1024,384]{2,1,0:T(8,128)(2,1)} %copy-done.8), kind=kOutput, calls=%fused_computation.219 | convolution fusion | flops 504233728 | bytes 2327552 | tf_op jit(solution)/shard_map/fqc,fkc->fqk/dot_general | solution.py:100
  57.8 4.4 %fusion.177 = (f32[256]{0:T(256)S(1)}, f32[256,2048]{1,0:T(8,128)}) fusion(bf16[256,384]{1,0:T(8,128)(2,1)S(1)} %convolution_convert_fusion.10, bf16[384,384]{1,0:T(8,128)(2,1)S(1)} %copy-done.6, bf16[1,2048,384]{2,1,0:T(8,128)(2,1)} %collective-permute-done.5), kind=kOutput, calls=%fused_computation.218 | convolution fusion | flops 1008467712 | bytes 4162560 | tf_op jit(solution)/shard_map/fqc,fkc->fqk/dot_general | solution.py:100
  62.2 2.2 %fusion.9 = f32[256]{0:T(256)S(1)} fusion(f32[256,2048]{1,0:T(8,128)} %get-tuple-element.18, f32[256]{0:T(256)S(1)} %maximum_maximum_fusion), kind=kLoop, calls=%fused_computation.14 | loop fusion | flops 1048320 | bytes 2099200 | tf_op jit(solution)/shard_map/reduce_sum | solution.py:104
  64.4 0.3 fusion.52
  64.9 0.5 fusion.46
  65.5 4.5 %fusion.16 = f32[256,384]{1,0:T(8,128)} fusion(bf16[384,384]{1,0:T(8,128)(2,1)S(1)} %copy-done.2, bf16[1,2048,384]{2,1,0:T(8,128)(2,1)} %collective-permute-done.5, f32[256,2048]{1,0:T(8,128)} %get-tuple-element.18, f32[256]{0:T(256)S(1)} %maximum_maximum_fusion), kind=kOutput, calls=%fused_computation.21 | convolution fusion | flops 1008467968 | bytes 4359168 | tf_op jit(solution)/shard_map/fqk,fkc->fqc/dot_general | solution.py:106
  70.0 1.7 %fusion.21 = f32[256,384]{1,0:T(8,128)S(1)} fusion(bf16[384,384]{1,0:T(8,128)(2,1)S(1)} %copy-done.2, bf16[1,512,384]{2,1,0:T(8,128)(2,1)S(1)} %collective-permute-done.3, f32[256,512]{1,0:T(8,128)} %get-tuple-element.22, f32[256]{0:T(256)S(1)} %maximum_maximum_fusion), kind=kOutput, calls=%fused_computation.32 | convolution fusion | flops 252116992 | bytes 1606656 | tf_op jit(solution)/shard_map/fqk,fkc->fqc/dot_general | solution.py:106
  71.7 0.5 fusion.20
  72.2 2.5 %fusion.25 = bf16[256,384]{1,0:T(8,128)(2,1)S(1)} fusion(f32[256,384]{1,0:T(8,128)} %fusion.16, f32[256,384]{1,0:T(8,128)S(1)} %fusion.20, bf16[384,384]{1,0:T(8,128)(2,1)S(1)} %copy-done.2, bf16[1,1024,384]{2,1,0:T(8,128)(2,1)} %copy-done.8, f32[256,1024]{1,0:T(8,128)} %get-tuple-element.20, f32[256]{0:T(256)S(1)} %maximum_maximum_fusion, ...), kind=kOutput, calls=%fused_computation.37 | convolution fusion | flops 504627200 | bytes 3115008 | tf_op jit(solution)/shard_map/fqk,fkc->fqc/dot_general | solution.py:106
  74.8 0.4 multiply_reduce_fusion
  75.6 0.3 fusion.176
  75.9 5.2 %collective-permute-start.7 = (bf16[1,1,128,384]{3,1,2,0:T(2,128)(2,1)S(1)}, bf16[1,1,128,384]{3,1,2,0:T(2,128)(2,1)S(1)}, u32[]{:S(2)}, u32[]{:S(2)}) collective-permute-start(bf16[1,1,128,384]{3,1,2,0:T(2,128)(2,1)S(1)} %get-tuple-element.16), channel_id=1, source_target_pairs={{1,0},{2,1},{3,2},{4,3},{5,4},{6,5},{7,6},{8,7},{9,8},{10,9},{11,1... | collective-permute-start | bytes 294920 | tf_op jit(solution)/shard_map/ppermute | solution.py:20
  81.1 2.4 %collective-permute-start.6 = (bf16[1,1,128,384]{3,1,2,0:T(2,128)(2,1)S(1)}, bf16[1,1,128,384]{3,1,2,0:T(2,128)(2,1)S(1)}, u32[]{:S(2)}, u32[]{:S(2)}) collective-permute-start(bf16[1,1,128,384]{3,1,2,0:T(2,128)(2,1)S(1)} %get-tuple-element.15), channel_id=1, source_target_pairs={{0,1},{1,2},{2,3},{3,4},{4,5},{5,6},{6,7},{7,8},{8,9},{9,10},{10,1... | collective-permute-start | bytes 294920 | tf_op jit(solution)/shard_map/ppermute | solution.py:19
  83.5 2.9 %fusion.40 = f32[2,8,17,384]{3,1,2,0:T(8,128)S(1)} fusion(bf16[3,3,3,384,384]{4,3,2,1,0:T(8,128)(2,1)} %param.18, bf16[4,1,7,2,384]{4,2,3,0,1:T(8,128)(2,1)S(1)} %copy-done.13, bf16[4,1,8,17,384]{4,2,3,0,1:T(8,128)(2,1)S(1)} %copy-done.10, pred[8,17]{0,1:T(8,128)(4,1)S(1)} %copy-done.16), kind=kOutput, calls=%fused_computation.51 | convolution fusion | flops 723449856 | bytes 3532936 | tf_op jit(solution)/shard_map/conv_general_dilated | solution.py:38
  86.5 0.3 copy.103
  87.0 2.2 %collective-permute-done.6 = bf16[1,1,128,384]{3,1,2,0:T(2,128)(2,1)S(1)} collective-permute-done((bf16[1,1,128,384]{3,1,2,0:T(2,128)(2,1)S(1)}, bf16[1,1,128,384]{3,1,2,0:T(2,128)(2,1)S(1)}, u32[]{:S(2)}, u32[]{:S(2)}) %collective-permute-start.6) | collective-permute-done | bytes 98336 | tf_op jit(solution)/shard_map/ppermute | solution.py:19
  89.3 0.7 maximum_bitcast_fusion
  90.2 1.2 %fusion.43 = f32[2,8,17,384]{3,1,2,0:T(8,128)S(1)} fusion(bf16[3,3,3,384,384]{4,3,2,1,0:T(8,128)(2,1)S(1)} %bitcast.408, bf16[4,1,7,2,384]{4,2,3,0,1:T(8,128)(2,1)S(1)} %slice.172, bf16[4,1,8,17,384]{4,2,3,0,1:T(8,128)(2,1)S(1)} %copy.46, pred[8,17]{0,1:T(8,128)(4,1)S(1)} %copy-done.16), kind=kOutput, calls=%fused_computation.52 | convolution fusion | flops 723449856 | bytes 3542016 | tf_op jit(solution)/shard_map/conv_general_dilated | solution.py:38
  91.4 1.2 %fusion.37 = bf16[2,8,17,384]{3,1,2,0:T(8,128)(2,1)S(1)} fusion(f32[2,8,17,384]{3,1,2,0:T(8,128)S(1)} %fusion.43, f32[2,8,17,384]{3,1,2,0:T(8,128)S(1)} %fusion.40, bf16[3,3,3,384,384]{4,3,2,1,0:T(8,128)(2,1)S(1)} %bitcast.408, bf16[4,1,7,2,384]{4,2,3,0,1:T(8,128)(2,1)S(1)} %slice.167, bf16[4,1,8,17,384]{4,2,3,0,1:T(8,128)(2,1)S(1)} %copy.38, ...), kind=kOutput, calls=%fused_computation.50 | convolution fusion | flops 723763200 | bytes 4168704 | tf_op jit(solution)/shard_map/conv_general_dilated | solution.py:38
  92.8 2.3 %collective-permute-start.9 = (bf16[1,1,128,384]{3,2,1,0:T(8,128)(2,1)S(1)}, bf16[1,1,128,384]{3,2,1,0:T(8,128)(2,1)S(1)}, u32[]{:S(2)}, u32[]{:S(2)}) collective-permute-start(bf16[1,1,128,384]{3,2,1,0:T(8,128)(2,1)S(1)} %slice.177), channel_id=1, source_target_pairs={{1,0},{2,1},{3,2},{4,3},{5,4},{6,5},{7,6},{8,7},{9,8},{10,9},{11,1... | collective-permute-start | bytes 294920 | tf_op jit(solution)/shard_map/ppermute | solution.py:20
  95.2 2.0 %collective-permute-start.8 = (bf16[1,1,128,384]{3,2,1,0:T(8,128)(2,1)S(1)}, bf16[1,1,128,384]{3,2,1,0:T(8,128)(2,1)S(1)}, u32[]{:S(2)}, u32[]{:S(2)}) collective-permute-start(bf16[1,1,128,384]{3,2,1,0:T(8,128)(2,1)S(1)} %slice.174), channel_id=1, source_target_pairs={{0,1},{1,2},{2,3},{3,4},{4,5},{5,6},{6,7},{7,8},{8,9},{9,10},{10,1... | collective-permute-start | bytes 294920 | tf_op jit(solution)/shard_map/ppermute | solution.py:19
  97.6 4.5 %collective-permute-done.8 = bf16[1,1,128,384]{3,2,1,0:T(8,128)(2,1)S(1)} collective-permute-done((bf16[1,1,128,384]{3,2,1,0:T(8,128)(2,1)S(1)}, bf16[1,1,128,384]{3,2,1,0:T(8,128)(2,1)S(1)}, u32[]{:S(2)}, u32[]{:S(2)}) %collective-permute-start.8) | collective-permute-done | bytes 98336 | tf_op jit(solution)/shard_map/ppermute | solution.py:19
  102.1 1.5 %convolution_bitcast_fusion = f32[1,4,130,3,3,192]{5,2,4,3,1,0:T(8,128)S(1)} fusion(bf16[3,3,384,192]{2,3,1,0:T(8,128)(2,1)S(1)} %copy-done, bf16[1,1,128,384]{3,2,1,0:T(8,128)(2,1)S(1)} %collective-permute-done.9, bf16[1,2,128,384]{3,2,1,0:T(8,128)(2,1)S(1)} %bitcast.405, bf16[1,1,128,384]{3,2,1,0:T(8,128)(2,1)S(1)} %collective-permute-done.8), kind=kOutput, calls=%fused_computation.12 | convolution fusion | flops 692490240 | bytes 5314560 | tf_op jit(solution)/shard_map/frwc,ijco->frwijo/dot_general | solution.py:55
  103.6 0.4 fusion.157
  103.9 0.2 fusion.160
  104.6 0.5 copy.76
  105.1 1.3 %convert_element_type.169 = bf16[1,4,49152]{2,1,0:T(4,128)(2,1)} reshape(bf16[1,2,2,128,2,192]{5,4,3,2,1,0:T(2,128)(2,1)S(1)} %copy.76) | data formatting | bytes 786432 | tf_op jit(solution)/shard_map/convert_element_type | solution.py:72
  (78 shorter events, 2.8 us)
Async XLA Ops:
  0.0 102.1 %copy-start = (bf16[3,3,384,192]{2,3,1,0:T(8,128)(2,1)S(1)}, bf16[3,3,384,192]{2,3,1,0:T(8,128)(2,1)}, u32[]{:S(2)}) copy-start(bf16[3,3,384,192]{2,3,1,0:T(8,128)(2,1)} %param.19) | copy-start | bytes 3981316
  0.0 34.2 %copy-start.1 = (bf16[1,2,128,384]{3,2,1,0:T(8,128)(2,1)S(1)}, bf16[1,2,128,384]{3,2,1,0:T(8,128)(2,1)}, u32[]{:S(2)}) copy-start(bf16[1,2,128,384]{3,2,1,0:T(8,128)(2,1)} %param.10) | copy-start | bytes 589828
  0.0 34.2 %copy-start.14 = (f32[384]{0:T(512)S(1)}, f32[384]{0:T(512)}, u32[]{:S(2)}) copy-start(f32[384]{0:T(512)} %param.11) | copy-start | bytes 4612
  0.0 26.8 %copy-start.4 = (bf16[2,2,128,384]{3,2,1,0:T(8,128)(2,1)S(1)}, bf16[2,2,128,384]{3,2,1,0:T(8,128)(2,1)}, u32[]{:S(2)}) copy-start(bf16[2,2,128,384]{3,2,1,0:T(8,128)(2,1)} %param.16) | copy-start | bytes 1179652
  0.0 34.3 %copy-start.12 = (bf16[384,384]{1,0:T(8,128)(2,1)S(1)}, bf16[384,384]{1,0:T(8,128)(2,1)}, u32[]{:S(2)}) copy-start(bf16[384,384]{1,0:T(8,128)(2,1)} %param.12) | copy-start | bytes 884740
  2.3 11.7 %collective-permute-start.2 = (bf16[1,256,384]{2,1,0:T(8,128)(2,1)S(1)}, bf16[1,256,384]{2,1,0:T(8,128)(2,1)S(1)}, u32[]{:S(2)}, u32[]{:S(2)}) collective-permute-start(bf16[1,256,384]{2,1,0:T(8,128)(2,1)S(1)} %fusion.100), channel_id=1, source_target_pairs={{0,8},{1,9},{2,10},{3,11},{4,12},{5,13},{6,14},{7,15},{8,0},{9,1},... | collective-permute-start | bytes 589832 | tf_op jit(solution)/shard_map/ppermute | solution.py:90
  14.0 11.1 %collective-permute-start.3 = (bf16[1,512,384]{2,1,0:T(8,128)(2,1)S(1)}, bf16[1,512,384]{2,1,0:T(8,128)(2,1)S(1)}, u32[]{:S(2)}, u32[]{:S(2)}) collective-permute-start(bf16[1,512,384]{2,1,0:T(8,128)(2,1)S(1)} %pad_maximum_fusion.3), channel_id=1, source_target_pairs={{0,4},{1,5},{2,6},{3,7},{4,0},{5,1},{6,2},{7,3},{8,12},{9,13},{10,... | collective-permute-start | bytes 1179656 | tf_op jit(solution)/shard_map/ppermute | solution.py:90
  25.2 20.8 %collective-permute-start.4 = (bf16[1,1024,384]{2,1,0:T(8,128)(2,1)S(1)}, bf16[1,1024,384]{2,1,0:T(8,128)(2,1)S(1)}, u32[]{:S(2)}, u32[]{:S(2)}) collective-permute-start(bf16[1,1024,384]{2,1,0:T(8,128)(2,1)S(1)} %pad_maximum_fusion.1), channel_id=1, source_target_pairs={{0,2},{1,3},{2,0},{3,1},{4,6},{5,7},{6,4},{7,5},{8,10},{9,11},{10,... | collective-permute-start | bytes 2359304 | tf_op jit(solution)/shard_map/ppermute | solution.py:90
  27.6 20.3 %collective-permute-start = (bf16[2,1,128,384]{3,2,1,0:T(8,128)(2,1)}, bf16[2,1,128,384]{3,2,1,0:T(8,128)(2,1)}, u32[]{:S(2)}, u32[]{:S(2)}) collective-permute-start(bf16[2,1,128,384]{3,2,1,0:T(8,128)(2,1)} %get-tuple-element.12), channel_id=1, source_target_pairs={{0,1},{1,2},{2,3},{3,4},{4,5},{5,6},{6,7},{7,8},{8,9},{9,10},{10,1... | collective-permute-start | bytes 589832 | tf_op jit(solution)/shard_map/ppermute | solution.py:19
  29.5 17.9 %copy-start.6 = (bf16[384,384]{1,0:T(8,128)(2,1)S(1)}, bf16[384,384]{1,0:T(8,128)(2,1)}, u32[]{:S(2)}) copy-start(bf16[384,384]{1,0:T(8,128)(2,1)} %param.13) | copy-start | bytes 884740
  29.5 19.4 %collective-permute-start.1 = (bf16[2,1,128,384]{3,2,1,0:T(8,128)(2,1)}, bf16[2,1,128,384]{3,2,1,0:T(8,128)(2,1)}, u32[]{:S(2)}, u32[]{:S(2)}) collective-permute-start(bf16[2,1,128,384]{3,2,1,0:T(8,128)(2,1)} %get-tuple-element.11), channel_id=1, source_target_pairs={{1,0},{2,1},{3,2},{4,3},{5,4},{6,5},{7,6},{8,7},{9,8},{10,9},{11,1... | collective-permute-start | bytes 589832 | tf_op jit(solution)/shard_map/ppermute | solution.py:20
  46.0 1.4 %copy-start.8 = (bf16[1,1024,384]{2,1,0:T(8,128)(2,1)}, bf16[1,1024,384]{2,1,0:T(8,128)(2,1)S(1)}, u32[]{:S(2)}) copy-start(bf16[1,1024,384]{2,1,0:T(8,128)(2,1)S(1)} %collective-permute-done.4) | copy-start | bytes 2359300
  47.4 10.4 %collective-permute-start.5 = (bf16[1,2048,384]{2,1,0:T(8,128)(2,1)}, bf16[1,2048,384]{2,1,0:T(8,128)(2,1)}, u32[]{:S(2)}, u32[]{:S(2)}) collective-permute-start(bf16[1,2048,384]{2,1,0:T(8,128)(2,1)} %pad_maximum_fusion), channel_id=1, source_target_pairs={{0,1},{1,0},{2,3},{3,2},{4,5},{5,4},{6,7},{7,6},{8,9},{9,8},{10,11... | collective-permute-start | bytes 4718600 | tf_op jit(solution)/shard_map/ppermute | solution.py:90
  51.3 0.8 copy-start.9
  62.2 2.2 %copy-start.7 = (f32[256,1024]{1,0:T(8,128)S(1)}, f32[256,1024]{1,0:T(8,128)}, u32[]{:S(2)}) copy-start(f32[256,1024]{1,0:T(8,128)} %get-tuple-element.20) | copy-start | bytes 3145732
  62.2 2.5 %copy-start.3 = (f32[256,512]{1,0:T(8,128)S(1)}, f32[256,512]{1,0:T(8,128)}, u32[]{:S(2)}) copy-start(f32[256,512]{1,0:T(8,128)} %get-tuple-element.22) | copy-start | bytes 1572868
  62.2 2.7 %copy-start.2 = (bf16[384,384]{1,0:T(8,128)(2,1)S(1)}, bf16[384,384]{1,0:T(8,128)(2,1)}, u32[]{:S(2)}) copy-start(bf16[384,384]{1,0:T(8,128)(2,1)} %param.14) | copy-start | bytes 884740
  72.2 2.6 %copy-start.11 = (bf16[384,384]{1,0:T(8,128)(2,1)S(1)}, bf16[384,384]{1,0:T(8,128)(2,1)}, u32[]{:S(2)}) copy-start(bf16[384,384]{1,0:T(8,128)(2,1)} %param.15) | copy-start | bytes 884740
  72.2 3.0 %copy-start.15 = (f32[384]{0:T(512)S(1)}, f32[384]{0:T(512)}, u32[]{:S(2)}) copy-start(f32[384]{0:T(512)} %param.17) | copy-start | bytes 4612
  74.7 8.7 %copy-start.10 = (bf16[4,1,8,17,384]{4,2,3,0,1:T(8,128)(2,1)S(1)}, bf16[4,1,8,17,384]{4,2,3,0,1:T(8,128)(2,1)}, u32[]{:S(2)}) copy-start(bf16[4,1,8,17,384]{4,2,3,0,1:T(8,128)(2,1)} %copy-done.9) | copy-start | bytes 1253380
  74.8 8.7 %copy-start.13 = (bf16[4,1,7,2,384]{4,2,3,0,1:T(8,128)(2,1)S(1)}, bf16[4,1,7,2,384]{4,2,3,0,1:T(8,128)(2,1)}, u32[]{:S(2)}) copy-start(bf16[4,1,7,2,384]{4,2,3,0,1:T(8,128)(2,1)} %slice.169) | copy-start | bytes 129028
  74.8 8.7 %copy-start.16 = (pred[8,17]{0,1:T(8,128)(4,1)S(1)}, pred[8,17]{0,1:T(8,128)(4,1)}, u32[]{:S(2)}) copy-start(pred[8,17]{0,1:T(8,128)(4,1)} %constant.37) | copy-start | bytes 412
  74.8 15.4 %slice-start = ((s8[7962624]{0:T(1024)(128)(4,1)}), s8[4194304]{0:T(1024)(128)(4,1)S(1)}, s32[]{:S(2)}) async-start(s8[7962624]{0:T(1024)(128)(4,1)} %bitcast.407), calls=%async_computation | async-start | bytes 8388608
  75.9 11.1 %collective-permute-start.7 = (bf16[1,1,128,384]{3,1,2,0:T(2,128)(2,1)S(1)}, bf16[1,1,128,384]{3,1,2,0:T(2,128)(2,1)S(1)}, u32[]{:S(2)}, u32[]{:S(2)}) collective-permute-start(bf16[1,1,128,384]{3,1,2,0:T(2,128)(2,1)S(1)} %get-tuple-element.16), channel_id=1, source_target_pairs={{1,0},{2,1},{3,2},{4,3},{5,4},{6,5},{7,6},{8,7},{9,8},{10,9},{11,1... | collective-permute-start | bytes 294920 | tf_op jit(solution)/shard_map/ppermute | solution.py:20
  81.1 5.4 %copy-start.5 = (bf16[4,1,128,384]{3,2,0,1:T(8,128)(2,1)S(1)}, bf16[4,1,128,384]{3,2,0,1:T(8,128)(2,1)}, u32[]{:S(2)}) copy-start(bf16[4,1,128,384]{3,2,0,1:T(8,128)(2,1)} %get-tuple-element.9) | copy-start | bytes 1179652
  81.1 9.1 %slice-start.1 = ((s8[7962624]{0:T(1024)(128)(4,1)}), s8[3768320]{0:T(1024)(128)(4,1)S(1)}, s32[]{:S(2)}) async-start(s8[7962624]{0:T(1024)(128)(4,1)} %bitcast.407), calls=%async_computation.1 | async-start | bytes 7536640
  81.1 8.2 %collective-permute-start.6 = (bf16[1,1,128,384]{3,1,2,0:T(2,128)(2,1)S(1)}, bf16[1,1,128,384]{3,1,2,0:T(2,128)(2,1)S(1)}, u32[]{:S(2)}, u32[]{:S(2)}) collective-permute-start(bf16[1,1,128,384]{3,1,2,0:T(2,128)(2,1)S(1)} %get-tuple-element.15), channel_id=1, source_target_pairs={{0,1},{1,2},{2,3},{3,4},{4,5},{5,6},{6,7},{7,8},{8,9},{9,10},{10,1... | collective-permute-start | bytes 294920 | tf_op jit(solution)/shard_map/ppermute | solution.py:19
  92.8 4.8 %collective-permute-start.9 = (bf16[1,1,128,384]{3,2,1,0:T(8,128)(2,1)S(1)}, bf16[1,1,128,384]{3,2,1,0:T(8,128)(2,1)S(1)}, u32[]{:S(2)}, u32[]{:S(2)}) collective-permute-start(bf16[1,1,128,384]{3,2,1,0:T(8,128)(2,1)S(1)} %slice.177), channel_id=1, source_target_pairs={{1,0},{2,1},{3,2},{4,3},{5,4},{6,5},{7,6},{8,7},{9,8},{10,9},{11,1... | collective-permute-start | bytes 294920 | tf_op jit(solution)/shard_map/ppermute | solution.py:20
  95.2 6.8 %collective-permute-start.8 = (bf16[1,1,128,384]{3,2,1,0:T(8,128)(2,1)S(1)}, bf16[1,1,128,384]{3,2,1,0:T(8,128)(2,1)S(1)}, u32[]{:S(2)}, u32[]{:S(2)}) collective-permute-start(bf16[1,1,128,384]{3,2,1,0:T(8,128)(2,1)S(1)} %slice.174), channel_id=1, source_target_pairs={{0,1},{1,2},{2,3},{3,4},{4,5},{5,6},{6,7},{7,8},{8,9},{9,10},{10,1... | collective-permute-start | bytes 294920 | tf_op jit(solution)/shard_map/ppermute | solution.py:19

commit v4 on v3

--- a/solution.py
+++ b/solution.py
@@ -85,13 +85,17 @@
     normed = rms_gain(flat.astype(jnp.float32), norm_attn).astype(jnp.bfloat16)
     queries = project(normed, w_query)
     size = lax.axis_size(ROWS)
-    pieces, held, bit = [normed], normed, size // 2
-    while bit >= 1:
-        other = lax.ppermute(held, ROWS, [(i, i ^ bit) for i in range(size)])
-        pieces.append(other)
-        if bit > 1:
+    chip_bits = [1 << k for k in range(1, size.bit_length() - 1)][::-1]
+    orders = (chip_bits, chip_bits[-1:] + chip_bits[:-1])
+    mine, held = [normed], normed
+    for step in range(len(chip_bits)):
+        perm = [(i, i ^ orders[i & 1][step]) for i in range(size)]
+        other = lax.ppermute(held, ROWS, perm)
+        mine.append(other)
+        if step + 1 < len(chip_bits):
             held = jnp.concatenate([held, other], axis=1)
-        bit //= 2
+    swap = [(i, i ^ 1) for i in range(size)]
+    pieces = mine + [lax.ppermute(piece, ROWS, swap) for piece in mine]
     scores, values = [], []
     for piece in pieces:
         keys = project(piece, w_key)

time: 107 us -> 110 us (1.028)
  the two profiles are of different devices: /device:TPU:24 before, /device:TPU:5 now
where the time goes in v4:
time: 110 us; the launch traced here: 109 us
  matrix products  45.3 us (41%)
  starting transfers between devices  25.8 us (23%)
  waiting for transfers between devices  17.7 us (16%)
  other arithmetic  12.2 us (11%)
  local copies, waits for them, and re-layouts  7.74 us (7%)
    dot_general x8, matrix products, body(): jnp.einsum('fqc,fkc->fqk', queries, keys, preferred_element_type=jnp.floa...  18.6 us
    dot_general x8, matrix products, body(): jnp.einsum('fqk,fkc->fqc', e.astype(jnp.bfloat16), v, preferred_element_t...  18.2 us
    ppermute x3, starting transfers between devices, padded_2(): before = lax.ppermute(last, axis, up)  12.1 us
    ppermute x3, waiting for transfers between devices, body(): other = lax.ppermute(held, ROWS, perm)  12 us
    ppermute x4, starting transfers between devices, body(): pieces = mine + [lax.ppermute(piece, ROWS, swap) for piece in mine]  6.14 us
    ppermute x3, starting transfers between devices, padded_2(): after = lax.ppermute(first, axis, down)  5.89 us
    ppermute x3, waiting for transfers between devices, padded_2(): after = lax.ppermute(first, axis, down)  5.66 us
    conv_general_dilated x3, matrix products, conv_rows(): lax.conv_general_dilated(haloed[tstep:tstep + 1], weight[tstep], window_s...  5.35 us
  transfers between devices with their start and end apart: 13, of which 4 were waited for; matrix products, arithmetic and copies ran while one was open for 25% of the time, Pallas kernels for 0%

profile of v4, /device:TPU:5, one launch (start us, length us, event | category | flops | bytes accessed | tf_op | source)
XLA Modules:
  0.0 109.3 jit_solution(8166110446698887244)
XLA Ops:
  0.0 1.2 %multiply_reduce_fusion.1 = f32[2,128]{1,0:T(2,128)S(1)} fusion(bf16[1,2,128,384]{3,2,1,0:T(8,128)(2,1)} %param.10), kind=kLoop, calls=%fused_computation.129 | loop fusion | flops 294656 | bytes 197632 | tf_op jit(solution)/shard_map/reduce_sum | solution.py:26
  1.2 1.0 fusion.108
  2.3 3.3 %collective-permute-start.5 = (bf16[1,256,384]{2,1,0:T(8,128)(2,1)S(1)}, bf16[1,256,384]{2,1,0:T(8,128)(2,1)}, u32[]{:S(2)}, u32[]{:S(2)}) collective-permute-start(bf16[1,256,384]{2,1,0:T(8,128)(2,1)S(1)} %fusion.108), channel_id=1, source_target_pairs={{0,1},{1,0},{2,3},{3,2},{4,5},{5,4},{6,7},{7,6},{8,9},{9,8},{10,11... | collective-permute-start | bytes 589832 | tf_op jit(solution)/shard_map/ppermute | solution.py:98
  5.6 1.8 %fusion.200 = (bf16[2,1,128,384]{3,2,1,0:T(8,128)(2,1)}, bf16[2,1,128,384]{3,2,1,0:T(8,128)(2,1)}) fusion(bf16[2,2,128,384]{3,2,1,0:T(8,128)(2,1)} %param.16), kind=kLoop, calls=%fused_computation.246 | loop fusion | bytes 786432 | tf_op jit(solution)/shard_map/slice | solution.py:18
  7.4 3.0 %collective-permute-start = (bf16[2,1,128,384]{3,2,1,0:T(8,128)(2,1)}, bf16[2,1,128,384]{3,2,1,0:T(8,128)(2,1)S(1)}, u32[]{:S(2)}, u32[]{:S(2)}) collective-permute-start(bf16[2,1,128,384]{3,2,1,0:T(8,128)(2,1)} %get-tuple-element.18), channel_id=1, source_target_pairs={{0,1},{1,2},{2,3},{3,4},{4,5},{5,6},{6,7},{7,8},{8,9},{9,10},{10,1... | collective-permute-start | bytes 589832 | tf_op jit(solution)/shard_map/ppermute | solution.py:19
  10.4 1.9 %collective-permute-start.1 = (bf16[2,1,128,384]{3,2,1,0:T(8,128)(2,1)}, bf16[2,1,128,384]{3,2,1,0:T(8,128)(2,1)S(1)}, u32[]{:S(2)}, u32[]{:S(2)}) collective-permute-start(bf16[2,1,128,384]{3,2,1,0:T(8,128)(2,1)} %get-tuple-element.17), channel_id=1, source_target_pairs={{1,0},{2,1},{3,2},{4,3},{5,4},{6,5},{7,6},{8,7},{9,8},{10,9},{11,1... | collective-permute-start | bytes 589832 | tf_op jit(solution)/shard_map/ppermute | solution.py:20
  12.4 1.0 fusion.110
  13.4 1.2 %convolution_convert_fusion.16 = bf16[256,384]{1,0:T(8,128)(2,1)S(1)} fusion(bf16[256,384]{1,0:T(8,128)(2,1)S(1)} %fusion.110, bf16[384,384]{1,0:T(8,128)(2,1)} %param.12), kind=kOutput, calls=%fused_computation.47 | convolution fusion | flops 75595776 | bytes 688128 | tf_op jit(solution)/shard_map/fqc,cd->fqd/dot_general | solution.py:30
  14.7 0.8 pad_maximum_fusion.2
  15.5 0.8 collective-permute-start.3
  16.3 1.1 fusion.221
  17.4 1.1 %collective-permute-done.1 = bf16[2,1,128,384]{3,2,1,0:T(8,128)(2,1)S(1)} collective-permute-done((bf16[2,1,128,384]{3,2,1,0:T(8,128)(2,1)}, bf16[2,1,128,384]{3,2,1,0:T(8,128)(2,1)S(1)}, u32[]{:S(2)}, u32[]{:S(2)}) %collective-permute-start.1) | collective-permute-done | bytes 196640 | tf_op jit(solution)/shard_map/ppermute | solution.py:20
  18.6 8.5 %collective-permute-done.3 = bf16[1,512,384]{2,1,0:T(8,128)(2,1)} collective-permute-done((bf16[1,512,384]{2,1,0:T(8,128)(2,1)}, bf16[1,512,384]{2,1,0:T(8,128)(2,1)}, u32[]{:S(2)}, u32[]{:S(2)}) %collective-permute-start.3) | collective-permute-done | bytes 393248 | tf_op jit(solution)/shard_map/ppermute | solution.py:93
  27.1 2.0 %pad_maximum_fusion = bf16[1,1024,384]{2,1,0:T(8,128)(2,1)} fusion(bf16[1,512,384]{2,1,0:T(8,128)(2,1)} %collective-permute-done.3, bf16[1,256,384]{2,1,0:T(8,128)(2,1)S(1)} %collective-permute-done.2, bf16[1,256,384]{2,1,0:T(8,128)(2,1)S(1)} %fusion.108), kind=kLoop, calls=%fused_computation.73 | loop fusion | flops 2359296 | bytes 1572864 | tf_op jit(solution)/shard_map/concatenate | solution.py:96
  29.0 0.7 collective-permute-start.4
  29.7 0.9 slice_bitcast_fusion.1
  31.1 0.7 slice.169
  31.9 0.9 collective-permute-start.6
  32.8 1.1 fusion.222
  33.9 2.0 %fusion.212 = (f32[256]{0:T(256)}, f32[256,256]{0,1:T(8,128)S(1)}) fusion(bf16[256,384]{1,0:T(8,128)(2,1)S(1)} %convolution_convert_fusion.16, bf16[384,384]{1,0:T(8,128)(2,1)S(1)} %copy-done.2, bf16[1,256,384]{2,1,0:T(8,128)(2,1)} %collective-permute-done.5), kind=kOutput, calls=%fused_computation.252 | convolution fusion | flops 126058240 | bytes 951296 | tf_op jit(solution)/shard_map/fqc,fkc->fqk/dot_general | solution.py:104
  35.9 1.1 fusion.209
  37.0 3.5 %collective-permute-done.4 = bf16[1,1024,384]{2,1,0:T(8,128)(2,1)} collective-permute-done((bf16[1,1024,384]{2,1,0:T(8,128)(2,1)}, bf16[1,1024,384]{2,1,0:T(8,128)(2,1)}, u32[]{:S(2)}, u32[]{:S(2)}) %collective-permute-start.4) | collective-permute-done | bytes 786464 | tf_op jit(solution)/shard_map/ppermute | solution.py:93
  40.5 2.0 %collective-permute-start.8 = (bf16[1,1024,384]{2,1,0:T(8,128)(2,1)}, bf16[1,1024,384]{2,1,0:T(8,128)(2,1)}, u32[]{:S(2)}, u32[]{:S(2)}) collective-permute-start(bf16[1,1024,384]{2,1,0:T(8,128)(2,1)} %collective-permute-done.4), channel_id=1, source_target_pairs={{0,1},{1,0},{2,3},{3,2},{4,5},{5,4},{6,7},{7,6},{8,9},{9,8},{10,11... | collective-permute-start | bytes 2359304 | tf_op jit(solution)/shard_map/ppermute | solution.py:98
  42.5 3.0 %fusion.218 = (f32[256]{0:T(256)}, f32[256,512]{1,0:T(8,128)}) fusion(bf16[256,384]{1,0:T(8,128)(2,1)S(1)} %convolution_convert_fusion.16, bf16[384,384]{1,0:T(8,128)(2,1)S(1)} %copy-done.2, bf16[1,512,384]{2,1,0:T(8,128)(2,1)} %collective-permute-done.3), kind=kOutput, calls=%fused_computation.254 | convolution fusion | flops 252116736 | bytes 1410048 | tf_op jit(solution)/shard_map/fqc,fkc->fqk/dot_general | solution.py:104
  45.5 3.1 %fusion.206 = (f32[256]{0:T(256)}, f32[256,512]{1,0:T(8,128)}) fusion(bf16[256,384]{1,0:T(8,128)(2,1)S(1)} %convolution_convert_fusion.16, bf16[384,384]{1,0:T(8,128)(2,1)S(1)} %copy-done.2, bf16[1,512,384]{2,1,0:T(8,128)(2,1)} %collective-permute-done.7), kind=kOutput, calls=%fused_computation.250 | convolution fusion | flops 252116736 | bytes 1410048 | tf_op jit(solution)/shard_map/fqc,fkc->fqk/dot_general | solution.py:104
  48.6 3.7 %fusion.215 = (f32[256]{0:T(256)}, f32[256,1024]{1,0:T(8,128)}) fusion(bf16[256,384]{1,0:T(8,128)(2,1)S(1)} %convolution_convert_fusion.16, bf16[384,384]{1,0:T(8,128)(2,1)S(1)} %copy-done.2, bf16[1,1024,384]{2,1,0:T(8,128)(2,1)} %collective-permute-done.4), kind=kOutput, calls=%fused_computation.253 | convolution fusion | flops 504233728 | bytes 2327552 | tf_op jit(solution)/shard_map/fqc,fkc->fqk/dot_general | solution.py:104
  52.2 3.6 %fusion.203 = (f32[256]{0:T(256)}, f32[256,1024]{1,0:T(8,128)}) fusion(bf16[256,384]{1,0:T(8,128)(2,1)S(1)} %convolution_convert_fusion.16, bf16[384,384]{1,0:T(8,128)(2,1)S(1)} %copy-done.2, bf16[1,1024,384]{2,1,0:T(8,128)(2,1)} %collective-permute-done.8), kind=kOutput, calls=%fused_computation.249 | convolution fusion | flops 504233728 | bytes 2327552 | tf_op jit(solution)/shard_map/fqc,fkc->fqk/dot_general | solution.py:104
  55.9 0.7 maximum_maximum_fusion
  56.6 1.5 %fusion.84 = (f32[256]{0:T(256)S(1)}, f32[256]{0:T(256)S(1)}) fusion(f32[256,512]{1,0:T(8,128)} %get-tuple-element.34, f32[256]{0:T(256)S(1)} %maximum_maximum_fusion, f32[256,512]{1,0:T(8,128)} %get-tuple-element.26), kind=kLoop, calls=%fused_computation.101 | loop fusion | flops 523776 | bytes 1051648 | tf_op jit(solution)/shard_map/reduce_sum | solution.py:108
  58.1 2.0 %fusion.46 = (f32[256]{0:T(256)S(1)}, f32[256]{0:T(256)S(1)}) fusion(f32[256,1024]{1,0:T(8,128)} %get-tuple-element.32, f32[256]{0:T(256)S(1)} %maximum_maximum_fusion, f32[256,1024]{1,0:T(8,128)} %get-tuple-element.24), kind=kLoop, calls=%fused_computation.68 | loop fusion | flops 1048064 | bytes 2100224 | tf_op jit(solution)/shard_map/reduce_sum | solution.py:108
  60.1 1.2 %fusion.41 = f32[256,384]{1,0:T(8,128)} fusion(bf16[256,384]{1,0:T(8,128)(2,1)S(1)} %fusion.110, bf16[384,384]{1,0:T(8,128)(2,1)S(1)} %copy-done.1, f32[256,256]{0,1:T(8,128)S(1)} %get-tuple-element.36, f32[256]{0:T(256)S(1)} %maximum_maximum_fusion), kind=kOutput, calls=%fused_computation.60 | convolution fusion | flops 126058496 | bytes 1147904 | tf_op jit(solution)/shard_map/fqk,fkc->fqc/dot_general | solution.py:110
  61.5 2.6 %fusion.14 = f32[256,384]{1,0:T(8,128)} fusion(bf16[384,384]{1,0:T(8,128)(2,1)S(1)} %copy-done.1, bf16[1,512,384]{2,1,0:T(8,128)(2,1)} %collective-permute-done.3, f32[256,512]{1,0:T(8,128)} %get-tuple-element.34, f32[256]{0:T(256)S(1)} %maximum_maximum_fusion), kind=kOutput, calls=%fused_computation.31 | convolution fusion | flops 252116992 | bytes 1606656 | tf_op jit(solution)/shard_map/fqk,fkc->fqc/dot_general | solution.py:110
  64.1 2.2 %fusion.42 = f32[256,384]{1,0:T(8,128)} fusion(bf16[384,384]{1,0:T(8,128)(2,1)S(1)} %copy-done.1, bf16[1,256,384]{2,1,0:T(8,128)(2,1)} %collective-permute-done.5, f32[256,256]{0,1:T(8,128)S(1)} %get-tuple-element.30, f32[256]{0:T(256)S(1)} %maximum_maximum_fusion), kind=kOutput, calls=%fused_computation.61 | convolution fusion | flops 126058496 | bytes 1147904 | tf_op jit(solution)/shard_map/fqk,fkc->fqc/dot_general | solution.py:110
  66.3 2.4 %fusion.15 = f32[256,384]{1,0:T(8,128)} fusion(bf16[384,384]{1,0:T(8,128)(2,1)S(1)} %copy-done.1, bf16[1,512,384]{2,1,0:T(8,128)(2,1)} %collective-permute-done.7, f32[256,512]{1,0:T(8,128)S(1)} %copy-done.4, f32[256]{0:T(256)S(1)} %maximum_maximum_fusion), kind=kOutput, calls=%fused_computation.32 | convolution fusion | flops 252116992 | bytes 1606656 | tf_op jit(solution)/shard_map/fqk,fkc->fqc/dot_general | solution.py:110
  68.7 2.4 %fusion.12 = f32[256,384]{1,0:T(8,128)} fusion(f32[256,384]{1,0:T(8,128)} %fusion.14, f32[256,384]{1,0:T(8,128)} %fusion.41, bf16[384,384]{1,0:T(8,128)(2,1)S(1)} %copy-done.1, bf16[1,256,384]{2,1,0:T(8,128)(2,1)S(1)} %collective-permute-done.2, f32[256,256]{0,1:T(8,128)S(1)} %get-tuple-element.38, f32[256]{0:T(256)S(1)} %maximum_maximum_fusion), kind=kOutput, calls=%fused_computation.29 | convolution fusion | flops 126255104 | bytes 1934336 | tf_op jit(solution)/shard_map/fqk,fkc->fqc/dot_general | solution.py:110
  71.1 3.4 %fusion.19 = f32[256,384]{1,0:T(8,128)} fusion(f32[256,384]{1,0:T(8,128)} %fusion.42, f32[256,384]{1,0:T(8,128)} %fusion.12, bf16[384,384]{1,0:T(8,128)(2,1)S(1)} %copy-done.1, bf16[1,1024,384]{2,1,0:T(8,128)(2,1)} %collective-permute-done.4, f32[256,1024]{1,0:T(8,128)} %get-tuple-element.32, f32[256]{0:T(256)S(1)} %maximum_maximum_fusion), kind=kOutput, calls=%fused_computation.36 | convolution fusion | flops 504430592 | bytes 3310592 | tf_op jit(solution)/shard_map/fqk,fkc->fqc/dot_general | solution.py:110
  74.5 1.5 %fusion.13 = f32[256,384]{1,0:T(8,128)S(1)} fusion(f32[256,384]{1,0:T(8,128)S(1)} %copy-done.6, f32[256,384]{1,0:T(8,128)} %fusion.19, bf16[384,384]{1,0:T(8,128)(2,1)S(1)} %copy-done.1, bf16[1,256,384]{2,1,0:T(8,128)(2,1)S(1)} %copy-done.9, f32[256,256]{0,1:T(8,128)S(1)} %get-tuple-element.28, f32[256]{0:T(256)S(1)} %maximum_maximum_fusion), kind=kOutput, calls=%fused_computation.30 | convolution fusion | flops 126255104 | bytes 1934336 | tf_op jit(solution)/shard_map/fqk,fkc->fqc/dot_general | solution.py:110
  76.1 2.5 %fusion.20 = bf16[256,384]{1,0:T(8,128)(2,1)S(1)} fusion(f32[256,384]{1,0:T(8,128)S(1)} %fusion.13, bf16[384,384]{1,0:T(8,128)(2,1)S(1)} %copy-done.1, bf16[1,1024,384]{2,1,0:T(8,128)(2,1)} %collective-permute-done.8, f32[256,1024]{1,0:T(8,128)} %get-tuple-element.24, f32[256]{0:T(256)S(1)} %maximum_maximum_fusion, f32[256]{0:T(256)S(1)} %add_add_fusion), kind=kOutput, calls=%fused_computation.38 | convolution fusion | flops 504528896 | bytes 2721792 | tf_op jit(solution)/shard_map/fqk,fkc->fqc/dot_general | solution.py:110
  79.7 2.1 %collective-permute-start.10 = (bf16[1,1,128,384]{3,1,2,0:T(2,128)(2,1)S(1)}, bf16[1,1,128,384]{3,1,2,0:T(2,128)(2,1)S(1)}, u32[]{:S(2)}, u32[]{:S(2)}) collective-permute-start(bf16[1,1,128,384]{3,1,2,0:T(2,128)(2,1)S(1)} %get-tuple-element.22), channel_id=1, source_target_pairs={{1,0},{2,1},{3,2},{4,3},{5,4},{6,5},{7,6},{8,7},{9,8},{10,9},{11,1... | collective-permute-start | bytes 294920 | tf_op jit(solution)/shard_map/ppermute | solution.py:20
  81.8 5.0 %collective-permute-start.9 = (bf16[1,1,128,384]{3,1,2,0:T(2,128)(2,1)S(1)}, bf16[1,1,128,384]{3,1,2,0:T(2,128)(2,1)S(1)}, u32[]{:S(2)}, u32[]{:S(2)}) collective-permute-start(bf16[1,1,128,384]{3,1,2,0:T(2,128)(2,1)S(1)} %get-tuple-element.21), channel_id=1, source_target_pairs={{0,1},{1,2},{2,3},{3,4},{4,5},{5,6},{6,7},{7,8},{8,9},{9,10},{10,1... | collective-permute-start | bytes 294920 | tf_op jit(solution)/shard_map/ppermute | solution.py:19
  86.8 2.9 %fusion.35 = f32[2,8,17,384]{3,1,2,0:T(8,128)S(1)} fusion(bf16[3,3,3,384,384]{4,3,2,1,0:T(8,128)(2,1)} %param.18, bf16[4,1,7,2,384]{4,2,3,0,1:T(8,128)(2,1)S(1)} %copy-done.13, bf16[4,1,8,17,384]{4,2,3,0,1:T(8,128)(2,1)S(1)} %copy-done.11, pred[8,17]{0,1:T(8,128)(4,1)S(1)} %copy-done.15), kind=kOutput, calls=%fused_computation.58 | convolution fusion | flops 723449856 | bytes 3532936 | tf_op jit(solution)/shard_map/conv_general_dilated | solution.py:38
  91.3 1.2 %fusion.38 = f32[2,8,17,384]{3,1,2,0:T(8,128)S(1)} fusion(bf16[3,3,3,384,384]{4,3,2,1,0:T(8,128)(2,1)S(1)} %bitcast.442, bf16[4,1,7,2,384]{4,2,3,0,1:T(8,128)(2,1)S(1)} %slice.172, bf16[4,1,8,17,384]{4,2,3,0,1:T(8,128)(2,1)S(1)} %copy.46, pred[8,17]{0,1:T(8,128)(4,1)S(1)} %copy-done.15), kind=kOutput, calls=%fused_computation.59 | convolution fusion | flops 723449856 | bytes 3542016 | tf_op jit(solution)/shard_map/conv_general_dilated | solution.py:38
  92.5 1.2 %fusion.32 = bf16[2,8,17,384]{3,1,2,0:T(8,128)(2,1)S(1)} fusion(f32[2,8,17,384]{3,1,2,0:T(8,128)S(1)} %fusion.38, f32[2,8,17,384]{3,1,2,0:T(8,128)S(1)} %fusion.35, bf16[3,3,3,384,384]{4,3,2,1,0:T(8,128)(2,1)S(1)} %bitcast.442, bf16[4,1,7,2,384]{4,2,3,0,1:T(8,128)(2,1)S(1)} %slice.167, bf16[4,1,8,17,384]{4,2,3,0,1:T(8,128)(2,1)S(1)} %copy.38, ...), kind=kOutput, calls=%fused_computation.57 | convolution fusion | flops 723763200 | bytes 4168704 | tf_op jit(solution)/shard_map/conv_general_dilated | solution.py:38
  93.9 4.1 %collective-permute-start.11 = (bf16[1,1,128,384]{3,2,1,0:T(8,128)(2,1)S(1)}, bf16[1,1,128,384]{3,2,1,0:T(8,128)(2,1)S(1)}, u32[]{:S(2)}, u32[]{:S(2)}) collective-permute-start(bf16[1,1,128,384]{3,2,1,0:T(8,128)(2,1)S(1)} %slice.174), channel_id=1, source_target_pairs={{0,1},{1,2},{2,3},{3,4},{4,5},{5,6},{6,7},{7,8},{8,9},{9,10},{10,1... | collective-permute-start | bytes 294920 | tf_op jit(solution)/shard_map/ppermute | solution.py:19
  98.1 1.9 %collective-permute-start.12 = (bf16[1,1,128,384]{3,2,1,0:T(8,128)(2,1)S(1)}, bf16[1,1,128,384]{3,2,1,0:T(8,128)(2,1)S(1)}, u32[]{:S(2)}, u32[]{:S(2)}) collective-permute-start(bf16[1,1,128,384]{3,2,1,0:T(8,128)(2,1)S(1)} %slice.177), channel_id=1, source_target_pairs={{1,0},{2,1},{3,2},{4,3},{5,4},{6,5},{7,6},{8,7},{9,8},{10,9},{11,1... | collective-permute-start | bytes 294920 | tf_op jit(solution)/shard_map/ppermute | solution.py:20
  100.4 4.5 %collective-permute-done.12 = bf16[1,1,128,384]{3,2,1,0:T(8,128)(2,1)S(1)} collective-permute-done((bf16[1,1,128,384]{3,2,1,0:T(8,128)(2,1)S(1)}, bf16[1,1,128,384]{3,2,1,0:T(8,128)(2,1)S(1)}, u32[]{:S(2)}, u32[]{:S(2)}) %collective-permute-start.12) | collective-permute-done | bytes 98336 | tf_op jit(solution)/shard_map/ppermute | solution.py:20
  104.9 1.5 %convolution_bitcast_fusion = f32[1,4,130,3,3,192]{5,2,4,3,1,0:T(8,128)S(1)} fusion(bf16[3,3,384,192]{2,3,1,0:T(8,128)(2,1)S(1)} %copy-done, bf16[1,1,128,384]{3,2,1,0:T(8,128)(2,1)S(1)} %collective-permute-done.12, bf16[1,2,128,384]{3,2,1,0:T(8,128)(2,1)S(1)} %bitcast.439, bf16[1,1,128,384]{3,2,1,0:T(8,128)(2,1)S(1)} %collective-permute-done.11), kind=kOutput, calls=%fused_computation.9 | convolution fusion | flops 692490240 | bytes 5314560 | tf_op jit(solution)/shard_map/frwc,ijco->frwijo/dot_general | solution.py:55
  108.0 1.3 %convert_element_type.214 = bf16[1,4,49152]{2,1,0:T(4,128)(2,1)} reshape(bf16[1,2,2,128,2,192]{5,4,3,2,1,0:T(2,128)(2,1)S(1)} %copy.76) | data formatting | bytes 786432 | tf_op jit(solution)/shard_map/convert_element_type | solution.py:72
  (86 shorter events, 5.6 us)
Async XLA Ops:
  0.0 104.9 %copy-start = (bf16[3,3,384,192]{2,3,1,0:T(8,128)(2,1)S(1)}, bf16[3,3,384,192]{2,3,1,0:T(8,128)(2,1)}, u32[]{:S(2)}) copy-start(bf16[3,3,384,192]{2,3,1,0:T(8,128)(2,1)} %param.19) | copy-start | bytes 3981316
  0.0 17.3 %copy-start.5 = (bf16[2,2,128,384]{3,2,1,0:T(8,128)(2,1)S(1)}, bf16[2,2,128,384]{3,2,1,0:T(8,128)(2,1)}, u32[]{:S(2)}) copy-start(bf16[2,2,128,384]{3,2,1,0:T(8,128)(2,1)} %param.16) | copy-start | bytes 1179652
  0.0 16.2 %copy-start.2 = (bf16[384,384]{1,0:T(8,128)(2,1)S(1)}, bf16[384,384]{1,0:T(8,128)(2,1)}, u32[]{:S(2)}) copy-start(bf16[384,384]{1,0:T(8,128)(2,1)} %param.13) | copy-start | bytes 884740
  2.3 12.4 %collective-permute-start.2 = (bf16[1,256,384]{2,1,0:T(8,128)(2,1)S(1)}, bf16[1,256,384]{2,1,0:T(8,128)(2,1)S(1)}, u32[]{:S(2)}, u32[]{:S(2)}) collective-permute-start(bf16[1,256,384]{2,1,0:T(8,128)(2,1)S(1)} %fusion.108), channel_id=1, source_target_pairs={{0,8},{1,3},{2,10},{3,1},{4,12},{5,7},{6,14},{7,5},{8,0},{9,11},{1... | collective-permute-start | bytes 589832 | tf_op jit(solution)/shard_map/ppermute | solution.py:93
  2.3 31.6 %collective-permute-start.5 = (bf16[1,256,384]{2,1,0:T(8,128)(2,1)S(1)}, bf16[1,256,384]{2,1,0:T(8,128)(2,1)}, u32[]{:S(2)}, u32[]{:S(2)}) collective-permute-start(bf16[1,256,384]{2,1,0:T(8,128)(2,1)S(1)} %fusion.108), channel_id=1, source_target_pairs={{0,1},{1,0},{2,3},{3,2},{4,5},{5,4},{6,7},{7,6},{8,9},{9,8},{10,11... | collective-permute-start | bytes 589832 | tf_op jit(solution)/shard_map/ppermute | solution.py:98
  7.4 9.9 %collective-permute-start = (bf16[2,1,128,384]{3,2,1,0:T(8,128)(2,1)}, bf16[2,1,128,384]{3,2,1,0:T(8,128)(2,1)S(1)}, u32[]{:S(2)}, u32[]{:S(2)}) collective-permute-start(bf16[2,1,128,384]{3,2,1,0:T(8,128)(2,1)} %get-tuple-element.18), channel_id=1, source_target_pairs={{0,1},{1,2},{2,3},{3,4},{4,5},{5,6},{6,7},{7,8},{8,9},{9,10},{10,1... | collective-permute-start | bytes 589832 | tf_op jit(solution)/shard_map/ppermute | solution.py:19
  10.4 8.1 %collective-permute-start.1 = (bf16[2,1,128,384]{3,2,1,0:T(8,128)(2,1)}, bf16[2,1,128,384]{3,2,1,0:T(8,128)(2,1)S(1)}, u32[]{:S(2)}, u32[]{:S(2)}) collective-permute-start(bf16[2,1,128,384]{3,2,1,0:T(8,128)(2,1)} %get-tuple-element.17), channel_id=1, source_target_pairs={{1,0},{2,1},{3,2},{4,3},{5,4},{6,5},{7,6},{8,7},{9,8},{10,9},{11,1... | collective-permute-start | bytes 589832 | tf_op jit(solution)/shard_map/ppermute | solution.py:20
  15.5 11.6 %collective-permute-start.3 = (bf16[1,512,384]{2,1,0:T(8,128)(2,1)}, bf16[1,512,384]{2,1,0:T(8,128)(2,1)}, u32[]{:S(2)}, u32[]{:S(2)}) collective-permute-start(bf16[1,512,384]{2,1,0:T(8,128)(2,1)} %pad_maximum_fusion.2), channel_id=1, source_target_pairs={{0,4},{1,9},{2,6},{3,11},{4,0},{5,13},{6,2},{7,15},{8,12},{9,1},{1... | collective-permute-start | bytes 1179656 | tf_op jit(solution)/shard_map/ppermute | solution.py:93
  29.0 11.5 %collective-permute-start.4 = (bf16[1,1024,384]{2,1,0:T(8,128)(2,1)}, bf16[1,1024,384]{2,1,0:T(8,128)(2,1)}, u32[]{:S(2)}, u32[]{:S(2)}) collective-permute-start(bf16[1,1024,384]{2,1,0:T(8,128)(2,1)} %pad_maximum_fusion), channel_id=1, source_target_pairs={{0,2},{1,5},{2,0},{3,7},{4,6},{5,1},{6,4},{7,3},{8,10},{9,13},{10,... | collective-permute-start | bytes 2359304 | tf_op jit(solution)/shard_map/ppermute | solution.py:93
  31.1 0.8 copy-start.10
  31.9 4.0 %collective-permute-start.6 = (bf16[1,256,384]{2,1,0:T(8,128)(2,1)S(1)}, bf16[1,256,384]{2,1,0:T(8,128)(2,1)S(1)}, u32[]{:S(2)}, u32[]{:S(2)}) collective-permute-start(bf16[1,256,384]{2,1,0:T(8,128)(2,1)S(1)} %collective-permute-done.2), channel_id=1, source_target_pairs={{0,1},{1,0},{2,3},{3,2},{4,5},{5,4},{6,7},{7,6},{8,9},{9,8},{10,11... | collective-permute-start | bytes 589832 | tf_op jit(solution)/shard_map/ppermute | solution.py:98
  35.9 9.6 %collective-permute-start.7 = (bf16[1,512,384]{2,1,0:T(8,128)(2,1)}, bf16[1,512,384]{2,1,0:T(8,128)(2,1)}, u32[]{:S(2)}, u32[]{:S(2)}) collective-permute-start(bf16[1,512,384]{2,1,0:T(8,128)(2,1)} %collective-permute-done.3), channel_id=1, source_target_pairs={{0,1},{1,0},{2,3},{3,2},{4,5},{5,4},{6,7},{7,6},{8,9},{9,8},{10,11... | collective-permute-start | bytes 1179656 | tf_op jit(solution)/shard_map/ppermute | solution.py:98
  35.9 12.7 %copy-start.8 = (bf16[1,256,384]{2,1,0:T(8,128)(2,1)}, bf16[1,256,384]{2,1,0:T(8,128)(2,1)S(1)}, u32[]{:S(2)}) copy-start(bf16[1,256,384]{2,1,0:T(8,128)(2,1)S(1)} %collective-permute-done.6) | copy-start | bytes 589828
  40.5 11.8 %collective-permute-start.8 = (bf16[1,1024,384]{2,1,0:T(8,128)(2,1)}, bf16[1,1024,384]{2,1,0:T(8,128)(2,1)}, u32[]{:S(2)}, u32[]{:S(2)}) collective-permute-start(bf16[1,1024,384]{2,1,0:T(8,128)(2,1)} %collective-permute-done.4), channel_id=1, source_target_pairs={{0,1},{1,0},{2,3},{3,2},{4,5},{5,4},{6,7},{7,6},{8,9},{9,8},{10,11... | collective-permute-start | bytes 2359304 | tf_op jit(solution)/shard_map/ppermute | solution.py:98
  52.2 7.8 %copy-start.1 = (bf16[384,384]{1,0:T(8,128)(2,1)S(1)}, bf16[384,384]{1,0:T(8,128)(2,1)}, u32[]{:S(2)}) copy-start(bf16[384,384]{1,0:T(8,128)(2,1)} %param.14) | copy-start | bytes 884740
  61.5 4.8 %copy-start.4 = (f32[256,512]{1,0:T(8,128)S(1)}, f32[256,512]{1,0:T(8,128)}, u32[]{:S(2)}) copy-start(f32[256,512]{1,0:T(8,128)} %get-tuple-element.26) | copy-start | bytes 1572868
  68.7 5.8 %copy-start.6 = (f32[256,384]{1,0:T(8,128)S(1)}, f32[256,384]{1,0:T(8,128)}, u32[]{:S(2)}) copy-start(f32[256,384]{1,0:T(8,128)} %fusion.15) | copy-start | bytes 1179652
  68.7 5.8 %copy-start.9 = (bf16[1,256,384]{2,1,0:T(8,128)(2,1)S(1)}, bf16[1,256,384]{2,1,0:T(8,128)(2,1)}, u32[]{:S(2)}) copy-start(bf16[1,256,384]{2,1,0:T(8,128)(2,1)} %copy-done.8) | copy-start | bytes 589828
  74.5 4.1 %copy-start.3 = (bf16[1,2,128,384]{3,2,1,0:T(8,128)(2,1)S(1)}, bf16[1,2,128,384]{3,2,1,0:T(8,128)(2,1)}, u32[]{:S(2)}) copy-start(bf16[1,2,128,384]{3,2,1,0:T(8,128)(2,1)} %param.10) | copy-start | bytes 589828
  76.1 2.5 %copy-start.12 = (bf16[384,384]{1,0:T(8,128)(2,1)S(1)}, bf16[384,384]{1,0:T(8,128)(2,1)}, u32[]{:S(2)}) copy-start(bf16[384,384]{1,0:T(8,128)(2,1)} %param.15) | copy-start | bytes 884740
  76.1 2.9 %copy-start.14 = (f32[384]{0:T(512)S(1)}, f32[384]{0:T(512)}, u32[]{:S(2)}) copy-start(f32[384]{0:T(512)} %param.17) | copy-start | bytes 4612
  76.1 10.7 %copy-start.11 = (bf16[4,1,8,17,384]{4,2,3,0,1:T(8,128)(2,1)S(1)}, bf16[4,1,8,17,384]{4,2,3,0,1:T(8,128)(2,1)}, u32[]{:S(2)}) copy-start(bf16[4,1,8,17,384]{4,2,3,0,1:T(8,128)(2,1)} %copy-done.10) | copy-start | bytes 1253380
  76.1 10.7 %copy-start.13 = (bf16[4,1,7,2,384]{4,2,3,0,1:T(8,128)(2,1)S(1)}, bf16[4,1,7,2,384]{4,2,3,0,1:T(8,128)(2,1)}, u32[]{:S(2)}) copy-start(bf16[4,1,7,2,384]{4,2,3,0,1:T(8,128)(2,1)} %slice.169) | copy-start | bytes 129028
  76.1 10.7 %copy-start.15 = (pred[8,17]{0,1:T(8,128)(4,1)S(1)}, pred[8,17]{0,1:T(8,128)(4,1)}, u32[]{:S(2)}) copy-start(pred[8,17]{0,1:T(8,128)(4,1)} %constant.36) | copy-start | bytes 412
  78.6 12.7 %slice-start = ((s8[7962624]{0:T(1024)(128)(4,1)}), s8[4194304]{0:T(1024)(128)(4,1)S(1)}, s32[]{:S(2)}) async-start(s8[7962624]{0:T(1024)(128)(4,1)} %bitcast.441), calls=%async_computation | async-start | bytes 8388608
  79.7 10.6 %collective-permute-start.10 = (bf16[1,1,128,384]{3,1,2,0:T(2,128)(2,1)S(1)}, bf16[1,1,128,384]{3,1,2,0:T(2,128)(2,1)S(1)}, u32[]{:S(2)}, u32[]{:S(2)}) collective-permute-start(bf16[1,1,128,384]{3,1,2,0:T(2,128)(2,1)S(1)} %get-tuple-element.22), channel_id=1, source_target_pairs={{1,0},{2,1},{3,2},{4,3},{5,4},{6,5},{7,6},{8,7},{9,8},{10,9},{11,1... | collective-permute-start | bytes 294920 | tf_op jit(solution)/shard_map/ppermute | solution.py:20
  81.8 8.0 %copy-start.7 = (bf16[4,1,128,384]{3,2,0,1:T(8,128)(2,1)S(1)}, bf16[4,1,128,384]{3,2,0,1:T(8,128)(2,1)}, u32[]{:S(2)}) copy-start(bf16[4,1,128,384]{3,2,0,1:T(8,128)(2,1)} %get-tuple-element.15) | copy-start | bytes 1179652
  81.8 9.5 %slice-start.1 = ((s8[7962624]{0:T(1024)(128)(4,1)}), s8[3768320]{0:T(1024)(128)(4,1)S(1)}, s32[]{:S(2)}) async-start(s8[7962624]{0:T(1024)(128)(4,1)} %bitcast.441), calls=%async_computation.1 | async-start | bytes 7536640
  81.8 8.5 %collective-permute-start.9 = (bf16[1,1,128,384]{3,1,2,0:T(2,128)(2,1)S(1)}, bf16[1,1,128,384]{3,1,2,0:T(2,128)(2,1)S(1)}, u32[]{:S(2)}, u32[]{:S(2)}) collective-permute-start(bf16[1,1,128,384]{3,1,2,0:T(2,128)(2,1)S(1)} %get-tuple-element.21), channel_id=1, source_target_pairs={{0,1},{1,2},{2,3},{3,4},{4,5},{5,6},{6,7},{7,8},{8,9},{9,10},{10,1... | collective-permute-start | bytes 294920 | tf_op jit(solution)/shard_map/ppermute | solution.py:19
  93.9 6.5 %collective-permute-start.11 = (bf16[1,1,128,384]{3,2,1,0:T(8,128)(2,1)S(1)}, bf16[1,1,128,384]{3,2,1,0:T(8,128)(2,1)S(1)}, u32[]{:S(2)}, u32[]{:S(2)}) collective-permute-start(bf16[1,1,128,384]{3,2,1,0:T(8,128)(2,1)S(1)} %slice.174), channel_id=1, source_target_pairs={{0,1},{1,2},{2,3},{3,4},{4,5},{5,6},{6,7},{7,8},{8,9},{9,10},{10,1... | collective-permute-start | bytes 294920 | tf_op jit(solution)/shard_map/ppermute | solution.py:19
  98.1 6.8 %collective-permute-start.12 = (bf16[1,1,128,384]{3,2,1,0:T(8,128)(2,1)S(1)}, bf16[1,1,128,384]{3,2,1,0:T(8,128)(2,1)S(1)}, u32[]{:S(2)}, u32[]{:S(2)}) collective-permute-start(bf16[1,1,128,384]{3,2,1,0:T(8,128)(2,1)S(1)} %slice.177), channel_id=1, source_target_pairs={{1,0},{2,1},{3,2},{4,3},{5,4},{6,5},{7,6},{8,7},{9,8},{10,9},{11,1... | collective-permute-start | bytes 294920 | tf_op jit(solution)/shard_map/ppermute | solution.py:20

commit v5 on v4

--- a/solution.py
+++ b/solution.py
@@ -30,6 +30,12 @@
     return jnp.einsum("fqc,cd->fqd", inputs, weight, preferred_element_type=jnp.float32).astype(
         jnp.bfloat16
     )
+
+
+def split_pair(values, axis):
+    high = values.astype(jnp.bfloat16)
+    low = (values - high.astype(jnp.float32)).astype(jnp.bfloat16)
+    return jnp.concatenate([high, low], axis=axis)
 
 
 def conv_rows(haloed, weight):
@@ -96,20 +102,24 @@
             held = jnp.concatenate([held, other], axis=1)
     swap = [(i, i ^ 1) for i in range(size)]
     pieces = mine + [lax.ppermute(piece, ROWS, swap) for piece in mine]
-    scores, values = [], []
+    q_keyed = jnp.einsum("fqc,dc->fqd", queries, w_key, preferred_element_type=jnp.float32)
+    q_pair = split_pair(q_keyed, axis=1)
+    count = queries.shape[1]
+    scores = []
     for piece in pieces:
-        keys = project(piece, w_key)
-        values.append(project(piece, w_value))
-        scores.append(
-            jnp.einsum("fqc,fkc->fqk", queries, keys, preferred_element_type=jnp.float32) * scale
-        )
+        both = jnp.einsum("fqc,fkc->fqk", q_pair, piece, preferred_element_type=jnp.float32)
+        scores.append((both[:, :count] + both[:, count:]) * scale)
     top = jnp.max(jnp.stack([jnp.max(s, axis=-1) for s in scores], axis=-1), axis=-1)[..., None]
     expos = [jnp.exp(s - top) for s in scores]
     denom = sum(jnp.sum(e, axis=-1, keepdims=True) for e in expos)
-    numer = sum(
-        jnp.einsum("fqk,fkc->fqc", e.astype(jnp.bfloat16), v, preferred_element_type=jnp.float32)
-        for e, v in zip(expos, values)
+    mixed_in = sum(
+        jnp.einsum("fqk,fkc->fqc", e.astype(jnp.bfloat16), p, preferred_element_type=jnp.float32)
+        for e, p in zip(expos, pieces)
     )
+    both = jnp.einsum(
+        "fqc,cd->fqd", split_pair(mixed_in, axis=1), w_value, preferred_element_type=jnp.float32
+    )
+    numer = both[:, :count] + both[:, count:]
     attended = (numer / denom).astype(jnp.bfloat16)
     mixed = (
         flat.astype(jnp.float32)

time: 110 us -> 77.7 us (0.71)
  the two profiles are of different devices: /device:TPU:5 before, /device:TPU:10 now
where the time goes in v5:
time: 77.7 us; the launch traced here: 77.3 us
  starting transfers between devices  23 us (30%)
  waiting for transfers between devices  23 us (30%)
  matrix products  13.9 us (18%)
  local copies, waits for them, and re-layouts  8.57 us (11%)
  other arithmetic  8.08 us (10%)
    ppermute x3, waiting for transfers between devices, body(): other = lax.ppermute(held, ROWS, perm)  14.3 us
    ppermute x3, starting transfers between devices, padded_2(): after = lax.ppermute(first, axis, down)  10.9 us
    ppermute x3, waiting for transfers between devices, padded_2(): before = lax.ppermute(last, axis, up)  8.02 us
    ppermute x3, starting transfers between devices, padded_2(): before = lax.ppermute(last, axis, up)  6.91 us
    ppermute x3, starting transfers between devices, body(): other = lax.ppermute(held, ROWS, perm)  5.04 us
    dot_general x8, matrix products, body(): jnp.einsum('fqc,fkc->fqk', q_pair, piece, preferred_element_type=jnp.floa...  3.7 us
    conv_general_dilated x3, matrix products, conv_rows(): lax.conv_general_dilated(haloed[tstep:tstep + 1], weight[tstep], window_s...  3.59 us
    convert_element_type x3, other arithmetic, body(): normed = rms_gain(flat.astype(jnp.float32), norm_attn).astype(jnp.bfloat16)  3.13 us
  transfers between devices with their start and end apart: 13, of which 5 were waited for; matrix products, arithmetic and copies ran while one was open for 18% of the time, Pallas kernels for 0%

profile of v5, /device:TPU:10, one launch (start us, length us, event | category | flops | bytes accessed | tf_op | source)
XLA Modules:
  0.0 77.3 jit_solution(6985828821108299858)
XLA Ops:
  0.0 1.2 %fusion.110 = f32[2,128]{1,0:T(2,128)S(1)} fusion(bf16[1,2,128,384]{3,2,1,0:T(8,128)(2,1)} %param.10), kind=kLoop, calls=%fused_computation.128 | loop fusion | flops 294656 | bytes 197632 | tf_op jit(solution)/shard_map/reduce_sum | solution.py:26
  1.2 1.0 %fusion.107 = bf16[1,256,384]{2,1,0:T(8,128)(2,1)S(1)} fusion(bf16[1,2,128,384]{3,2,1,0:T(8,128)(2,1)} %param.10, f32[384]{0:T(512)} %param.11, f32[256]{0:T(256)S(1)} %get-tuple-element.28), kind=kLoop, calls=%fused_computation.122 | loop fusion | flops 393216 | bytes 395776 | tf_op jit(solution)/shard_map/convert_element_type | solution.py:91
  2.2 2.7 %collective-permute-start.2 = (bf16[1,256,384]{2,1,0:T(8,128)(2,1)S(1)}, bf16[1,256,384]{2,1,0:T(8,128)(2,1)S(1)}, u32[]{:S(2)}, u32[]{:S(2)}) collective-permute-start(bf16[1,256,384]{2,1,0:T(8,128)(2,1)S(1)} %fusion.107), channel_id=1, source_target_pairs={{0,8},{1,3},{2,10},{3,1},{4,12},{5,7},{6,14},{7,5},{8,0},{9,11},{1... | collective-permute-start | bytes 589832 | tf_op jit(solution)/shard_map/ppermute | solution.py:99
  4.9 1.8 %fusion.230 = (bf16[2,1,128,384]{3,2,1,0:T(8,128)(2,1)}, bf16[2,1,128,384]{3,2,1,0:T(8,128)(2,1)}) fusion(bf16[2,2,128,384]{3,2,1,0:T(8,128)(2,1)} %param.16), kind=kLoop, calls=%fused_computation.282 | loop fusion | bytes 786432 | tf_op jit(solution)/shard_map/slice | solution.py:18
  6.7 2.4 %collective-permute-start = (bf16[2,1,128,384]{3,2,1,0:T(8,128)(2,1)}, bf16[2,1,128,384]{3,2,1,0:T(8,128)(2,1)}, u32[]{:S(2)}, u32[]{:S(2)}) collective-permute-start(bf16[2,1,128,384]{3,2,1,0:T(8,128)(2,1)} %get-tuple-element.18), channel_id=1, source_target_pairs={{0,1},{1,2},{2,3},{3,4},{4,5},{5,6},{6,7},{7,8},{8,9},{9,10},{10,1... | collective-permute-start | bytes 589832 | tf_op jit(solution)/shard_map/ppermute | solution.py:19
  9.1 4.0 %collective-permute-start.1 = (bf16[2,1,128,384]{3,2,1,0:T(8,128)(2,1)}, bf16[2,1,128,384]{3,2,1,0:T(8,128)(2,1)}, u32[]{:S(2)}, u32[]{:S(2)}) collective-permute-start(bf16[2,1,128,384]{3,2,1,0:T(8,128)(2,1)} %get-tuple-element.17), channel_id=1, source_target_pairs={{1,0},{2,1},{3,2},{4,3},{5,4},{6,5},{7,6},{8,7},{9,8},{10,9},{11,1... | collective-permute-start | bytes 589832 | tf_op jit(solution)/shard_map/ppermute | solution.py:20
  13.2 1.0 %fusion.109 = bf16[256,384]{1,0:T(8,128)(2,1)S(1)} fusion(bf16[1,2,128,384]{3,2,1,0:T(8,128)(2,1)} %param.10, f32[384]{0:T(512)} %param.11, f32[256]{0:T(256)S(1)} %get-tuple-element.28), kind=kLoop, calls=%fused_computation.125 | loop fusion | flops 393216 | bytes 395776 | tf_op jit(solution)/shard_map/convert_element_type | solution.py:91
  14.2 1.0 %fusion.112 = bf16[1,2,128,384]{3,2,1,0:T(8,128)(2,1)S(1)} fusion(bf16[1,2,128,384]{3,2,1,0:T(8,128)(2,1)} %param.10, f32[384]{0:T(512)} %param.11, f32[2,128]{1,0:T(2,128)S(1)} %get-tuple-element.27), kind=kLoop, calls=%fused_computation.130 | loop fusion | flops 393216 | bytes 395776 | tf_op jit(solution)/shard_map/convert_element_type | solution.py:91
  15.3 1.5 %convert_bitcast_fusion.1 = (bf16[1,256,384]{2,1,0:T(8,128)(2,1)S(1)}, bf16[1,256,384]{2,1,0:T(8,128)(2,1)S(1)}) fusion(bf16[384,384]{1,0:T(8,128)(2,1)S(1)} %copy-done.3, bf16[256,384]{1,0:T(8,128)(2,1)S(1)} %fusion.109, bf16[384,384]{1,0:T(8,128)(2,1)} %param.12), kind=kOutput, calls=%fused_computation.251 | convolution fusion | flops 151486464 | bytes 1179648 | tf_op jit(solution)/shard_map/fqc,dc->fqd/dot_general | solution.py:105
  16.8 0.3 convolution_bitcast_fusion.9
  17.3 0.9 %constant_dynamic-update-slice_fusion.2 = bf16[2,4,128,384]{3,2,1,0:T(8,128)(2,1)S(1)} fusion(bf16[2,1,128,384]{3,2,1,0:T(8,128)(2,1)} %collective-permute-done), kind=kLoop, calls=%fused_computation.254 | loop fusion | bytes 393216
  18.4 1.0 %constant_dynamic-update-slice_fusion = bf16[2,4,128,384]{3,2,1,0:T(8,128)(2,1)S(1)} fusion(bf16[2,4,128,384]{3,2,1,0:T(8,128)(2,1)S(1)} %constant_dynamic-update-slice_fusion.1, bf16[2,1,128,384]{3,2,1,0:T(8,128)(2,1)} %collective-permute-done.1), kind=kLoop, calls=%fused_computation.252 | loop fusion | bytes 393216 | tf_op jit(solution)/shard_map/concatenate | solution.py:21
  19.4 0.3 copy.104
  20.1 0.3 convolution_bitcast_fusion.8
  20.4 5.7 %collective-permute-done.3 = bf16[1,512,384]{2,1,0:T(8,128)(2,1)S(1)} collective-permute-done((bf16[1,512,384]{2,1,0:T(8,128)(2,1)S(1)}, bf16[1,512,384]{2,1,0:T(8,128)(2,1)S(1)}, u32[]{:S(2)}, u32[]{:S(2)}) %collective-permute-start.3) | collective-permute-done | bytes 393248 | tf_op jit(solution)/shard_map/ppermute | solution.py:99
  26.2 2.3 %collective-permute-start.4 = (bf16[1,1024,384]{2,1,0:T(8,128)(2,1)S(1)}, bf16[1,1024,384]{2,1,0:T(8,128)(2,1)S(1)}, u32[]{:S(2)}, u32[]{:S(2)}) collective-permute-start(bf16[1,1024,384]{2,1,0:T(8,128)(2,1)S(1)} %pad_maximum_fusion), channel_id=1, source_target_pairs={{0,2},{1,5},{2,0},{3,7},{4,6},{5,1},{6,4},{7,3},{8,10},{9,13},{10,... | collective-permute-start | bytes 2359304 | tf_op jit(solution)/shard_map/ppermute | solution.py:99
  28.5 0.3 convolution_bitcast_fusion.7
  29.0 0.3 convolution_bitcast_fusion.6
  29.5 0.5 convolution_bitcast_fusion.4
  29.9 8.6 %collective-permute-done.4 = bf16[1,1024,384]{2,1,0:T(8,128)(2,1)S(1)} collective-permute-done((bf16[1,1024,384]{2,1,0:T(8,128)(2,1)S(1)}, bf16[1,1024,384]{2,1,0:T(8,128)(2,1)S(1)}, u32[]{:S(2)}, u32[]{:S(2)}) %collective-permute-start.4) | collective-permute-done | bytes 786464 | tf_op jit(solution)/shard_map/ppermute | solution.py:99
  38.6 0.5 convolution_bitcast_fusion.3
  39.2 0.7 convolution_bitcast_fusion.2
  40.1 0.7 collective-permute-done.8
  40.8 0.7 convolution_bitcast_fusion.1
  41.7 0.5 fusion.41
  43.0 0.5 fusion.46
  43.5 0.3 fusion.100
  44.2 0.5 fusion.49
  44.7 0.3 fusion.103
  45.4 0.3 convert_bitcast_fusion
  45.7 0.5 copy-done.4
  46.2 0.4 convolution_bitcast_fusion.5
  46.6 0.4 multiply_reduce_fusion
  47.8 4.9 %collective-permute-start.10 = (bf16[1,1,128,384]{3,1,2,0:T(2,128)(2,1)S(1)}, bf16[1,1,128,384]{3,1,2,0:T(2,128)(2,1)S(1)}, u32[]{:S(2)}, u32[]{:S(2)}) collective-permute-start(bf16[1,1,128,384]{3,1,2,0:T(2,128)(2,1)S(1)} %get-tuple-element.26), channel_id=1, source_target_pairs={{1,0},{2,1},{3,2},{4,3},{5,4},{6,5},{7,6},{8,7},{9,8},{10,9},{11,1... | collective-permute-start | bytes 294920 | tf_op jit(solution)/shard_map/ppermute | solution.py:20
  52.7 2.1 %collective-permute-start.9 = (bf16[1,1,128,384]{3,1,2,0:T(2,128)(2,1)S(1)}, bf16[1,1,128,384]{3,1,2,0:T(2,128)(2,1)S(1)}, u32[]{:S(2)}, u32[]{:S(2)}) collective-permute-start(bf16[1,1,128,384]{3,1,2,0:T(2,128)(2,1)S(1)} %get-tuple-element.25), channel_id=1, source_target_pairs={{0,1},{1,2},{2,3},{3,4},{4,5},{5,6},{6,7},{7,8},{8,9},{9,10},{10,1... | collective-permute-start | bytes 294920 | tf_op jit(solution)/shard_map/ppermute | solution.py:19
  54.9 1.2 %fusion.29 = f32[2,8,17,384]{3,1,2,0:T(8,128)S(1)} fusion(bf16[3,3,3,384,384]{4,3,2,1,0:T(8,128)(2,1)S(1)} %bitcast.466, bf16[4,1,7,2,384]{4,2,3,0,1:T(8,128)(2,1)S(1)} %slice.241, bf16[4,1,8,17,384]{4,2,3,0,1:T(8,128)(2,1)S(1)} %copy.41, pred[8,17]{0,1:T(8,128)(4,1)S(1)} %copy-done.7), kind=kOutput, calls=%fused_computation.37 | convolution fusion | flops 723449856 | bytes 3542016 | tf_op jit(solution)/shard_map/conv_general_dilated | solution.py:44
  56.1 0.3 copy.103
  56.6 4.0 %collective-permute-done.9 = bf16[1,1,128,384]{3,1,2,0:T(2,128)(2,1)S(1)} collective-permute-done((bf16[1,1,128,384]{3,1,2,0:T(2,128)(2,1)S(1)}, bf16[1,1,128,384]{3,1,2,0:T(2,128)(2,1)S(1)}, u32[]{:S(2)}, u32[]{:S(2)}) %collective-permute-start.9) | collective-permute-done | bytes 98336 | tf_op jit(solution)/shard_map/ppermute | solution.py:19
  60.6 0.7 maximum_bitcast_fusion.3
  61.5 1.2 %fusion.32 = f32[2,8,17,384]{3,1,2,0:T(8,128)S(1)} fusion(bf16[3,3,3,384,384]{4,3,2,1,0:T(8,128)(2,1)S(1)} %bitcast.466, bf16[4,1,7,2,384]{4,2,3,0,1:T(8,128)(2,1)S(1)} %slice.262, bf16[4,1,8,17,384]{4,2,3,0,1:T(8,128)(2,1)S(1)} %copy.46, pred[8,17]{0,1:T(8,128)(4,1)S(1)} %copy-done.7), kind=kOutput, calls=%fused_computation.38 | convolution fusion | flops 723449856 | bytes 3542016 | tf_op jit(solution)/shard_map/conv_general_dilated | solution.py:44
  62.7 1.2 %fusion.26 = bf16[2,8,17,384]{3,1,2,0:T(8,128)(2,1)S(1)} fusion(f32[2,8,17,384]{3,1,2,0:T(8,128)S(1)} %fusion.32, f32[2,8,17,384]{3,1,2,0:T(8,128)S(1)} %fusion.29, bf16[3,3,3,384,384]{4,3,2,1,0:T(8,128)(2,1)S(1)} %bitcast.466, bf16[4,1,7,2,384]{4,2,3,0,1:T(8,128)(2,1)S(1)} %slice.239, bf16[4,1,8,17,384]{4,2,3,0,1:T(8,128)(2,1)S(1)} %copy.38, ...), kind=kOutput, calls=%fused_computation.36 | convolution fusion | flops 723763200 | bytes 4168704 | tf_op jit(solution)/shard_map/conv_general_dilated | solution.py:44
  64.1 1.9 %collective-permute-start.12 = (bf16[1,1,128,384]{3,2,1,0:T(8,128)(2,1)S(1)}, bf16[1,1,128,384]{3,2,1,0:T(8,128)(2,1)S(1)}, u32[]{:S(2)}, u32[]{:S(2)}) collective-permute-start(bf16[1,1,128,384]{3,2,1,0:T(8,128)(2,1)S(1)} %slice.267), channel_id=1, source_target_pairs={{1,0},{2,1},{3,2},{4,3},{5,4},{6,5},{7,6},{8,7},{9,8},{10,9},{11,1... | collective-permute-start | bytes 294920 | tf_op jit(solution)/shard_map/ppermute | solution.py:20
  66.1 2.4 %collective-permute-start.11 = (bf16[1,1,128,384]{3,2,1,0:T(8,128)(2,1)S(1)}, bf16[1,1,128,384]{3,2,1,0:T(8,128)(2,1)S(1)}, u32[]{:S(2)}, u32[]{:S(2)}) collective-permute-start(bf16[1,1,128,384]{3,2,1,0:T(8,128)(2,1)S(1)} %slice.264), channel_id=1, source_target_pairs={{0,1},{1,2},{2,3},{3,4},{4,5},{5,6},{6,7},{7,8},{8,9},{9,10},{10,1... | collective-permute-start | bytes 294920 | tf_op jit(solution)/shard_map/ppermute | solution.py:19
  68.9 4.1 %collective-permute-done.11 = bf16[1,1,128,384]{3,2,1,0:T(8,128)(2,1)S(1)} collective-permute-done((bf16[1,1,128,384]{3,2,1,0:T(8,128)(2,1)S(1)}, bf16[1,1,128,384]{3,2,1,0:T(8,128)(2,1)S(1)}, u32[]{:S(2)}, u32[]{:S(2)}) %collective-permute-start.11) | collective-permute-done | bytes 98336 | tf_op jit(solution)/shard_map/ppermute | solution.py:19
  72.9 1.5 %convolution_bitcast_fusion = f32[1,4,130,3,3,192]{5,2,4,3,1,0:T(8,128)S(1)} fusion(bf16[3,3,384,192]{2,3,1,0:T(8,128)(2,1)S(1)} %copy-done, bf16[1,1,128,384]{3,2,1,0:T(8,128)(2,1)S(1)} %collective-permute-done.12, bf16[1,2,128,384]{3,2,1,0:T(8,128)(2,1)S(1)} %bitcast.463, bf16[1,1,128,384]{3,2,1,0:T(8,128)(2,1)S(1)} %collective-permute-done.11), kind=kOutput, calls=%fused_computation.9 | convolution fusion | flops 692490240 | bytes 5314560 | tf_op jit(solution)/shard_map/frwc,ijco->frwijo/dot_general | solution.py:61
  74.4 0.4 fusion.195
  75.4 0.5 copy.76
  76.0 1.3 %convert_element_type.181 = bf16[1,4,49152]{2,1,0:T(4,128)(2,1)} reshape(bf16[1,2,2,128,2,192]{5,4,3,2,1,0:T(2,128)(2,1)S(1)} %copy.76) | data formatting | bytes 786432 | tf_op jit(solution)/shard_map/convert_element_type | solution.py:78
  (80 shorter events, 5.2 us)
Async XLA Ops:
  0.0 72.9 %copy-start = (bf16[3,3,384,192]{2,3,1,0:T(8,128)(2,1)S(1)}, bf16[3,3,384,192]{2,3,1,0:T(8,128)(2,1)}, u32[]{:S(2)}) copy-start(bf16[3,3,384,192]{2,3,1,0:T(8,128)(2,1)} %param.19) | copy-start | bytes 3981316
  0.0 15.3 %copy-start.3 = (bf16[384,384]{1,0:T(8,128)(2,1)S(1)}, bf16[384,384]{1,0:T(8,128)(2,1)}, u32[]{:S(2)}) copy-start(bf16[384,384]{1,0:T(8,128)(2,1)} %param.13) | copy-start | bytes 884740
  2.2 15.0 %collective-permute-start.2 = (bf16[1,256,384]{2,1,0:T(8,128)(2,1)S(1)}, bf16[1,256,384]{2,1,0:T(8,128)(2,1)S(1)}, u32[]{:S(2)}, u32[]{:S(2)}) collective-permute-start(bf16[1,256,384]{2,1,0:T(8,128)(2,1)S(1)} %fusion.107), channel_id=1, source_target_pairs={{0,8},{1,3},{2,10},{3,1},{4,12},{5,7},{6,14},{7,5},{8,0},{9,11},{1... | collective-permute-start | bytes 589832 | tf_op jit(solution)/shard_map/ppermute | solution.py:99
  4.9 23.7 %collective-permute-start.5 = (bf16[1,256,384]{2,1,0:T(8,128)(2,1)S(1)}, bf16[1,256,384]{2,1,0:T(8,128)(2,1)S(1)}, u32[]{:S(2)}, u32[]{:S(2)}) collective-permute-start(bf16[1,256,384]{2,1,0:T(8,128)(2,1)S(1)} %fusion.107), channel_id=1, source_target_pairs={{0,1},{1,0},{2,3},{3,2},{4,5},{5,4},{6,7},{7,6},{8,9},{9,8},{10,11... | collective-permute-start | bytes 589832 | tf_op jit(solution)/shard_map/ppermute | solution.py:104
  6.7 10.6 %collective-permute-start = (bf16[2,1,128,384]{3,2,1,0:T(8,128)(2,1)}, bf16[2,1,128,384]{3,2,1,0:T(8,128)(2,1)}, u32[]{:S(2)}, u32[]{:S(2)}) collective-permute-start(bf16[2,1,128,384]{3,2,1,0:T(8,128)(2,1)} %get-tuple-element.18), channel_id=1, source_target_pairs={{0,1},{1,2},{2,3},{3,4},{4,5},{5,6},{6,7},{7,8},{8,9},{9,10},{10,1... | collective-permute-start | bytes 589832 | tf_op jit(solution)/shard_map/ppermute | solution.py:19
  9.1 9.3 %collective-permute-start.1 = (bf16[2,1,128,384]{3,2,1,0:T(8,128)(2,1)}, bf16[2,1,128,384]{3,2,1,0:T(8,128)(2,1)}, u32[]{:S(2)}, u32[]{:S(2)}) collective-permute-start(bf16[2,1,128,384]{3,2,1,0:T(8,128)(2,1)} %get-tuple-element.17), channel_id=1, source_target_pairs={{1,0},{2,1},{3,2},{4,3},{5,4},{6,5},{7,6},{8,7},{9,8},{10,9},{11,1... | collective-permute-start | bytes 589832 | tf_op jit(solution)/shard_map/ppermute | solution.py:20
  15.3 3.0 %copy-start.2 = (bf16[2,2,128,384]{3,2,1,0:T(8,128)(2,1)S(1)}, bf16[2,2,128,384]{3,2,1,0:T(8,128)(2,1)}, u32[]{:S(2)}) copy-start(bf16[2,2,128,384]{3,2,1,0:T(8,128)(2,1)} %param.16) | copy-start | bytes 1179652
  17.2 8.9 %collective-permute-start.3 = (bf16[1,512,384]{2,1,0:T(8,128)(2,1)S(1)}, bf16[1,512,384]{2,1,0:T(8,128)(2,1)S(1)}, u32[]{:S(2)}, u32[]{:S(2)}) collective-permute-start(bf16[1,512,384]{2,1,0:T(8,128)(2,1)S(1)} %pad_maximum_fusion.2), channel_id=1, source_target_pairs={{0,4},{1,9},{2,6},{3,11},{4,0},{5,13},{6,2},{7,15},{8,12},{9,1},{1... | collective-permute-start | bytes 1179656 | tf_op jit(solution)/shard_map/ppermute | solution.py:99
  20.0 9.0 %collective-permute-start.6 = (bf16[1,256,384]{2,1,0:T(8,128)(2,1)S(1)}, bf16[1,256,384]{2,1,0:T(8,128)(2,1)S(1)}, u32[]{:S(2)}, u32[]{:S(2)}) collective-permute-start(bf16[1,256,384]{2,1,0:T(8,128)(2,1)S(1)} %collective-permute-done.2), channel_id=1, source_target_pairs={{0,1},{1,0},{2,3},{3,2},{4,5},{5,4},{6,7},{7,6},{8,9},{9,8},{10,11... | collective-permute-start | bytes 589832 | tf_op jit(solution)/shard_map/ppermute | solution.py:104
  26.2 12.3 %collective-permute-start.4 = (bf16[1,1024,384]{2,1,0:T(8,128)(2,1)S(1)}, bf16[1,1024,384]{2,1,0:T(8,128)(2,1)S(1)}, u32[]{:S(2)}, u32[]{:S(2)}) collective-permute-start(bf16[1,1024,384]{2,1,0:T(8,128)(2,1)S(1)} %pad_maximum_fusion), channel_id=1, source_target_pairs={{0,2},{1,5},{2,0},{3,7},{4,6},{5,1},{6,4},{7,3},{8,10},{9,13},{10,... | collective-permute-start | bytes 2359304 | tf_op jit(solution)/shard_map/ppermute | solution.py:99
  29.3 9.3 %collective-permute-start.7 = (bf16[1,512,384]{2,1,0:T(8,128)(2,1)S(1)}, bf16[1,512,384]{2,1,0:T(8,128)(2,1)S(1)}, u32[]{:S(2)}, u32[]{:S(2)}) collective-permute-start(bf16[1,512,384]{2,1,0:T(8,128)(2,1)S(1)} %collective-permute-done.3), channel_id=1, source_target_pairs={{0,1},{1,0},{2,3},{3,2},{4,5},{5,4},{6,7},{7,6},{8,9},{9,8},{10,11... | collective-permute-start | bytes 1179656 | tf_op jit(solution)/shard_map/ppermute | solution.py:104
  38.5 2.3 %collective-permute-start.8 = (bf16[1,1024,384]{2,1,0:T(8,128)(2,1)S(1)}, bf16[1,1024,384]{2,1,0:T(8,128)(2,1)S(1)}, u32[]{:S(2)}, u32[]{:S(2)}) collective-permute-start(bf16[1,1024,384]{2,1,0:T(8,128)(2,1)S(1)} %collective-permute-done.4), channel_id=1, source_target_pairs={{0,1},{1,0},{2,3},{3,2},{4,5},{5,4},{6,7},{7,6},{8,9},{9,8},{10,11... | collective-permute-start | bytes 2359304 | tf_op jit(solution)/shard_map/ppermute | solution.py:104
  42.3 12.5 %slice-start = ((s8[7962624]{0:T(1024)(128)(4,1)}), s8[4194304]{0:T(1024)(128)(4,1)S(1)}, s32[]{:S(2)}) async-start(s8[7962624]{0:T(1024)(128)(4,1)} %bitcast.465), calls=%async_computation | async-start | bytes 8388608
  44.2 10.7 %slice-start.1 = ((s8[7962624]{0:T(1024)(128)(4,1)}), s8[3768320]{0:T(1024)(128)(4,1)S(1)}, s32[]{:S(2)}) async-start(s8[7962624]{0:T(1024)(128)(4,1)} %bitcast.465), calls=%async_computation.1 | async-start | bytes 7536640
  45.0 1.2 %copy-start.4 = (bf16[384,384]{1,0:T(8,128)(2,1)S(1)}, bf16[384,384]{1,0:T(8,128)(2,1)}, u32[]{:S(2)}) copy-start(bf16[384,384]{1,0:T(8,128)(2,1)} %param.14) | copy-start | bytes 884740
  45.3 1.3 %copy-start.1 = (bf16[1,2,128,384]{3,2,1,0:T(8,128)(2,1)S(1)}, bf16[1,2,128,384]{3,2,1,0:T(8,128)(2,1)}, u32[]{:S(2)}) copy-start(bf16[1,2,128,384]{3,2,1,0:T(8,128)(2,1)} %param.10) | copy-start | bytes 589828
  45.3 1.3 %copy-start.6 = (bf16[384,384]{1,0:T(8,128)(2,1)S(1)}, bf16[384,384]{1,0:T(8,128)(2,1)}, u32[]{:S(2)}) copy-start(bf16[384,384]{1,0:T(8,128)(2,1)} %param.15) | copy-start | bytes 884740
  45.6 1.5 %copy-start.5 = (f32[384]{0:T(512)S(1)}, f32[384]{0:T(512)}, u32[]{:S(2)}) copy-start(f32[384]{0:T(512)} %param.17) | copy-start | bytes 4612
  46.6 8.2 %copy-start.7 = (pred[8,17]{0,1:T(8,128)(4,1)S(1)}, pred[8,17]{0,1:T(8,128)(4,1)}, u32[]{:S(2)}) copy-start(pred[8,17]{0,1:T(8,128)(4,1)} %constant.36) | copy-start | bytes 412
  47.8 8.8 %collective-permute-start.10 = (bf16[1,1,128,384]{3,1,2,0:T(2,128)(2,1)S(1)}, bf16[1,1,128,384]{3,1,2,0:T(2,128)(2,1)S(1)}, u32[]{:S(2)}, u32[]{:S(2)}) collective-permute-start(bf16[1,1,128,384]{3,1,2,0:T(2,128)(2,1)S(1)} %get-tuple-element.26), channel_id=1, source_target_pairs={{1,0},{2,1},{3,2},{4,3},{5,4},{6,5},{7,6},{8,7},{9,8},{10,9},{11,1... | collective-permute-start | bytes 294920 | tf_op jit(solution)/shard_map/ppermute | solution.py:20
  52.7 7.9 %collective-permute-start.9 = (bf16[1,1,128,384]{3,1,2,0:T(2,128)(2,1)S(1)}, bf16[1,1,128,384]{3,1,2,0:T(2,128)(2,1)S(1)}, u32[]{:S(2)}, u32[]{:S(2)}) collective-permute-start(bf16[1,1,128,384]{3,1,2,0:T(2,128)(2,1)S(1)} %get-tuple-element.25), channel_id=1, source_target_pairs={{0,1},{1,2},{2,3},{3,4},{4,5},{5,6},{6,7},{7,8},{8,9},{9,10},{10,1... | collective-permute-start | bytes 294920 | tf_op jit(solution)/shard_map/ppermute | solution.py:19
  64.1 4.8 %collective-permute-start.12 = (bf16[1,1,128,384]{3,2,1,0:T(8,128)(2,1)S(1)}, bf16[1,1,128,384]{3,2,1,0:T(8,128)(2,1)S(1)}, u32[]{:S(2)}, u32[]{:S(2)}) collective-permute-start(bf16[1,1,128,384]{3,2,1,0:T(8,128)(2,1)S(1)} %slice.267), channel_id=1, source_target_pairs={{1,0},{2,1},{3,2},{4,3},{5,4},{6,5},{7,6},{8,7},{9,8},{10,9},{11,1... | collective-permute-start | bytes 294920 | tf_op jit(solution)/shard_map/ppermute | solution.py:20
  66.1 6.8 %collective-permute-start.11 = (bf16[1,1,128,384]{3,2,1,0:T(8,128)(2,1)S(1)}, bf16[1,1,128,384]{3,2,1,0:T(8,128)(2,1)S(1)}, u32[]{:S(2)}, u32[]{:S(2)}) collective-permute-start(bf16[1,1,128,384]{3,2,1,0:T(8,128)(2,1)S(1)} %slice.264), channel_id=1, source_target_pairs={{0,1},{1,2},{2,3},{3,4},{4,5},{5,6},{6,7},{7,8},{8,9},{9,10},{10,1... | collective-permute-start | bytes 294920 | tf_op jit(solution)/shard_map/ppermute | solution.py:19

commit v6 on v5

--- a/solution.py
+++ b/solution.py
@@ -84,7 +84,7 @@
     nframes, nrows, ncols, chans = frames.shape
     scale = chans ** (-0.5)
 
-    cache_haloed = padded_2(cache_one, ((ROWS, 1),), 1)
+    cache_haloed = padded_2(cache_one, ((ROWS, 1),), 2)
     cache_part = conv_rows(cache_haloed, conv_weight[:2])
 
     flat = frames.reshape(nframes, nrows * ncols, chans)
@@ -130,9 +130,12 @@
         .astype(jnp.bfloat16)
         .reshape(nframes, nrows, ncols, chans)
     )
-    activ_haloed = padded_2(activ, ((ROWS, 1),), 1)
-    conv_out = (cache_part + conv_rows(activ_haloed, conv_weight[2:])).astype(jnp.bfloat16)
-    extended = padded_2(conv_out, ((ROWS, 1),), 1)
+    activ_haloed = padded_2(activ, ((ROWS, 1),), 2)
+    extended = cache_part + conv_rows(activ_haloed, conv_weight[2:])
+    where = lax.axis_index(ROWS)
+    line = jnp.arange(nrows + 2)
+    inside = ((line > 0) | (where > 0)) & ((line < nrows + 1) | (where < size - 1))
+    extended = jnp.where(inside[None, :, None, None], extended, 0.0).astype(jnp.bfloat16)
     return upsample_conv(extended, w_up)
 
 

time: 77.7 us -> 79.6 us (1.024)
  the two profiles are of different devices: /device:TPU:10 before, /device:TPU:5 now
where the time goes in v6:
time: 79.6 us; the launch traced here: 78.9 us
  matrix products  24.3 us (31%)
  local copies, waits for them, and re-layouts  19.8 us (25%)
  starting transfers between devices  19.6 us (25%)
  other arithmetic  8.5 us (11%)
  waiting for transfers between devices  6.08 us (8%)
    conv_general_dilated x3, matrix products, conv_rows(): lax.conv_general_dilated(haloed[tstep:tstep + 1], weight[tstep], window_s...  12.6 us
    conv_general_dilated x9, local copies, waits for them, and re-layouts, conv_rows(): lax.conv_general_dilated(haloed[tstep:tstep + 1], weight[tstep], window_s...  7.95 us
    ppermute x2, starting transfers between devices, padded_2(): before = lax.ppermute(last, axis, up)  7.4 us
    ppermute x4, starting transfers between devices, body(): pieces = mine + [lax.ppermute(piece, ROWS, swap) for piece in mine]  7.06 us
    unnamed x51, local copies, waits for them, and re-layouts  5.55 us
    dot_general x8, matrix products, body(): jnp.einsum('fqc,fkc->fqk', q_pair, piece, preferred_element_type=jnp.floa...  4.84 us
    ppermute x2, starting transfers between devices, padded_2(): after = lax.ppermute(first, axis, down)  4.19 us
    dot_general x8, matrix products, body(): jnp.einsum('fqk,fkc->fqc', e.astype(jnp.bfloat16), p, preferred_element_t...  4 us
  transfers between devices with their start and end apart: 11, of which 3 were waited for; matrix products, arithmetic and copies ran while one was open for 38% of the time, Pallas kernels for 0%

profile of v6, /device:TPU:5, one launch (start us, length us, event | category | flops | bytes accessed | tf_op | source)
XLA Modules:
  0.0 78.9 jit_solution(8706553999103485948)
XLA Ops:
  0.0 1.2 %fusion.100 = f32[2,128]{1,0:T(2,128)S(1)} fusion(bf16[1,2,128,384]{3,2,1,0:T(8,128)(2,1)} %param.10), kind=kLoop, calls=%fused_computation.118 | loop fusion | flops 294656 | bytes 197632 | tf_op jit(solution)/shard_map/reduce_sum | solution.py:26
  1.2 1.0 %fusion.97 = bf16[1,256,384]{2,1,0:T(8,128)(2,1)S(1)} fusion(bf16[1,2,128,384]{3,2,1,0:T(8,128)(2,1)} %param.10, f32[384]{0:T(512)} %param.11, f32[256]{0:T(256)S(1)} %get-tuple-element.22), kind=kLoop, calls=%fused_computation.112 | loop fusion | flops 393216 | bytes 395776 | tf_op jit(solution)/shard_map/convert_element_type | solution.py:91
  2.3 3.3 %collective-permute-start.5 = (bf16[1,256,384]{2,1,0:T(8,128)(2,1)S(1)}, bf16[1,256,384]{2,1,0:T(8,128)(2,1)S(1)}, u32[]{:S(2)}, u32[]{:S(2)}) collective-permute-start(bf16[1,256,384]{2,1,0:T(8,128)(2,1)S(1)} %fusion.97), channel_id=1, source_target_pairs={{0,1},{1,0},{2,3},{3,2},{4,5},{5,4},{6,7},{7,6},{8,9},{9,8},{10,11... | collective-permute-start | bytes 589832 | tf_op jit(solution)/shard_map/ppermute | solution.py:104
  5.6 3.0 %collective-permute-start = (bf16[2,2,128,384]{3,2,1,0:T(8,128)(2,1)}, bf16[2,2,128,384]{3,2,1,0:T(8,128)(2,1)}, u32[]{:S(2)}, u32[]{:S(2)}) collective-permute-start(bf16[2,2,128,384]{3,2,1,0:T(8,128)(2,1)} %param.16), channel_id=1, source_target_pairs={{0,1},{1,2},{2,3},{3,4},{4,5},{5,6},{6,7},{7,8},{8,9},{9,10},{10,1... | collective-permute-start | bytes 1179656 | tf_op jit(solution)/shard_map/ppermute | solution.py:19
  8.6 1.9 %collective-permute-start.1 = (bf16[2,2,128,384]{3,2,1,0:T(8,128)(2,1)}, bf16[2,2,128,384]{3,2,1,0:T(8,128)(2,1)}, u32[]{:S(2)}, u32[]{:S(2)}) collective-permute-start(bf16[2,2,128,384]{3,2,1,0:T(8,128)(2,1)} %param.16), channel_id=1, source_target_pairs={{1,0},{2,1},{3,2},{4,3},{5,4},{6,5},{7,6},{8,7},{9,8},{10,9},{11,1... | collective-permute-start | bytes 1179656 | tf_op jit(solution)/shard_map/ppermute | solution.py:20
  10.6 1.0 %fusion.99 = bf16[256,384]{1,0:T(8,128)(2,1)S(1)} fusion(bf16[1,2,128,384]{3,2,1,0:T(8,128)(2,1)} %param.10, f32[384]{0:T(512)} %param.11, f32[256]{0:T(256)S(1)} %get-tuple-element.22), kind=kLoop, calls=%fused_computation.115 | loop fusion | flops 393216 | bytes 395776 | tf_op jit(solution)/shard_map/convert_element_type | solution.py:91
  11.6 1.0 %fusion.102 = bf16[1,2,128,384]{3,2,1,0:T(8,128)(2,1)S(1)} fusion(bf16[1,2,128,384]{3,2,1,0:T(8,128)(2,1)} %param.10, f32[384]{0:T(512)} %param.11, f32[2,128]{1,0:T(2,128)S(1)} %get-tuple-element.21), kind=kLoop, calls=%fused_computation.120 | loop fusion | flops 393216 | bytes 395776 | tf_op jit(solution)/shard_map/convert_element_type | solution.py:91
  12.7 0.5 convert_bitcast_fusion.1
  13.7 0.9 %collective-permute-start.3 = (bf16[1,512,384]{2,1,0:T(8,128)(2,1)S(1)}, bf16[1,512,384]{2,1,0:T(8,128)(2,1)S(1)}, u32[]{:S(2)}, u32[]{:S(2)}) collective-permute-start(bf16[1,512,384]{2,1,0:T(8,128)(2,1)S(1)} %pad_maximum_fusion.2), channel_id=1, source_target_pairs={{0,4},{1,9},{2,6},{3,11},{4,0},{5,13},{6,2},{7,15},{8,12},{9,1},{1... | collective-permute-start | bytes 1179656 | tf_op jit(solution)/shard_map/ppermute | solution.py:99
  14.5 1.4 %collective-permute-start.6 = (bf16[1,256,384]{2,1,0:T(8,128)(2,1)S(1)}, bf16[1,256,384]{2,1,0:T(8,128)(2,1)S(1)}, u32[]{:S(2)}, u32[]{:S(2)}) collective-permute-start(bf16[1,256,384]{2,1,0:T(8,128)(2,1)S(1)} %collective-permute-done.2), channel_id=1, source_target_pairs={{0,1},{1,0},{2,3},{3,2},{4,5},{5,4},{6,7},{7,6},{8,9},{9,8},{10,11... | collective-permute-start | bytes 589832 | tf_op jit(solution)/shard_map/ppermute | solution.py:104
  16.8 1.2 %constant_dynamic-update-slice_fusion.2 = bf16[2,6,128,384]{3,2,1,0:T(8,128)(2,1)S(1)} fusion(bf16[2,2,128,384]{3,2,1,0:T(8,128)(2,1)} %collective-permute-done), kind=kLoop, calls=%fused_computation.242 | loop fusion | bytes 786432
  18.0 1.8 %collective-permute-done.1 = bf16[2,2,128,384]{3,2,1,0:T(8,128)(2,1)} collective-permute-done((bf16[2,2,128,384]{3,2,1,0:T(8,128)(2,1)}, bf16[2,2,128,384]{3,2,1,0:T(8,128)(2,1)}, u32[]{:S(2)}, u32[]{:S(2)}) %collective-permute-start.1) | collective-permute-done | bytes 393248 | tf_op jit(solution)/shard_map/ppermute | solution.py:20
  19.8 1.1 %constant_dynamic-update-slice_fusion = bf16[2,6,128,384]{3,2,1,0:T(8,128)(2,1)S(1)} fusion(bf16[2,6,128,384]{3,2,1,0:T(8,128)(2,1)S(1)} %constant_dynamic-update-slice_fusion.1, bf16[2,2,128,384]{3,2,1,0:T(8,128)(2,1)} %collective-permute-done.1), kind=kLoop, calls=%fused_computation.240 | loop fusion | bytes 786432 | tf_op jit(solution)/shard_map/concatenate | solution.py:21
  20.9 1.0 %slice_bitcast_fusion = (bf16[6,1,128,384]{3,2,0,1:T(8,128)(2,1)}, bf16[6,1,128,384]{3,2,0,1:T(8,128)(2,1)S(1)}) fusion(bf16[2,6,128,384]{3,2,1,0:T(8,128)(2,1)S(1)} %constant_dynamic-update-slice_fusion), kind=kLoop, calls=%fused_computation.75 | loop fusion | bytes 2359296 | tf_op jit(solution)/shard_map/slice | solution.py:45
  21.9 3.6 %collective-permute-done.3 = bf16[1,512,384]{2,1,0:T(8,128)(2,1)S(1)} collective-permute-done((bf16[1,512,384]{2,1,0:T(8,128)(2,1)S(1)}, bf16[1,512,384]{2,1,0:T(8,128)(2,1)S(1)}, u32[]{:S(2)}, u32[]{:S(2)}) %collective-permute-start.3) | collective-permute-done | bytes 393248 | tf_op jit(solution)/shard_map/ppermute | solution.py:99
  25.5 1.0 %pad_maximum_fusion = bf16[1,1024,384]{2,1,0:T(8,128)(2,1)} fusion(bf16[1,512,384]{2,1,0:T(8,128)(2,1)S(1)} %collective-permute-done.3, bf16[1,256,384]{2,1,0:T(8,128)(2,1)S(1)} %collective-permute-done.2, bf16[1,256,384]{2,1,0:T(8,128)(2,1)S(1)} %fusion.97), kind=kLoop, calls=%fused_computation.53 | loop fusion | flops 2359296 | bytes 1572864 | tf_op jit(solution)/shard_map/concatenate | solution.py:102
  27.2 1.0 %pad.5 = bf16[6,1,136,384]{3,2,0,1:T(8,128)(2,1)} pad(bf16[6,1,128,384]{3,2,0,1:T(8,128)(2,1)S(1)} %get-tuple-element.16, bf16[]{:T(256)} %constant.35.clone.1), padding=0_0x0_0x1_7x0_0 | pad | bytes 1216514 | tf_op jit(solution)/shard_map/slice | solution.py:45
  28.2 2.2 %reshape.954 = bf16[6,1,8,17,384]{4,3,2,0,1:T(8,128)(2,1)} reshape(bf16[6,1,136,384]{3,2,0,1:T(8,128)(2,1)} %pad.5) | data formatting | bytes 1253376 | tf_op jit(solution)/shard_map/conv_general_dilated | solution.py:44
  30.4 1.3 %copy.37 = bf16[6,1,8,17,384]{4,2,3,0,1:T(8,128)(2,1)S(1)} copy(bf16[6,1,8,17,384]{4,3,2,0,1:T(8,128)(2,1)} %reshape.954) | data formatting | bytes 1253376 | tf_op jit(solution)/shard_map/conv_general_dilated | solution.py:44
  31.7 0.8 %copy-done.13 = bf16[6,1,8,17,384]{4,2,3,0,1:T(8,128)(2,1)} copy-done((bf16[6,1,8,17,384]{4,2,3,0,1:T(8,128)(2,1)}, bf16[6,1,8,17,384]{4,2,3,0,1:T(8,128)(2,1)S(1)}, u32[]{:S(2)}) %copy-start.13) | copy-done | bytes 626712
  32.5 0.6 slice.211
  33.1 1.0 %pad.7 = bf16[6,1,136,384]{3,2,0,1:T(8,128)(2,1)} pad(bf16[6,1,128,384]{3,2,0,1:T(8,128)(2,1)S(1)} %copy-done.4, bf16[]{:T(256)} %constant.35.clone.1), padding=0_0x0_0x1_7x0_0 | pad | bytes 1216514 | tf_op jit(solution)/shard_map/slice | solution.py:45
  34.1 2.2 %reshape.959 = bf16[6,1,8,17,384]{4,3,2,0,1:T(8,128)(2,1)} reshape(bf16[6,1,136,384]{3,2,0,1:T(8,128)(2,1)} %pad.7) | data formatting | bytes 1253376 | tf_op jit(solution)/shard_map/conv_general_dilated | solution.py:44
  36.3 1.3 %copy.39 = bf16[6,1,8,17,384]{4,2,3,0,1:T(8,128)(2,1)S(1)} copy(bf16[6,1,8,17,384]{4,3,2,0,1:T(8,128)(2,1)} %reshape.959) | data formatting | bytes 1253376 | tf_op jit(solution)/shard_map/conv_general_dilated | solution.py:44
  37.7 3.9 %fusion.13 = f32[4,8,17,384]{3,1,2,0:T(8,128)S(1)} fusion(bf16[3,3,3,384,384]{4,3,2,1,0:T(8,128)(2,1)} %param.18, bf16[6,1,7,2,384]{4,2,3,0,1:T(8,128)(2,1)S(1)} %copy-done.19, bf16[6,1,8,17,384]{4,2,3,0,1:T(8,128)(2,1)S(1)} %copy-done.14, pred[8,17]{0,1:T(8,128)(4,1)S(1)} %copy-done.22), kind=kOutput, calls=%fused_computation.20 | convolution fusion | flops 1446199296 | bytes 4181128 | tf_op jit(solution)/shard_map/conv_general_dilated | solution.py:44
  41.7 2.3 %collective-permute-start.7 = (bf16[1,512,384]{2,1,0:T(8,128)(2,1)S(1)}, bf16[1,512,384]{2,1,0:T(8,128)(2,1)S(1)}, u32[]{:S(2)}, u32[]{:S(2)}) collective-permute-start(bf16[1,512,384]{2,1,0:T(8,128)(2,1)S(1)} %copy-done.8), channel_id=1, source_target_pairs={{0,1},{1,0},{2,3},{3,2},{4,5},{5,4},{6,7},{7,6},{8,9},{9,8},{10,11... | collective-permute-start | bytes 1179656 | tf_op jit(solution)/shard_map/ppermute | solution.py:104
  44.1 0.5 convolution_bitcast_fusion.4
  44.7 0.6 collective-permute-done.7
  45.3 0.5 convolution_bitcast_fusion.3
  45.9 1.9 %convolution_bitcast_fusion.2 = f32[1,512,1024]{2,1,0:T(8,128)S(1)} fusion(bf16[1,1024,384]{2,1,0:T(8,128)(2,1)} %collective-permute-done.4, bf16[1,256,384]{2,1,0:T(8,128)(2,1)S(1)} %get-tuple-element.20, bf16[1,256,384]{2,1,0:T(8,128)(2,1)S(1)} %get-tuple-element.19), kind=kOutput, calls=%fused_computation.11 | convolution fusion | flops 403439616 | bytes 3276800 | tf_op jit(solution)/shard_map/fqc,fkc->fqk/dot_general | solution.py:110
  48.0 0.7 convolution_bitcast_fusion.1
  49.0 0.7 copy-done.6
  50.4 0.5 fusion.44
  51.3 1.7 %fusion.51 = f32[256,384]{1,0:T(8,128)S(1)} fusion(bf16[1,1024,384]{2,1,0:T(8,128)(2,1)} %collective-permute-done.4, f32[256]{0:T(256)S(1)} %maximum_maximum_fusion, f32[1,512,1024]{2,1,0:T(8,128)S(1)} %convolution_bitcast_fusion.2), kind=kOutput, calls=%fused_computation.57 | convolution fusion | flops 202375168 | bytes 3277824 | tf_op jit(solution)/shard_map/fqk,fkc->fqc/dot_general | solution.py:116
  53.7 0.5 fusion.48
  54.5 0.6 copy-done.10
  55.4 0.7 copy-done.18
  56.1 0.4 convolution_bitcast_fusion.5
  56.5 0.4 multiply_reduce_fusion
  57.2 2.3 %collective-permute-start.10 = (bf16[1,2,128,384]{3,2,1,0:T(8,128)(2,1)S(1)}, bf16[1,2,128,384]{3,2,1,0:T(8,128)(2,1)S(1)}, u32[]{:S(2)}, u32[]{:S(2)}) collective-permute-start(bf16[1,2,128,384]{3,2,1,0:T(8,128)(2,1)S(1)} %bitcast.472), channel_id=1, source_target_pairs={{1,0},{2,1},{3,2},{4,3},{5,4},{6,5},{7,6},{8,7},{9,8},{10,9},{11,1... | collective-permute-start | bytes 589832 | tf_op jit(solution)/shard_map/ppermute | solution.py:20
  59.5 4.4 %collective-permute-start.9 = (bf16[1,2,128,384]{3,2,1,0:T(8,128)(2,1)S(1)}, bf16[1,2,128,384]{3,2,1,0:T(8,128)(2,1)S(1)}, u32[]{:S(2)}, u32[]{:S(2)}) collective-permute-start(bf16[1,2,128,384]{3,2,1,0:T(8,128)(2,1)S(1)} %bitcast.473), channel_id=1, source_target_pairs={{0,1},{1,2},{2,3},{3,4},{4,5},{5,6},{6,7},{7,8},{8,9},{9,10},{10,1... | collective-permute-start | bytes 589832 | tf_op jit(solution)/shard_map/ppermute | solution.py:19
  63.8 4.8 %fusion.28 = f32[4,8,17,384]{3,1,2,0:T(8,128)} fusion(f32[4,8,17,384]{3,1,2,0:T(8,128)S(1)} %fusion.13, bf16[3,3,3,384,384]{4,3,2,1,0:T(8,128)(2,1)} %param.18, bf16[6,1,7,2,384]{4,2,3,0,1:T(8,128)(2,1)S(1)} %slice.213, bf16[6,1,8,17,384]{4,2,3,0,1:T(8,128)(2,1)S(1)} %copy.39, pred[8,17]{0,1:T(8,128)(4,1)S(1)} %copy-done.22), kind=kOutput, calls=%fused_computation.25 | convolution fusion | flops 1446408192 | bytes 5016712 | tf_op jit(solution)/shard_map/conv_general_dilated | solution.py:44
  69.2 1.0 %copy-done.23 = f32[4,8,17,384]{3,1,2,0:T(8,128)S(1)} copy-done((f32[4,8,17,384]{3,1,2,0:T(8,128)S(1)}, f32[4,8,17,384]{3,1,2,0:T(8,128)}, u32[]{:S(2)}) %copy-start.23) | copy-done | bytes 835608
  70.3 3.9 %fusion.31 = bf16[4,8,17,384]{3,1,2,0:T(8,128)(2,1)S(1)} fusion(f32[4,8,17,384]{3,1,2,0:T(8,128)S(1)} %copy-done.23, bf16[3,3,3,384,384]{4,3,2,1,0:T(8,128)(2,1)} %param.18, bf16[6,1,7,2,384]{4,2,3,0,1:T(8,128)(2,1)S(1)} %slice.232, bf16[6,1,8,17,384]{4,2,3,0,1:T(8,128)(2,1)S(1)} %copy.41, pred[4]{0:T(512)(128)(4,1)S(1)} %or_and_fusion, ...), kind=kOutput, calls=%fused_computation.26 | convolution fusion | flops 1446825984 | bytes 4598924 | tf_op jit(solution)/shard_map/conv_general_dilated | solution.py:44
  74.5 1.5 %convolution_bitcast_fusion = f32[1,4,130,3,3,192]{5,2,4,3,1,0:T(8,128)S(1)} fusion(bf16[3,3,384,192]{2,3,1,0:T(8,128)(2,1)S(1)} %copy-done, bf16[1,4,128,384]{3,2,1,0:T(8,128)(2,1)S(1)} %bitcast.471), kind=kOutput, calls=%fused_computation.9 | convolution fusion | flops 690094080 | bytes 5314560 | tf_op jit(solution)/shard_map/frwc,ijco->frwijo/dot_general | solution.py:61
  76.0 0.4 fusion.184
  77.0 0.5 copy.69
  77.6 1.3 %convert_element_type.181 = bf16[1,4,49152]{2,1,0:T(4,128)(2,1)} reshape(bf16[1,2,2,128,2,192]{5,4,3,2,1,0:T(2,128)(2,1)S(1)} %copy.69) | data formatting | bytes 786432 | tf_op jit(solution)/shard_map/convert_element_type | solution.py:78
  (95 shorter events, 6.9 us)
Async XLA Ops:
  0.0 74.5 %copy-start = (bf16[3,3,384,192]{2,3,1,0:T(8,128)(2,1)S(1)}, bf16[3,3,384,192]{2,3,1,0:T(8,128)(2,1)}, u32[]{:S(2)}) copy-start(bf16[3,3,384,192]{2,3,1,0:T(8,128)(2,1)} %param.19) | copy-start | bytes 3981316
  0.0 12.7 %copy-start.17 = (bf16[384,384]{1,0:T(8,128)(2,1)S(1)}, bf16[384,384]{1,0:T(8,128)(2,1)}, u32[]{:S(2)}) copy-start(bf16[384,384]{1,0:T(8,128)(2,1)} %param.12) | copy-start | bytes 884740
  0.0 12.7 %copy-start.16 = (bf16[384,384]{1,0:T(8,128)(2,1)S(1)}, bf16[384,384]{1,0:T(8,128)(2,1)}, u32[]{:S(2)}) copy-start(bf16[384,384]{1,0:T(8,128)(2,1)} %param.13) | copy-start | bytes 884740
  2.3 11.4 %collective-permute-start.2 = (bf16[1,256,384]{2,1,0:T(8,128)(2,1)S(1)}, bf16[1,256,384]{2,1,0:T(8,128)(2,1)S(1)}, u32[]{:S(2)}, u32[]{:S(2)}) collective-permute-start(bf16[1,256,384]{2,1,0:T(8,128)(2,1)S(1)} %fusion.97), channel_id=1, source_target_pairs={{0,8},{1,3},{2,10},{3,1},{4,12},{5,7},{6,14},{7,5},{8,0},{9,11},{1... | collective-permute-start | bytes 589832 | tf_op jit(solution)/shard_map/ppermute | solution.py:99
  2.3 14.0 %collective-permute-start.5 = (bf16[1,256,384]{2,1,0:T(8,128)(2,1)S(1)}, bf16[1,256,384]{2,1,0:T(8,128)(2,1)S(1)}, u32[]{:S(2)}, u32[]{:S(2)}) collective-permute-start(bf16[1,256,384]{2,1,0:T(8,128)(2,1)S(1)} %fusion.97), channel_id=1, source_target_pairs={{0,1},{1,0},{2,3},{3,2},{4,5},{5,4},{6,7},{7,6},{8,9},{9,8},{10,11... | collective-permute-start | bytes 589832 | tf_op jit(solution)/shard_map/ppermute | solution.py:104
  5.6 11.2 %collective-permute-start = (bf16[2,2,128,384]{3,2,1,0:T(8,128)(2,1)}, bf16[2,2,128,384]{3,2,1,0:T(8,128)(2,1)}, u32[]{:S(2)}, u32[]{:S(2)}) collective-permute-start(bf16[2,2,128,384]{3,2,1,0:T(8,128)(2,1)} %param.16), channel_id=1, source_target_pairs={{0,1},{1,2},{2,3},{3,4},{4,5},{5,6},{6,7},{7,8},{8,9},{9,10},{10,1... | collective-permute-start | bytes 1179656 | tf_op jit(solution)/shard_map/ppermute | solution.py:19
  8.6 11.2 %collective-permute-start.1 = (bf16[2,2,128,384]{3,2,1,0:T(8,128)(2,1)}, bf16[2,2,128,384]{3,2,1,0:T(8,128)(2,1)}, u32[]{:S(2)}, u32[]{:S(2)}) collective-permute-start(bf16[2,2,128,384]{3,2,1,0:T(8,128)(2,1)} %param.16), channel_id=1, source_target_pairs={{1,0},{2,1},{3,2},{4,3},{5,4},{6,5},{7,6},{8,7},{9,8},{10,9},{11,1... | collective-permute-start | bytes 1179656 | tf_op jit(solution)/shard_map/ppermute | solution.py:20
  12.7 1.0 %copy-start.5 = (bf16[1,2,128,384]{3,2,1,0:T(8,128)(2,1)}, bf16[1,2,128,384]{3,2,1,0:T(8,128)(2,1)S(1)}, u32[]{:S(2)}) copy-start(bf16[1,2,128,384]{3,2,1,0:T(8,128)(2,1)S(1)} %fusion.102) | copy-start | bytes 589828
  13.7 11.8 %collective-permute-start.3 = (bf16[1,512,384]{2,1,0:T(8,128)(2,1)S(1)}, bf16[1,512,384]{2,1,0:T(8,128)(2,1)S(1)}, u32[]{:S(2)}, u32[]{:S(2)}) collective-permute-start(bf16[1,512,384]{2,1,0:T(8,128)(2,1)S(1)} %pad_maximum_fusion.2), channel_id=1, source_target_pairs={{0,4},{1,9},{2,6},{3,11},{4,0},{5,13},{6,2},{7,15},{8,12},{9,1},{1... | collective-permute-start | bytes 1179656 | tf_op jit(solution)/shard_map/ppermute | solution.py:99
  14.5 12.0 %collective-permute-start.6 = (bf16[1,256,384]{2,1,0:T(8,128)(2,1)S(1)}, bf16[1,256,384]{2,1,0:T(8,128)(2,1)S(1)}, u32[]{:S(2)}, u32[]{:S(2)}) collective-permute-start(bf16[1,256,384]{2,1,0:T(8,128)(2,1)S(1)} %collective-permute-done.2), channel_id=1, source_target_pairs={{0,1},{1,0},{2,3},{3,2},{4,5},{5,4},{6,7},{7,6},{8,9},{9,8},{10,11... | collective-permute-start | bytes 589832 | tf_op jit(solution)/shard_map/ppermute | solution.py:104
  16.3 1.7 %copy-start.15 = (bf16[2,2,128,384]{3,2,1,0:T(8,128)(2,1)S(1)}, bf16[2,2,128,384]{3,2,1,0:T(8,128)(2,1)}, u32[]{:S(2)}) copy-start(bf16[2,2,128,384]{3,2,1,0:T(8,128)(2,1)} %param.16) | copy-start | bytes 1179652
  16.3 1.7 %copy-start.11 = (bf16[1,256,384]{2,1,0:T(8,128)(2,1)}, bf16[1,256,384]{2,1,0:T(8,128)(2,1)S(1)}, u32[]{:S(2)}) copy-start(bf16[1,256,384]{2,1,0:T(8,128)(2,1)S(1)} %collective-permute-done.5) | copy-start | bytes 589828
  16.7 5.2 %copy-start.1 = (f32[1,512,256]{1,2,0:T(8,128)}, f32[1,512,256]{1,2,0:T(8,128)S(1)}, u32[]{:S(2)}) copy-start(f32[1,512,256]{1,2,0:T(8,128)S(1)} %convolution_bitcast_fusion.7) | copy-start | bytes 1572868
  25.5 1.0 %copy-start.7 = (bf16[1,512,384]{2,1,0:T(8,128)(2,1)}, bf16[1,512,384]{2,1,0:T(8,128)(2,1)S(1)}, u32[]{:S(2)}) copy-start(bf16[1,512,384]{2,1,0:T(8,128)(2,1)S(1)} %collective-permute-done.3) | copy-start | bytes 1179652
  26.5 18.0 %collective-permute-start.4 = (bf16[1,1024,384]{2,1,0:T(8,128)(2,1)}, bf16[1,1024,384]{2,1,0:T(8,128)(2,1)}, u32[]{:S(2)}, u32[]{:S(2)}) collective-permute-start(bf16[1,1024,384]{2,1,0:T(8,128)(2,1)} %pad_maximum_fusion), channel_id=1, source_target_pairs={{0,2},{1,5},{2,0},{3,7},{4,6},{5,1},{6,4},{7,3},{8,10},{9,13},{10,... | collective-permute-start | bytes 2359304 | tf_op jit(solution)/shard_map/ppermute | solution.py:99
  26.5 0.7 copy-start.9
  30.4 2.8 %copy-start.4 = (bf16[6,1,128,384]{3,2,0,1:T(8,128)(2,1)S(1)}, bf16[6,1,128,384]{3,2,0,1:T(8,128)(2,1)}, u32[]{:S(2)}) copy-start(bf16[6,1,128,384]{3,2,0,1:T(8,128)(2,1)} %get-tuple-element.15) | copy-start | bytes 1769476
  31.7 0.8 %copy-start.13 = (bf16[6,1,8,17,384]{4,2,3,0,1:T(8,128)(2,1)}, bf16[6,1,8,17,384]{4,2,3,0,1:T(8,128)(2,1)S(1)}, u32[]{:S(2)}) copy-start(bf16[6,1,8,17,384]{4,2,3,0,1:T(8,128)(2,1)S(1)} %copy.37) | copy-start | bytes 1880068
  34.1 3.5 %copy-start.22 = (pred[8,17]{0,1:T(8,128)(4,1)S(1)}, pred[8,17]{0,1:T(8,128)(4,1)}, u32[]{:S(2)}) copy-start(pred[8,17]{0,1:T(8,128)(4,1)} %constant.52) | copy-start | bytes 412
  36.3 1.4 %copy-start.14 = (bf16[6,1,8,17,384]{4,2,3,0,1:T(8,128)(2,1)S(1)}, bf16[6,1,8,17,384]{4,2,3,0,1:T(8,128)(2,1)}, u32[]{:S(2)}) copy-start(bf16[6,1,8,17,384]{4,2,3,0,1:T(8,128)(2,1)} %copy-done.13) | copy-start | bytes 1880068
  36.3 1.4 %copy-start.19 = (bf16[6,1,7,2,384]{4,2,3,0,1:T(8,128)(2,1)S(1)}, bf16[6,1,7,2,384]{4,2,3,0,1:T(8,128)(2,1)}, u32[]{:S(2)}) copy-start(bf16[6,1,7,2,384]{4,2,3,0,1:T(8,128)(2,1)} %slice.211) | copy-start | bytes 193540
  37.7 3.9 %copy-start.8 = (bf16[1,512,384]{2,1,0:T(8,128)(2,1)S(1)}, bf16[1,512,384]{2,1,0:T(8,128)(2,1)}, u32[]{:S(2)}) copy-start(bf16[1,512,384]{2,1,0:T(8,128)(2,1)} %copy-done.7) | copy-start | bytes 1179652
  41.7 3.7 %collective-permute-start.7 = (bf16[1,512,384]{2,1,0:T(8,128)(2,1)S(1)}, bf16[1,512,384]{2,1,0:T(8,128)(2,1)S(1)}, u32[]{:S(2)}, u32[]{:S(2)}) collective-permute-start(bf16[1,512,384]{2,1,0:T(8,128)(2,1)S(1)} %copy-done.8), channel_id=1, source_target_pairs={{0,1},{1,0},{2,3},{3,2},{4,5},{5,4},{6,7},{7,6},{8,9},{9,8},{10,11... | collective-permute-start | bytes 1179656 | tf_op jit(solution)/shard_map/ppermute | solution.py:104
  44.5 3.5 %collective-permute-start.8 = (bf16[1,1024,384]{2,1,0:T(8,128)(2,1)}, bf16[1,1024,384]{2,1,0:T(8,128)(2,1)S(1)}, u32[]{:S(2)}, u32[]{:S(2)}) collective-permute-start(bf16[1,1024,384]{2,1,0:T(8,128)(2,1)} %collective-permute-done.4), channel_id=1, source_target_pairs={{0,1},{1,0},{2,3},{3,2},{4,5},{5,4},{6,7},{7,6},{8,9},{9,8},{10,11... | collective-permute-start | bytes 2359304 | tf_op jit(solution)/shard_map/ppermute | solution.py:104
  48.7 0.9 %copy-start.6 = (bf16[1,2,128,384]{3,2,1,0:T(8,128)(2,1)S(1)}, bf16[1,2,128,384]{3,2,1,0:T(8,128)(2,1)}, u32[]{:S(2)}) copy-start(bf16[1,2,128,384]{3,2,1,0:T(8,128)(2,1)} %copy-done.5) | copy-start | bytes 589828
  48.7 1.2 %copy-start.2 = (f32[1,512,256]{1,2,0:T(8,128)S(1)}, f32[1,512,256]{1,2,0:T(8,128)}, u32[]{:S(2)}) copy-start(f32[1,512,256]{1,2,0:T(8,128)} %copy-done.1) | copy-start | bytes 1572868
  51.3 1.7 %copy-start.12 = (bf16[1,256,384]{2,1,0:T(8,128)(2,1)S(1)}, bf16[1,256,384]{2,1,0:T(8,128)(2,1)}, u32[]{:S(2)}) copy-start(bf16[1,256,384]{2,1,0:T(8,128)(2,1)} %copy-done.11) | copy-start | bytes 589828
  54.2 0.9 %copy-start.10 = (bf16[1,256,384]{2,1,0:T(8,128)(2,1)S(1)}, bf16[1,256,384]{2,1,0:T(8,128)(2,1)}, u32[]{:S(2)}) copy-start(bf16[1,256,384]{2,1,0:T(8,128)(2,1)} %copy-done.9) | copy-start | bytes 589828
  55.1 1.0 %copy-start.18 = (bf16[384,384]{1,0:T(8,128)(2,1)S(1)}, bf16[384,384]{1,0:T(8,128)(2,1)}, u32[]{:S(2)}) copy-start(bf16[384,384]{1,0:T(8,128)(2,1)} %param.14) | copy-start | bytes 884740
  55.1 1.4 %copy-start.3 = (bf16[1,2,128,384]{3,2,1,0:T(8,128)(2,1)S(1)}, bf16[1,2,128,384]{3,2,1,0:T(8,128)(2,1)}, u32[]{:S(2)}) copy-start(bf16[1,2,128,384]{3,2,1,0:T(8,128)(2,1)} %param.10) | copy-start | bytes 589828
  55.1 1.4 %copy-start.21 = (bf16[384,384]{1,0:T(8,128)(2,1)S(1)}, bf16[384,384]{1,0:T(8,128)(2,1)}, u32[]{:S(2)}) copy-start(bf16[384,384]{1,0:T(8,128)(2,1)} %param.15) | copy-start | bytes 884740
  56.1 0.9 %copy-start.20 = (f32[384]{0:T(512)S(1)}, f32[384]{0:T(512)}, u32[]{:S(2)}) copy-start(f32[384]{0:T(512)} %param.17) | copy-start | bytes 4612
  57.2 11.5 %collective-permute-start.10 = (bf16[1,2,128,384]{3,2,1,0:T(8,128)(2,1)S(1)}, bf16[1,2,128,384]{3,2,1,0:T(8,128)(2,1)S(1)}, u32[]{:S(2)}, u32[]{:S(2)}) collective-permute-start(bf16[1,2,128,384]{3,2,1,0:T(8,128)(2,1)S(1)} %bitcast.472), channel_id=1, source_target_pairs={{1,0},{2,1},{3,2},{4,3},{5,4},{6,5},{7,6},{8,7},{9,8},{10,9},{11,1... | collective-permute-start | bytes 589832 | tf_op jit(solution)/shard_map/ppermute | solution.py:20
  59.5 9.2 %collective-permute-start.9 = (bf16[1,2,128,384]{3,2,1,0:T(8,128)(2,1)S(1)}, bf16[1,2,128,384]{3,2,1,0:T(8,128)(2,1)S(1)}, u32[]{:S(2)}, u32[]{:S(2)}) collective-permute-start(bf16[1,2,128,384]{3,2,1,0:T(8,128)(2,1)S(1)} %bitcast.473), channel_id=1, source_target_pairs={{0,1},{1,2},{2,3},{3,4},{4,5},{5,6},{6,7},{7,8},{8,9},{9,10},{10,1... | collective-permute-start | bytes 589832 | tf_op jit(solution)/shard_map/ppermute | solution.py:19
  69.1 1.2 %copy-start.23 = (f32[4,8,17,384]{3,1,2,0:T(8,128)S(1)}, f32[4,8,17,384]{3,1,2,0:T(8,128)}, u32[]{:S(2)}) copy-start(f32[4,8,17,384]{3,1,2,0:T(8,128)} %fusion.28) | copy-start | bytes 2506756

commit v7 on v5

--- a/solution.py
+++ b/solution.py
@@ -30,6 +30,15 @@
     return jnp.einsum("fqc,cd->fqd", inputs, weight, preferred_element_type=jnp.float32).astype(
         jnp.bfloat16
     )
+
+
+def exchange(values, bits, size):
+    masks = [0]
+    for bit in bits:
+        masks = masks + [mask | bit for mask in masks]
+    return [
+        lax.ppermute(values, ROWS, [(i, i ^ mask) for i in range(size)]) for mask in masks[1:]
+    ]
 
 
 def split_pair(values, axis):
@@ -91,17 +100,17 @@
     normed = rms_gain(flat.astype(jnp.float32), norm_attn).astype(jnp.bfloat16)
     queries = project(normed, w_query)
     size = lax.axis_size(ROWS)
-    chip_bits = [1 << k for k in range(1, size.bit_length() - 1)][::-1]
-    orders = (chip_bits, chip_bits[-1:] + chip_bits[:-1])
-    mine, held = [normed], normed
-    for step in range(len(chip_bits)):
-        perm = [(i, i ^ orders[i & 1][step]) for i in range(size)]
-        other = lax.ppermute(held, ROWS, perm)
-        mine.append(other)
-        if step + 1 < len(chip_bits):
-            held = jnp.concatenate([held, other], axis=1)
-    swap = [(i, i ^ 1) for i in range(size)]
-    pieces = mine + [lax.ppermute(piece, ROWS, swap) for piece in mine]
+    chip_bits = [1 << k for k in range(1, size.bit_length() - 1)]
+    low, high = chip_bits[:1], chip_bits[1:]
+    half = normed.shape[1] // 2
+    first, second = normed[:, :half], normed[:, half:]
+    first_in = exchange(first, high, size)
+    second_in = exchange(second, low, size)
+    gathered = jnp.concatenate([first, second] + first_in + second_in, axis=1)
+    first_out = exchange(jnp.concatenate([first] + first_in, axis=1), low, size)
+    second_out = exchange(jnp.concatenate([second] + second_in, axis=1), high, size)
+    mine = [gathered] + first_out + second_out
+    pieces = mine + [exchange(piece, [1], size)[0] for piece in mine]
     q_keyed = jnp.einsum("fqc,dc->fqd", queries, w_key, preferred_element_type=jnp.float32)
     q_pair = split_pair(q_keyed, axis=1)
     count = queries.shape[1]

time: 77.7 us -> 77.3 us (level)
  the two profiles are of different devices: /device:TPU:10 before, /device:TPU:8 now
where the time goes in v7:
time: 77.3 us; the launch traced here: 76.9 us
  starting transfers between devices  28.8 us (37%)
  waiting for transfers between devices  19.1 us (25%)
  matrix products  14.8 us (19%)
  other arithmetic  7.04 us (9%)
  local copies, waits for them, and re-layouts  6.31 us (8%)
    ppermute x13, starting transfers between devices, exchange(): lax.ppermute(values, ROWS, [(i, i ^ mask) for i in range(size)])  11.5 us
    ppermute x3, starting transfers between devices, padded_2(): after = lax.ppermute(first, axis, down)  10.9 us
    ppermute x13, waiting for transfers between devices, exchange(): lax.ppermute(values, ROWS, [(i, i ^ mask) for i in range(size)])  9.84 us
    ppermute x3, waiting for transfers between devices, padded_2(): before = lax.ppermute(last, axis, up)  8.03 us
    ppermute x3, starting transfers between devices, padded_2(): before = lax.ppermute(last, axis, up)  6.42 us
    dot_general x10, matrix products, body(): jnp.einsum('fqc,fkc->fqk', q_pair, piece, preferred_element_type=jnp.floa...  4.07 us
    conv_general_dilated x3, matrix products, conv_rows(): lax.conv_general_dilated(haloed[tstep:tstep + 1], weight[tstep], window_s...  3.58 us
    dot_general x10, matrix products, body(): jnp.einsum('fqk,fkc->fqc', e.astype(jnp.bfloat16), p, preferred_element_t...  3.33 us
  transfers between devices with their start and end apart: 19, of which 4 were waited for; matrix products, arithmetic and copies ran while one was open for 15% of the time, Pallas kernels for 0%

profile of v7, /device:TPU:8, one launch (start us, length us, event | category | flops | bytes accessed | tf_op | source)
XLA Modules:
  0.0 76.9 jit_solution(10632137675544529652)
XLA Ops:
  0.0 1.1 %multiply_reduce_fusion.1 = f32[2,128]{1,0:T(2,128)S(1)} fusion(bf16[1,2,128,384]{3,2,1,0:T(8,128)(2,1)} %param.10), kind=kLoop, calls=%fused_computation.131 | loop fusion | flops 294656 | bytes 197632 | tf_op jit(solution)/shard_map/reduce_sum | solution.py:26
  1.2 1.1 %constant_dynamic-update-slice_fusion.7 = (bf16[1,768,384]{2,1,0:T(8,128)(2,1)S(1)}, bf16[1,256,384]{2,1,0:T(8,128)(2,1)S(1)}) fusion(f32[384]{0:T(512)} %param.11, f32[256]{0:T(256)S(1)} %rsqrt_bitcast_fusion, bf16[1,2,128,384]{3,2,1,0:T(8,128)(2,1)} %param.10), kind=kLoop, calls=%fused_computation.281 | loop fusion | flops 393215 | bytes 592384
  2.3 1.6 %collective-permute-start.4 = (bf16[1,128,384]{2,1,0:T(8,128)(2,1)S(1)}, bf16[1,128,384]{2,1,0:T(8,128)(2,1)S(1)}, u32[]{:S(2)}, u32[]{:S(2)}) collective-permute-start(bf16[1,128,384]{2,1,0:T(8,128)(2,1)S(1)} %get-tuple-element.29), channel_id=1, source_target_pairs={{0,12},{1,13},{2,14},{3,15},{4,8},{5,9},{6,10},{7,11},{8,4},{9,5},... | collective-permute-start | bytes 294920 | tf_op jit(solution)/shard_map/ppermute | solution.py:40
  3.9 1.1 %collective-permute-start.3 = (bf16[1,128,384]{2,1,0:T(8,128)(2,1)S(1)}, bf16[1,128,384]{2,1,0:T(8,128)(2,1)S(1)}, u32[]{:S(2)}, u32[]{:S(2)}) collective-permute-start(bf16[1,128,384]{2,1,0:T(8,128)(2,1)S(1)} %get-tuple-element.29), channel_id=1, source_target_pairs={{0,8},{1,9},{2,10},{3,11},{4,12},{5,13},{6,14},{7,15},{8,0},{9,1},... | collective-permute-start | bytes 294920 | tf_op jit(solution)/shard_map/ppermute | solution.py:40
  5.0 1.4 %collective-permute-start.2 = (bf16[1,128,384]{2,1,0:T(8,128)(2,1)S(1)}, bf16[1,128,384]{2,1,0:T(8,128)(2,1)S(1)}, u32[]{:S(2)}, u32[]{:S(2)}) collective-permute-start(bf16[1,128,384]{2,1,0:T(8,128)(2,1)S(1)} %get-tuple-element.29), channel_id=1, source_target_pairs={{0,4},{1,5},{2,6},{3,7},{4,0},{5,1},{6,2},{7,3},{8,12},{9,13},{10,... | collective-permute-start | bytes 294920 | tf_op jit(solution)/shard_map/ppermute | solution.py:40
  6.4 1.5 %collective-permute-start.5 = (bf16[1,128,384]{2,1,0:T(8,128)(2,1)S(1)}, bf16[1,128,384]{2,1,0:T(8,128)(2,1)S(1)}, u32[]{:S(2)}, u32[]{:S(2)}) collective-permute-start(bf16[1,128,384]{2,1,0:T(8,128)(2,1)S(1)} %get-tuple-element.30), channel_id=1, source_target_pairs={{0,2},{1,3},{2,0},{3,1},{4,6},{5,7},{6,4},{7,5},{8,10},{9,11},{10,... | collective-permute-start | bytes 294920 | tf_op jit(solution)/shard_map/ppermute | solution.py:40
  7.9 1.7 %fusion.252 = (bf16[2,1,128,384]{3,2,1,0:T(8,128)(2,1)S(1)}, bf16[2,1,128,384]{3,2,1,0:T(8,128)(2,1)}) fusion(bf16[2,2,128,384]{3,2,1,0:T(8,128)(2,1)} %param.16), kind=kLoop, calls=%fused_computation.310 | loop fusion | bytes 786432 | tf_op jit(solution)/shard_map/slice | solution.py:18
  9.6 1.9 %collective-permute-start = (bf16[2,1,128,384]{3,2,1,0:T(8,128)(2,1)}, bf16[2,1,128,384]{3,2,1,0:T(8,128)(2,1)S(1)}, u32[]{:S(2)}, u32[]{:S(2)}) collective-permute-start(bf16[2,1,128,384]{3,2,1,0:T(8,128)(2,1)} %get-tuple-element.20), channel_id=1, source_target_pairs={{0,1},{1,2},{2,3},{3,4},{4,5},{5,6},{6,7},{7,8},{8,9},{9,10},{10,1... | collective-permute-start | bytes 589832 | tf_op jit(solution)/shard_map/ppermute | solution.py:19
  11.6 1.0 %fusion.107 = bf16[256,384]{1,0:T(8,128)(2,1)S(1)} fusion(bf16[1,2,128,384]{3,2,1,0:T(8,128)(2,1)} %param.10, f32[384]{0:T(512)} %param.11, f32[256]{0:T(256)S(1)} %rsqrt_bitcast_fusion), kind=kLoop, calls=%fused_computation.124 | loop fusion | flops 393216 | bytes 395776 | tf_op jit(solution)/shard_map/convert_element_type | solution.py:100
  12.6 1.6 %convert_bitcast_fusion.1 = (bf16[1,256,384]{2,1,0:T(8,128)(2,1)S(1)}, bf16[1,256,384]{2,1,0:T(8,128)(2,1)S(1)}) fusion(bf16[384,384]{1,0:T(8,128)(2,1)} %param.13, bf16[256,384]{1,0:T(8,128)(2,1)S(1)} %fusion.107, bf16[384,384]{1,0:T(8,128)(2,1)} %param.12), kind=kOutput, calls=%fused_computation.273 | convolution fusion | flops 151486464 | bytes 1179648 | tf_op jit(solution)/shard_map/fqc,dc->fqd/dot_general | solution.py:114
  14.2 4.5 %collective-permute-start.1 = (bf16[2,1,128,384]{3,2,1,0:T(8,128)(2,1)S(1)}, bf16[2,1,128,384]{3,2,1,0:T(8,128)(2,1)S(1)}, u32[]{:S(2)}, u32[]{:S(2)}) collective-permute-start(bf16[2,1,128,384]{3,2,1,0:T(8,128)(2,1)S(1)} %get-tuple-element.19), channel_id=1, source_target_pairs={{1,0},{2,1},{3,2},{4,3},{5,4},{6,5},{7,6},{8,7},{9,8},{10,9},{11,1... | collective-permute-start | bytes 589832 | tf_op jit(solution)/shard_map/ppermute | solution.py:20
  18.8 1.5 %collective-permute-start.9 = (bf16[1,256,384]{2,1,0:T(8,128)(2,1)S(1)}, bf16[1,256,384]{2,1,0:T(8,128)(2,1)S(1)}, u32[]{:S(2)}, u32[]{:S(2)}) collective-permute-start(bf16[1,256,384]{2,1,0:T(8,128)(2,1)S(1)} %pad_maximum_fusion.2), channel_id=1, source_target_pairs={{0,12},{1,13},{2,14},{3,15},{4,8},{5,9},{6,10},{7,11},{8,4},{9,5},... | collective-permute-start | bytes 589832 | tf_op jit(solution)/shard_map/ppermute | solution.py:40
  20.3 1.5 %collective-permute-start.8 = (bf16[1,256,384]{2,1,0:T(8,128)(2,1)S(1)}, bf16[1,256,384]{2,1,0:T(8,128)(2,1)S(1)}, u32[]{:S(2)}, u32[]{:S(2)}) collective-permute-start(bf16[1,256,384]{2,1,0:T(8,128)(2,1)S(1)} %pad_maximum_fusion.2), channel_id=1, source_target_pairs={{0,8},{1,9},{2,10},{3,11},{4,12},{5,13},{6,14},{7,15},{8,0},{9,1},... | collective-permute-start | bytes 589832 | tf_op jit(solution)/shard_map/ppermute | solution.py:40
  21.9 1.5 %collective-permute-start.7 = (bf16[1,256,384]{2,1,0:T(8,128)(2,1)S(1)}, bf16[1,256,384]{2,1,0:T(8,128)(2,1)S(1)}, u32[]{:S(2)}, u32[]{:S(2)}) collective-permute-start(bf16[1,256,384]{2,1,0:T(8,128)(2,1)S(1)} %pad_maximum_fusion.2), channel_id=1, source_target_pairs={{0,4},{1,5},{2,6},{3,7},{4,0},{5,1},{6,2},{7,3},{8,12},{9,13},{10,... | collective-permute-start | bytes 589832 | tf_op jit(solution)/shard_map/ppermute | solution.py:40
  23.5 0.6 convolution_bitcast_fusion.2
  24.5 1.2 %collective-permute-done.1 = bf16[2,1,128,384]{3,2,1,0:T(8,128)(2,1)S(1)} collective-permute-done((bf16[2,1,128,384]{3,2,1,0:T(8,128)(2,1)S(1)}, bf16[2,1,128,384]{3,2,1,0:T(8,128)(2,1)S(1)}, u32[]{:S(2)}, u32[]{:S(2)}) %collective-permute-start.1) | collective-permute-done | bytes 196640 | tf_op jit(solution)/shard_map/ppermute | solution.py:20
  26.5 9.8 %collective-permute-done.9 = bf16[1,256,384]{2,1,0:T(8,128)(2,1)S(1)} collective-permute-done((bf16[1,256,384]{2,1,0:T(8,128)(2,1)S(1)}, bf16[1,256,384]{2,1,0:T(8,128)(2,1)S(1)}, u32[]{:S(2)}, u32[]{:S(2)}) %collective-permute-start.9) | collective-permute-done | bytes 196640 | tf_op jit(solution)/shard_map/ppermute | solution.py:40
  36.7 0.5 collective-permute-start.13
  37.2 0.3 convolution_bitcast_fusion.10
  38.2 0.3 convolution_bitcast_fusion.6
  38.6 0.3 convolution_bitcast_fusion.7
  39.0 0.5 collective-permute-start.11
  39.5 0.5 convolution_bitcast_fusion.4
  40.0 0.3 convolution_bitcast_fusion.8
  40.4 0.6 convolution_bitcast_fusion.1
  41.2 0.5 convolution_bitcast_fusion.3
  41.8 0.3 fusion.161
  42.4 0.4 fusion.44
  42.8 0.5 fusion.48
  44.1 0.4 fusion.101
  44.5 0.5 fusion.16
  45.9 0.4 convert_bitcast_fusion
  46.3 0.4 convolution_bitcast_fusion.5
  46.7 0.4 multiply_reduce_fusion
  47.9 4.4 %collective-permute-start.16 = (bf16[1,1,128,384]{3,1,2,0:T(2,128)(2,1)S(1)}, bf16[1,1,128,384]{3,1,2,0:T(2,128)(2,1)S(1)}, u32[]{:S(2)}, u32[]{:S(2)}) collective-permute-start(bf16[1,1,128,384]{3,1,2,0:T(2,128)(2,1)S(1)} %get-tuple-element.28), channel_id=1, source_target_pairs={{1,0},{2,1},{3,2},{4,3},{5,4},{6,5},{7,6},{8,7},{9,8},{10,9},{11,1... | collective-permute-start | bytes 294920 | tf_op jit(solution)/shard_map/ppermute | solution.py:20
  52.3 2.1 %collective-permute-start.15 = (bf16[1,1,128,384]{3,1,2,0:T(2,128)(2,1)S(1)}, bf16[1,1,128,384]{3,1,2,0:T(2,128)(2,1)S(1)}, u32[]{:S(2)}, u32[]{:S(2)}) collective-permute-start(bf16[1,1,128,384]{3,1,2,0:T(2,128)(2,1)S(1)} %get-tuple-element.27), channel_id=1, source_target_pairs={{0,1},{1,2},{2,3},{3,4},{4,5},{5,6},{6,7},{7,8},{8,9},{9,10},{10,1... | collective-permute-start | bytes 294920 | tf_op jit(solution)/shard_map/ppermute | solution.py:19
  54.5 1.2 %fusion.31 = f32[2,8,17,384]{3,1,2,0:T(8,128)S(1)} fusion(bf16[3,3,3,384,384]{4,3,2,1,0:T(8,128)(2,1)S(1)} %bitcast.488, bf16[4,1,7,2,384]{4,2,3,0,1:T(8,128)(2,1)S(1)} %slice.266, bf16[4,1,8,17,384]{4,2,3,0,1:T(8,128)(2,1)S(1)} %copy.41, pred[8,17]{0,1:T(8,128)(4,1)S(1)} %copy-done.6), kind=kOutput, calls=%fused_computation.41 | convolution fusion | flops 723449856 | bytes 3542016 | tf_op jit(solution)/shard_map/conv_general_dilated | solution.py:53
  56.3 4.0 %collective-permute-done.15 = bf16[1,1,128,384]{3,1,2,0:T(2,128)(2,1)S(1)} collective-permute-done((bf16[1,1,128,384]{3,1,2,0:T(2,128)(2,1)S(1)}, bf16[1,1,128,384]{3,1,2,0:T(2,128)(2,1)S(1)}, u32[]{:S(2)}, u32[]{:S(2)}) %collective-permute-start.15) | collective-permute-done | bytes 98336 | tf_op jit(solution)/shard_map/ppermute | solution.py:19
  60.2 0.7 maximum_bitcast_fusion.3
  61.1 1.2 %fusion.34 = f32[2,8,17,384]{3,1,2,0:T(8,128)S(1)} fusion(bf16[3,3,3,384,384]{4,3,2,1,0:T(8,128)(2,1)S(1)} %bitcast.488, bf16[4,1,7,2,384]{4,2,3,0,1:T(8,128)(2,1)S(1)} %slice.293, bf16[4,1,8,17,384]{4,2,3,0,1:T(8,128)(2,1)S(1)} %copy.46, pred[8,17]{0,1:T(8,128)(4,1)S(1)} %copy-done.6), kind=kOutput, calls=%fused_computation.42 | convolution fusion | flops 723449856 | bytes 3542016 | tf_op jit(solution)/shard_map/conv_general_dilated | solution.py:53
  62.3 1.2 %fusion.28 = bf16[2,8,17,384]{3,1,2,0:T(8,128)(2,1)S(1)} fusion(f32[2,8,17,384]{3,1,2,0:T(8,128)S(1)} %fusion.34, f32[2,8,17,384]{3,1,2,0:T(8,128)S(1)} %fusion.31, bf16[3,3,3,384,384]{4,3,2,1,0:T(8,128)(2,1)S(1)} %bitcast.488, bf16[4,1,7,2,384]{4,2,3,0,1:T(8,128)(2,1)S(1)} %slice.264, bf16[4,1,8,17,384]{4,2,3,0,1:T(8,128)(2,1)S(1)} %copy.38, ...), kind=kOutput, calls=%fused_computation.40 | convolution fusion | flops 723763200 | bytes 4168704 | tf_op jit(solution)/shard_map/conv_general_dilated | solution.py:53
  63.7 1.9 %collective-permute-start.18 = (bf16[1,1,128,384]{3,2,1,0:T(8,128)(2,1)S(1)}, bf16[1,1,128,384]{3,2,1,0:T(8,128)(2,1)S(1)}, u32[]{:S(2)}, u32[]{:S(2)}) collective-permute-start(bf16[1,1,128,384]{3,2,1,0:T(8,128)(2,1)S(1)} %slice.298), channel_id=1, source_target_pairs={{1,0},{2,1},{3,2},{4,3},{5,4},{6,5},{7,6},{8,7},{9,8},{10,9},{11,1... | collective-permute-start | bytes 294920 | tf_op jit(solution)/shard_map/ppermute | solution.py:20
  65.7 2.4 %collective-permute-start.17 = (bf16[1,1,128,384]{3,2,1,0:T(8,128)(2,1)S(1)}, bf16[1,1,128,384]{3,2,1,0:T(8,128)(2,1)S(1)}, u32[]{:S(2)}, u32[]{:S(2)}) collective-permute-start(bf16[1,1,128,384]{3,2,1,0:T(8,128)(2,1)S(1)} %slice.295), channel_id=1, source_target_pairs={{0,1},{1,2},{2,3},{3,4},{4,5},{5,6},{6,7},{7,8},{8,9},{9,10},{10,1... | collective-permute-start | bytes 294920 | tf_op jit(solution)/shard_map/ppermute | solution.py:19
  68.5 4.1 %collective-permute-done.17 = bf16[1,1,128,384]{3,2,1,0:T(8,128)(2,1)S(1)} collective-permute-done((bf16[1,1,128,384]{3,2,1,0:T(8,128)(2,1)S(1)}, bf16[1,1,128,384]{3,2,1,0:T(8,128)(2,1)S(1)}, u32[]{:S(2)}, u32[]{:S(2)}) %collective-permute-start.17) | collective-permute-done | bytes 98336 | tf_op jit(solution)/shard_map/ppermute | solution.py:19
  72.6 1.5 %convolution_bitcast_fusion = f32[1,4,130,3,3,192]{5,2,4,3,1,0:T(8,128)S(1)} fusion(bf16[3,3,384,192]{2,3,1,0:T(8,128)(2,1)S(1)} %copy-done, bf16[1,1,128,384]{3,2,1,0:T(8,128)(2,1)S(1)} %collective-permute-done.18, bf16[1,2,128,384]{3,2,1,0:T(8,128)(2,1)S(1)} %bitcast.485, bf16[1,1,128,384]{3,2,1,0:T(8,128)(2,1)S(1)} %collective-permute-done.17), kind=kOutput, calls=%fused_computation.9 | convolution fusion | flops 692490240 | bytes 5314560 | tf_op jit(solution)/shard_map/frwc,ijco->frwijo/dot_general | solution.py:70
  74.0 0.4 fusion.214
  75.1 0.5 copy.76
  75.6 1.3 %convert_element_type.171 = bf16[1,4,49152]{2,1,0:T(4,128)(2,1)} reshape(bf16[1,2,2,128,2,192]{5,4,3,2,1,0:T(2,128)(2,1)S(1)} %copy.76) | data formatting | bytes 786432 | tf_op jit(solution)/shard_map/convert_element_type | solution.py:87
  (100 shorter events, 7.4 us)
Async XLA Ops:
  0.0 72.6 %copy-start = (bf16[3,3,384,192]{2,3,1,0:T(8,128)(2,1)S(1)}, bf16[3,3,384,192]{2,3,1,0:T(8,128)(2,1)}, u32[]{:S(2)}) copy-start(bf16[3,3,384,192]{2,3,1,0:T(8,128)(2,1)} %param.19) | copy-start | bytes 3981316
  2.3 19.6 %collective-permute-start.4 = (bf16[1,128,384]{2,1,0:T(8,128)(2,1)S(1)}, bf16[1,128,384]{2,1,0:T(8,128)(2,1)S(1)}, u32[]{:S(2)}, u32[]{:S(2)}) collective-permute-start(bf16[1,128,384]{2,1,0:T(8,128)(2,1)S(1)} %get-tuple-element.29), channel_id=1, source_target_pairs={{0,12},{1,13},{2,14},{3,15},{4,8},{5,9},{6,10},{7,11},{8,4},{9,5},... | collective-permute-start | bytes 294920 | tf_op jit(solution)/shard_map/ppermute | solution.py:40
  3.9 16.4 %collective-permute-start.3 = (bf16[1,128,384]{2,1,0:T(8,128)(2,1)S(1)}, bf16[1,128,384]{2,1,0:T(8,128)(2,1)S(1)}, u32[]{:S(2)}, u32[]{:S(2)}) collective-permute-start(bf16[1,128,384]{2,1,0:T(8,128)(2,1)S(1)} %get-tuple-element.29), channel_id=1, source_target_pairs={{0,8},{1,9},{2,10},{3,11},{4,12},{5,13},{6,14},{7,15},{8,0},{9,1},... | collective-permute-start | bytes 294920 | tf_op jit(solution)/shard_map/ppermute | solution.py:40
  5.0 13.8 %collective-permute-start.2 = (bf16[1,128,384]{2,1,0:T(8,128)(2,1)S(1)}, bf16[1,128,384]{2,1,0:T(8,128)(2,1)S(1)}, u32[]{:S(2)}, u32[]{:S(2)}) collective-permute-start(bf16[1,128,384]{2,1,0:T(8,128)(2,1)S(1)} %get-tuple-element.29), channel_id=1, source_target_pairs={{0,4},{1,5},{2,6},{3,7},{4,0},{5,1},{6,2},{7,3},{8,12},{9,13},{10,... | collective-permute-start | bytes 294920 | tf_op jit(solution)/shard_map/ppermute | solution.py:40
  6.4 7.8 %collective-permute-start.5 = (bf16[1,128,384]{2,1,0:T(8,128)(2,1)S(1)}, bf16[1,128,384]{2,1,0:T(8,128)(2,1)S(1)}, u32[]{:S(2)}, u32[]{:S(2)}) collective-permute-start(bf16[1,128,384]{2,1,0:T(8,128)(2,1)S(1)} %get-tuple-element.30), channel_id=1, source_target_pairs={{0,2},{1,3},{2,0},{3,1},{4,6},{5,7},{6,4},{7,5},{8,10},{9,11},{10,... | collective-permute-start | bytes 294920 | tf_op jit(solution)/shard_map/ppermute | solution.py:40
  9.6 14.7 %collective-permute-start = (bf16[2,1,128,384]{3,2,1,0:T(8,128)(2,1)}, bf16[2,1,128,384]{3,2,1,0:T(8,128)(2,1)S(1)}, u32[]{:S(2)}, u32[]{:S(2)}) collective-permute-start(bf16[2,1,128,384]{3,2,1,0:T(8,128)(2,1)} %get-tuple-element.20), channel_id=1, source_target_pairs={{0,1},{1,2},{2,3},{3,4},{4,5},{5,6},{6,7},{7,8},{8,9},{9,10},{10,1... | collective-permute-start | bytes 589832 | tf_op jit(solution)/shard_map/ppermute | solution.py:19
  14.2 11.6 %collective-permute-start.1 = (bf16[2,1,128,384]{3,2,1,0:T(8,128)(2,1)S(1)}, bf16[2,1,128,384]{3,2,1,0:T(8,128)(2,1)S(1)}, u32[]{:S(2)}, u32[]{:S(2)}) collective-permute-start(bf16[2,1,128,384]{3,2,1,0:T(8,128)(2,1)S(1)} %get-tuple-element.19), channel_id=1, source_target_pairs={{1,0},{2,1},{3,2},{4,3},{5,4},{6,5},{7,6},{8,7},{9,8},{10,9},{11,1... | collective-permute-start | bytes 589832 | tf_op jit(solution)/shard_map/ppermute | solution.py:20
  18.8 17.5 %collective-permute-start.9 = (bf16[1,256,384]{2,1,0:T(8,128)(2,1)S(1)}, bf16[1,256,384]{2,1,0:T(8,128)(2,1)S(1)}, u32[]{:S(2)}, u32[]{:S(2)}) collective-permute-start(bf16[1,256,384]{2,1,0:T(8,128)(2,1)S(1)} %pad_maximum_fusion.2), channel_id=1, source_target_pairs={{0,12},{1,13},{2,14},{3,15},{4,8},{5,9},{6,10},{7,11},{8,4},{9,5},... | collective-permute-start | bytes 589832 | tf_op jit(solution)/shard_map/ppermute | solution.py:40
  20.3 16.4 %collective-permute-start.8 = (bf16[1,256,384]{2,1,0:T(8,128)(2,1)S(1)}, bf16[1,256,384]{2,1,0:T(8,128)(2,1)S(1)}, u32[]{:S(2)}, u32[]{:S(2)}) collective-permute-start(bf16[1,256,384]{2,1,0:T(8,128)(2,1)S(1)} %pad_maximum_fusion.2), channel_id=1, source_target_pairs={{0,8},{1,9},{2,10},{3,11},{4,12},{5,13},{6,14},{7,15},{8,0},{9,1},... | collective-permute-start | bytes 589832 | tf_op jit(solution)/shard_map/ppermute | solution.py:40
  21.9 15.7 %collective-permute-start.7 = (bf16[1,256,384]{2,1,0:T(8,128)(2,1)S(1)}, bf16[1,256,384]{2,1,0:T(8,128)(2,1)S(1)}, u32[]{:S(2)}, u32[]{:S(2)}) collective-permute-start(bf16[1,256,384]{2,1,0:T(8,128)(2,1)S(1)} %pad_maximum_fusion.2), channel_id=1, source_target_pairs={{0,4},{1,5},{2,6},{3,7},{4,0},{5,1},{6,2},{7,3},{8,12},{9,13},{10,... | collective-permute-start | bytes 589832 | tf_op jit(solution)/shard_map/ppermute | solution.py:40
  23.5 1.0 %copy-start.2 = (bf16[2,2,128,384]{3,2,1,0:T(8,128)(2,1)S(1)}, bf16[2,2,128,384]{3,2,1,0:T(8,128)(2,1)}, u32[]{:S(2)}) copy-start(bf16[2,2,128,384]{3,2,1,0:T(8,128)(2,1)} %param.16) | copy-start | bytes 1179652
  24.3 16.1 %collective-permute-start.10 = (bf16[1,768,384]{2,1,0:T(8,128)(2,1)S(1)}, bf16[1,768,384]{2,1,0:T(8,128)(2,1)S(1)}, u32[]{:S(2)}, u32[]{:S(2)}) collective-permute-start(bf16[1,768,384]{2,1,0:T(8,128)(2,1)S(1)} %constant_dynamic-update-slice_fusion.3), channel_id=1, source_target_pairs={{0,1},{1,0},{2,3},{3,2},{4,5},{5,4},{6,7},{7,6},{8,9},{9,8},{10,11... | collective-permute-start | bytes 1769480 | tf_op jit(solution)/shard_map/ppermute | solution.py:40
  25.8 13.2 %collective-permute-start.6 = (bf16[1,512,384]{2,1,0:T(8,128)(2,1)S(1)}, bf16[1,512,384]{2,1,0:T(8,128)(2,1)S(1)}, u32[]{:S(2)}, u32[]{:S(2)}) collective-permute-start(bf16[1,512,384]{2,1,0:T(8,128)(2,1)S(1)} %pad_maximum_fusion.1), channel_id=1, source_target_pairs={{0,2},{1,3},{2,0},{3,1},{4,6},{5,7},{6,4},{7,5},{8,10},{9,11},{10,... | collective-permute-start | bytes 1179656 | tf_op jit(solution)/shard_map/ppermute | solution.py:40
  36.7 1.5 %collective-permute-start.14 = (bf16[1,256,384]{2,1,0:T(8,128)(2,1)S(1)}, bf16[1,256,384]{2,1,0:T(8,128)(2,1)S(1)}, u32[]{:S(2)}, u32[]{:S(2)}) collective-permute-start(bf16[1,256,384]{2,1,0:T(8,128)(2,1)S(1)} %collective-permute-done.9), channel_id=1, source_target_pairs={{0,1},{1,0},{2,3},{3,2},{4,5},{5,4},{6,7},{7,6},{8,9},{9,8},{10,11... | collective-permute-start | bytes 589832 | tf_op jit(solution)/shard_map/ppermute | solution.py:40
  36.7 1.8 %collective-permute-start.13 = (bf16[1,256,384]{2,1,0:T(8,128)(2,1)S(1)}, bf16[1,256,384]{2,1,0:T(8,128)(2,1)S(1)}, u32[]{:S(2)}, u32[]{:S(2)}) collective-permute-start(bf16[1,256,384]{2,1,0:T(8,128)(2,1)S(1)} %collective-permute-done.8), channel_id=1, source_target_pairs={{0,1},{1,0},{2,3},{3,2},{4,5},{5,4},{6,7},{7,6},{8,9},{9,8},{10,11... | collective-permute-start | bytes 589832 | tf_op jit(solution)/shard_map/ppermute | solution.py:40
  37.6 2.5 %collective-permute-start.12 = (bf16[1,256,384]{2,1,0:T(8,128)(2,1)S(1)}, bf16[1,256,384]{2,1,0:T(8,128)(2,1)S(1)}, u32[]{:S(2)}, u32[]{:S(2)}) collective-permute-start(bf16[1,256,384]{2,1,0:T(8,128)(2,1)S(1)} %collective-permute-done.7), channel_id=1, source_target_pairs={{0,1},{1,0},{2,3},{3,2},{4,5},{5,4},{6,7},{7,6},{8,9},{9,8},{10,11... | collective-permute-start | bytes 589832 | tf_op jit(solution)/shard_map/ppermute | solution.py:40
  39.0 2.2 %collective-permute-start.11 = (bf16[1,512,384]{2,1,0:T(8,128)(2,1)S(1)}, bf16[1,512,384]{2,1,0:T(8,128)(2,1)S(1)}, u32[]{:S(2)}, u32[]{:S(2)}) collective-permute-start(bf16[1,512,384]{2,1,0:T(8,128)(2,1)S(1)} %collective-permute-done.6), channel_id=1, source_target_pairs={{0,1},{1,0},{2,3},{3,2},{4,5},{5,4},{6,7},{7,6},{8,9},{9,8},{10,11... | collective-permute-start | bytes 1179656 | tf_op jit(solution)/shard_map/ppermute | solution.py:40
  44.1 10.4 %slice-start = ((s8[7962624]{0:T(1024)(128)(4,1)}), s8[4194304]{0:T(1024)(128)(4,1)S(1)}, s32[]{:S(2)}) async-start(s8[7962624]{0:T(1024)(128)(4,1)} %bitcast.487), calls=%async_computation | async-start | bytes 8388608
  45.0 1.3 %copy-start.3 = (bf16[384,384]{1,0:T(8,128)(2,1)S(1)}, bf16[384,384]{1,0:T(8,128)(2,1)}, u32[]{:S(2)}) copy-start(bf16[384,384]{1,0:T(8,128)(2,1)} %param.14) | copy-start | bytes 884740
  45.5 1.2 %copy-start.1 = (bf16[1,2,128,384]{3,2,1,0:T(8,128)(2,1)S(1)}, bf16[1,2,128,384]{3,2,1,0:T(8,128)(2,1)}, u32[]{:S(2)}) copy-start(bf16[1,2,128,384]{3,2,1,0:T(8,128)(2,1)} %param.10) | copy-start | bytes 589828
  45.6 1.2 %copy-start.5 = (bf16[384,384]{1,0:T(8,128)(2,1)S(1)}, bf16[384,384]{1,0:T(8,128)(2,1)}, u32[]{:S(2)}) copy-start(bf16[384,384]{1,0:T(8,128)(2,1)} %param.15) | copy-start | bytes 884740
  45.8 1.4 %copy-start.4 = (f32[384]{0:T(512)S(1)}, f32[384]{0:T(512)}, u32[]{:S(2)}) copy-start(f32[384]{0:T(512)} %param.17) | copy-start | bytes 4612
  45.9 8.6 %slice-start.1 = ((s8[7962624]{0:T(1024)(128)(4,1)}), s8[3768320]{0:T(1024)(128)(4,1)S(1)}, s32[]{:S(2)}) async-start(s8[7962624]{0:T(1024)(128)(4,1)} %bitcast.487), calls=%async_computation.1 | async-start | bytes 7536640
  46.3 8.2 %copy-start.6 = (pred[8,17]{0,1:T(8,128)(4,1)S(1)}, pred[8,17]{0,1:T(8,128)(4,1)}, u32[]{:S(2)}) copy-start(pred[8,17]{0,1:T(8,128)(4,1)} %constant.36) | copy-start | bytes 412
  47.9 8.4 %collective-permute-start.16 = (bf16[1,1,128,384]{3,1,2,0:T(2,128)(2,1)S(1)}, bf16[1,1,128,384]{3,1,2,0:T(2,128)(2,1)S(1)}, u32[]{:S(2)}, u32[]{:S(2)}) collective-permute-start(bf16[1,1,128,384]{3,1,2,0:T(2,128)(2,1)S(1)} %get-tuple-element.28), channel_id=1, source_target_pairs={{1,0},{2,1},{3,2},{4,3},{5,4},{6,5},{7,6},{8,7},{9,8},{10,9},{11,1... | collective-permute-start | bytes 294920 | tf_op jit(solution)/shard_map/ppermute | solution.py:20
  52.3 7.9 %collective-permute-start.15 = (bf16[1,1,128,384]{3,1,2,0:T(2,128)(2,1)S(1)}, bf16[1,1,128,384]{3,1,2,0:T(2,128)(2,1)S(1)}, u32[]{:S(2)}, u32[]{:S(2)}) collective-permute-start(bf16[1,1,128,384]{3,1,2,0:T(2,128)(2,1)S(1)} %get-tuple-element.27), channel_id=1, source_target_pairs={{0,1},{1,2},{2,3},{3,4},{4,5},{5,6},{6,7},{7,8},{8,9},{9,10},{10,1... | collective-permute-start | bytes 294920 | tf_op jit(solution)/shard_map/ppermute | solution.py:19
  63.7 4.8 %collective-permute-start.18 = (bf16[1,1,128,384]{3,2,1,0:T(8,128)(2,1)S(1)}, bf16[1,1,128,384]{3,2,1,0:T(8,128)(2,1)S(1)}, u32[]{:S(2)}, u32[]{:S(2)}) collective-permute-start(bf16[1,1,128,384]{3,2,1,0:T(8,128)(2,1)S(1)} %slice.298), channel_id=1, source_target_pairs={{1,0},{2,1},{3,2},{4,3},{5,4},{6,5},{7,6},{8,7},{9,8},{10,9},{11,1... | collective-permute-start | bytes 294920 | tf_op jit(solution)/shard_map/ppermute | solution.py:20
  65.7 6.8 %collective-permute-start.17 = (bf16[1,1,128,384]{3,2,1,0:T(8,128)(2,1)S(1)}, bf16[1,1,128,384]{3,2,1,0:T(8,128)(2,1)S(1)}, u32[]{:S(2)}, u32[]{:S(2)}) collective-permute-start(bf16[1,1,128,384]{3,2,1,0:T(8,128)(2,1)S(1)} %slice.295), channel_id=1, source_target_pairs={{0,1},{1,2},{2,3},{3,4},{4,5},{5,6},{6,7},{7,8},{8,9},{9,10},{10,1... | collective-permute-start | bytes 294920 | tf_op jit(solution)/shard_map/ppermute | solution.py:19

commit v8 on v7

--- a/solution.py
+++ b/solution.py
@@ -48,18 +48,21 @@
 
 
 def conv_rows(haloed, weight):
+    nt, rp, ncols, chans = haloed.shape
+    rows_out = rp - 2
+    padded = jnp.pad(haloed, ((0, 0), (0, 0), (1, 1), (0, 0)))
+    wide = jnp.concatenate([padded[:, :, shift : shift + ncols] for shift in range(3)], axis=-1)
     total = None
-    for tstep in range(weight.shape[0]):
-        part = lax.conv_general_dilated(
-            haloed[tstep : tstep + 1],
-            weight[tstep],
-            window_strides=(1, 1),
-            padding=((0, 0), (1, 1)),
-            dimension_numbers=("NHWC", "HWIO", "NHWC"),
-            preferred_element_type=jnp.float32,
-        )
-        total = part if total is None else total + part
-    return total
+    for tstep in range(nt):
+        for rstep in range(3):
+            part = wide[tstep, rstep : rstep + rows_out].reshape(-1, 3 * chans)
+            term = jnp.dot(
+                part,
+                weight[tstep, rstep].reshape(3 * chans, -1),
+                preferred_element_type=jnp.float32,
+            )
+            total = term if total is None else total + term
+    return total.reshape(1, rows_out, ncols, -1)
 
 
 def upsample_conv(extended, w_up):
@@ -93,7 +96,7 @@
     nframes, nrows, ncols, chans = frames.shape
     scale = chans ** (-0.5)
 
-    cache_haloed = padded_2(cache_one, ((ROWS, 1),), 1)
+    cache_haloed = padded_2(cache_one, ((ROWS, 1),), 2)
     cache_part = conv_rows(cache_haloed, conv_weight[:2])
 
     flat = frames.reshape(nframes, nrows * ncols, chans)
@@ -139,9 +142,12 @@
         .astype(jnp.bfloat16)
         .reshape(nframes, nrows, ncols, chans)
     )
-    activ_haloed = padded_2(activ, ((ROWS, 1),), 1)
-    conv_out = (cache_part + conv_rows(activ_haloed, conv_weight[2:])).astype(jnp.bfloat16)
-    extended = padded_2(conv_out, ((ROWS, 1),), 1)
+    activ_haloed = padded_2(activ, ((ROWS, 1),), 2)
+    extended = cache_part + conv_rows(activ_haloed, conv_weight[2:])
+    where = lax.axis_index(ROWS)
+    line = jnp.arange(nrows + 2)
+    inside = ((line > 0) | (where > 0)) & ((line < nrows + 1) | (where < size - 1))
+    extended = jnp.where(inside[None, :, None, None], extended, 0.0).astype(jnp.bfloat16)
     return upsample_conv(extended, w_up)
 
 

time: 77.3 us -> 89 us (1.15)
  local copies, waits for them, and re-layouts: 6.31 us -> 21.2 us
  waiting for transfers between devices: 19.1 us -> 11.9 us
  matrix products: 14.8 us -> 19.5 us
  starting transfers between devices: 28.8 us -> 24.3 us
  other arithmetic: 7.04 us -> 10.6 us
    unnamed x26 -> x35, local copies, waits for them, and re-layouts: 0.95 us -> 8.32 us
    dot_general x0 -> x9, matrix products: none -> 7.15 us  [conv_rows(): jnp.dot(part, weight[tstep, rstep].reshape(3 * chans, -1), preferred_elem...]
    slice x5, local copies, waits for them, and re-layouts: 2.41 us -> 7.79 us  [the longest x1 5.49 us: conv_rows(): weight[tstep, rstep].reshape(3 * chans, -1)]
    conv_general_dilated x3 -> x0, matrix products: 3.58 us -> none  [conv_rows(): lax.conv_general_dilated(haloed[tstep:tstep + 1], weight[tstep], window_s...]
    ppermute x3 -> x2, waiting for transfers between devices: 8.03 us -> 4.72 us  [padded_2(): before = lax.ppermute(last, axis, up)]
    ppermute x13, waiting for transfers between devices: 9.84 us -> 7 us  [exchange(): lax.ppermute(values, ROWS, [(i, i ^ mask) for i in range(size)])]
    ppermute x3 -> x2, starting transfers between devices: 6.42 us -> 4.18 us  [padded_2(): before = lax.ppermute(last, axis, up)]
    ppermute x3 -> x2, starting transfers between devices: 10.9 us -> 8.84 us  [padded_2(): after = lax.ppermute(first, axis, down)]
  transfers between devices with their start and end apart: 19 -> 17, of which waited for: 4 -> 5; matrix products, arithmetic and copies ran while one was open for 15% -> 39% of each run, Pallas kernels for 0% -> 0%
where the time goes in v8:
time: 89 us; the launch traced here: 88.1 us
  starting transfers between devices  24.3 us (27%)
  local copies, waits for them, and re-layouts  21.2 us (24%)
  matrix products  19.5 us (22%)
  waiting for transfers between devices  11.9 us (13%)
  other arithmetic  10.6 us (12%)
    ppermute x13, starting transfers between devices, exchange(): lax.ppermute(values, ROWS, [(i, i ^ mask) for i in range(size)])  11.2 us
    ppermute x2, starting transfers between devices, padded_2(): after = lax.ppermute(first, axis, down)  8.84 us
    unnamed x35, local copies, waits for them, and re-layouts  8.32 us
    dot_general x9, matrix products, conv_rows(): jnp.dot(part, weight[tstep, rstep].reshape(3 * chans, -1), preferred_elem...  7.15 us
    ppermute x13, waiting for transfers between devices, exchange(): lax.ppermute(values, ROWS, [(i, i ^ mask) for i in range(size)])  7 us
    slice x1, local copies, waits for them, and re-layouts, conv_rows(): weight[tstep, rstep].reshape(3 * chans, -1)  5.49 us
    dot_general x10, matrix products, body(): jnp.einsum('fqc,fkc->fqk', q_pair, piece, preferred_element_type=jnp.floa...  5.13 us
    ppermute x2, waiting for transfers between devices, padded_2(): before = lax.ppermute(last, axis, up)  4.72 us
  transfers between devices with their start and end apart: 17, of which 5 were waited for; matrix products, arithmetic and copies ran while one was open for 39% of the time, Pallas kernels for 0%

profile of v8, /device:TPU:8, one launch (start us, length us, event | category | flops | bytes accessed | tf_op | source)
XLA Modules:
  0.0 88.1 jit_solution(8972485594804877384)
XLA Ops:
  0.0 2.0 %collective-permute-start = (bf16[2,2,128,384]{3,2,1,0:T(8,128)(2,1)}, bf16[2,2,128,384]{3,2,1,0:T(8,128)(2,1)}, u32[]{:S(2)}, u32[]{:S(2)}) collective-permute-start(bf16[2,2,128,384]{3,2,1,0:T(8,128)(2,1)} %param.16), channel_id=1, source_target_pairs={{0,1},{1,2},{2,3},{3,4},{4,5},{5,6},{6,7},{7,8},{8,9},{9,10},{10,1... | collective-permute-start | bytes 1179656 | tf_op jit(solution)/shard_map/ppermute | solution.py:19
  2.1 4.5 %collective-permute-start.1 = (bf16[2,2,128,384]{3,2,1,0:T(8,128)(2,1)}, bf16[2,2,128,384]{3,2,1,0:T(8,128)(2,1)}, u32[]{:S(2)}, u32[]{:S(2)}) collective-permute-start(bf16[2,2,128,384]{3,2,1,0:T(8,128)(2,1)} %param.16), channel_id=1, source_target_pairs={{1,0},{2,1},{3,2},{4,3},{5,4},{6,5},{7,6},{8,7},{9,8},{10,9},{11,1... | collective-permute-start | bytes 1179656 | tf_op jit(solution)/shard_map/ppermute | solution.py:20
  6.6 1.0 %multiply_reduce_fusion.1 = f32[2,128]{1,0:T(2,128)S(1)} fusion(bf16[1,2,128,384]{3,2,1,0:T(8,128)(2,1)} %param.10), kind=kLoop, calls=%fused_computation.103 | loop fusion | flops 294656 | bytes 197632 | tf_op jit(solution)/shard_map/reduce_sum | solution.py:26
  7.7 1.7 %constant_dynamic-update-slice_fusion.7 = (bf16[1,768,384]{2,1,0:T(8,128)(2,1)}, bf16[1,256,384]{2,1,0:T(8,128)(2,1)S(1)}) fusion(f32[384]{0:T(512)} %param.11, f32[256]{0:T(256)S(1)} %rsqrt_bitcast_fusion, bf16[1,2,128,384]{3,2,1,0:T(8,128)(2,1)} %param.10), kind=kLoop, calls=%fused_computation.248 | loop fusion | flops 393215 | bytes 592384
  9.4 0.7 fusion.187
  10.1 1.6 %collective-permute-start.4 = (bf16[1,128,384]{2,1,0:T(8,128)(2,1)}, bf16[1,128,384]{2,1,0:T(8,128)(2,1)}, u32[]{:S(2)}, u32[]{:S(2)}) collective-permute-start(bf16[1,128,384]{2,1,0:T(8,128)(2,1)} %get-tuple-element.43), channel_id=1, source_target_pairs={{0,12},{1,13},{2,14},{3,15},{4,8},{5,9},{6,10},{7,11},{8,4},{9,5},... | collective-permute-start | bytes 294920 | tf_op jit(solution)/shard_map/ppermute | solution.py:40
  11.7 1.0 %collective-permute-start.3 = (bf16[1,128,384]{2,1,0:T(8,128)(2,1)}, bf16[1,128,384]{2,1,0:T(8,128)(2,1)}, u32[]{:S(2)}, u32[]{:S(2)}) collective-permute-start(bf16[1,128,384]{2,1,0:T(8,128)(2,1)} %get-tuple-element.43), channel_id=1, source_target_pairs={{0,8},{1,9},{2,10},{3,11},{4,12},{5,13},{6,14},{7,15},{8,0},{9,1},... | collective-permute-start | bytes 294920 | tf_op jit(solution)/shard_map/ppermute | solution.py:40
  12.7 0.8 collective-permute-start.5
  13.5 1.5 %fusion.54 = bf16[256,384]{1,0:T(8,128)(2,1)} fusion(bf16[1,2,128,384]{3,2,1,0:T(8,128)(2,1)S(1)} %copy-done.6, f32[384]{0:T(512)} %param.11, f32[256]{0:T(256)S(1)} %rsqrt_bitcast_fusion), kind=kLoop, calls=%fused_computation.96 | loop fusion | flops 393216 | bytes 395776 | tf_op jit(solution)/shard_map/convert_element_type | solution.py:103
  15.0 5.5 %fusion.183 = (bf16[1,1,3,384,384]{4,3,2,1,0:T(8,128)(2,1)}, bf16[1,1,3,384,384]{4,3,2,1,0:T(8,128)(2,1)S(1)}, bf16[1,1,3,384,384]{4,3,2,1,0:T(8,128)(2,1)S(1)},...) fusion(bf16[3,3,3,384,384]{4,3,2,1,0:T(8,128)(2,1)} %param.18), kind=kLoop, calls=%fused_computation.266 | loop fusion | bytes 15925248 | tf_op jit(solution)/shard_map/slice | solution.py:61
  20.5 1.6 %convert_bitcast_fusion.1 = (bf16[1,256,384]{2,1,0:T(8,128)(2,1)S(1)}, bf16[1,256,384]{2,1,0:T(8,128)(2,1)S(1)}) fusion(bf16[384,384]{1,0:T(8,128)(2,1)} %param.13, bf16[256,384]{1,0:T(8,128)(2,1)} %fusion.54, bf16[384,384]{1,0:T(8,128)(2,1)} %param.12), kind=kOutput, calls=%fused_computation.240 | convolution fusion | flops 151486464 | bytes 1179648 | tf_op jit(solution)/shard_map/fqc,dc->fqd/dot_general | solution.py:117
  22.2 1.3 %collective-permute-start.2 = (bf16[1,128,384]{2,1,0:T(8,128)(2,1)}, bf16[1,128,384]{2,1,0:T(8,128)(2,1)S(1)}, u32[]{:S(2)}, u32[]{:S(2)}) collective-permute-start(bf16[1,128,384]{2,1,0:T(8,128)(2,1)} %get-tuple-element.43), channel_id=1, source_target_pairs={{0,4},{1,5},{2,6},{3,7},{4,0},{5,1},{6,2},{7,3},{8,12},{9,13},{10,... | collective-permute-start | bytes 294920 | tf_op jit(solution)/shard_map/ppermute | solution.py:40
  23.5 1.0 %pad_maximum_fusion.4 = bf16[1,256,384]{2,1,0:T(8,128)(2,1)S(1)} fusion(bf16[1,128,384]{2,1,0:T(8,128)(2,1)} %collective-permute-done.5, bf16[1,128,384]{2,1,0:T(8,128)(2,1)} %get-tuple-element.44), kind=kLoop, calls=%fused_computation.203 | loop fusion | flops 393216 | bytes 393216 | tf_op jit(solution)/shard_map/concatenate | solution.py:114
  24.5 2.6 %collective-permute-done.2 = bf16[1,128,384]{2,1,0:T(8,128)(2,1)S(1)} collective-permute-done((bf16[1,128,384]{2,1,0:T(8,128)(2,1)}, bf16[1,128,384]{2,1,0:T(8,128)(2,1)S(1)}, u32[]{:S(2)}, u32[]{:S(2)}) %collective-permute-start.2) | collective-permute-done | bytes 98336 | tf_op jit(solution)/shard_map/ppermute | solution.py:40
  27.1 2.9 %collective-permute-start.9 = (bf16[1,256,384]{2,1,0:T(8,128)(2,1)S(1)}, bf16[1,256,384]{2,1,0:T(8,128)(2,1)S(1)}, u32[]{:S(2)}, u32[]{:S(2)}) collective-permute-start(bf16[1,256,384]{2,1,0:T(8,128)(2,1)S(1)} %pad_maximum_fusion.4), channel_id=1, source_target_pairs={{0,12},{1,13},{2,14},{3,15},{4,8},{5,9},{6,10},{7,11},{8,4},{9,5},... | collective-permute-start | bytes 589832 | tf_op jit(solution)/shard_map/ppermute | solution.py:40
  29.9 0.7 constant_dynamic-update-slice_fusion.6
  30.6 0.7 collective-permute-start.8
  31.3 1.5 %constant_dynamic-update-slice_fusion.5 = bf16[1,768,384]{2,1,0:T(8,128)(2,1)} fusion(bf16[1,768,384]{2,1,0:T(8,128)(2,1)} %constant_dynamic-update-slice_fusion.6, bf16[1,128,384]{2,1,0:T(8,128)(2,1)} %collective-permute-done.3), kind=kLoop, calls=%fused_computation.246 | loop fusion | bytes 196608
  32.9 0.7 collective-permute-start.7
  33.6 1.5 %constant_dynamic-update-slice_fusion.4 = bf16[1,768,384]{2,1,0:T(8,128)(2,1)} fusion(bf16[1,768,384]{2,1,0:T(8,128)(2,1)} %constant_dynamic-update-slice_fusion.5, bf16[1,128,384]{2,1,0:T(8,128)(2,1)} %collective-permute-done.4), kind=kLoop, calls=%fused_computation.245 | loop fusion | bytes 196608
  35.1 1.5 %constant_dynamic-update-slice_fusion.3 = bf16[1,768,384]{2,1,0:T(8,128)(2,1)} fusion(bf16[1,768,384]{2,1,0:T(8,128)(2,1)} %constant_dynamic-update-slice_fusion.4, bf16[1,128,384]{2,1,0:T(8,128)(2,1)} %collective-permute-done.5), kind=kLoop, calls=%fused_computation.244 | loop fusion | bytes 196608 | tf_op jit(solution)/shard_map/concatenate | solution.py:112
  36.7 1.7 %convolution_bitcast_fusion.2 = f32[1,512,768]{2,1,0:T(8,128)S(1)} fusion(bf16[1,768,384]{2,1,0:T(8,128)(2,1)} %constant_dynamic-update-slice_fusion.3, bf16[1,256,384]{2,1,0:T(8,128)(2,1)S(1)} %get-tuple-element.42, bf16[1,256,384]{2,1,0:T(8,128)(2,1)S(1)} %get-tuple-element.41), kind=kOutput, calls=%fused_computation.6 | convolution fusion | flops 302776320 | bytes 2555904 | tf_op jit(solution)/shard_map/fqc,fkc->fqk/dot_general | solution.py:122
  38.5 1.1 %pad_maximum_fusion.3 = bf16[1,512,384]{2,1,0:T(8,128)(2,1)S(1)} fusion(bf16[1,128,384]{2,1,0:T(8,128)(2,1)} %collective-permute-done.4, bf16[1,128,384]{2,1,0:T(8,128)(2,1)} %collective-permute-done.3, bf16[1,128,384]{2,1,0:T(8,128)(2,1)S(1)} %collective-permute-done.2, bf16[1,128,384]{2,1,0:T(8,128)(2,1)} %get-tuple-element.43), kind=kLoop, calls=%fused_computation.82 | loop fusion | flops 1572864 | bytes 786432 | tf_op jit(solution)/shard_map/concatenate | solution.py:113
  39.6 2.4 %collective-permute-done.9 = bf16[1,256,384]{2,1,0:T(8,128)(2,1)S(1)} collective-permute-done((bf16[1,256,384]{2,1,0:T(8,128)(2,1)S(1)}, bf16[1,256,384]{2,1,0:T(8,128)(2,1)S(1)}, u32[]{:S(2)}, u32[]{:S(2)}) %collective-permute-start.9) | collective-permute-done | bytes 196640 | tf_op jit(solution)/shard_map/ppermute | solution.py:40
  42.3 2.0 %collective-permute-done.8 = bf16[1,256,384]{2,1,0:T(8,128)(2,1)S(1)} collective-permute-done((bf16[1,256,384]{2,1,0:T(8,128)(2,1)S(1)}, bf16[1,256,384]{2,1,0:T(8,128)(2,1)S(1)}, u32[]{:S(2)}, u32[]{:S(2)}) %collective-permute-start.8) | collective-permute-done | bytes 196640 | tf_op jit(solution)/shard_map/ppermute | solution.py:40
  44.3 0.9 %collective-permute-start.6 = (bf16[1,512,384]{2,1,0:T(8,128)(2,1)S(1)}, bf16[1,512,384]{2,1,0:T(8,128)(2,1)S(1)}, u32[]{:S(2)}, u32[]{:S(2)}) collective-permute-start(bf16[1,512,384]{2,1,0:T(8,128)(2,1)S(1)} %pad_maximum_fusion.3), channel_id=1, source_target_pairs={{0,2},{1,3},{2,0},{3,1},{4,6},{5,7},{6,4},{7,5},{8,10},{9,11},{10,... | collective-permute-start | bytes 1179656 | tf_op jit(solution)/shard_map/ppermute | solution.py:40
  46.1 0.6 collective-permute-start.13
  46.7 1.0 %constant_dynamic-update-slice_fusion.2 = bf16[2,6,128,384]{3,2,1,0:T(8,128)(2,1)S(1)} fusion(bf16[2,2,128,384]{3,2,1,0:T(8,128)(2,1)} %collective-permute-done), kind=kLoop, calls=%fused_computation.243 | loop fusion | bytes 786432
  47.9 1.1 %constant_dynamic-update-slice_fusion = bf16[2,6,128,384]{3,2,1,0:T(8,128)(2,1)S(1)} fusion(bf16[2,6,128,384]{3,2,1,0:T(8,128)(2,1)S(1)} %constant_dynamic-update-slice_fusion.1, bf16[2,2,128,384]{3,2,1,0:T(8,128)(2,1)} %collective-permute-done.1), kind=kLoop, calls=%fused_computation.241 | loop fusion | bytes 786432 | tf_op jit(solution)/shard_map/concatenate | solution.py:21
  48.9 0.6 pad_slice_fusion.1
  49.5 0.7 pad_maximum_fusion
  50.3 1.0 %fusion.184 = (bf16[1,4,128,1152]{3,2,1,0:T(8,128)(2,1)S(1)}, bf16[1,4,128,1152]{3,2,1,0:T(8,128)(2,1)S(1)}, bf16[1,4,128,1152]{3,2,1,0:T(8,128)(2,1)S(1)}, bf16...) fusion(bf16[2,6,128,1152]{3,2,1,0:T(8,128)(2,1)S(1)} %pad_maximum, ...), kind=kLoop, calls=%fused_computation.267 | loop fusion | bytes 14155776 | tf_op jit(solution)/shard_map/slice | solution.py:58
  51.5 0.8 fusion.192
  52.6 0.8 convolution_add_fusion.5
  53.8 0.8 convolution_add_fusion.4
  55.0 0.8 convolution_add_fusion.3
  55.8 0.8 convolution_add_fusion.2
  58.9 0.6 convolution_bitcast_fusion.1
  66.4 4.3 %collective-permute-start.16 = (bf16[1,2,128,384]{3,2,1,0:T(8,128)(2,1)S(1)}, bf16[1,2,128,384]{3,2,1,0:T(8,128)(2,1)S(1)}, u32[]{:S(2)}, u32[]{:S(2)}) collective-permute-start(bf16[1,2,128,384]{3,2,1,0:T(8,128)(2,1)S(1)} %bitcast.486), channel_id=1, source_target_pairs={{1,0},{2,1},{3,2},{4,3},{5,4},{6,5},{7,6},{8,7},{9,8},{10,9},{11,1... | collective-permute-start | bytes 589832 | tf_op jit(solution)/shard_map/ppermute | solution.py:20
  70.7 2.1 %collective-permute-start.15 = (bf16[1,2,128,384]{3,2,1,0:T(8,128)(2,1)S(1)}, bf16[1,2,128,384]{3,2,1,0:T(8,128)(2,1)S(1)}, u32[]{:S(2)}, u32[]{:S(2)}) collective-permute-start(bf16[1,2,128,384]{3,2,1,0:T(8,128)(2,1)S(1)} %bitcast.487), channel_id=1, source_target_pairs={{0,1},{1,2},{2,3},{3,4},{4,5},{5,6},{6,7},{7,8},{8,9},{9,10},{10,1... | collective-permute-start | bytes 589832 | tf_op jit(solution)/shard_map/ppermute | solution.py:19
  72.9 0.8 convolution_add_fusion.1
  73.9 4.7 %collective-permute-done.15 = bf16[1,2,128,384]{3,2,1,0:T(8,128)(2,1)S(1)} collective-permute-done((bf16[1,2,128,384]{3,2,1,0:T(8,128)(2,1)S(1)}, bf16[1,2,128,384]{3,2,1,0:T(8,128)(2,1)S(1)}, u32[]{:S(2)}, u32[]{:S(2)}) %collective-permute-start.15) | collective-permute-done | bytes 196640 | tf_op jit(solution)/shard_map/ppermute | solution.py:19
  79.7 0.7 copy-done.9
  80.4 0.8 fusion.194
  81.6 0.8 fusion.193
  82.8 0.8 fusion.2
  83.7 1.5 %convolution_bitcast_fusion = f32[1,4,130,3,3,192]{5,2,4,3,1,0:T(8,128)S(1)} fusion(bf16[3,3,384,192]{2,3,1,0:T(8,128)(2,1)S(1)} %copy-done, bf16[1,4,128,384]{3,2,1,0:T(8,128)(2,1)S(1)} %select_convert_fusion), kind=kOutput, calls=%fused_computation.1 | convolution fusion | flops 690094080 | bytes 5314560 | tf_op jit(solution)/shard_map/frwc,ijco->frwijo/dot_general | solution.py:73
  86.8 1.3 %convert_element_type.183 = bf16[1,4,49152]{2,1,0:T(4,128)(2,1)} reshape(bf16[1,2,2,128,2,192]{5,4,3,2,1,0:T(2,128)(2,1)S(1)} %copy.61) | data formatting | bytes 786432 | tf_op jit(solution)/shard_map/convert_element_type | solution.py:90
  (97 shorter events, 15.6 us)
Async XLA Ops:
  0.0 83.7 %copy-start = (bf16[3,3,384,192]{2,3,1,0:T(8,128)(2,1)S(1)}, bf16[3,3,384,192]{2,3,1,0:T(8,128)(2,1)}, u32[]{:S(2)}) copy-start(bf16[3,3,384,192]{2,3,1,0:T(8,128)(2,1)} %param.19) | copy-start | bytes 3981316
  0.0 13.5 %copy-start.6 = (bf16[1,2,128,384]{3,2,1,0:T(8,128)(2,1)S(1)}, bf16[1,2,128,384]{3,2,1,0:T(8,128)(2,1)}, u32[]{:S(2)}) copy-start(bf16[1,2,128,384]{3,2,1,0:T(8,128)(2,1)} %param.10) | copy-start | bytes 589828
  0.0 46.1 %collective-permute-start = (bf16[2,2,128,384]{3,2,1,0:T(8,128)(2,1)}, bf16[2,2,128,384]{3,2,1,0:T(8,128)(2,1)}, u32[]{:S(2)}, u32[]{:S(2)}) collective-permute-start(bf16[2,2,128,384]{3,2,1,0:T(8,128)(2,1)} %param.16), channel_id=1, source_target_pairs={{0,1},{1,2},{2,3},{3,4},{4,5},{5,6},{6,7},{7,8},{8,9},{9,10},{10,1... | collective-permute-start | bytes 1179656 | tf_op jit(solution)/shard_map/ppermute | solution.py:19
  2.1 45.7 %collective-permute-start.1 = (bf16[2,2,128,384]{3,2,1,0:T(8,128)(2,1)}, bf16[2,2,128,384]{3,2,1,0:T(8,128)(2,1)}, u32[]{:S(2)}, u32[]{:S(2)}) collective-permute-start(bf16[2,2,128,384]{3,2,1,0:T(8,128)(2,1)} %param.16), channel_id=1, source_target_pairs={{1,0},{2,1},{3,2},{4,3},{5,4},{6,5},{7,6},{8,7},{9,8},{10,9},{11,1... | collective-permute-start | bytes 1179656 | tf_op jit(solution)/shard_map/ppermute | solution.py:20
  10.1 22.8 %collective-permute-start.4 = (bf16[1,128,384]{2,1,0:T(8,128)(2,1)}, bf16[1,128,384]{2,1,0:T(8,128)(2,1)}, u32[]{:S(2)}, u32[]{:S(2)}) collective-permute-start(bf16[1,128,384]{2,1,0:T(8,128)(2,1)} %get-tuple-element.43), channel_id=1, source_target_pairs={{0,12},{1,13},{2,14},{3,15},{4,8},{5,9},{6,10},{7,11},{8,4},{9,5},... | collective-permute-start | bytes 294920 | tf_op jit(solution)/shard_map/ppermute | solution.py:40
  11.7 18.9 %collective-permute-start.3 = (bf16[1,128,384]{2,1,0:T(8,128)(2,1)}, bf16[1,128,384]{2,1,0:T(8,128)(2,1)}, u32[]{:S(2)}, u32[]{:S(2)}) collective-permute-start(bf16[1,128,384]{2,1,0:T(8,128)(2,1)} %get-tuple-element.43), channel_id=1, source_target_pairs={{0,8},{1,9},{2,10},{3,11},{4,12},{5,13},{6,14},{7,15},{8,0},{9,1},... | collective-permute-start | bytes 294920 | tf_op jit(solution)/shard_map/ppermute | solution.py:40
  12.7 9.5 %collective-permute-start.5 = (bf16[1,128,384]{2,1,0:T(8,128)(2,1)}, bf16[1,128,384]{2,1,0:T(8,128)(2,1)}, u32[]{:S(2)}, u32[]{:S(2)}) collective-permute-start(bf16[1,128,384]{2,1,0:T(8,128)(2,1)} %get-tuple-element.44), channel_id=1, source_target_pairs={{0,2},{1,3},{2,0},{3,1},{4,6},{5,7},{6,4},{7,5},{8,10},{9,11},{10,... | collective-permute-start | bytes 294920 | tf_op jit(solution)/shard_map/ppermute | solution.py:40
  22.2 4.9 %collective-permute-start.2 = (bf16[1,128,384]{2,1,0:T(8,128)(2,1)}, bf16[1,128,384]{2,1,0:T(8,128)(2,1)S(1)}, u32[]{:S(2)}, u32[]{:S(2)}) collective-permute-start(bf16[1,128,384]{2,1,0:T(8,128)(2,1)} %get-tuple-element.43), channel_id=1, source_target_pairs={{0,4},{1,5},{2,6},{3,7},{4,0},{5,1},{6,2},{7,3},{8,12},{9,13},{10,... | collective-permute-start | bytes 294920 | tf_op jit(solution)/shard_map/ppermute | solution.py:40
  27.1 14.9 %collective-permute-start.9 = (bf16[1,256,384]{2,1,0:T(8,128)(2,1)S(1)}, bf16[1,256,384]{2,1,0:T(8,128)(2,1)S(1)}, u32[]{:S(2)}, u32[]{:S(2)}) collective-permute-start(bf16[1,256,384]{2,1,0:T(8,128)(2,1)S(1)} %pad_maximum_fusion.4), channel_id=1, source_target_pairs={{0,12},{1,13},{2,14},{3,15},{4,8},{5,9},{6,10},{7,11},{8,4},{9,5},... | collective-permute-start | bytes 589832 | tf_op jit(solution)/shard_map/ppermute | solution.py:40
  30.6 13.7 %collective-permute-start.8 = (bf16[1,256,384]{2,1,0:T(8,128)(2,1)S(1)}, bf16[1,256,384]{2,1,0:T(8,128)(2,1)S(1)}, u32[]{:S(2)}, u32[]{:S(2)}) collective-permute-start(bf16[1,256,384]{2,1,0:T(8,128)(2,1)S(1)} %pad_maximum_fusion.4), channel_id=1, source_target_pairs={{0,8},{1,9},{2,10},{3,11},{4,12},{5,13},{6,14},{7,15},{8,0},{9,1},... | collective-permute-start | bytes 589832 | tf_op jit(solution)/shard_map/ppermute | solution.py:40
  32.9 12.7 %collective-permute-start.7 = (bf16[1,256,384]{2,1,0:T(8,128)(2,1)S(1)}, bf16[1,256,384]{2,1,0:T(8,128)(2,1)S(1)}, u32[]{:S(2)}, u32[]{:S(2)}) collective-permute-start(bf16[1,256,384]{2,1,0:T(8,128)(2,1)S(1)} %pad_maximum_fusion.4), channel_id=1, source_target_pairs={{0,4},{1,5},{2,6},{3,7},{4,0},{5,1},{6,2},{7,3},{8,12},{9,13},{10,... | collective-permute-start | bytes 589832 | tf_op jit(solution)/shard_map/ppermute | solution.py:40
  38.3 3.6 %copy-start.5 = (bf16[1,768,384]{2,1,0:T(8,128)(2,1)S(1)}, bf16[1,768,384]{2,1,0:T(8,128)(2,1)}, u32[]{:S(2)}) copy-start(bf16[1,768,384]{2,1,0:T(8,128)(2,1)} %constant_dynamic-update-slice_fusion.3) | copy-start | bytes 1769476
  42.0 16.9 %collective-permute-start.10 = (bf16[1,768,384]{2,1,0:T(8,128)(2,1)S(1)}, bf16[1,768,384]{2,1,0:T(8,128)(2,1)S(1)}, u32[]{:S(2)}, u32[]{:S(2)}) collective-permute-start(bf16[1,768,384]{2,1,0:T(8,128)(2,1)S(1)} %copy-done.5), channel_id=1, source_target_pairs={{0,1},{1,0},{2,3},{3,2},{4,5},{5,4},{6,7},{7,6},{8,9},{9,8},{10,11... | collective-permute-start | bytes 1769480 | tf_op jit(solution)/shard_map/ppermute | solution.py:40
  44.3 13.1 %collective-permute-start.6 = (bf16[1,512,384]{2,1,0:T(8,128)(2,1)S(1)}, bf16[1,512,384]{2,1,0:T(8,128)(2,1)S(1)}, u32[]{:S(2)}, u32[]{:S(2)}) collective-permute-start(bf16[1,512,384]{2,1,0:T(8,128)(2,1)S(1)} %pad_maximum_fusion.3), channel_id=1, source_target_pairs={{0,2},{1,3},{2,0},{3,1},{4,6},{5,7},{6,4},{7,5},{8,10},{9,11},{10,... | collective-permute-start | bytes 1179656 | tf_op jit(solution)/shard_map/ppermute | solution.py:40
  45.6 2.1 %copy-start.11 = (bf16[2,2,128,384]{3,2,1,0:T(8,128)(2,1)S(1)}, bf16[2,2,128,384]{3,2,1,0:T(8,128)(2,1)}, u32[]{:S(2)}) copy-start(bf16[2,2,128,384]{3,2,1,0:T(8,128)(2,1)} %param.16) | copy-start | bytes 1179652
  45.6 10.9 %collective-permute-start.14 = (bf16[1,256,384]{2,1,0:T(8,128)(2,1)S(1)}, bf16[1,256,384]{2,1,0:T(8,128)(2,1)S(1)}, u32[]{:S(2)}, u32[]{:S(2)}) collective-permute-start(bf16[1,256,384]{2,1,0:T(8,128)(2,1)S(1)} %collective-permute-done.9), channel_id=1, source_target_pairs={{0,1},{1,0},{2,3},{3,2},{4,5},{5,4},{6,7},{7,6},{8,9},{9,8},{10,11... | collective-permute-start | bytes 589832 | tf_op jit(solution)/shard_map/ppermute | solution.py:40
  46.1 10.9 %collective-permute-start.13 = (bf16[1,256,384]{2,1,0:T(8,128)(2,1)S(1)}, bf16[1,256,384]{2,1,0:T(8,128)(2,1)S(1)}, u32[]{:S(2)}, u32[]{:S(2)}) collective-permute-start(bf16[1,256,384]{2,1,0:T(8,128)(2,1)S(1)} %collective-permute-done.8), channel_id=1, source_target_pairs={{0,1},{1,0},{2,3},{3,2},{4,5},{5,4},{6,7},{7,6},{8,9},{9,8},{10,11... | collective-permute-start | bytes 589832 | tf_op jit(solution)/shard_map/ppermute | solution.py:40
  47.8 10.7 %collective-permute-start.12 = (bf16[1,256,384]{2,1,0:T(8,128)(2,1)S(1)}, bf16[1,256,384]{2,1,0:T(8,128)(2,1)S(1)}, u32[]{:S(2)}, u32[]{:S(2)}) collective-permute-start(bf16[1,256,384]{2,1,0:T(8,128)(2,1)S(1)} %collective-permute-done.7), channel_id=1, source_target_pairs={{0,1},{1,0},{2,3},{3,2},{4,5},{5,4},{6,7},{7,6},{8,9},{9,8},{10,11... | collective-permute-start | bytes 589832 | tf_op jit(solution)/shard_map/ppermute | solution.py:40
  50.3 1.2 %copy-start.10 = (bf16[1,1,3,384,384]{4,3,2,1,0:T(8,128)(2,1)S(1)}, bf16[1,1,3,384,384]{4,3,2,1,0:T(8,128)(2,1)}, u32[]{:S(2)}) copy-start(bf16[1,1,3,384,384]{4,3,2,1,0:T(8,128)(2,1)} %get-tuple-element.20) | copy-start | bytes 2654212
  51.4 1.2 %copy-start.3 = (bf16[1,1,3,384,384]{4,3,2,1,0:T(8,128)(2,1)S(1)}, bf16[1,1,3,384,384]{4,3,2,1,0:T(8,128)(2,1)}, u32[]{:S(2)}) copy-start(bf16[1,1,3,384,384]{4,3,2,1,0:T(8,128)(2,1)} %get-tuple-element.21) | copy-start | bytes 2654212
  52.6 1.2 %copy-start.2 = (bf16[1,1,3,384,384]{4,3,2,1,0:T(8,128)(2,1)S(1)}, bf16[1,1,3,384,384]{4,3,2,1,0:T(8,128)(2,1)}, u32[]{:S(2)}) copy-start(bf16[1,1,3,384,384]{4,3,2,1,0:T(8,128)(2,1)} %get-tuple-element.19) | copy-start | bytes 2654212
  53.8 1.2 %copy-start.1 = (bf16[1,1,3,384,384]{4,3,2,1,0:T(8,128)(2,1)S(1)}, bf16[1,1,3,384,384]{4,3,2,1,0:T(8,128)(2,1)}, u32[]{:S(2)}) copy-start(bf16[1,1,3,384,384]{4,3,2,1,0:T(8,128)(2,1)} %get-tuple-element.18) | copy-start | bytes 2654212
  57.4 2.3 %collective-permute-start.11 = (bf16[1,512,384]{2,1,0:T(8,128)(2,1)S(1)}, bf16[1,512,384]{2,1,0:T(8,128)(2,1)S(1)}, u32[]{:S(2)}, u32[]{:S(2)}) collective-permute-start(bf16[1,512,384]{2,1,0:T(8,128)(2,1)S(1)} %collective-permute-done.6), channel_id=1, source_target_pairs={{0,1},{1,0},{2,3},{3,2},{4,5},{5,4},{6,7},{7,6},{8,9},{9,8},{10,11... | collective-permute-start | bytes 1179656 | tf_op jit(solution)/shard_map/ppermute | solution.py:40
  64.2 1.0 %copy-start.12 = (bf16[384,384]{1,0:T(8,128)(2,1)S(1)}, bf16[384,384]{1,0:T(8,128)(2,1)}, u32[]{:S(2)}) copy-start(bf16[384,384]{1,0:T(8,128)(2,1)} %param.14) | copy-start | bytes 884740
  64.6 1.0 %copy-start.7 = (bf16[1,2,128,384]{3,2,1,0:T(8,128)(2,1)S(1)}, bf16[1,2,128,384]{3,2,1,0:T(8,128)(2,1)}, u32[]{:S(2)}) copy-start(bf16[1,2,128,384]{3,2,1,0:T(8,128)(2,1)} %param.10) | copy-start | bytes 589828
  64.6 1.1 %copy-start.14 = (bf16[384,384]{1,0:T(8,128)(2,1)S(1)}, bf16[384,384]{1,0:T(8,128)(2,1)}, u32[]{:S(2)}) copy-start(bf16[384,384]{1,0:T(8,128)(2,1)} %param.15) | copy-start | bytes 884740
  65.5 0.7 copy-start.13
  66.4 7.5 %collective-permute-start.16 = (bf16[1,2,128,384]{3,2,1,0:T(8,128)(2,1)S(1)}, bf16[1,2,128,384]{3,2,1,0:T(8,128)(2,1)S(1)}, u32[]{:S(2)}, u32[]{:S(2)}) collective-permute-start(bf16[1,2,128,384]{3,2,1,0:T(8,128)(2,1)S(1)} %bitcast.486), channel_id=1, source_target_pairs={{1,0},{2,1},{3,2},{4,3},{5,4},{6,5},{7,6},{8,7},{9,8},{10,9},{11,1... | collective-permute-start | bytes 589832 | tf_op jit(solution)/shard_map/ppermute | solution.py:20
  70.7 7.9 %collective-permute-start.15 = (bf16[1,2,128,384]{3,2,1,0:T(8,128)(2,1)S(1)}, bf16[1,2,128,384]{3,2,1,0:T(8,128)(2,1)S(1)}, u32[]{:S(2)}, u32[]{:S(2)}) collective-permute-start(bf16[1,2,128,384]{3,2,1,0:T(8,128)(2,1)S(1)} %bitcast.487), channel_id=1, source_target_pairs={{0,1},{1,2},{2,3},{3,4},{4,5},{5,6},{6,7},{7,8},{8,9},{9,10},{10,1... | collective-permute-start | bytes 589832 | tf_op jit(solution)/shard_map/ppermute | solution.py:19
  79.3 1.2 %copy-start.9 = (bf16[1,1,3,384,384]{4,3,2,1,0:T(8,128)(2,1)S(1)}, bf16[1,1,3,384,384]{4,3,2,1,0:T(8,128)(2,1)}, u32[]{:S(2)}) copy-start(bf16[1,1,3,384,384]{4,3,2,1,0:T(8,128)(2,1)} %get-tuple-element.22) | copy-start | bytes 2654212
  80.4 1.2 %copy-start.8 = (bf16[1,1,3,384,384]{4,3,2,1,0:T(8,128)(2,1)S(1)}, bf16[1,1,3,384,384]{4,3,2,1,0:T(8,128)(2,1)}, u32[]{:S(2)}) copy-start(bf16[1,1,3,384,384]{4,3,2,1,0:T(8,128)(2,1)} %get-tuple-element.23) | copy-start | bytes 2654212
  81.6 1.2 %copy-start.4 = (bf16[1,1,3,384,384]{4,3,2,1,0:T(8,128)(2,1)S(1)}, bf16[1,1,3,384,384]{4,3,2,1,0:T(8,128)(2,1)}, u32[]{:S(2)}) copy-start(bf16[1,1,3,384,384]{4,3,2,1,0:T(8,128)(2,1)} %get-tuple-element.15) | copy-start | bytes 2654212

commit v9 on v8

--- a/solution.py
+++ b/solution.py
@@ -2,6 +2,7 @@
 import jax.numpy as jnp
 from jax import lax
 from jax.sharding import PartitionSpec as P
+
 
 EPS = 1e-06
 
@@ -66,7 +67,7 @@
 
 
 def upsample_conv(extended, w_up):
-    nf, rp, ncols, chans = extended.shape
+    nf, rp, ncols, _ = extended.shape
     nrows = rp - 2
     outs = w_up.shape[-1]
     padded = jnp.pad(extended, ((0, 0), (0, 0), (1, 1), (0, 0)))
@@ -90,7 +91,7 @@
     return result.astype(jnp.bfloat16).reshape(nf, 2 * nrows, 2 * ncols * outs)
 
 
-def body(
+def layer(
     frames, norm_attn, w_query, w_key, w_value, w_out, cache_one, norm_conv, conv_weight, w_up
 ):
     nframes, nrows, ncols, chans = frames.shape
@@ -167,5 +168,5 @@
         P(),
     )
     return jax.shard_map(
-        body, mesh=mesh, in_specs=placed, out_specs=P("clips", ROWS, None), check_vma=False
+        layer, mesh=mesh, in_specs=placed, out_specs=P("clips", ROWS, None), check_vma=False
     )

time: 89 us -> 89 us (level)
  no operation moved by 1% of the time
where the time goes in v9:
time: 89 us; the launch traced here: 88.1 us
  starting transfers between devices  24.3 us (27%)
  local copies, waits for them, and re-layouts  21.2 us (24%)
  matrix products  19.5 us (22%)
  waiting for transfers between devices  11.9 us (13%)
  other arithmetic  10.6 us (12%)
    ppermute x13, starting transfers between devices, exchange(): lax.ppermute(values, ROWS, [(i, i ^ mask) for i in range(size)])  11.2 us
    ppermute x2, starting transfers between devices, padded_2(): after = lax.ppermute(first, axis, down)  8.85 us
    unnamed x35, local copies, waits for them, and re-layouts  8.32 us
    dot_general x9, matrix products, conv_rows(): jnp.dot(part, weight[tstep, rstep].reshape(3 * chans, -1), preferred_elem...  7.15 us
    ppermute x13, waiting for transfers between devices, exchange(): lax.ppermute(values, ROWS, [(i, i ^ mask) for i in range(size)])  7 us
    slice x1, local copies, waits for them, and re-layouts, conv_rows(): weight[tstep, rstep].reshape(3 * chans, -1)  5.49 us
    dot_general x10, matrix products, layer(): jnp.einsum('fqc,fkc->fqk', q_pair, piece, preferred_element_type=jnp.floa...  5.13 us
    ppermute x2, waiting for transfers between devices, padded_2(): before = lax.ppermute(last, axis, up)  4.72 us
  transfers between devices with their start and end apart: 17, of which 5 were waited for; matrix products, arithmetic and copies ran while one was open for 39% of the time, Pallas kernels for 0%

profile of v9, /device:TPU:8, one launch (start us, length us, event | category | flops | bytes accessed | tf_op | source)
XLA Modules:
  0.0 88.1 jit_solution(8972485594804877384)
XLA Ops:
  0.0 2.0 %collective-permute-start = (bf16[2,2,128,384]{3,2,1,0:T(8,128)(2,1)}, bf16[2,2,128,384]{3,2,1,0:T(8,128)(2,1)}, u32[]{:S(2)}, u32[]{:S(2)}) collective-permute-start(bf16[2,2,128,384]{3,2,1,0:T(8,128)(2,1)} %param.16), channel_id=1, source_target_pairs={{0,1},{1,2},{2,3},{3,4},{4,5},{5,6},{6,7},{7,8},{8,9},{9,10},{10,1... | collective-permute-start | bytes 1179656 | tf_op jit(solution)/shard_map/ppermute | solution.py:20
  2.1 4.5 %collective-permute-start.1 = (bf16[2,2,128,384]{3,2,1,0:T(8,128)(2,1)}, bf16[2,2,128,384]{3,2,1,0:T(8,128)(2,1)}, u32[]{:S(2)}, u32[]{:S(2)}) collective-permute-start(bf16[2,2,128,384]{3,2,1,0:T(8,128)(2,1)} %param.16), channel_id=1, source_target_pairs={{1,0},{2,1},{3,2},{4,3},{5,4},{6,5},{7,6},{8,7},{9,8},{10,9},{11,1... | collective-permute-start | bytes 1179656 | tf_op jit(solution)/shard_map/ppermute | solution.py:21
  6.6 1.0 %multiply_reduce_fusion.1 = f32[2,128]{1,0:T(2,128)S(1)} fusion(bf16[1,2,128,384]{3,2,1,0:T(8,128)(2,1)} %param.10), kind=kLoop, calls=%fused_computation.103 | loop fusion | flops 294656 | bytes 197632 | tf_op jit(solution)/shard_map/reduce_sum | solution.py:27
  7.7 1.7 %constant_dynamic-update-slice_fusion.7 = (bf16[1,768,384]{2,1,0:T(8,128)(2,1)}, bf16[1,256,384]{2,1,0:T(8,128)(2,1)S(1)}) fusion(f32[384]{0:T(512)} %param.11, f32[256]{0:T(256)S(1)} %rsqrt_bitcast_fusion, bf16[1,2,128,384]{3,2,1,0:T(8,128)(2,1)} %param.10), kind=kLoop, calls=%fused_computation.248 | loop fusion | flops 393215 | bytes 592384
  9.4 0.7 fusion.187
  10.1 1.6 %collective-permute-start.4 = (bf16[1,128,384]{2,1,0:T(8,128)(2,1)}, bf16[1,128,384]{2,1,0:T(8,128)(2,1)}, u32[]{:S(2)}, u32[]{:S(2)}) collective-permute-start(bf16[1,128,384]{2,1,0:T(8,128)(2,1)} %get-tuple-element.43), channel_id=1, source_target_pairs={{0,12},{1,13},{2,14},{3,15},{4,8},{5,9},{6,10},{7,11},{8,4},{9,5},... | collective-permute-start | bytes 294920 | tf_op jit(solution)/shard_map/ppermute | solution.py:41
  11.7 1.0 %collective-permute-start.3 = (bf16[1,128,384]{2,1,0:T(8,128)(2,1)}, bf16[1,128,384]{2,1,0:T(8,128)(2,1)}, u32[]{:S(2)}, u32[]{:S(2)}) collective-permute-start(bf16[1,128,384]{2,1,0:T(8,128)(2,1)} %get-tuple-element.43), channel_id=1, source_target_pairs={{0,8},{1,9},{2,10},{3,11},{4,12},{5,13},{6,14},{7,15},{8,0},{9,1},... | collective-permute-start | bytes 294920 | tf_op jit(solution)/shard_map/ppermute | solution.py:41
  12.7 0.8 collective-permute-start.5
  13.5 1.5 %fusion.54 = bf16[256,384]{1,0:T(8,128)(2,1)} fusion(bf16[1,2,128,384]{3,2,1,0:T(8,128)(2,1)S(1)} %copy-done.6, f32[384]{0:T(512)} %param.11, f32[256]{0:T(256)S(1)} %rsqrt_bitcast_fusion), kind=kLoop, calls=%fused_computation.96 | loop fusion | flops 393216 | bytes 395776 | tf_op jit(solution)/shard_map/convert_element_type | solution.py:104
  15.0 5.5 %fusion.183 = (bf16[1,1,3,384,384]{4,3,2,1,0:T(8,128)(2,1)}, bf16[1,1,3,384,384]{4,3,2,1,0:T(8,128)(2,1)S(1)}, bf16[1,1,3,384,384]{4,3,2,1,0:T(8,128)(2,1)S(1)},...) fusion(bf16[3,3,3,384,384]{4,3,2,1,0:T(8,128)(2,1)} %param.18), kind=kLoop, calls=%fused_computation.266 | loop fusion | bytes 15925248 | tf_op jit(solution)/shard_map/slice | solution.py:62
  20.5 1.6 %convert_bitcast_fusion.1 = (bf16[1,256,384]{2,1,0:T(8,128)(2,1)S(1)}, bf16[1,256,384]{2,1,0:T(8,128)(2,1)S(1)}) fusion(bf16[384,384]{1,0:T(8,128)(2,1)} %param.13, bf16[256,384]{1,0:T(8,128)(2,1)} %fusion.54, bf16[384,384]{1,0:T(8,128)(2,1)} %param.12), kind=kOutput, calls=%fused_computation.240 | convolution fusion | flops 151486464 | bytes 1179648 | tf_op jit(solution)/shard_map/fqc,dc->fqd/dot_general | solution.py:118
  22.2 1.3 %collective-permute-start.2 = (bf16[1,128,384]{2,1,0:T(8,128)(2,1)}, bf16[1,128,384]{2,1,0:T(8,128)(2,1)S(1)}, u32[]{:S(2)}, u32[]{:S(2)}) collective-permute-start(bf16[1,128,384]{2,1,0:T(8,128)(2,1)} %get-tuple-element.43), channel_id=1, source_target_pairs={{0,4},{1,5},{2,6},{3,7},{4,0},{5,1},{6,2},{7,3},{8,12},{9,13},{10,... | collective-permute-start | bytes 294920 | tf_op jit(solution)/shard_map/ppermute | solution.py:41
  23.5 1.0 %pad_maximum_fusion.4 = bf16[1,256,384]{2,1,0:T(8,128)(2,1)S(1)} fusion(bf16[1,128,384]{2,1,0:T(8,128)(2,1)} %collective-permute-done.5, bf16[1,128,384]{2,1,0:T(8,128)(2,1)} %get-tuple-element.44), kind=kLoop, calls=%fused_computation.203 | loop fusion | flops 393216 | bytes 393216 | tf_op jit(solution)/shard_map/concatenate | solution.py:115
  24.5 2.6 %collective-permute-done.2 = bf16[1,128,384]{2,1,0:T(8,128)(2,1)S(1)} collective-permute-done((bf16[1,128,384]{2,1,0:T(8,128)(2,1)}, bf16[1,128,384]{2,1,0:T(8,128)(2,1)S(1)}, u32[]{:S(2)}, u32[]{:S(2)}) %collective-permute-start.2) | collective-permute-done | bytes 98336 | tf_op jit(solution)/shard_map/ppermute | solution.py:41
  27.1 2.9 %collective-permute-start.9 = (bf16[1,256,384]{2,1,0:T(8,128)(2,1)S(1)}, bf16[1,256,384]{2,1,0:T(8,128)(2,1)S(1)}, u32[]{:S(2)}, u32[]{:S(2)}) collective-permute-start(bf16[1,256,384]{2,1,0:T(8,128)(2,1)S(1)} %pad_maximum_fusion.4), channel_id=1, source_target_pairs={{0,12},{1,13},{2,14},{3,15},{4,8},{5,9},{6,10},{7,11},{8,4},{9,5},... | collective-permute-start | bytes 589832 | tf_op jit(solution)/shard_map/ppermute | solution.py:41
  29.9 0.7 constant_dynamic-update-slice_fusion.6
  30.6 0.7 collective-permute-start.8
  31.3 1.5 %constant_dynamic-update-slice_fusion.5 = bf16[1,768,384]{2,1,0:T(8,128)(2,1)} fusion(bf16[1,768,384]{2,1,0:T(8,128)(2,1)} %constant_dynamic-update-slice_fusion.6, bf16[1,128,384]{2,1,0:T(8,128)(2,1)} %collective-permute-done.3), kind=kLoop, calls=%fused_computation.246 | loop fusion | bytes 196608
  32.9 0.7 collective-permute-start.7
  33.6 1.5 %constant_dynamic-update-slice_fusion.4 = bf16[1,768,384]{2,1,0:T(8,128)(2,1)} fusion(bf16[1,768,384]{2,1,0:T(8,128)(2,1)} %constant_dynamic-update-slice_fusion.5, bf16[1,128,384]{2,1,0:T(8,128)(2,1)} %collective-permute-done.4), kind=kLoop, calls=%fused_computation.245 | loop fusion | bytes 196608
  35.1 1.5 %constant_dynamic-update-slice_fusion.3 = bf16[1,768,384]{2,1,0:T(8,128)(2,1)} fusion(bf16[1,768,384]{2,1,0:T(8,128)(2,1)} %constant_dynamic-update-slice_fusion.4, bf16[1,128,384]{2,1,0:T(8,128)(2,1)} %collective-permute-done.5), kind=kLoop, calls=%fused_computation.244 | loop fusion | bytes 196608 | tf_op jit(solution)/shard_map/concatenate | solution.py:113
  36.7 1.7 %convolution_bitcast_fusion.2 = f32[1,512,768]{2,1,0:T(8,128)S(1)} fusion(bf16[1,768,384]{2,1,0:T(8,128)(2,1)} %constant_dynamic-update-slice_fusion.3, bf16[1,256,384]{2,1,0:T(8,128)(2,1)S(1)} %get-tuple-element.42, bf16[1,256,384]{2,1,0:T(8,128)(2,1)S(1)} %get-tuple-element.41), kind=kOutput, calls=%fused_computation.6 | convolution fusion | flops 302776320 | bytes 2555904 | tf_op jit(solution)/shard_map/fqc,fkc->fqk/dot_general | solution.py:123
  38.5 1.1 %pad_maximum_fusion.3 = bf16[1,512,384]{2,1,0:T(8,128)(2,1)S(1)} fusion(bf16[1,128,384]{2,1,0:T(8,128)(2,1)} %collective-permute-done.4, bf16[1,128,384]{2,1,0:T(8,128)(2,1)} %collective-permute-done.3, bf16[1,128,384]{2,1,0:T(8,128)(2,1)S(1)} %collective-permute-done.2, bf16[1,128,384]{2,1,0:T(8,128)(2,1)} %get-tuple-element.43), kind=kLoop, calls=%fused_computation.82 | loop fusion | flops 1572864 | bytes 786432 | tf_op jit(solution)/shard_map/concatenate | solution.py:114
  39.6 2.4 %collective-permute-done.9 = bf16[1,256,384]{2,1,0:T(8,128)(2,1)S(1)} collective-permute-done((bf16[1,256,384]{2,1,0:T(8,128)(2,1)S(1)}, bf16[1,256,384]{2,1,0:T(8,128)(2,1)S(1)}, u32[]{:S(2)}, u32[]{:S(2)}) %collective-permute-start.9) | collective-permute-done | bytes 196640 | tf_op jit(solution)/shard_map/ppermute | solution.py:41
  42.3 2.0 %collective-permute-done.8 = bf16[1,256,384]{2,1,0:T(8,128)(2,1)S(1)} collective-permute-done((bf16[1,256,384]{2,1,0:T(8,128)(2,1)S(1)}, bf16[1,256,384]{2,1,0:T(8,128)(2,1)S(1)}, u32[]{:S(2)}, u32[]{:S(2)}) %collective-permute-start.8) | collective-permute-done | bytes 196640 | tf_op jit(solution)/shard_map/ppermute | solution.py:41
  44.3 0.9 %collective-permute-start.6 = (bf16[1,512,384]{2,1,0:T(8,128)(2,1)S(1)}, bf16[1,512,384]{2,1,0:T(8,128)(2,1)S(1)}, u32[]{:S(2)}, u32[]{:S(2)}) collective-permute-start(bf16[1,512,384]{2,1,0:T(8,128)(2,1)S(1)} %pad_maximum_fusion.3), channel_id=1, source_target_pairs={{0,2},{1,3},{2,0},{3,1},{4,6},{5,7},{6,4},{7,5},{8,10},{9,11},{10,... | collective-permute-start | bytes 1179656 | tf_op jit(solution)/shard_map/ppermute | solution.py:41
  46.1 0.6 collective-permute-start.13
  46.7 1.0 %constant_dynamic-update-slice_fusion.2 = bf16[2,6,128,384]{3,2,1,0:T(8,128)(2,1)S(1)} fusion(bf16[2,2,128,384]{3,2,1,0:T(8,128)(2,1)} %collective-permute-done), kind=kLoop, calls=%fused_computation.243 | loop fusion | bytes 786432
  47.9 1.1 %constant_dynamic-update-slice_fusion = bf16[2,6,128,384]{3,2,1,0:T(8,128)(2,1)S(1)} fusion(bf16[2,6,128,384]{3,2,1,0:T(8,128)(2,1)S(1)} %constant_dynamic-update-slice_fusion.1, bf16[2,2,128,384]{3,2,1,0:T(8,128)(2,1)} %collective-permute-done.1), kind=kLoop, calls=%fused_computation.241 | loop fusion | bytes 786432 | tf_op jit(solution)/shard_map/concatenate | solution.py:22
  48.9 0.6 pad_slice_fusion.1
  49.5 0.7 pad_maximum_fusion
  50.3 1.0 %fusion.184 = (bf16[1,4,128,1152]{3,2,1,0:T(8,128)(2,1)S(1)}, bf16[1,4,128,1152]{3,2,1,0:T(8,128)(2,1)S(1)}, bf16[1,4,128,1152]{3,2,1,0:T(8,128)(2,1)S(1)}, bf16...) fusion(bf16[2,6,128,1152]{3,2,1,0:T(8,128)(2,1)S(1)} %pad_maximum, ...), kind=kLoop, calls=%fused_computation.267 | loop fusion | bytes 14155776 | tf_op jit(solution)/shard_map/slice | solution.py:59
  51.5 0.8 fusion.192
  52.6 0.8 convolution_add_fusion.5
  53.8 0.8 convolution_add_fusion.4
  55.0 0.8 convolution_add_fusion.3
  55.8 0.8 convolution_add_fusion.2
  58.9 0.6 convolution_bitcast_fusion.1
  66.4 4.3 %collective-permute-start.16 = (bf16[1,2,128,384]{3,2,1,0:T(8,128)(2,1)S(1)}, bf16[1,2,128,384]{3,2,1,0:T(8,128)(2,1)S(1)}, u32[]{:S(2)}, u32[]{:S(2)}) collective-permute-start(bf16[1,2,128,384]{3,2,1,0:T(8,128)(2,1)S(1)} %bitcast.486), channel_id=1, source_target_pairs={{1,0},{2,1},{3,2},{4,3},{5,4},{6,5},{7,6},{8,7},{9,8},{10,9},{11,1... | collective-permute-start | bytes 589832 | tf_op jit(solution)/shard_map/ppermute | solution.py:21
  70.7 2.1 %collective-permute-start.15 = (bf16[1,2,128,384]{3,2,1,0:T(8,128)(2,1)S(1)}, bf16[1,2,128,384]{3,2,1,0:T(8,128)(2,1)S(1)}, u32[]{:S(2)}, u32[]{:S(2)}) collective-permute-start(bf16[1,2,128,384]{3,2,1,0:T(8,128)(2,1)S(1)} %bitcast.487), channel_id=1, source_target_pairs={{0,1},{1,2},{2,3},{3,4},{4,5},{5,6},{6,7},{7,8},{8,9},{9,10},{10,1... | collective-permute-start | bytes 589832 | tf_op jit(solution)/shard_map/ppermute | solution.py:20
  72.9 0.8 convolution_add_fusion.1
  73.9 4.7 %collective-permute-done.15 = bf16[1,2,128,384]{3,2,1,0:T(8,128)(2,1)S(1)} collective-permute-done((bf16[1,2,128,384]{3,2,1,0:T(8,128)(2,1)S(1)}, bf16[1,2,128,384]{3,2,1,0:T(8,128)(2,1)S(1)}, u32[]{:S(2)}, u32[]{:S(2)}) %collective-permute-start.15) | collective-permute-done | bytes 196640 | tf_op jit(solution)/shard_map/ppermute | solution.py:20
  79.7 0.7 copy-done.9
  80.4 0.8 fusion.194
  81.6 0.8 fusion.193
  82.8 0.8 fusion.2
  83.7 1.5 %convolution_bitcast_fusion = f32[1,4,130,3,3,192]{5,2,4,3,1,0:T(8,128)S(1)} fusion(bf16[3,3,384,192]{2,3,1,0:T(8,128)(2,1)S(1)} %copy-done, bf16[1,4,128,384]{3,2,1,0:T(8,128)(2,1)S(1)} %select_convert_fusion), kind=kOutput, calls=%fused_computation.1 | convolution fusion | flops 690094080 | bytes 5314560 | tf_op jit(solution)/shard_map/frwc,ijco->frwijo/dot_general | solution.py:74
  86.8 1.3 %convert_element_type.183 = bf16[1,4,49152]{2,1,0:T(4,128)(2,1)} reshape(bf16[1,2,2,128,2,192]{5,4,3,2,1,0:T(2,128)(2,1)S(1)} %copy.61) | data formatting | bytes 786432 | tf_op jit(solution)/shard_map/convert_element_type | solution.py:91
  (97 shorter events, 15.6 us)
Async XLA Ops:
  0.0 83.7 %copy-start = (bf16[3,3,384,192]{2,3,1,0:T(8,128)(2,1)S(1)}, bf16[3,3,384,192]{2,3,1,0:T(8,128)(2,1)}, u32[]{:S(2)}) copy-start(bf16[3,3,384,192]{2,3,1,0:T(8,128)(2,1)} %param.19) | copy-start | bytes 3981316
  0.0 13.5 %copy-start.6 = (bf16[1,2,128,384]{3,2,1,0:T(8,128)(2,1)S(1)}, bf16[1,2,128,384]{3,2,1,0:T(8,128)(2,1)}, u32[]{:S(2)}) copy-start(bf16[1,2,128,384]{3,2,1,0:T(8,128)(2,1)} %param.10) | copy-start | bytes 589828
  0.0 46.1 %collective-permute-start = (bf16[2,2,128,384]{3,2,1,0:T(8,128)(2,1)}, bf16[2,2,128,384]{3,2,1,0:T(8,128)(2,1)}, u32[]{:S(2)}, u32[]{:S(2)}) collective-permute-start(bf16[2,2,128,384]{3,2,1,0:T(8,128)(2,1)} %param.16), channel_id=1, source_target_pairs={{0,1},{1,2},{2,3},{3,4},{4,5},{5,6},{6,7},{7,8},{8,9},{9,10},{10,1... | collective-permute-start | bytes 1179656 | tf_op jit(solution)/shard_map/ppermute | solution.py:20
  2.1 45.7 %collective-permute-start.1 = (bf16[2,2,128,384]{3,2,1,0:T(8,128)(2,1)}, bf16[2,2,128,384]{3,2,1,0:T(8,128)(2,1)}, u32[]{:S(2)}, u32[]{:S(2)}) collective-permute-start(bf16[2,2,128,384]{3,2,1,0:T(8,128)(2,1)} %param.16), channel_id=1, source_target_pairs={{1,0},{2,1},{3,2},{4,3},{5,4},{6,5},{7,6},{8,7},{9,8},{10,9},{11,1... | collective-permute-start | bytes 1179656 | tf_op jit(solution)/shard_map/ppermute | solution.py:21
  10.1 22.8 %collective-permute-start.4 = (bf16[1,128,384]{2,1,0:T(8,128)(2,1)}, bf16[1,128,384]{2,1,0:T(8,128)(2,1)}, u32[]{:S(2)}, u32[]{:S(2)}) collective-permute-start(bf16[1,128,384]{2,1,0:T(8,128)(2,1)} %get-tuple-element.43), channel_id=1, source_target_pairs={{0,12},{1,13},{2,14},{3,15},{4,8},{5,9},{6,10},{7,11},{8,4},{9,5},... | collective-permute-start | bytes 294920 | tf_op jit(solution)/shard_map/ppermute | solution.py:41
  11.7 18.9 %collective-permute-start.3 = (bf16[1,128,384]{2,1,0:T(8,128)(2,1)}, bf16[1,128,384]{2,1,0:T(8,128)(2,1)}, u32[]{:S(2)}, u32[]{:S(2)}) collective-permute-start(bf16[1,128,384]{2,1,0:T(8,128)(2,1)} %get-tuple-element.43), channel_id=1, source_target_pairs={{0,8},{1,9},{2,10},{3,11},{4,12},{5,13},{6,14},{7,15},{8,0},{9,1},... | collective-permute-start | bytes 294920 | tf_op jit(solution)/shard_map/ppermute | solution.py:41
  12.7 9.5 %collective-permute-start.5 = (bf16[1,128,384]{2,1,0:T(8,128)(2,1)}, bf16[1,128,384]{2,1,0:T(8,128)(2,1)}, u32[]{:S(2)}, u32[]{:S(2)}) collective-permute-start(bf16[1,128,384]{2,1,0:T(8,128)(2,1)} %get-tuple-element.44), channel_id=1, source_target_pairs={{0,2},{1,3},{2,0},{3,1},{4,6},{5,7},{6,4},{7,5},{8,10},{9,11},{10,... | collective-permute-start | bytes 294920 | tf_op jit(solution)/shard_map/ppermute | solution.py:41
  22.2 4.9 %collective-permute-start.2 = (bf16[1,128,384]{2,1,0:T(8,128)(2,1)}, bf16[1,128,384]{2,1,0:T(8,128)(2,1)S(1)}, u32[]{:S(2)}, u32[]{:S(2)}) collective-permute-start(bf16[1,128,384]{2,1,0:T(8,128)(2,1)} %get-tuple-element.43), channel_id=1, source_target_pairs={{0,4},{1,5},{2,6},{3,7},{4,0},{5,1},{6,2},{7,3},{8,12},{9,13},{10,... | collective-permute-start | bytes 294920 | tf_op jit(solution)/shard_map/ppermute | solution.py:41
  27.1 14.9 %collective-permute-start.9 = (bf16[1,256,384]{2,1,0:T(8,128)(2,1)S(1)}, bf16[1,256,384]{2,1,0:T(8,128)(2,1)S(1)}, u32[]{:S(2)}, u32[]{:S(2)}) collective-permute-start(bf16[1,256,384]{2,1,0:T(8,128)(2,1)S(1)} %pad_maximum_fusion.4), channel_id=1, source_target_pairs={{0,12},{1,13},{2,14},{3,15},{4,8},{5,9},{6,10},{7,11},{8,4},{9,5},... | collective-permute-start | bytes 589832 | tf_op jit(solution)/shard_map/ppermute | solution.py:41
  30.6 13.7 %collective-permute-start.8 = (bf16[1,256,384]{2,1,0:T(8,128)(2,1)S(1)}, bf16[1,256,384]{2,1,0:T(8,128)(2,1)S(1)}, u32[]{:S(2)}, u32[]{:S(2)}) collective-permute-start(bf16[1,256,384]{2,1,0:T(8,128)(2,1)S(1)} %pad_maximum_fusion.4), channel_id=1, source_target_pairs={{0,8},{1,9},{2,10},{3,11},{4,12},{5,13},{6,14},{7,15},{8,0},{9,1},... | collective-permute-start | bytes 589832 | tf_op jit(solution)/shard_map/ppermute | solution.py:41
  32.9 12.7 %collective-permute-start.7 = (bf16[1,256,384]{2,1,0:T(8,128)(2,1)S(1)}, bf16[1,256,384]{2,1,0:T(8,128)(2,1)S(1)}, u32[]{:S(2)}, u32[]{:S(2)}) collective-permute-start(bf16[1,256,384]{2,1,0:T(8,128)(2,1)S(1)} %pad_maximum_fusion.4), channel_id=1, source_target_pairs={{0,4},{1,5},{2,6},{3,7},{4,0},{5,1},{6,2},{7,3},{8,12},{9,13},{10,... | collective-permute-start | bytes 589832 | tf_op jit(solution)/shard_map/ppermute | solution.py:41
  38.3 3.6 %copy-start.5 = (bf16[1,768,384]{2,1,0:T(8,128)(2,1)S(1)}, bf16[1,768,384]{2,1,0:T(8,128)(2,1)}, u32[]{:S(2)}) copy-start(bf16[1,768,384]{2,1,0:T(8,128)(2,1)} %constant_dynamic-update-slice_fusion.3) | copy-start | bytes 1769476
  42.0 16.9 %collective-permute-start.10 = (bf16[1,768,384]{2,1,0:T(8,128)(2,1)S(1)}, bf16[1,768,384]{2,1,0:T(8,128)(2,1)S(1)}, u32[]{:S(2)}, u32[]{:S(2)}) collective-permute-start(bf16[1,768,384]{2,1,0:T(8,128)(2,1)S(1)} %copy-done.5), channel_id=1, source_target_pairs={{0,1},{1,0},{2,3},{3,2},{4,5},{5,4},{6,7},{7,6},{8,9},{9,8},{10,11... | collective-permute-start | bytes 1769480 | tf_op jit(solution)/shard_map/ppermute | solution.py:41
  44.3 13.1 %collective-permute-start.6 = (bf16[1,512,384]{2,1,0:T(8,128)(2,1)S(1)}, bf16[1,512,384]{2,1,0:T(8,128)(2,1)S(1)}, u32[]{:S(2)}, u32[]{:S(2)}) collective-permute-start(bf16[1,512,384]{2,1,0:T(8,128)(2,1)S(1)} %pad_maximum_fusion.3), channel_id=1, source_target_pairs={{0,2},{1,3},{2,0},{3,1},{4,6},{5,7},{6,4},{7,5},{8,10},{9,11},{10,... | collective-permute-start | bytes 1179656 | tf_op jit(solution)/shard_map/ppermute | solution.py:41
  45.6 2.1 %copy-start.11 = (bf16[2,2,128,384]{3,2,1,0:T(8,128)(2,1)S(1)}, bf16[2,2,128,384]{3,2,1,0:T(8,128)(2,1)}, u32[]{:S(2)}) copy-start(bf16[2,2,128,384]{3,2,1,0:T(8,128)(2,1)} %param.16) | copy-start | bytes 1179652
  45.6 10.9 %collective-permute-start.14 = (bf16[1,256,384]{2,1,0:T(8,128)(2,1)S(1)}, bf16[1,256,384]{2,1,0:T(8,128)(2,1)S(1)}, u32[]{:S(2)}, u32[]{:S(2)}) collective-permute-start(bf16[1,256,384]{2,1,0:T(8,128)(2,1)S(1)} %collective-permute-done.9), channel_id=1, source_target_pairs={{0,1},{1,0},{2,3},{3,2},{4,5},{5,4},{6,7},{7,6},{8,9},{9,8},{10,11... | collective-permute-start | bytes 589832 | tf_op jit(solution)/shard_map/ppermute | solution.py:41
  46.1 10.9 %collective-permute-start.13 = (bf16[1,256,384]{2,1,0:T(8,128)(2,1)S(1)}, bf16[1,256,384]{2,1,0:T(8,128)(2,1)S(1)}, u32[]{:S(2)}, u32[]{:S(2)}) collective-permute-start(bf16[1,256,384]{2,1,0:T(8,128)(2,1)S(1)} %collective-permute-done.8), channel_id=1, source_target_pairs={{0,1},{1,0},{2,3},{3,2},{4,5},{5,4},{6,7},{7,6},{8,9},{9,8},{10,11... | collective-permute-start | bytes 589832 | tf_op jit(solution)/shard_map/ppermute | solution.py:41
  47.8 10.7 %collective-permute-start.12 = (bf16[1,256,384]{2,1,0:T(8,128)(2,1)S(1)}, bf16[1,256,384]{2,1,0:T(8,128)(2,1)S(1)}, u32[]{:S(2)}, u32[]{:S(2)}) collective-permute-start(bf16[1,256,384]{2,1,0:T(8,128)(2,1)S(1)} %collective-permute-done.7), channel_id=1, source_target_pairs={{0,1},{1,0},{2,3},{3,2},{4,5},{5,4},{6,7},{7,6},{8,9},{9,8},{10,11... | collective-permute-start | bytes 589832 | tf_op jit(solution)/shard_map/ppermute | solution.py:41
  50.3 1.2 %copy-start.10 = (bf16[1,1,3,384,384]{4,3,2,1,0:T(8,128)(2,1)S(1)}, bf16[1,1,3,384,384]{4,3,2,1,0:T(8,128)(2,1)}, u32[]{:S(2)}) copy-start(bf16[1,1,3,384,384]{4,3,2,1,0:T(8,128)(2,1)} %get-tuple-element.20) | copy-start | bytes 2654212
  51.4 1.2 %copy-start.3 = (bf16[1,1,3,384,384]{4,3,2,1,0:T(8,128)(2,1)S(1)}, bf16[1,1,3,384,384]{4,3,2,1,0:T(8,128)(2,1)}, u32[]{:S(2)}) copy-start(bf16[1,1,3,384,384]{4,3,2,1,0:T(8,128)(2,1)} %get-tuple-element.21) | copy-start | bytes 2654212
  52.6 1.2 %copy-start.2 = (bf16[1,1,3,384,384]{4,3,2,1,0:T(8,128)(2,1)S(1)}, bf16[1,1,3,384,384]{4,3,2,1,0:T(8,128)(2,1)}, u32[]{:S(2)}) copy-start(bf16[1,1,3,384,384]{4,3,2,1,0:T(8,128)(2,1)} %get-tuple-element.19) | copy-start | bytes 2654212
  53.8 1.2 %copy-start.1 = (bf16[1,1,3,384,384]{4,3,2,1,0:T(8,128)(2,1)S(1)}, bf16[1,1,3,384,384]{4,3,2,1,0:T(8,128)(2,1)}, u32[]{:S(2)}) copy-start(bf16[1,1,3,384,384]{4,3,2,1,0:T(8,128)(2,1)} %get-tuple-element.18) | copy-start | bytes 2654212
  57.4 2.3 %collective-permute-start.11 = (bf16[1,512,384]{2,1,0:T(8,128)(2,1)S(1)}, bf16[1,512,384]{2,1,0:T(8,128)(2,1)S(1)}, u32[]{:S(2)}, u32[]{:S(2)}) collective-permute-start(bf16[1,512,384]{2,1,0:T(8,128)(2,1)S(1)} %collective-permute-done.6), channel_id=1, source_target_pairs={{0,1},{1,0},{2,3},{3,2},{4,5},{5,4},{6,7},{7,6},{8,9},{9,8},{10,11... | collective-permute-start | bytes 1179656 | tf_op jit(solution)/shard_map/ppermute | solution.py:41
  64.2 1.0 %copy-start.12 = (bf16[384,384]{1,0:T(8,128)(2,1)S(1)}, bf16[384,384]{1,0:T(8,128)(2,1)}, u32[]{:S(2)}) copy-start(bf16[384,384]{1,0:T(8,128)(2,1)} %param.14) | copy-start | bytes 884740
  64.6 1.0 %copy-start.7 = (bf16[1,2,128,384]{3,2,1,0:T(8,128)(2,1)S(1)}, bf16[1,2,128,384]{3,2,1,0:T(8,128)(2,1)}, u32[]{:S(2)}) copy-start(bf16[1,2,128,384]{3,2,1,0:T(8,128)(2,1)} %param.10) | copy-start | bytes 589828
  64.6 1.1 %copy-start.14 = (bf16[384,384]{1,0:T(8,128)(2,1)S(1)}, bf16[384,384]{1,0:T(8,128)(2,1)}, u32[]{:S(2)}) copy-start(bf16[384,384]{1,0:T(8,128)(2,1)} %param.15) | copy-start | bytes 884740
  65.5 0.7 copy-start.13
  66.4 7.5 %collective-permute-start.16 = (bf16[1,2,128,384]{3,2,1,0:T(8,128)(2,1)S(1)}, bf16[1,2,128,384]{3,2,1,0:T(8,128)(2,1)S(1)}, u32[]{:S(2)}, u32[]{:S(2)}) collective-permute-start(bf16[1,2,128,384]{3,2,1,0:T(8,128)(2,1)S(1)} %bitcast.486), channel_id=1, source_target_pairs={{1,0},{2,1},{3,2},{4,3},{5,4},{6,5},{7,6},{8,7},{9,8},{10,9},{11,1... | collective-permute-start | bytes 589832 | tf_op jit(solution)/shard_map/ppermute | solution.py:21
  70.7 7.9 %collective-permute-start.15 = (bf16[1,2,128,384]{3,2,1,0:T(8,128)(2,1)S(1)}, bf16[1,2,128,384]{3,2,1,0:T(8,128)(2,1)S(1)}, u32[]{:S(2)}, u32[]{:S(2)}) collective-permute-start(bf16[1,2,128,384]{3,2,1,0:T(8,128)(2,1)S(1)} %bitcast.487), channel_id=1, source_target_pairs={{0,1},{1,2},{2,3},{3,4},{4,5},{5,6},{6,7},{7,8},{8,9},{9,10},{10,1... | collective-permute-start | bytes 589832 | tf_op jit(solution)/shard_map/ppermute | solution.py:20
  79.3 1.2 %copy-start.9 = (bf16[1,1,3,384,384]{4,3,2,1,0:T(8,128)(2,1)S(1)}, bf16[1,1,3,384,384]{4,3,2,1,0:T(8,128)(2,1)}, u32[]{:S(2)}) copy-start(bf16[1,1,3,384,384]{4,3,2,1,0:T(8,128)(2,1)} %get-tuple-element.22) | copy-start | bytes 2654212
  80.4 1.2 %copy-start.8 = (bf16[1,1,3,384,384]{4,3,2,1,0:T(8,128)(2,1)S(1)}, bf16[1,1,3,384,384]{4,3,2,1,0:T(8,128)(2,1)}, u32[]{:S(2)}) copy-start(bf16[1,1,3,384,384]{4,3,2,1,0:T(8,128)(2,1)} %get-tuple-element.23) | copy-start | bytes 2654212
  81.6 1.2 %copy-start.4 = (bf16[1,1,3,384,384]{4,3,2,1,0:T(8,128)(2,1)S(1)}, bf16[1,1,3,384,384]{4,3,2,1,0:T(8,128)(2,1)}, u32[]{:S(2)}) copy-start(bf16[1,1,3,384,384]{4,3,2,1,0:T(8,128)(2,1)} %get-tuple-element.15) | copy-start | bytes 2654212

commit v10 on v7

--- a/solution.py
+++ b/solution.py
@@ -11,13 +11,19 @@
 
 def padded_2(array, sides, width):
     for axis, dim in sides:
-        size, length = (lax.axis_size(axis), array.shape[dim])
-        up = [(i, (i + 1) % size) for i in range(size - 1)]
-        down = [(j, i) for i, j in up]
-        last = lax.slice_in_dim(array, length - width, length, axis=dim)
+        size = lax.axis_size(axis)
+        even = (lax.axis_index(axis) % 2) == 0
         first = lax.slice_in_dim(array, 0, width, axis=dim)
-        before = lax.ppermute(last, axis, up)
-        after = lax.ppermute(first, axis, down)
+        last = lax.slice_in_dim(array, array.shape[dim] - width, array.shape[dim], axis=dim)
+        on_chip = lax.ppermute(
+            jnp.where(even, last, first), axis, [(i, i ^ 1) for i in range(size)]
+        )
+        pairs = [(i, i + 1) for i in range(1, size - 1, 2)]
+        across = lax.ppermute(
+            jnp.where(even, first, last), axis, pairs + [(j, i) for i, j in pairs]
+        )
+        before = jnp.where(even, across, on_chip)
+        after = jnp.where(even, on_chip, across)
         array = jnp.concatenate([before, array, after], axis=dim)
     return array
 

time: 77.3 us -> 69 us (0.89)
  the two profiles are of different devices: /device:TPU:8 before, /device:TPU:5 now
where the time goes in v10:
time: 69 us; the launch traced here: 68.7 us
  starting transfers between devices  22.9 us (33%)
  waiting for transfers between devices  17.7 us (26%)
  matrix products  14.9 us (22%)
  other arithmetic  8.43 us (12%)
  local copies, waits for them, and re-layouts  4.19 us (6%)
  between operations  0.76 us (1%)
    ppermute x13, starting transfers between devices, exchange(): lax.ppermute(values, ROWS, [(i, i ^ mask) for i in range(size)])  13.3 us
    ppermute x13, waiting for transfers between devices, exchange(): lax.ppermute(values, ROWS, [(i, i ^ mask) for i in range(size)])  10.4 us
    ppermute x3, starting transfers between devices, padded_2(): lax.ppermute(jnp.where(even, first, last), axis, pairs + [(j, i) for i, j...  9.38 us
    ppermute x3, waiting for transfers between devices, padded_2(): lax.ppermute(jnp.where(even, first, last), axis, pairs + [(j, i) for i, j...  7.23 us
    dot_general x10, matrix products, body(): jnp.einsum('fqc,fkc->fqk', q_pair, piece, preferred_element_type=jnp.floa...  4.07 us
    conv_general_dilated x3, matrix products, conv_rows(): lax.conv_general_dilated(haloed[tstep:tstep + 1], weight[tstep], window_s...  3.58 us
    dot_general x10, matrix products, body(): jnp.einsum('fqk,fkc->fqc', e.astype(jnp.bfloat16), p, preferred_element_t...  3.34 us
    select_n x3, other arithmetic, padded_2(): jnp.where(even, first, last)  1.79 us
  transfers between devices with their start and end apart: 19, of which 4 were waited for; matrix products, arithmetic and copies ran while one was open for 17% of the time, Pallas kernels for 0%

profile of v10, /device:TPU:5, one launch (start us, length us, event | category | flops | bytes accessed | tf_op | source)
XLA Modules:
  0.0 68.7 jit_solution(8441298168893619431)
XLA Ops:
  0.0 1.1 %multiply_reduce_fusion.1 = f32[2,128]{1,0:T(2,128)S(1)} fusion(bf16[1,2,128,384]{3,2,1,0:T(8,128)(2,1)} %param.10), kind=kLoop, calls=%fused_computation.132 | loop fusion | flops 294656 | bytes 197632 | tf_op jit(solution)/shard_map/reduce_sum | solution.py:32
  1.2 1.1 %constant_dynamic-update-slice_fusion.4 = (bf16[1,768,384]{2,1,0:T(8,128)(2,1)S(1)}, bf16[1,256,384]{2,1,0:T(8,128)(2,1)S(1)}) fusion(f32[384]{0:T(512)} %param.11, f32[256]{0:T(256)S(1)} %rsqrt_bitcast_fusion, bf16[1,2,128,384]{3,2,1,0:T(8,128)(2,1)} %param.10), kind=kLoop, calls=%fused_computation.291 | loop fusion | flops 393215 | bytes 592384
  2.3 3.4 %collective-permute-start.4 = (bf16[1,128,384]{2,1,0:T(8,128)(2,1)S(1)}, bf16[1,128,384]{2,1,0:T(8,128)(2,1)S(1)}, u32[]{:S(2)}, u32[]{:S(2)}) collective-permute-start(bf16[1,128,384]{2,1,0:T(8,128)(2,1)S(1)} %get-tuple-element.35), channel_id=1, source_target_pairs={{0,12},{1,13},{2,14},{3,15},{4,8},{5,9},{6,10},{7,11},{8,4},{9,5},... | collective-permute-start | bytes 294920 | tf_op jit(solution)/shard_map/ppermute | solution.py:46
  5.7 0.4 collective-permute-start.2
  6.2 1.7 %broadcast_select_fusion.3 = (bf16[2,1,128,384]{3,2,1,0:T(8,128)(2,1)}, bf16[2,1,128,384]{3,2,1,0:T(8,128)(2,1)S(1)}) fusion(pred[]{:T(512)S(6)} %eq.9, bf16[2,2,128,384]{3,2,1,0:T(8,128)(2,1)} %param.16), kind=kLoop, calls=%fused_computation.260 | loop fusion | flops 196608 | bytes 786433 | tf_op jit(solution)/shard_map/jit(_where)/select_n | solution.py:23
  8.0 5.4 %collective-permute-start = (bf16[2,1,128,384]{3,2,1,0:T(8,128)(2,1)}, bf16[2,1,128,384]{3,2,1,0:T(8,128)(2,1)S(1)}, u32[]{:S(2)}, u32[]{:S(2)}) collective-permute-start(bf16[2,1,128,384]{3,2,1,0:T(8,128)(2,1)} %get-tuple-element.21), channel_id=1, source_target_pairs={{1,2},{3,4},{5,6},{7,8},{9,10},{11,12},{13,14},{2,1},{4,3},{6,5},{... | collective-permute-start | bytes 589832 | tf_op jit(solution)/shard_map/ppermute | solution.py:22
  13.3 1.0 %fusion.107 = bf16[256,384]{1,0:T(8,128)(2,1)S(1)} fusion(bf16[1,2,128,384]{3,2,1,0:T(8,128)(2,1)} %param.10, f32[384]{0:T(512)} %param.11, f32[256]{0:T(256)S(1)} %rsqrt_bitcast_fusion), kind=kLoop, calls=%fused_computation.125 | loop fusion | flops 393216 | bytes 395776 | tf_op jit(solution)/shard_map/convert_element_type | solution.py:106
  14.4 1.6 %convert_bitcast_fusion.1 = (bf16[1,256,384]{2,1,0:T(8,128)(2,1)S(1)}, bf16[1,256,384]{2,1,0:T(8,128)(2,1)S(1)}) fusion(bf16[384,384]{1,0:T(8,128)(2,1)} %param.13, bf16[256,384]{1,0:T(8,128)(2,1)S(1)} %fusion.107, bf16[384,384]{1,0:T(8,128)(2,1)} %param.12), kind=kOutput, calls=%fused_computation.280 | convolution fusion | flops 151486464 | bytes 1179648 | tf_op jit(solution)/shard_map/fqc,dc->fqd/dot_general | solution.py:120
  16.1 1.6 %collective-permute-start.9 = (bf16[1,256,384]{2,1,0:T(8,128)(2,1)S(1)}, bf16[1,256,384]{2,1,0:T(8,128)(2,1)S(1)}, u32[]{:S(2)}, u32[]{:S(2)}) collective-permute-start(bf16[1,256,384]{2,1,0:T(8,128)(2,1)S(1)} %pad_maximum_fusion.3), channel_id=1, source_target_pairs={{0,12},{1,13},{2,14},{3,15},{4,8},{5,9},{6,10},{7,11},{8,4},{9,5},... | collective-permute-start | bytes 589832 | tf_op jit(solution)/shard_map/ppermute | solution.py:46
  17.7 1.2 %collective-permute-start.8 = (bf16[1,256,384]{2,1,0:T(8,128)(2,1)S(1)}, bf16[1,256,384]{2,1,0:T(8,128)(2,1)S(1)}, u32[]{:S(2)}, u32[]{:S(2)}) collective-permute-start(bf16[1,256,384]{2,1,0:T(8,128)(2,1)S(1)} %pad_maximum_fusion.3), channel_id=1, source_target_pairs={{0,8},{1,9},{2,10},{3,11},{4,12},{5,13},{6,14},{7,15},{8,0},{9,1},... | collective-permute-start | bytes 589832 | tf_op jit(solution)/shard_map/ppermute | solution.py:46
  18.9 1.0 %collective-permute-start.7 = (bf16[1,256,384]{2,1,0:T(8,128)(2,1)S(1)}, bf16[1,256,384]{2,1,0:T(8,128)(2,1)S(1)}, u32[]{:S(2)}, u32[]{:S(2)}) collective-permute-start(bf16[1,256,384]{2,1,0:T(8,128)(2,1)S(1)} %pad_maximum_fusion.3), channel_id=1, source_target_pairs={{0,4},{1,5},{2,6},{3,7},{4,0},{5,1},{6,2},{7,3},{8,12},{9,13},{10,... | collective-permute-start | bytes 589832 | tf_op jit(solution)/shard_map/ppermute | solution.py:46
  19.9 0.6 convolution_bitcast_fusion.2
  20.8 1.4 %collective-permute-start.10 = (bf16[1,768,384]{2,1,0:T(8,128)(2,1)S(1)}, bf16[1,768,384]{2,1,0:T(8,128)(2,1)S(1)}, u32[]{:S(2)}, u32[]{:S(2)}) collective-permute-start(bf16[1,768,384]{2,1,0:T(8,128)(2,1)S(1)} %constant_dynamic-update-slice_fusion), channel_id=1, source_target_pairs={{0,1},{1,0},{2,3},{3,2},{4,5},{5,4},{6,7},{7,6},{8,9},{9,8},{10,11... | collective-permute-start | bytes 1769480 | tf_op jit(solution)/shard_map/ppermute | solution.py:46
  22.4 0.3 copy.102
  23.0 1.0 %collective-permute-done.9 = bf16[1,256,384]{2,1,0:T(8,128)(2,1)S(1)} collective-permute-done((bf16[1,256,384]{2,1,0:T(8,128)(2,1)S(1)}, bf16[1,256,384]{2,1,0:T(8,128)(2,1)S(1)}, u32[]{:S(2)}, u32[]{:S(2)}) %collective-permute-start.9) | collective-permute-done | bytes 196640 | tf_op jit(solution)/shard_map/ppermute | solution.py:46
  24.0 0.3 convolution_bitcast_fusion.9
  24.4 2.5 %collective-permute-start.14 = (bf16[1,256,384]{2,1,0:T(8,128)(2,1)S(1)}, bf16[1,256,384]{2,1,0:T(8,128)(2,1)S(1)}, u32[]{:S(2)}, u32[]{:S(2)}) collective-permute-start(bf16[1,256,384]{2,1,0:T(8,128)(2,1)S(1)} %collective-permute-done.9), channel_id=1, source_target_pairs={{0,1},{1,0},{2,3},{3,2},{4,5},{5,4},{6,7},{7,6},{8,9},{9,8},{10,11... | collective-permute-start | bytes 589832 | tf_op jit(solution)/shard_map/ppermute | solution.py:46
  26.8 9.4 %collective-permute-done.8 = bf16[1,256,384]{2,1,0:T(8,128)(2,1)S(1)} collective-permute-done((bf16[1,256,384]{2,1,0:T(8,128)(2,1)S(1)}, bf16[1,256,384]{2,1,0:T(8,128)(2,1)S(1)}, u32[]{:S(2)}, u32[]{:S(2)}) %collective-permute-start.8) | collective-permute-done | bytes 196640 | tf_op jit(solution)/shard_map/ppermute | solution.py:46
  36.2 1.1 %collective-permute-start.13 = (bf16[1,256,384]{2,1,0:T(8,128)(2,1)S(1)}, bf16[1,256,384]{2,1,0:T(8,128)(2,1)S(1)}, u32[]{:S(2)}, u32[]{:S(2)}) collective-permute-start(bf16[1,256,384]{2,1,0:T(8,128)(2,1)S(1)} %collective-permute-done.8), channel_id=1, source_target_pairs={{0,1},{1,0},{2,3},{3,2},{4,5},{5,4},{6,7},{7,6},{8,9},{9,8},{10,11... | collective-permute-start | bytes 589832 | tf_op jit(solution)/shard_map/ppermute | solution.py:46
  37.3 0.3 convolution_bitcast_fusion.10
  37.7 0.3 convolution_bitcast_fusion.11
  38.2 0.3 convolution_bitcast_fusion.6
  38.6 0.3 convolution_bitcast_fusion.7
  39.0 0.6 collective-permute-start.11
  39.5 0.5 convolution_bitcast_fusion.4
  40.1 0.3 convolution_bitcast_fusion.8
  40.5 0.6 convolution_bitcast_fusion.1
  41.3 0.5 convolution_bitcast_fusion.3
  41.9 0.3 fusion.161
  42.4 0.4 fusion.44
  42.8 0.5 fusion.48
  44.2 0.4 fusion.101
  44.5 0.5 fusion.16
  45.9 0.4 convert_bitcast_fusion
  46.4 0.4 convolution_bitcast_fusion.5
  46.8 0.4 multiply_reduce_fusion
  47.5 2.1 %collective-permute-start.15 = (bf16[1,1,128,384]{3,2,1,0:T(8,128)(2,1)S(1)}, bf16[1,1,128,384]{3,2,1,0:T(8,128)(2,1)S(1)}, u32[]{:S(2)}, u32[]{:S(2)}) collective-permute-start(bf16[1,1,128,384]{3,2,1,0:T(8,128)(2,1)S(1)} %get-tuple-element.33), channel_id=1, source_target_pairs={{1,2},{3,4},{5,6},{7,8},{9,10},{11,12},{13,14},{2,1},{4,3},{6,5},{... | collective-permute-start | bytes 294920 | tf_op jit(solution)/shard_map/ppermute | solution.py:22
  49.7 1.2 %fusion.31 = f32[2,8,17,384]{3,1,2,0:T(8,128)S(1)} fusion(bf16[3,3,3,384,384]{4,3,2,1,0:T(8,128)(2,1)S(1)} %bitcast.489, bf16[4,1,7,2,384]{4,2,3,0,1:T(8,128)(2,1)S(1)} %slice.266, bf16[4,1,8,17,384]{4,2,3,0,1:T(8,128)(2,1)S(1)} %copy.41, pred[8,17]{0,1:T(8,128)(4,1)S(1)} %copy-done.6), kind=kOutput, calls=%fused_computation.41 | convolution fusion | flops 723449856 | bytes 3542016 | tf_op jit(solution)/shard_map/conv_general_dilated | solution.py:59
  50.9 0.3 copy.101
  51.5 2.8 %collective-permute-done.15 = bf16[1,1,128,384]{3,2,1,0:T(8,128)(2,1)S(1)} collective-permute-done((bf16[1,1,128,384]{3,2,1,0:T(8,128)(2,1)S(1)}, bf16[1,1,128,384]{3,2,1,0:T(8,128)(2,1)S(1)}, u32[]{:S(2)}, u32[]{:S(2)}) %collective-permute-start.15) | collective-permute-done | bytes 98336 | tf_op jit(solution)/shard_map/ppermute | solution.py:22
  55.0 1.2 %fusion.34 = f32[2,8,17,384]{3,1,2,0:T(8,128)S(1)} fusion(bf16[3,3,3,384,384]{4,3,2,1,0:T(8,128)(2,1)S(1)} %bitcast.489, bf16[4,1,7,2,384]{4,2,3,0,1:T(8,128)(2,1)S(1)} %slice.293, bf16[4,1,8,17,384]{4,2,3,0,1:T(8,128)(2,1)S(1)} %copy.44, pred[8,17]{0,1:T(8,128)(4,1)S(1)} %copy-done.6), kind=kOutput, calls=%fused_computation.42 | convolution fusion | flops 723449856 | bytes 3542016 | tf_op jit(solution)/shard_map/conv_general_dilated | solution.py:59
  56.2 1.2 %fusion.28 = bf16[2,8,17,384]{3,1,2,0:T(8,128)(2,1)S(1)} fusion(f32[2,8,17,384]{3,1,2,0:T(8,128)S(1)} %fusion.34, f32[2,8,17,384]{3,1,2,0:T(8,128)S(1)} %fusion.31, bf16[3,3,3,384,384]{4,3,2,1,0:T(8,128)(2,1)S(1)} %bitcast.489, bf16[4,1,7,2,384]{4,2,3,0,1:T(8,128)(2,1)S(1)} %slice.264, bf16[4,1,8,17,384]{4,2,3,0,1:T(8,128)(2,1)S(1)} %copy.38, ...), kind=kOutput, calls=%fused_computation.40 | convolution fusion | flops 723763200 | bytes 4168704 | tf_op jit(solution)/shard_map/conv_general_dilated | solution.py:59
  57.5 1.9 %collective-permute-start.17 = (bf16[1,1,128,384]{3,2,1,0:T(8,128)(2,1)S(1)}, bf16[1,1,128,384]{3,2,1,0:T(8,128)(2,1)S(1)}, u32[]{:S(2)}, u32[]{:S(2)}) collective-permute-start(bf16[1,1,128,384]{3,2,1,0:T(8,128)(2,1)S(1)} %slice.296), channel_id=1, source_target_pairs={{1,2},{3,4},{5,6},{7,8},{9,10},{11,12},{13,14},{2,1},{4,3},{6,5},{... | collective-permute-start | bytes 294920 | tf_op jit(solution)/shard_map/ppermute | solution.py:22
  60.0 4.4 %collective-permute-done.17 = bf16[1,1,128,384]{3,2,1,0:T(8,128)(2,1)S(1)} collective-permute-done((bf16[1,1,128,384]{3,2,1,0:T(8,128)(2,1)S(1)}, bf16[1,1,128,384]{3,2,1,0:T(8,128)(2,1)S(1)}, u32[]{:S(2)}, u32[]{:S(2)}) %collective-permute-start.17) | collective-permute-done | bytes 98336 | tf_op jit(solution)/shard_map/ppermute | solution.py:22
  64.4 1.5 %convolution_bitcast_fusion = f32[1,4,130,3,3,192]{5,2,4,3,1,0:T(8,128)S(1)} fusion(bf16[3,3,384,192]{2,3,1,0:T(8,128)(2,1)S(1)} %copy-done, bf16[1,1,128,384]{3,2,1,0:T(8,128)(2,1)S(1)} %get-tuple-element.30, bf16[1,2,128,384]{3,2,1,0:T(8,128)(2,1)S(1)} %bitcast.487, bf16[1,1,128,384]{3,2,1,0:T(8,128)(2,1)S(1)} %get-tuple-element.29), kind=kOutput, calls=%fused_computation.9 | convolution fusion | flops 692490240 | bytes 5314560 | tf_op jit(solution)/shard_map/frwc,ijco->frwijo/dot_general | solution.py:76
  65.9 0.4 fusion.214
  66.9 0.5 copy.74
  67.5 1.3 %convert_element_type.171 = bf16[1,4,49152]{2,1,0:T(4,128)(2,1)} reshape(bf16[1,2,2,128,2,192]{5,4,3,2,1,0:T(2,128)(2,1)S(1)} %copy.74) | data formatting | bytes 786432 | tf_op jit(solution)/shard_map/convert_element_type | solution.py:93
  (101 shorter events, 6.2 us)
Async XLA Ops:
  0.0 64.4 %copy-start = (bf16[3,3,384,192]{2,3,1,0:T(8,128)(2,1)S(1)}, bf16[3,3,384,192]{2,3,1,0:T(8,128)(2,1)}, u32[]{:S(2)}) copy-start(bf16[3,3,384,192]{2,3,1,0:T(8,128)(2,1)} %param.19) | copy-start | bytes 3981316
  2.3 16.7 %collective-permute-start.4 = (bf16[1,128,384]{2,1,0:T(8,128)(2,1)S(1)}, bf16[1,128,384]{2,1,0:T(8,128)(2,1)S(1)}, u32[]{:S(2)}, u32[]{:S(2)}) collective-permute-start(bf16[1,128,384]{2,1,0:T(8,128)(2,1)S(1)} %get-tuple-element.35), channel_id=1, source_target_pairs={{0,12},{1,13},{2,14},{3,15},{4,8},{5,9},{6,10},{7,11},{8,4},{9,5},... | collective-permute-start | bytes 294920 | tf_op jit(solution)/shard_map/ppermute | solution.py:46
  5.6 12.0 %collective-permute-start.3 = (bf16[1,128,384]{2,1,0:T(8,128)(2,1)S(1)}, bf16[1,128,384]{2,1,0:T(8,128)(2,1)S(1)}, u32[]{:S(2)}, u32[]{:S(2)}) collective-permute-start(bf16[1,128,384]{2,1,0:T(8,128)(2,1)S(1)} %get-tuple-element.35), channel_id=1, source_target_pairs={{0,8},{1,9},{2,10},{3,11},{4,12},{5,13},{6,14},{7,15},{8,0},{9,1},... | collective-permute-start | bytes 294920 | tf_op jit(solution)/shard_map/ppermute | solution.py:46
  5.7 10.4 %collective-permute-start.2 = (bf16[1,128,384]{2,1,0:T(8,128)(2,1)S(1)}, bf16[1,128,384]{2,1,0:T(8,128)(2,1)S(1)}, u32[]{:S(2)}, u32[]{:S(2)}) collective-permute-start(bf16[1,128,384]{2,1,0:T(8,128)(2,1)S(1)} %get-tuple-element.35), channel_id=1, source_target_pairs={{0,4},{1,5},{2,6},{3,7},{4,0},{5,1},{6,2},{7,3},{8,12},{9,13},{10,... | collective-permute-start | bytes 294920 | tf_op jit(solution)/shard_map/ppermute | solution.py:46
  6.0 9.9 %collective-permute-start.5 = (bf16[1,128,384]{2,1,0:T(8,128)(2,1)S(1)}, bf16[1,128,384]{2,1,0:T(8,128)(2,1)S(1)}, u32[]{:S(2)}, u32[]{:S(2)}) collective-permute-start(bf16[1,128,384]{2,1,0:T(8,128)(2,1)S(1)} %get-tuple-element.36), channel_id=1, source_target_pairs={{0,2},{1,3},{2,0},{3,1},{4,6},{5,7},{6,4},{7,5},{8,10},{9,11},{10,... | collective-permute-start | bytes 294920 | tf_op jit(solution)/shard_map/ppermute | solution.py:46
  8.0 12.8 %collective-permute-start = (bf16[2,1,128,384]{3,2,1,0:T(8,128)(2,1)}, bf16[2,1,128,384]{3,2,1,0:T(8,128)(2,1)S(1)}, u32[]{:S(2)}, u32[]{:S(2)}) collective-permute-start(bf16[2,1,128,384]{3,2,1,0:T(8,128)(2,1)} %get-tuple-element.21), channel_id=1, source_target_pairs={{1,2},{3,4},{5,6},{7,8},{9,10},{11,12},{13,14},{2,1},{4,3},{6,5},{... | collective-permute-start | bytes 589832 | tf_op jit(solution)/shard_map/ppermute | solution.py:22
  16.0 6.2 %collective-permute-start.1 = (bf16[2,1,128,384]{3,2,1,0:T(8,128)(2,1)S(1)}, bf16[2,1,128,384]{3,2,1,0:T(8,128)(2,1)S(1)}, u32[]{:S(2)}, u32[]{:S(2)}) collective-permute-start(bf16[2,1,128,384]{3,2,1,0:T(8,128)(2,1)S(1)} %get-tuple-element.22), channel_id=1, source_target_pairs={{0,1},{1,0},{2,3},{3,2},{4,5},{5,4},{6,7},{7,6},{8,9},{9,8},{10,11... | collective-permute-start | bytes 589832 | tf_op jit(solution)/shard_map/ppermute | solution.py:18
  16.1 7.9 %collective-permute-start.9 = (bf16[1,256,384]{2,1,0:T(8,128)(2,1)S(1)}, bf16[1,256,384]{2,1,0:T(8,128)(2,1)S(1)}, u32[]{:S(2)}, u32[]{:S(2)}) collective-permute-start(bf16[1,256,384]{2,1,0:T(8,128)(2,1)S(1)} %pad_maximum_fusion.3), channel_id=1, source_target_pairs={{0,12},{1,13},{2,14},{3,15},{4,8},{5,9},{6,10},{7,11},{8,4},{9,5},... | collective-permute-start | bytes 589832 | tf_op jit(solution)/shard_map/ppermute | solution.py:46
  17.7 18.5 %collective-permute-start.8 = (bf16[1,256,384]{2,1,0:T(8,128)(2,1)S(1)}, bf16[1,256,384]{2,1,0:T(8,128)(2,1)S(1)}, u32[]{:S(2)}, u32[]{:S(2)}) collective-permute-start(bf16[1,256,384]{2,1,0:T(8,128)(2,1)S(1)} %pad_maximum_fusion.3), channel_id=1, source_target_pairs={{0,8},{1,9},{2,10},{3,11},{4,12},{5,13},{6,14},{7,15},{8,0},{9,1},... | collective-permute-start | bytes 589832 | tf_op jit(solution)/shard_map/ppermute | solution.py:46
  18.9 18.7 %collective-permute-start.7 = (bf16[1,256,384]{2,1,0:T(8,128)(2,1)S(1)}, bf16[1,256,384]{2,1,0:T(8,128)(2,1)S(1)}, u32[]{:S(2)}, u32[]{:S(2)}) collective-permute-start(bf16[1,256,384]{2,1,0:T(8,128)(2,1)S(1)} %pad_maximum_fusion.3), channel_id=1, source_target_pairs={{0,4},{1,5},{2,6},{3,7},{4,0},{5,1},{6,2},{7,3},{8,12},{9,13},{10,... | collective-permute-start | bytes 589832 | tf_op jit(solution)/shard_map/ppermute | solution.py:46
  19.9 2.3 %copy-start.2 = (bf16[2,2,128,384]{3,2,1,0:T(8,128)(2,1)S(1)}, bf16[2,2,128,384]{3,2,1,0:T(8,128)(2,1)}, u32[]{:S(2)}) copy-start(bf16[2,2,128,384]{3,2,1,0:T(8,128)(2,1)} %param.16) | copy-start | bytes 1179652
  20.8 19.7 %collective-permute-start.10 = (bf16[1,768,384]{2,1,0:T(8,128)(2,1)S(1)}, bf16[1,768,384]{2,1,0:T(8,128)(2,1)S(1)}, u32[]{:S(2)}, u32[]{:S(2)}) collective-permute-start(bf16[1,768,384]{2,1,0:T(8,128)(2,1)S(1)} %constant_dynamic-update-slice_fusion), channel_id=1, source_target_pairs={{0,1},{1,0},{2,3},{3,2},{4,5},{5,4},{6,7},{7,6},{8,9},{9,8},{10,11... | collective-permute-start | bytes 1769480 | tf_op jit(solution)/shard_map/ppermute | solution.py:46
  22.2 16.8 %collective-permute-start.6 = (bf16[1,512,384]{2,1,0:T(8,128)(2,1)S(1)}, bf16[1,512,384]{2,1,0:T(8,128)(2,1)S(1)}, u32[]{:S(2)}, u32[]{:S(2)}) collective-permute-start(bf16[1,512,384]{2,1,0:T(8,128)(2,1)S(1)} %pad_maximum_fusion.2), channel_id=1, source_target_pairs={{0,2},{1,3},{2,0},{3,1},{4,6},{5,7},{6,4},{7,5},{8,10},{9,11},{10,... | collective-permute-start | bytes 1179656 | tf_op jit(solution)/shard_map/ppermute | solution.py:46
  24.4 13.8 %collective-permute-start.14 = (bf16[1,256,384]{2,1,0:T(8,128)(2,1)S(1)}, bf16[1,256,384]{2,1,0:T(8,128)(2,1)S(1)}, u32[]{:S(2)}, u32[]{:S(2)}) collective-permute-start(bf16[1,256,384]{2,1,0:T(8,128)(2,1)S(1)} %collective-permute-done.9), channel_id=1, source_target_pairs={{0,1},{1,0},{2,3},{3,2},{4,5},{5,4},{6,7},{7,6},{8,9},{9,8},{10,11... | collective-permute-start | bytes 589832 | tf_op jit(solution)/shard_map/ppermute | solution.py:46
  36.2 2.3 %collective-permute-start.13 = (bf16[1,256,384]{2,1,0:T(8,128)(2,1)S(1)}, bf16[1,256,384]{2,1,0:T(8,128)(2,1)S(1)}, u32[]{:S(2)}, u32[]{:S(2)}) collective-permute-start(bf16[1,256,384]{2,1,0:T(8,128)(2,1)S(1)} %collective-permute-done.8), channel_id=1, source_target_pairs={{0,1},{1,0},{2,3},{3,2},{4,5},{5,4},{6,7},{7,6},{8,9},{9,8},{10,11... | collective-permute-start | bytes 589832 | tf_op jit(solution)/shard_map/ppermute | solution.py:46
  37.6 2.5 %collective-permute-start.12 = (bf16[1,256,384]{2,1,0:T(8,128)(2,1)S(1)}, bf16[1,256,384]{2,1,0:T(8,128)(2,1)S(1)}, u32[]{:S(2)}, u32[]{:S(2)}) collective-permute-start(bf16[1,256,384]{2,1,0:T(8,128)(2,1)S(1)} %collective-permute-done.7), channel_id=1, source_target_pairs={{0,1},{1,0},{2,3},{3,2},{4,5},{5,4},{6,7},{7,6},{8,9},{9,8},{10,11... | collective-permute-start | bytes 589832 | tf_op jit(solution)/shard_map/ppermute | solution.py:46
  39.0 2.3 %collective-permute-start.11 = (bf16[1,512,384]{2,1,0:T(8,128)(2,1)S(1)}, bf16[1,512,384]{2,1,0:T(8,128)(2,1)S(1)}, u32[]{:S(2)}, u32[]{:S(2)}) collective-permute-start(bf16[1,512,384]{2,1,0:T(8,128)(2,1)S(1)} %collective-permute-done.6), channel_id=1, source_target_pairs={{0,1},{1,0},{2,3},{3,2},{4,5},{5,4},{6,7},{7,6},{8,9},{9,8},{10,11... | collective-permute-start | bytes 1179656 | tf_op jit(solution)/shard_map/ppermute | solution.py:46
  44.1 5.5 %slice-start = ((s8[7962624]{0:T(1024)(128)(4,1)}), s8[4194304]{0:T(1024)(128)(4,1)S(1)}, s32[]{:S(2)}) async-start(s8[7962624]{0:T(1024)(128)(4,1)} %bitcast.488), calls=%async_computation | async-start | bytes 8388608
  45.1 1.3 %copy-start.3 = (bf16[384,384]{1,0:T(8,128)(2,1)S(1)}, bf16[384,384]{1,0:T(8,128)(2,1)}, u32[]{:S(2)}) copy-start(bf16[384,384]{1,0:T(8,128)(2,1)} %param.14) | copy-start | bytes 884740
  45.6 1.2 %copy-start.1 = (bf16[1,2,128,384]{3,2,1,0:T(8,128)(2,1)S(1)}, bf16[1,2,128,384]{3,2,1,0:T(8,128)(2,1)}, u32[]{:S(2)}) copy-start(bf16[1,2,128,384]{3,2,1,0:T(8,128)(2,1)} %param.10) | copy-start | bytes 589828
  45.6 1.2 %copy-start.5 = (bf16[384,384]{1,0:T(8,128)(2,1)S(1)}, bf16[384,384]{1,0:T(8,128)(2,1)}, u32[]{:S(2)}) copy-start(bf16[384,384]{1,0:T(8,128)(2,1)} %param.15) | copy-start | bytes 884740
  45.9 1.4 %copy-start.4 = (f32[384]{0:T(512)S(1)}, f32[384]{0:T(512)}, u32[]{:S(2)}) copy-start(f32[384]{0:T(512)} %param.17) | copy-start | bytes 4612
  45.9 3.8 %slice-start.1 = ((s8[7962624]{0:T(1024)(128)(4,1)}), s8[3768320]{0:T(1024)(128)(4,1)S(1)}, s32[]{:S(2)}) async-start(s8[7962624]{0:T(1024)(128)(4,1)} %bitcast.488), calls=%async_computation.1 | async-start | bytes 7536640
  46.3 3.4 %copy-start.6 = (pred[8,17]{0,1:T(8,128)(4,1)S(1)}, pred[8,17]{0,1:T(8,128)(4,1)}, u32[]{:S(2)}) copy-start(pred[8,17]{0,1:T(8,128)(4,1)} %constant.61) | copy-start | bytes 412
  47.5 6.8 %collective-permute-start.15 = (bf16[1,1,128,384]{3,2,1,0:T(8,128)(2,1)S(1)}, bf16[1,1,128,384]{3,2,1,0:T(8,128)(2,1)S(1)}, u32[]{:S(2)}, u32[]{:S(2)}) collective-permute-start(bf16[1,1,128,384]{3,2,1,0:T(8,128)(2,1)S(1)} %get-tuple-element.33), channel_id=1, source_target_pairs={{1,2},{3,4},{5,6},{7,8},{9,10},{11,12},{13,14},{2,1},{4,3},{6,5},{... | collective-permute-start | bytes 294920 | tf_op jit(solution)/shard_map/ppermute | solution.py:22
  49.6 4.7 %collective-permute-start.16 = (bf16[1,1,128,384]{3,2,1,0:T(8,128)(2,1)S(1)}, bf16[1,1,128,384]{3,2,1,0:T(8,128)(2,1)S(1)}, u32[]{:S(2)}, u32[]{:S(2)}) collective-permute-start(bf16[1,1,128,384]{3,2,1,0:T(8,128)(2,1)S(1)} %get-tuple-element.34), channel_id=1, source_target_pairs={{0,1},{1,0},{2,3},{3,2},{4,5},{5,4},{6,7},{7,6},{8,9},{9,8},{10,11... | collective-permute-start | bytes 294920 | tf_op jit(solution)/shard_map/ppermute | solution.py:18
  57.5 6.8 %collective-permute-start.17 = (bf16[1,1,128,384]{3,2,1,0:T(8,128)(2,1)S(1)}, bf16[1,1,128,384]{3,2,1,0:T(8,128)(2,1)S(1)}, u32[]{:S(2)}, u32[]{:S(2)}) collective-permute-start(bf16[1,1,128,384]{3,2,1,0:T(8,128)(2,1)S(1)} %slice.296), channel_id=1, source_target_pairs={{1,2},{3,4},{5,6},{7,8},{9,10},{11,12},{13,14},{2,1},{4,3},{6,5},{... | collective-permute-start | bytes 294920 | tf_op jit(solution)/shard_map/ppermute | solution.py:22
  59.6 4.8 %collective-permute-start.18 = (bf16[1,1,128,384]{3,2,1,0:T(8,128)(2,1)S(1)}, bf16[1,1,128,384]{3,2,1,0:T(8,128)(2,1)S(1)}, u32[]{:S(2)}, u32[]{:S(2)}) collective-permute-start(bf16[1,1,128,384]{3,2,1,0:T(8,128)(2,1)S(1)} %slice.297), channel_id=1, source_target_pairs={{0,1},{1,0},{2,3},{3,2},{4,5},{5,4},{6,7},{7,6},{8,9},{9,8},{10,11... | collective-permute-start | bytes 294920 | tf_op jit(solution)/shard_map/ppermute | solution.py:18

commit v11 on v10

--- a/solution.py
+++ b/solution.py
@@ -28,6 +28,11 @@
     return array
 
 
+def halo_pair(array, axis, width):
+    haloed = padded_2(array, ((axis, 1),), width)
+    return haloed[:, :width], haloed[:, -width:]
+
+
 def rms_gain(values, gain):
     return values * lax.rsqrt(jnp.mean(values * values, axis=-1, keepdims=True) + EPS) * gain
 
@@ -45,6 +50,17 @@
     return [
         lax.ppermute(values, ROWS, [(i, i ^ mask) for i in range(size)]) for mask in masks[1:]
     ]
+
+
+def tap_row(rows, weight):
+    return lax.conv_general_dilated(
+        rows,
+        weight[None],
+        window_strides=(1, 1),
+        padding=((0, 0), (1, 1)),
+        dimension_numbers=("NHWC", "HWIO", "NHWC"),
+        preferred_element_type=jnp.float32,
+    )
 
 
 def split_pair(values, axis):
@@ -68,14 +84,24 @@
     return total
 
 
-def upsample_conv(extended, w_up):
-    nf, rp, ncols, chans = extended.shape
-    nrows = rp - 2
+def upsample_conv(before, middle, after, w_up):
+    nf, nrows, ncols, chans = middle.shape
     outs = w_up.shape[-1]
-    padded = jnp.pad(extended, ((0, 0), (0, 0), (1, 1), (0, 0)))
-    taps = jnp.einsum(
-        "frwc,ijco->frwijo", padded, w_up, preferred_element_type=jnp.float32
-    )
+
+    def taps_of(rows):
+        padded = jnp.pad(rows, ((0, 0), (0, 0), (1, 1), (0, 0)))
+        return jnp.einsum("frwc,ijco->frwijo", padded, w_up, preferred_element_type=jnp.float32)
+
+    mid, top, bottom = taps_of(middle), taps_of(before), taps_of(after)
+    shifted = {
+        0: lambda dr, co: jnp.concatenate(
+            [top[:, :, co : co + ncols, dr], mid[:, : nrows - 1, co : co + ncols, dr]], axis=1
+        ),
+        1: lambda dr, co: mid[:, :, co : co + ncols, dr],
+        2: lambda dr, co: jnp.concatenate(
+            [mid[:, 1:, co : co + ncols, dr], bottom[:, :, co : co + ncols, dr]], axis=1
+        ),
+    }
     phases_a = []
     for a in range(2):
         phases_b = []
@@ -85,7 +111,7 @@
                 ro = (a + dr + 1) // 2
                 for dc in range(3):
                     co = (b + dc + 1) // 2
-                    term = taps[:, ro : ro + nrows, co : co + ncols, dr, dc, :]
+                    term = shifted[ro](dr, co)[:, :, :, dc, :]
                     acc = term if acc is None else acc + term
             phases_b.append(acc)
         phases_a.append(jnp.stack(phases_b, axis=3))
@@ -145,10 +171,14 @@
         .astype(jnp.bfloat16)
         .reshape(nframes, nrows, ncols, chans)
     )
-    activ_haloed = padded_2(activ, ((ROWS, 1),), 1)
-    conv_out = (cache_part + conv_rows(activ_haloed, conv_weight[2:])).astype(jnp.bfloat16)
-    extended = padded_2(conv_out, ((ROWS, 1),), 1)
-    return upsample_conv(extended, w_up)
+    above, below = halo_pair(activ, ROWS, 1)
+    weight = conv_weight[2]
+    total = cache_part + tap_row(activ, weight[1])
+    total = total + tap_row(jnp.concatenate([above, activ[:, :-1]], axis=1), weight[0])
+    total = total + tap_row(jnp.concatenate([activ[:, 1:], below], axis=1), weight[2])
+    conv_out = total.astype(jnp.bfloat16)
+    before, after = halo_pair(conv_out, ROWS, 1)
+    return upsample_conv(before, conv_out, after, w_up)
 
 
 def solution(mesh):

time: 69 us -> 77.2 us (1.12)
  the two profiles are of different devices: /device:TPU:5 before, /device:TPU:21 now
where the time goes in v11:
time: 77.2 us; the launch traced here: 76.7 us
  starting transfers between devices  20.6 us (27%)
  matrix products  17.9 us (23%)
  waiting for transfers between devices  13.3 us (17%)
  local copies, waits for them, and re-layouts  12.3 us (16%)
  other arithmetic  11.6 us (15%)
  between operations  0.89 us (1%)
    ppermute x3, starting transfers between devices, padded_2(): lax.ppermute(jnp.where(even, first, last), axis, pairs + [(j, i) for i, j...  10.6 us
    ppermute x13, starting transfers between devices, exchange(): lax.ppermute(values, ROWS, [(i, i ^ mask) for i in range(size)])  9 us
    ppermute x13, waiting for transfers between devices, exchange(): lax.ppermute(values, ROWS, [(i, i ^ mask) for i in range(size)])  7.52 us
    ppermute x3, waiting for transfers between devices, padded_2(): lax.ppermute(jnp.where(even, first, last), axis, pairs + [(j, i) for i, j...  5.8 us
    another operation x4, other arithmetic  4.65 us
    conv_general_dilated x2, matrix products, conv_rows(): lax.conv_general_dilated(haloed[tstep:tstep + 1], weight[tstep], window_s...  4.32 us
    dot_general x10, matrix products, body(): jnp.einsum('fqc,fkc->fqk', q_pair, piece, preferred_element_type=jnp.floa...  4.07 us
    unnamed x36, local copies, waits for them, and re-layouts  3.9 us
  transfers between devices with their start and end apart: 19, of which 3 were waited for; matrix products, arithmetic and copies ran while one was open for 22% of the time, Pallas kernels for 0%

profile of v11, /device:TPU:21, one launch (start us, length us, event | category | flops | bytes accessed | tf_op | source)
XLA Modules:
  0.0 76.7 jit_solution(6571614360016752824)
XLA Ops:
  0.0 1.2 %multiply_reduce_fusion.1 = f32[2,128]{1,0:T(2,128)S(1)} fusion(bf16[1,2,128,384]{3,2,1,0:T(8,128)(2,1)} %param.10), kind=kLoop, calls=%fused_computation.153 | loop fusion | flops 294656 | bytes 197632 | tf_op jit(solution)/shard_map/reduce_sum | solution.py:37
  1.2 1.1 %constant_dynamic-update-slice_fusion.4 = (bf16[1,768,384]{2,1,0:T(8,128)(2,1)S(1)}, bf16[1,256,384]{2,1,0:T(8,128)(2,1)S(1)}) fusion(f32[384]{0:T(512)} %param.11, f32[256]{0:T(256)S(1)} %rsqrt_bitcast_fusion, bf16[1,2,128,384]{3,2,1,0:T(8,128)(2,1)} %param.10), kind=kLoop, calls=%fused_computation.317 | loop fusion | flops 393215 | bytes 592384
  2.3 1.4 %collective-permute-start.2 = (bf16[1,128,384]{2,1,0:T(8,128)(2,1)S(1)}, bf16[1,128,384]{2,1,0:T(8,128)(2,1)S(1)}, u32[]{:S(2)}, u32[]{:S(2)}) collective-permute-start(bf16[1,128,384]{2,1,0:T(8,128)(2,1)S(1)} %get-tuple-element.56), channel_id=1, source_target_pairs={{0,4},{1,5},{2,6},{3,7},{4,0},{5,1},{6,2},{7,3},{8,12},{9,13},{10,... | collective-permute-start | bytes 294920 | tf_op jit(solution)/shard_map/ppermute | solution.py:51
  3.7 1.3 %collective-permute-start.4 = (bf16[1,128,384]{2,1,0:T(8,128)(2,1)S(1)}, bf16[1,128,384]{2,1,0:T(8,128)(2,1)S(1)}, u32[]{:S(2)}, u32[]{:S(2)}) collective-permute-start(bf16[1,128,384]{2,1,0:T(8,128)(2,1)S(1)} %get-tuple-element.56), channel_id=1, source_target_pairs={{0,12},{1,13},{2,14},{3,15},{4,8},{5,9},{6,10},{7,11},{8,4},{9,5},... | collective-permute-start | bytes 294920 | tf_op jit(solution)/shard_map/ppermute | solution.py:51
  5.2 1.8 %broadcast_select_fusion.3 = (bf16[2,1,128,384]{3,2,1,0:T(8,128)(2,1)}, bf16[2,1,128,384]{3,2,1,0:T(8,128)(2,1)}) fusion(pred[]{:T(512)S(6)} %eq.9, bf16[2,2,128,384]{3,2,1,0:T(8,128)(2,1)} %param.16), kind=kLoop, calls=%fused_computation.283 | loop fusion | flops 196608 | bytes 786433 | tf_op jit(solution)/shard_map/jit(_where)/select_n | solution.py:23
  7.0 6.7 %collective-permute-start = (bf16[2,1,128,384]{3,2,1,0:T(8,128)(2,1)}, bf16[2,1,128,384]{3,2,1,0:T(8,128)(2,1)S(1)}, u32[]{:S(2)}, u32[]{:S(2)}) collective-permute-start(bf16[2,1,128,384]{3,2,1,0:T(8,128)(2,1)} %get-tuple-element.44), channel_id=1, source_target_pairs={{1,2},{3,4},{5,6},{7,8},{9,10},{11,12},{13,14},{2,1},{4,3},{6,5},{... | collective-permute-start | bytes 589832 | tf_op jit(solution)/shard_map/ppermute | solution.py:22
  13.9 1.6 %convert_bitcast_fusion.1 = (bf16[1,256,384]{2,1,0:T(8,128)(2,1)S(1)}, bf16[1,256,384]{2,1,0:T(8,128)(2,1)S(1)}) fusion(bf16[384,384]{1,0:T(8,128)(2,1)} %param.13, bf16[256,384]{1,0:T(8,128)(2,1)S(1)} %fusion.86, bf16[384,384]{1,0:T(8,128)(2,1)} %param.12), kind=kOutput, calls=%fused_computation.306 | convolution fusion | flops 151486464 | bytes 1179648 | tf_op jit(solution)/shard_map/fqc,dc->fqd/dot_general | solution.py:146
  15.7 0.5 collective-permute-start.8
  16.3 1.1 %collective-permute-start.10 = (bf16[1,768,384]{2,1,0:T(8,128)(2,1)S(1)}, bf16[1,768,384]{2,1,0:T(8,128)(2,1)S(1)}, u32[]{:S(2)}, u32[]{:S(2)}) collective-permute-start(bf16[1,768,384]{2,1,0:T(8,128)(2,1)S(1)} %constant_dynamic-update-slice_fusion), channel_id=1, source_target_pairs={{0,1},{1,0},{2,3},{3,2},{4,5},{5,4},{6,7},{7,6},{8,9},{9,8},{10,11... | collective-permute-start | bytes 1769480 | tf_op jit(solution)/shard_map/ppermute | solution.py:51
  17.4 0.6 convolution_bitcast_fusion.2
  18.2 2.3 %collective-permute-start.9 = (bf16[1,256,384]{2,1,0:T(8,128)(2,1)S(1)}, bf16[1,256,384]{2,1,0:T(8,128)(2,1)S(1)}, u32[]{:S(2)}, u32[]{:S(2)}) collective-permute-start(bf16[1,256,384]{2,1,0:T(8,128)(2,1)S(1)} %pad_maximum_fusion.9), channel_id=1, source_target_pairs={{0,12},{1,13},{2,14},{3,15},{4,8},{5,9},{6,10},{7,11},{8,4},{9,5},... | collective-permute-start | bytes 589832 | tf_op jit(solution)/shard_map/ppermute | solution.py:51
  22.3 3.1 %fusion.26 = f32[2,8,17,384]{3,1,2,0:T(8,128)S(1)} fusion(bf16[3,3,3,384,384]{4,3,2,1,0:T(8,128)(2,1)} %param.18, bf16[4,1,7,2,384]{4,2,3,0,1:T(8,128)(2,1)S(1)} %slice.405, bf16[4,1,8,17,384]{4,2,3,0,1:T(8,128)(2,1)S(1)} %copy.23, pred[8,17]{0,1:T(8,128)(4,1)S(1)} %copy-done.11), kind=kOutput, calls=%fused_computation.43 | convolution fusion | flops 723449856 | bytes 3532936 | tf_op jit(solution)/shard_map/conv_general_dilated | solution.py:75
  25.4 1.2 %fusion.23 = f32[2,8,17,384]{3,1,2,0:T(8,128)S(1)} fusion(f32[2,8,17,384]{3,1,2,0:T(8,128)S(1)} %fusion.26, bf16[3,3,3,384,384]{4,3,2,1,0:T(8,128)(2,1)S(1)} %bitcast.312, bf16[4,1,7,2,384]{4,2,3,0,1:T(8,128)(2,1)S(1)} %slice.403, bf16[4,1,8,17,384]{4,2,3,0,1:T(8,128)(2,1)S(1)} %copy.20, pred[8,17]{0,1:T(8,128)(4,1)S(1)} %copy-done.11), kind=kOutput, calls=%fused_computation.42 | convolution fusion | flops 723554304 | bytes 3959808 | tf_op jit(solution)/shard_map/conv_general_dilated | solution.py:75
  27.9 7.5 %collective-permute-done.9 = bf16[1,256,384]{2,1,0:T(8,128)(2,1)S(1)} collective-permute-done((bf16[1,256,384]{2,1,0:T(8,128)(2,1)S(1)}, bf16[1,256,384]{2,1,0:T(8,128)(2,1)S(1)}, u32[]{:S(2)}, u32[]{:S(2)}) %collective-permute-start.9) | collective-permute-done | bytes 196640 | tf_op jit(solution)/shard_map/ppermute | solution.py:51
  35.4 1.5 %collective-permute-start.14 = (bf16[1,256,384]{2,1,0:T(8,128)(2,1)S(1)}, bf16[1,256,384]{2,1,0:T(8,128)(2,1)S(1)}, u32[]{:S(2)}, u32[]{:S(2)}) collective-permute-start(bf16[1,256,384]{2,1,0:T(8,128)(2,1)S(1)} %collective-permute-done.9), channel_id=1, source_target_pairs={{0,1},{1,0},{2,3},{3,2},{4,5},{5,4},{6,7},{7,6},{8,9},{9,8},{10,11... | collective-permute-start | bytes 589832 | tf_op jit(solution)/shard_map/ppermute | solution.py:51
  38.2 0.5 convolution_bitcast_fusion.6
  39.2 0.6 convolution_bitcast_fusion.1
  40.0 0.5 convolution_bitcast_fusion.5
  40.6 0.4 fusion.40
  42.7 0.5 fusion.44
  43.2 0.5 fusion.16
  44.6 0.4 convert_bitcast_fusion
  45.0 0.5 copy-done.7
  45.5 0.4 convolution_bitcast_fusion.7
  45.9 0.4 multiply_reduce_fusion
  46.4 0.4 multiply_convert_fusion
  46.8 1.9 %collective-permute-start.15 = (bf16[1,1,128,384]{3,2,1,0:T(8,128)(2,1)S(1)}, bf16[1,1,128,384]{3,2,1,0:T(8,128)(2,1)S(1)}, u32[]{:S(2)}, u32[]{:S(2)}) collective-permute-start(bf16[1,1,128,384]{3,2,1,0:T(8,128)(2,1)S(1)} %get-tuple-element.51), channel_id=1, source_target_pairs={{1,2},{3,4},{5,6},{7,8},{9,10},{11,12},{13,14},{2,1},{4,3},{6,5},{... | collective-permute-start | bytes 294920 | tf_op jit(solution)/shard_map/ppermute | solution.py:22
  48.8 0.6 collective-permute-start.16
  49.7 0.5 fusion.7
  50.3 3.4 %collective-permute-done.15 = bf16[1,1,128,384]{3,2,1,0:T(8,128)(2,1)S(1)} collective-permute-done((bf16[1,1,128,384]{3,2,1,0:T(8,128)(2,1)S(1)}, bf16[1,1,128,384]{3,2,1,0:T(8,128)(2,1)S(1)}, u32[]{:S(2)}, u32[]{:S(2)}) %collective-permute-start.15) | collective-permute-done | bytes 98336 | tf_op jit(solution)/shard_map/ppermute | solution.py:22
  54.6 0.5 fusion.8
  55.2 0.5 fusion.17
  56.1 0.8 %convolution_bitcast_fusion = f32[1,2,130,3,3,192]{5,2,4,3,1,0:T(8,128)S(1)} fusion(bf16[3,3,384,192]{2,3,1,0:T(8,128)(2,1)S(1)} %copy-done, bf16[1,2,128,384]{3,2,1,0:T(8,128)(2,1)S(1)} %bitcast.310), kind=kOutput, calls=%fused_computation.6 | convolution fusion | flops 345047040 | bytes 3320832 | tf_op jit(solution)/shard_map/frwc,ijco->frwijo/dot_general | solution.py:93
  56.9 2.6 %slice_bitcast_fusion.6 = (f32[1,2,128,3,192]{4,2,3,1,0:T(8,128)}, f32[1,2,128,3,192]{4,2,3,1,0:T(8,128)}, f32[1,2,128,3,192]{4,2,3,1,0:T(8,128)}, f32[1,2,128,3...) fusion(f32[1,2,130,3,3,192]{5,2,4,3,1,0:T(8,128)S(1)} %convolut, ...), kind=kLoop, calls=%fused_computation.68 | loop fusion | bytes 10616832 | tf_op jit(solution)/shard_map/squeeze | solution.py:100
  59.6 0.6 copy-done.1
  60.3 1.9 %collective-permute-start.17 = (bf16[1,1,128,384]{3,2,1,0:T(8,128)(2,1)S(1)}, bf16[1,1,128,384]{3,2,1,0:T(8,128)(2,1)S(1)}, u32[]{:S(2)}, u32[]{:S(2)}) collective-permute-start(bf16[1,1,128,384]{3,2,1,0:T(8,128)(2,1)S(1)} %slice.437), channel_id=1, source_target_pairs={{1,2},{3,4},{5,6},{7,8},{9,10},{11,12},{13,14},{2,1},{4,3},{6,5},{... | collective-permute-start | bytes 294920 | tf_op jit(solution)/shard_map/ppermute | solution.py:22
  62.3 0.4 collective-permute-start.18
  62.7 2.0 %slice_bitcast_fusion.19 = (f32[1,1,128,3,192]{4,2,3,1,0:T(8,128)S(1)}, f32[1,1,128,3,192]{4,2,3,1,0:T(8,128)S(1)}, f32[1,1,128,3,192]{4,2,3,1,0:T(8,128)S(1)}, ...) fusion(f32[1,2,130,3,3,192]{5,2,4,3,1,0:T(8,128)} %copy-done.1), kind=kLoop, calls=%fused_computation.124 | loop fusion | bytes 3538944 | tf_op jit(solution)/shard_map/squeeze | solution.py:98
  64.7 2.4 %collective-permute-done.17 = bf16[1,1,128,384]{3,2,1,0:T(8,128)(2,1)S(1)} collective-permute-done((bf16[1,1,128,384]{3,2,1,0:T(8,128)(2,1)S(1)}, bf16[1,1,128,384]{3,2,1,0:T(8,128)(2,1)S(1)}, u32[]{:S(2)}, u32[]{:S(2)}) %collective-permute-start.17) | collective-permute-done | bytes 98336 | tf_op jit(solution)/shard_map/ppermute | solution.py:22
  67.1 0.7 convolution_bitcast_fusion.4
  67.9 0.7 convolution_bitcast_fusion.3
  68.8 1.0 %copy-done.2 = f32[1,2,128,3,192]{4,2,3,1,0:T(8,128)S(1)} copy-done((f32[1,2,128,3,192]{4,2,3,1,0:T(8,128)S(1)}, f32[1,2,128,3,192]{4,2,3,1,0:T(8,128)}, u32[]{:S(2)}) %copy-start.2) | copy-done | bytes 589848
  70.0 1.2 %fusion.105 = bf16[1,2,128,1,192]{4,2,3,1,0:T(8,128)(2,1)S(1)} fusion(f32[1,1,128,3,192]{4,2,3,1,0:T(8,128)S(1)} %get-tuple-element.32, f32[1,1,128,3,192]{4,2,3,1,0:T(8,128)S(1)} %get-tuple-element.20, f32[1,2,128,3,192]{4,2,3,1,0:T(8,128)S(1)} %copy-done.2, f32[1,2,128,3,192]{4,2,3,1,0:T(8,128)} %get-tuple-element.21, ...), kind=kLoop, calls=%fused_computation.168 | loop fusion | flops 589824 | bytes 2457600 | tf_op jit(solution)/shard_map/convert.8
  71.2 1.1 %fusion.119 = bf16[1,2,128,1,192]{4,2,3,1,0:T(8,128)(2,1)S(1)} fusion(f32[1,2,128,3,192]{4,2,3,1,0:T(8,128)} %get-tuple-element.27, f32[1,2,128,3,192]{4,2,3,1,0:T(8,128)S(1)} %copy-done.2, f32[1,1,128,3,192]{4,2,3,1,0:T(8,128)S(1)} %get-tuple-element.17, f32[1,1,128,3,192]{4,2,3,1,0:T(8,128)S(1)} %get-tuple-element.31, ...), kind=kLoop, calls=%fused_computation.190 | loop fusion | flops 589824 | bytes 2457600 | tf_op jit(solution)/shard_map/convert.9
  72.4 1.1 %fusion.95 = bf16[1,2,128,1,192]{4,2,3,1,0:T(8,128)(2,1)S(1)} fusion(f32[1,1,128,3,192]{4,2,3,1,0:T(8,128)S(1)} %get-tuple-element.18, f32[1,1,128,3,192]{4,2,3,1,0:T(8,128)S(1)} %get-tuple-element.35, f32[1,1,128,3,192]{4,2,3,1,0:T(8,128)S(1)} %get-tuple-element.33, f32[1,1,128,3,192]{4,2,3,1,0:T(8,128)S(1)} %get-tuple-element.16, ...), kind=kLoop, calls=%fused_computation.158 | loop fusion | flops 589824 | bytes 2457600 | tf_op jit(solution)/shard_map/convert.5
  73.6 1.1 %fusion.108 = bf16[1,2,128,1,192]{4,2,3,1,0:T(8,128)(2,1)S(1)} fusion(f32[1,1,128,3,192]{4,2,3,1,0:T(8,128)S(1)} %get-tuple-element.34, f32[1,1,128,3,192]{4,2,3,1,0:T(8,128)S(1)} %get-tuple-element.19, f32[1,1,128,3,192]{4,2,3,1,0:T(8,128)S(1)} %get-tuple-element.35, f32[1,1,128,3,192]{4,2,3,1,0:T(8,128)S(1)} %get-tuple-element.18, ...), kind=kLoop, calls=%fused_computation.172 | loop fusion | flops 589824 | bytes 2457600 | tf_op jit(solution)/shard_map/convert.6
  74.9 0.5 copy.44
  75.4 1.3 %convert_element_type.174 = bf16[1,4,49152]{2,1,0:T(4,128)(2,1)} reshape(bf16[1,2,2,128,2,192]{5,4,3,2,1,0:T(2,128)(2,1)S(1)} %copy.44) | data formatting | bytes 786432 | tf_op jit(solution)/shard_map/convert_element_type | solution.py:119
  (129 shorter events, 11.0 us)
Async XLA Ops:
  0.0 56.1 %copy-start = (bf16[3,3,384,192]{2,3,1,0:T(8,128)(2,1)S(1)}, bf16[3,3,384,192]{2,3,1,0:T(8,128)(2,1)}, u32[]{:S(2)}) copy-start(bf16[3,3,384,192]{2,3,1,0:T(8,128)(2,1)} %param.19) | copy-start | bytes 3981316
  0.0 13.8 %copy-start.5 = (bf16[1,2,128,384]{3,2,1,0:T(8,128)(2,1)S(1)}, bf16[1,2,128,384]{3,2,1,0:T(8,128)(2,1)}, u32[]{:S(2)}) copy-start(bf16[1,2,128,384]{3,2,1,0:T(8,128)(2,1)} %param.10) | copy-start | bytes 589828
  0.0 13.8 %copy-start.8 = (f32[384]{0:T(512)S(1)}, f32[384]{0:T(512)}, u32[]{:S(2)}) copy-start(f32[384]{0:T(512)} %param.11) | copy-start | bytes 4612
  2.3 13.3 %collective-permute-start.2 = (bf16[1,128,384]{2,1,0:T(8,128)(2,1)S(1)}, bf16[1,128,384]{2,1,0:T(8,128)(2,1)S(1)}, u32[]{:S(2)}, u32[]{:S(2)}) collective-permute-start(bf16[1,128,384]{2,1,0:T(8,128)(2,1)S(1)} %get-tuple-element.56), channel_id=1, source_target_pairs={{0,4},{1,5},{2,6},{3,7},{4,0},{5,1},{6,2},{7,3},{8,12},{9,13},{10,... | collective-permute-start | bytes 294920 | tf_op jit(solution)/shard_map/ppermute | solution.py:51
  3.6 12.1 %collective-permute-start.3 = (bf16[1,128,384]{2,1,0:T(8,128)(2,1)S(1)}, bf16[1,128,384]{2,1,0:T(8,128)(2,1)S(1)}, u32[]{:S(2)}, u32[]{:S(2)}) collective-permute-start(bf16[1,128,384]{2,1,0:T(8,128)(2,1)S(1)} %get-tuple-element.56), channel_id=1, source_target_pairs={{0,8},{1,9},{2,10},{3,11},{4,12},{5,13},{6,14},{7,15},{8,0},{9,1},... | collective-permute-start | bytes 294920 | tf_op jit(solution)/shard_map/ppermute | solution.py:51
  3.7 12.5 %collective-permute-start.4 = (bf16[1,128,384]{2,1,0:T(8,128)(2,1)S(1)}, bf16[1,128,384]{2,1,0:T(8,128)(2,1)S(1)}, u32[]{:S(2)}, u32[]{:S(2)}) collective-permute-start(bf16[1,128,384]{2,1,0:T(8,128)(2,1)S(1)} %get-tuple-element.56), channel_id=1, source_target_pairs={{0,12},{1,13},{2,14},{3,15},{4,8},{5,9},{6,10},{7,11},{8,4},{9,5},... | collective-permute-start | bytes 294920 | tf_op jit(solution)/shard_map/ppermute | solution.py:51
  5.0 10.5 %collective-permute-start.5 = (bf16[1,128,384]{2,1,0:T(8,128)(2,1)S(1)}, bf16[1,128,384]{2,1,0:T(8,128)(2,1)S(1)}, u32[]{:S(2)}, u32[]{:S(2)}) collective-permute-start(bf16[1,128,384]{2,1,0:T(8,128)(2,1)S(1)} %get-tuple-element.57), channel_id=1, source_target_pairs={{0,2},{1,3},{2,0},{3,1},{4,6},{5,7},{6,4},{7,5},{8,10},{9,11},{10,... | collective-permute-start | bytes 294920 | tf_op jit(solution)/shard_map/ppermute | solution.py:51
  7.0 11.2 %collective-permute-start = (bf16[2,1,128,384]{3,2,1,0:T(8,128)(2,1)}, bf16[2,1,128,384]{3,2,1,0:T(8,128)(2,1)S(1)}, u32[]{:S(2)}, u32[]{:S(2)}) collective-permute-start(bf16[2,1,128,384]{3,2,1,0:T(8,128)(2,1)} %get-tuple-element.44), channel_id=1, source_target_pairs={{1,2},{3,4},{5,6},{7,8},{9,10},{11,12},{13,14},{2,1},{4,3},{6,5},{... | collective-permute-start | bytes 589832 | tf_op jit(solution)/shard_map/ppermute | solution.py:22
  15.5 5.0 %collective-permute-start.1 = (bf16[2,1,128,384]{3,2,1,0:T(8,128)(2,1)}, bf16[2,1,128,384]{3,2,1,0:T(8,128)(2,1)S(1)}, u32[]{:S(2)}, u32[]{:S(2)}) collective-permute-start(bf16[2,1,128,384]{3,2,1,0:T(8,128)(2,1)} %get-tuple-element.45), channel_id=1, source_target_pairs={{0,1},{1,0},{2,3},{3,2},{4,5},{5,4},{6,7},{7,6},{8,9},{9,8},{10,11... | collective-permute-start | bytes 589832 | tf_op jit(solution)/shard_map/ppermute | solution.py:18
  15.6 11.0 %collective-permute-start.7 = (bf16[1,256,384]{2,1,0:T(8,128)(2,1)S(1)}, bf16[1,256,384]{2,1,0:T(8,128)(2,1)S(1)}, u32[]{:S(2)}, u32[]{:S(2)}) collective-permute-start(bf16[1,256,384]{2,1,0:T(8,128)(2,1)S(1)} %pad_maximum_fusion.9), channel_id=1, source_target_pairs={{0,4},{1,5},{2,6},{3,7},{4,0},{5,1},{6,2},{7,3},{8,12},{9,13},{10,... | collective-permute-start | bytes 589832 | tf_op jit(solution)/shard_map/ppermute | solution.py:51
  15.7 11.7 %collective-permute-start.8 = (bf16[1,256,384]{2,1,0:T(8,128)(2,1)S(1)}, bf16[1,256,384]{2,1,0:T(8,128)(2,1)S(1)}, u32[]{:S(2)}, u32[]{:S(2)}) collective-permute-start(bf16[1,256,384]{2,1,0:T(8,128)(2,1)S(1)} %pad_maximum_fusion.9), channel_id=1, source_target_pairs={{0,8},{1,9},{2,10},{3,11},{4,12},{5,13},{6,14},{7,15},{8,0},{9,1},... | collective-permute-start | bytes 589832 | tf_op jit(solution)/shard_map/ppermute | solution.py:51
  16.3 22.9 %collective-permute-start.10 = (bf16[1,768,384]{2,1,0:T(8,128)(2,1)S(1)}, bf16[1,768,384]{2,1,0:T(8,128)(2,1)S(1)}, u32[]{:S(2)}, u32[]{:S(2)}) collective-permute-start(bf16[1,768,384]{2,1,0:T(8,128)(2,1)S(1)} %constant_dynamic-update-slice_fusion), channel_id=1, source_target_pairs={{0,1},{1,0},{2,3},{3,2},{4,5},{5,4},{6,7},{7,6},{8,9},{9,8},{10,11... | collective-permute-start | bytes 1769480 | tf_op jit(solution)/shard_map/ppermute | solution.py:51
  18.0 2.5 %copy-start.6 = (bf16[2,2,128,384]{3,2,1,0:T(8,128)(2,1)S(1)}, bf16[2,2,128,384]{3,2,1,0:T(8,128)(2,1)}, u32[]{:S(2)}) copy-start(bf16[2,2,128,384]{3,2,1,0:T(8,128)(2,1)} %param.16) | copy-start | bytes 1179652
  18.2 17.2 %collective-permute-start.9 = (bf16[1,256,384]{2,1,0:T(8,128)(2,1)S(1)}, bf16[1,256,384]{2,1,0:T(8,128)(2,1)S(1)}, u32[]{:S(2)}, u32[]{:S(2)}) collective-permute-start(bf16[1,256,384]{2,1,0:T(8,128)(2,1)S(1)} %pad_maximum_fusion.9), channel_id=1, source_target_pairs={{0,12},{1,13},{2,14},{3,15},{4,8},{5,9},{6,10},{7,11},{8,4},{9,5},... | collective-permute-start | bytes 589832 | tf_op jit(solution)/shard_map/ppermute | solution.py:51
  20.5 17.7 %collective-permute-start.6 = (bf16[1,512,384]{2,1,0:T(8,128)(2,1)S(1)}, bf16[1,512,384]{2,1,0:T(8,128)(2,1)S(1)}, u32[]{:S(2)}, u32[]{:S(2)}) collective-permute-start(bf16[1,512,384]{2,1,0:T(8,128)(2,1)S(1)} %pad_maximum_fusion.2), channel_id=1, source_target_pairs={{0,2},{1,3},{2,0},{3,1},{4,6},{5,7},{6,4},{7,5},{8,10},{9,11},{10,... | collective-permute-start | bytes 1179656 | tf_op jit(solution)/shard_map/ppermute | solution.py:51
  20.5 4.9 %slice-start = ((s8[7962624]{0:T(1024)(128)(4,1)}), s8[4194304]{0:T(1024)(128)(4,1)S(1)}, s32[]{:S(2)}) async-start(s8[7962624]{0:T(1024)(128)(4,1)} %bitcast.311), calls=%async_computation | async-start | bytes 8388608
  21.2 1.0 %copy-start.11 = (pred[8,17]{0,1:T(8,128)(4,1)S(1)}, pred[8,17]{0,1:T(8,128)(4,1)}, u32[]{:S(2)}) copy-start(pred[8,17]{0,1:T(8,128)(4,1)} %constant.73) | copy-start | bytes 412
  21.8 3.6 %slice-start.1 = ((s8[7962624]{0:T(1024)(128)(4,1)}), s8[3768320]{0:T(1024)(128)(4,1)S(1)}, s32[]{:S(2)}) async-start(s8[7962624]{0:T(1024)(128)(4,1)} %bitcast.311), calls=%async_computation.1 | async-start | bytes 7536640
  27.0 10.3 %collective-permute-start.12 = (bf16[1,256,384]{2,1,0:T(8,128)(2,1)S(1)}, bf16[1,256,384]{2,1,0:T(8,128)(2,1)S(1)}, u32[]{:S(2)}, u32[]{:S(2)}) collective-permute-start(bf16[1,256,384]{2,1,0:T(8,128)(2,1)S(1)} %collective-permute-done.7), channel_id=1, source_target_pairs={{0,1},{1,0},{2,3},{3,2},{4,5},{5,4},{6,7},{7,6},{8,9},{9,8},{10,11... | collective-permute-start | bytes 589832 | tf_op jit(solution)/shard_map/ppermute | solution.py:51
  27.4 10.4 %collective-permute-start.13 = (bf16[1,256,384]{2,1,0:T(8,128)(2,1)S(1)}, bf16[1,256,384]{2,1,0:T(8,128)(2,1)S(1)}, u32[]{:S(2)}, u32[]{:S(2)}) collective-permute-start(bf16[1,256,384]{2,1,0:T(8,128)(2,1)S(1)} %collective-permute-done.8), channel_id=1, source_target_pairs={{0,1},{1,0},{2,3},{3,2},{4,5},{5,4},{6,7},{7,6},{8,9},{9,8},{10,11... | collective-permute-start | bytes 589832 | tf_op jit(solution)/shard_map/ppermute | solution.py:51
  35.4 3.4 %collective-permute-start.14 = (bf16[1,256,384]{2,1,0:T(8,128)(2,1)S(1)}, bf16[1,256,384]{2,1,0:T(8,128)(2,1)S(1)}, u32[]{:S(2)}, u32[]{:S(2)}) collective-permute-start(bf16[1,256,384]{2,1,0:T(8,128)(2,1)S(1)} %collective-permute-done.9), channel_id=1, source_target_pairs={{0,1},{1,0},{2,3},{3,2},{4,5},{5,4},{6,7},{7,6},{8,9},{9,8},{10,11... | collective-permute-start | bytes 589832 | tf_op jit(solution)/shard_map/ppermute | solution.py:51
  38.2 1.8 %collective-permute-start.11 = (bf16[1,512,384]{2,1,0:T(8,128)(2,1)S(1)}, bf16[1,512,384]{2,1,0:T(8,128)(2,1)S(1)}, u32[]{:S(2)}, u32[]{:S(2)}) collective-permute-start(bf16[1,512,384]{2,1,0:T(8,128)(2,1)S(1)} %collective-permute-done.6), channel_id=1, source_target_pairs={{0,1},{1,0},{2,3},{3,2},{4,5},{5,4},{6,7},{7,6},{8,9},{9,8},{10,11... | collective-permute-start | bytes 1179656 | tf_op jit(solution)/shard_map/ppermute | solution.py:51
  44.6 1.0 %copy-start.7 = (bf16[384,384]{1,0:T(8,128)(2,1)S(1)}, bf16[384,384]{1,0:T(8,128)(2,1)}, u32[]{:S(2)}) copy-start(bf16[384,384]{1,0:T(8,128)(2,1)} %param.14) | copy-start | bytes 884740
  44.6 1.4 %copy-start.10 = (bf16[384,384]{1,0:T(8,128)(2,1)S(1)}, bf16[384,384]{1,0:T(8,128)(2,1)}, u32[]{:S(2)}) copy-start(bf16[384,384]{1,0:T(8,128)(2,1)} %param.15) | copy-start | bytes 884740
  45.5 0.9 %copy-start.9 = (f32[384]{0:T(512)S(1)}, f32[384]{0:T(512)}, u32[]{:S(2)}) copy-start(f32[384]{0:T(512)} %param.17) | copy-start | bytes 4612
  46.8 6.8 %collective-permute-start.15 = (bf16[1,1,128,384]{3,2,1,0:T(8,128)(2,1)S(1)}, bf16[1,1,128,384]{3,2,1,0:T(8,128)(2,1)S(1)}, u32[]{:S(2)}, u32[]{:S(2)}) collective-permute-start(bf16[1,1,128,384]{3,2,1,0:T(8,128)(2,1)S(1)} %get-tuple-element.51), channel_id=1, source_target_pairs={{1,2},{3,4},{5,6},{7,8},{9,10},{11,12},{13,14},{2,1},{4,3},{6,5},{... | collective-permute-start | bytes 294920 | tf_op jit(solution)/shard_map/ppermute | solution.py:22
  48.8 4.9 %collective-permute-start.16 = (bf16[1,1,128,384]{3,2,1,0:T(8,128)(2,1)S(1)}, bf16[1,1,128,384]{3,2,1,0:T(8,128)(2,1)S(1)}, u32[]{:S(2)}, u32[]{:S(2)}) collective-permute-start(bf16[1,1,128,384]{3,2,1,0:T(8,128)(2,1)S(1)} %get-tuple-element.52), channel_id=1, source_target_pairs={{0,1},{1,0},{2,3},{3,2},{4,5},{5,4},{6,7},{7,6},{8,9},{9,8},{10,11... | collective-permute-start | bytes 294920 | tf_op jit(solution)/shard_map/ppermute | solution.py:18
  56.9 3.2 %copy-start.1 = (f32[1,2,130,3,3,192]{5,2,4,3,1,0:T(8,128)}, f32[1,2,130,3,3,192]{5,2,4,3,1,0:T(8,128)S(1)}, u32[]{:S(2)}) copy-start(f32[1,2,130,3,3,192]{5,2,4,3,1,0:T(8,128)S(1)} %convolution_bitcast_fusion) | copy-start | bytes 5391364
  60.3 6.8 %collective-permute-start.17 = (bf16[1,1,128,384]{3,2,1,0:T(8,128)(2,1)S(1)}, bf16[1,1,128,384]{3,2,1,0:T(8,128)(2,1)S(1)}, u32[]{:S(2)}, u32[]{:S(2)}) collective-permute-start(bf16[1,1,128,384]{3,2,1,0:T(8,128)(2,1)S(1)} %slice.437), channel_id=1, source_target_pairs={{1,2},{3,4},{5,6},{7,8},{9,10},{11,12},{13,14},{2,1},{4,3},{6,5},{... | collective-permute-start | bytes 294920 | tf_op jit(solution)/shard_map/ppermute | solution.py:22
  62.3 4.8 %collective-permute-start.18 = (bf16[1,1,128,384]{3,2,1,0:T(8,128)(2,1)S(1)}, bf16[1,1,128,384]{3,2,1,0:T(8,128)(2,1)S(1)}, u32[]{:S(2)}, u32[]{:S(2)}) collective-permute-start(bf16[1,1,128,384]{3,2,1,0:T(8,128)(2,1)S(1)} %slice.438), channel_id=1, source_target_pairs={{0,1},{1,0},{2,3},{3,2},{4,5},{5,4},{6,7},{7,6},{8,9},{9,8},{10,11... | collective-permute-start | bytes 294920 | tf_op jit(solution)/shard_map/ppermute | solution.py:18
  68.6 1.1 %copy-start.2 = (f32[1,2,128,3,192]{4,2,3,1,0:T(8,128)S(1)}, f32[1,2,128,3,192]{4,2,3,1,0:T(8,128)}, u32[]{:S(2)}) copy-start(f32[1,2,128,3,192]{4,2,3,1,0:T(8,128)} %get-tuple-element.24) | copy-start | bytes 1769476
  68.6 1.4 %copy-start.4 = (f32[1,2,128,3,192]{4,2,3,1,0:T(8,128)S(1)}, f32[1,2,128,3,192]{4,2,3,1,0:T(8,128)}, u32[]{:S(2)}) copy-start(f32[1,2,128,3,192]{4,2,3,1,0:T(8,128)} %get-tuple-element.26) | copy-start | bytes 1769476
  70.0 1.2 %copy-start.3 = (f32[1,2,128,3,192]{4,2,3,1,0:T(8,128)S(1)}, f32[1,2,128,3,192]{4,2,3,1,0:T(8,128)}, u32[]{:S(2)}) copy-start(f32[1,2,128,3,192]{4,2,3,1,0:T(8,128)} %get-tuple-element.23) | copy-start | bytes 1769476

commit v12 on v10

--- a/solution.py
+++ b/solution.py
@@ -99,7 +99,7 @@
     nframes, nrows, ncols, chans = frames.shape
     scale = chans ** (-0.5)
 
-    cache_haloed = padded_2(cache_one, ((ROWS, 1),), 1)
+    cache_haloed = padded_2(cache_one, ((ROWS, 1),), 2)
     cache_part = conv_rows(cache_haloed, conv_weight[:2])
 
     flat = frames.reshape(nframes, nrows * ncols, chans)
@@ -145,9 +145,12 @@
         .astype(jnp.bfloat16)
         .reshape(nframes, nrows, ncols, chans)
     )
-    activ_haloed = padded_2(activ, ((ROWS, 1),), 1)
-    conv_out = (cache_part + conv_rows(activ_haloed, conv_weight[2:])).astype(jnp.bfloat16)
-    extended = padded_2(conv_out, ((ROWS, 1),), 1)
+    activ_haloed = padded_2(activ, ((ROWS, 1),), 2)
+    extended = cache_part + conv_rows(activ_haloed, conv_weight[2:])
+    where = lax.axis_index(ROWS)
+    line = jnp.arange(nrows + 2)
+    inside = ((line > 0) | (where > 0)) & ((line < nrows + 1) | (where < size - 1))
+    extended = jnp.where(inside[None, :, None, None], extended, 0.0).astype(jnp.bfloat16)
     return upsample_conv(extended, w_up)
 
 

time: 69 us -> 99.9 us (1.45); the launches traced: 68.7 us -> 98.4 us
  matrix products: 14.9 us -> 39.4 us
  local copies, waits for them, and re-layouts: 4.19 us -> 18.6 us
  waiting for transfers between devices: 17.7 us -> 3.59 us
  starting transfers between devices: 22.9 us -> 25.9 us
  other arithmetic: 8.43 us -> 10.2 us
    conv_general_dilated x3, matrix products: 3.58 us -> 13.5 us  [conv_rows(): lax.conv_general_dilated(haloed[tstep:tstep + 1], weight[tstep], window_s...]
    dot_general x10, matrix products: 4.07 us -> 12 us  [body(): jnp.einsum('fqc,fkc->fqk', q_pair, piece, preferred_element_type=jnp.floa...]
    dot_general x10, matrix products: 3.34 us -> 11.1 us  [body(): jnp.einsum('fqk,fkc->fqc', e.astype(jnp.bfloat16), p, preferred_element_t...]
    ppermute x3 -> x2, waiting for transfers between devices: 7.23 us -> 0.01 us  [padded_2(): lax.ppermute(jnp.where(even, first, last), axis, pairs + [(j, i) for i, j...]
    conv_general_dilated x6 -> x9, local copies, waits for them, and re-layouts: 0.21 us -> 7.19 us  [conv_rows(): lax.conv_general_dilated(haloed[tstep:tstep + 1], weight[tstep], window_s...]
    ppermute x13, waiting for transfers between devices: 10.4 us -> 3.58 us  [exchange(): lax.ppermute(values, ROWS, [(i, i ^ mask) for i in range(size)])]
    unnamed x25 -> x54, local copies, waits for them, and re-layouts: 1.09 us -> 5.49 us
    slice x3, local copies, waits for them, and re-layouts: 0.4 us -> 2.93 us  [conv_rows(): haloed[tstep:tstep + 1]]
  transfers between devices with their start and end apart: 19 -> 17, of which waited for: 4 -> 2; matrix products, arithmetic and copies ran while one was open for 17% -> 40% of each run, Pallas kernels for 0% -> 0%
where the time goes in v12:
time: 99.9 us; the launch traced here: 98.4 us
  matrix products  39.4 us (39%)
  starting transfers between devices  25.9 us (26%)
  local copies, waits for them, and re-layouts  18.6 us (19%)
  other arithmetic  10.2 us (10%)
  waiting for transfers between devices  3.59 us (4%)
    ppermute x13, starting transfers between devices, exchange(): lax.ppermute(values, ROWS, [(i, i ^ mask) for i in range(size)])  14.7 us
    conv_general_dilated x3, matrix products, conv_rows(): lax.conv_general_dilated(haloed[tstep:tstep + 1], weight[tstep], window_s...  13.5 us
    dot_general x10, matrix products, body(): jnp.einsum('fqc,fkc->fqk', q_pair, piece, preferred_element_type=jnp.floa...  12 us
    dot_general x10, matrix products, body(): jnp.einsum('fqk,fkc->fqc', e.astype(jnp.bfloat16), p, preferred_element_t...  11.1 us
    ppermute x2, starting transfers between devices, padded_2(): lax.ppermute(jnp.where(even, first, last), axis, pairs + [(j, i) for i, j...  11.1 us
    conv_general_dilated x9, local copies, waits for them, and re-layouts, conv_rows(): lax.conv_general_dilated(haloed[tstep:tstep + 1], weight[tstep], window_s...  7.19 us
    unnamed x54, local copies, waits for them, and re-layouts  5.49 us
    ppermute x13, waiting for transfers between devices, exchange(): lax.ppermute(values, ROWS, [(i, i ^ mask) for i in range(size)])  3.58 us
  transfers between devices with their start and end apart: 17, of which 2 were waited for; matrix products, arithmetic and copies ran while one was open for 40% of the time, Pallas kernels for 0%

profile of v12, /device:TPU:5, one launch (start us, length us, event | category | flops | bytes accessed | tf_op | source)
XLA Modules:
  0.0 98.4 jit_solution(3792254275434694374)
XLA Ops:
  0.0 1.2 %multiply_reduce_fusion.1 = f32[2,128]{1,0:T(2,128)S(1)} fusion(bf16[1,2,128,384]{3,2,1,0:T(8,128)(2,1)} %param.10), kind=kLoop, calls=%fused_computation.122 | loop fusion | flops 294656 | bytes 197632 | tf_op jit(solution)/shard_map/reduce_sum | solution.py:32
  1.2 1.8 %constant_dynamic-update-slice_fusion.4 = (bf16[1,768,384]{2,1,0:T(8,128)(2,1)}, bf16[1,256,384]{2,1,0:T(8,128)(2,1)S(1)}) fusion(f32[384]{0:T(512)} %param.11, f32[256]{0:T(256)S(1)} %rsqrt_bitcast_fusion, bf16[1,2,128,384]{3,2,1,0:T(8,128)(2,1)} %param.10), kind=kLoop, calls=%fused_computation.271 | loop fusion | flops 393215 | bytes 592384
  3.0 1.4 %collective-permute-start.2 = (bf16[1,128,384]{2,1,0:T(8,128)(2,1)S(1)}, bf16[1,128,384]{2,1,0:T(8,128)(2,1)S(1)}, u32[]{:S(2)}, u32[]{:S(2)}) collective-permute-start(bf16[1,128,384]{2,1,0:T(8,128)(2,1)S(1)} %get-tuple-element.27), channel_id=1, source_target_pairs={{0,4},{1,5},{2,6},{3,7},{4,0},{5,1},{6,2},{7,3},{8,12},{9,13},{10,... | collective-permute-start | bytes 294920 | tf_op jit(solution)/shard_map/ppermute | solution.py:46
  4.4 2.3 %collective-permute-start.3 = (bf16[1,128,384]{2,1,0:T(8,128)(2,1)S(1)}, bf16[1,128,384]{2,1,0:T(8,128)(2,1)S(1)}, u32[]{:S(2)}, u32[]{:S(2)}) collective-permute-start(bf16[1,128,384]{2,1,0:T(8,128)(2,1)S(1)} %get-tuple-element.27), channel_id=1, source_target_pairs={{0,8},{1,9},{2,10},{3,11},{4,12},{5,13},{6,14},{7,15},{8,0},{9,1},... | collective-permute-start | bytes 294920 | tf_op jit(solution)/shard_map/ppermute | solution.py:46
  6.9 4.9 %collective-permute-start = (bf16[2,2,128,384]{3,2,1,0:T(8,128)(2,1)}, bf16[2,2,128,384]{3,2,1,0:T(8,128)(2,1)}, u32[]{:S(2)}, u32[]{:S(2)}) collective-permute-start(bf16[2,2,128,384]{3,2,1,0:T(8,128)(2,1)} %param.16), channel_id=1, source_target_pairs={{1,2},{3,4},{5,6},{7,8},{9,10},{11,12},{13,14},{2,1},{4,3},{6,5},{... | collective-permute-start | bytes 1179656 | tf_op jit(solution)/shard_map/ppermute | solution.py:22
  11.8 1.0 %fusion.97 = bf16[256,384]{1,0:T(8,128)(2,1)S(1)} fusion(bf16[1,2,128,384]{3,2,1,0:T(8,128)(2,1)} %param.10, f32[384]{0:T(512)} %param.11, f32[256]{0:T(256)S(1)} %rsqrt_bitcast_fusion), kind=kLoop, calls=%fused_computation.115 | loop fusion | flops 393216 | bytes 395776 | tf_op jit(solution)/shard_map/convert_element_type | solution.py:106
  13.5 1.4 %collective-permute-start.7 = (bf16[1,256,384]{2,1,0:T(8,128)(2,1)S(1)}, bf16[1,256,384]{2,1,0:T(8,128)(2,1)S(1)}, u32[]{:S(2)}, u32[]{:S(2)}) collective-permute-start(bf16[1,256,384]{2,1,0:T(8,128)(2,1)S(1)} %pad_maximum_fusion.3), channel_id=1, source_target_pairs={{0,4},{1,5},{2,6},{3,7},{4,0},{5,1},{6,2},{7,3},{8,12},{9,13},{10,... | collective-permute-start | bytes 589832 | tf_op jit(solution)/shard_map/ppermute | solution.py:46
  15.5 1.9 %collective-permute-start.8 = (bf16[1,256,384]{2,1,0:T(8,128)(2,1)S(1)}, bf16[1,256,384]{2,1,0:T(8,128)(2,1)}, u32[]{:S(2)}, u32[]{:S(2)}) collective-permute-start(bf16[1,256,384]{2,1,0:T(8,128)(2,1)S(1)} %pad_maximum_fusion.3), channel_id=1, source_target_pairs={{0,8},{1,9},{2,10},{3,11},{4,12},{5,13},{6,14},{7,15},{8,0},{9,1},... | collective-permute-start | bytes 589832 | tf_op jit(solution)/shard_map/ppermute | solution.py:46
  18.1 0.7 constant_dynamic-update-slice_fusion.1
  19.4 0.8 collective-permute-start.10
  20.3 1.7 %convolution_bitcast_fusion.2 = f32[1,512,768]{2,1,0:T(8,128)S(1)} fusion(bf16[1,768,384]{2,1,0:T(8,128)(2,1)} %constant_dynamic-update-slice_fusion, bf16[1,256,384]{2,1,0:T(8,128)(2,1)S(1)} %get-tuple-element.26, bf16[1,256,384]{2,1,0:T(8,128)(2,1)S(1)} %get-tuple-element.25), kind=kOutput, calls=%fused_computation.11 | convolution fusion | flops 302776320 | bytes 2555904 | tf_op jit(solution)/shard_map/fqc,fkc->fqk/dot_general | solution.py:125
  22.2 0.8 pad_maximum_fusion.2
  23.3 5.0 %collective-permute-start.9 = (bf16[1,256,384]{2,1,0:T(8,128)(2,1)S(1)}, bf16[1,256,384]{2,1,0:T(8,128)(2,1)}, u32[]{:S(2)}, u32[]{:S(2)}) collective-permute-start(bf16[1,256,384]{2,1,0:T(8,128)(2,1)S(1)} %pad_maximum_fusion.3), channel_id=1, source_target_pairs={{0,12},{1,13},{2,14},{3,15},{4,8},{5,9},{6,10},{7,11},{8,4},{9,5},... | collective-permute-start | bytes 589832 | tf_op jit(solution)/shard_map/ppermute | solution.py:46
  28.8 1.4 %convolution_bitcast_fusion.10 = f32[1,512,256]{1,2,0:T(8,128)S(1)} fusion(bf16[1,256,384]{2,1,0:T(8,128)(2,1)} %collective-permute-done.8, bf16[1,256,384]{2,1,0:T(8,128)(2,1)S(1)} %get-tuple-element.26, bf16[1,256,384]{2,1,0:T(8,128)(2,1)S(1)} %get-tuple-element.25), kind=kOutput, calls=%fused_computation.31 | convolution fusion | flops 101449728 | bytes 1114112 | tf_op jit(solution)/shard_map/fqc,fkc->fqk/dot_general | solution.py:125
  30.2 3.2 %collective-permute-done.9 = bf16[1,256,384]{2,1,0:T(8,128)(2,1)} collective-permute-done((bf16[1,256,384]{2,1,0:T(8,128)(2,1)S(1)}, bf16[1,256,384]{2,1,0:T(8,128)(2,1)}, u32[]{:S(2)}, u32[]{:S(2)}) %collective-permute-start.9) | collective-permute-done | bytes 196640 | tf_op jit(solution)/shard_map/ppermute | solution.py:46
  33.4 1.1 %collective-permute-start.12 = (bf16[1,256,384]{2,1,0:T(8,128)(2,1)S(1)}, bf16[1,256,384]{2,1,0:T(8,128)(2,1)}, u32[]{:S(2)}, u32[]{:S(2)}) collective-permute-start(bf16[1,256,384]{2,1,0:T(8,128)(2,1)S(1)} %collective-permute-done.7), channel_id=1, source_target_pairs={{0,1},{1,0},{2,3},{3,2},{4,5},{5,4},{6,7},{7,6},{8,9},{9,8},{10,11... | collective-permute-start | bytes 589832 | tf_op jit(solution)/shard_map/ppermute | solution.py:46
  34.5 1.2 %convolution_bitcast_fusion.9 = f32[1,512,256]{1,2,0:T(8,128)S(1)} fusion(bf16[1,256,384]{2,1,0:T(8,128)(2,1)} %collective-permute-done.9, bf16[1,256,384]{2,1,0:T(8,128)(2,1)S(1)} %get-tuple-element.26, bf16[1,256,384]{2,1,0:T(8,128)(2,1)S(1)} %get-tuple-element.25), kind=kOutput, calls=%fused_computation.30 | convolution fusion | flops 101449728 | bytes 1114112 | tf_op jit(solution)/shard_map/fqc,fkc->fqk/dot_general | solution.py:125
  35.9 0.7 copy-done.5
  37.1 1.1 %broadcast_select_fusion.1 = (bf16[2,2,128,384]{3,2,1,0:T(8,128)(2,1)S(1)}, bf16[2,2,128,384]{3,2,1,0:T(8,128)(2,1)S(1)}) fusion(bf16[2,2,128,384]{3,2,1,0:T(8,128)(2,1)} %collective-permute-done, bf16[2,2,128,384]{3,2,1,0:T(8,128)(2,1)S(1)} %collective-permute-done.1, pred[]{:T(512)S(6)} %eq.7), kind=kLoop, calls=%fused_computation.124 | loop fusion | flops 393216 | bytes 1572865 | tf_op jit(solution)/shard_map/jit(_where)/select_n | solution.py:25
  38.2 1.2 %pad_maximum_fusion = bf16[2,6,128,384]{3,2,1,0:T(8,128)(2,1)S(1)} fusion(bf16[2,2,128,384]{3,2,1,0:T(8,128)(2,1)S(1)} %get-tuple-element.20, bf16[2,2,128,384]{3,2,1,0:T(8,128)(2,1)} %param.16, bf16[2,2,128,384]{3,2,1,0:T(8,128)(2,1)S(1)} %get-tuple-element.19), kind=kLoop, calls=%fused_computation.43 | loop fusion | flops 1179648 | bytes 2359296 | tf_op jit(solution)/shard_map/concatenate | solution.py:27
  39.3 1.0 slice_bitcast_fusion
  40.3 1.0 %pad.5 = bf16[6,1,136,384]{3,2,0,1:T(8,128)(2,1)} pad(bf16[6,1,128,384]{3,2,0,1:T(8,128)(2,1)S(1)} %get-tuple-element.18, bf16[]{:T(256)} %constant.47.clone.1), padding=0_0x0_0x1_7x0_0 | pad | bytes 1216514 | tf_op jit(solution)/shard_map/slice | solution.py:60
  41.3 2.2 %reshape.975 = bf16[6,1,8,17,384]{4,3,2,0,1:T(8,128)(2,1)} reshape(bf16[6,1,136,384]{3,2,0,1:T(8,128)(2,1)} %pad.5) | data formatting | bytes 1253376 | tf_op jit(solution)/shard_map/conv_general_dilated | solution.py:59
  43.5 1.2 %copy.37 = bf16[6,1,8,17,384]{4,2,3,0,1:T(8,128)(2,1)S(1)} copy(bf16[6,1,8,17,384]{4,3,2,0,1:T(8,128)(2,1)} %reshape.975) | data formatting | bytes 1253376 | tf_op jit(solution)/shard_map/conv_general_dilated | solution.py:59
  44.8 4.8 %fusion.13 = f32[4,8,17,384]{3,1,2,0:T(8,128)} fusion(bf16[3,3,3,384,384]{4,3,2,1,0:T(8,128)(2,1)} %param.18, bf16[6,1,7,2,384]{4,2,3,0,1:T(8,128)(2,1)S(1)} %slice.236, bf16[6,1,8,17,384]{4,2,3,0,1:T(8,128)(2,1)S(1)} %copy.37, pred[8,17]{0,1:T(8,128)(4,1)S(1)} %copy-done.22), kind=kOutput, calls=%fused_computation.20 | convolution fusion | flops 1446199296 | bytes 4181128 | tf_op jit(solution)/shard_map/conv_general_dilated | solution.py:59
  49.6 1.0 %pad.7 = bf16[6,1,136,384]{3,2,0,1:T(8,128)(2,1)} pad(bf16[6,1,128,384]{3,2,0,1:T(8,128)(2,1)S(1)} %copy-done.7, bf16[]{:T(256)} %constant.47.clone.1), padding=0_0x0_0x1_7x0_0 | pad | bytes 1216514 | tf_op jit(solution)/shard_map/slice | solution.py:60
  50.6 2.2 %reshape.980 = bf16[6,1,8,17,384]{4,3,2,0,1:T(8,128)(2,1)} reshape(bf16[6,1,136,384]{3,2,0,1:T(8,128)(2,1)} %pad.7) | data formatting | bytes 1253376 | tf_op jit(solution)/shard_map/conv_general_dilated | solution.py:59
  52.8 1.2 %copy.39 = bf16[6,1,8,17,384]{4,2,3,0,1:T(8,128)(2,1)S(1)} copy(bf16[6,1,8,17,384]{4,3,2,0,1:T(8,128)(2,1)} %reshape.980) | data formatting | bytes 1253376 | tf_op jit(solution)/shard_map/conv_general_dilated | solution.py:59
  54.1 1.3 %convolution_bitcast_fusion.8 = f32[1,512,256]{1,2,0:T(8,128)S(1)} fusion(bf16[1,256,384]{2,1,0:T(8,128)(2,1)} %collective-permute-done.12, bf16[1,256,384]{2,1,0:T(8,128)(2,1)S(1)} %get-tuple-element.26, bf16[1,256,384]{2,1,0:T(8,128)(2,1)S(1)} %get-tuple-element.25), kind=kOutput, calls=%fused_computation.29 | convolution fusion | flops 101449728 | bytes 1114112 | tf_op jit(solution)/shard_map/fqc,fkc->fqk/dot_general | solution.py:125
  55.4 1.3 %convolution_bitcast_fusion.7 = f32[1,512,256]{1,2,0:T(8,128)S(1)} fusion(bf16[1,256,384]{2,1,0:T(8,128)(2,1)} %collective-permute-done.13, bf16[1,256,384]{2,1,0:T(8,128)(2,1)S(1)} %get-tuple-element.26, bf16[1,256,384]{2,1,0:T(8,128)(2,1)S(1)} %get-tuple-element.25), kind=kOutput, calls=%fused_computation.28 | convolution fusion | flops 101449728 | bytes 1114112 | tf_op jit(solution)/shard_map/fqc,fkc->fqk/dot_general | solution.py:125
  56.8 1.5 %convolution_bitcast_fusion.4 = f32[1,512,512]{1,2,0:T(8,128)S(1)} fusion(bf16[1,512,384]{2,1,0:T(8,128)(2,1)} %collective-permute-done.6, bf16[1,256,384]{2,1,0:T(8,128)(2,1)S(1)} %get-tuple-element.26, bf16[1,256,384]{2,1,0:T(8,128)(2,1)S(1)} %get-tuple-element.25), kind=kOutput, calls=%fused_computation.17 | convolution fusion | flops 202113024 | bytes 1835008 | tf_op jit(solution)/shard_map/fqc,fkc->fqk/dot_general | solution.py:125
  58.4 1.2 %convolution_bitcast_fusion.6 = f32[1,512,256]{1,2,0:T(8,128)S(1)} fusion(bf16[1,256,384]{2,1,0:T(8,128)(2,1)} %collective-permute-done.14, bf16[1,256,384]{2,1,0:T(8,128)(2,1)S(1)} %get-tuple-element.26, bf16[1,256,384]{2,1,0:T(8,128)(2,1)S(1)} %get-tuple-element.25), kind=kOutput, calls=%fused_computation.27 | convolution fusion | flops 101449728 | bytes 1114112 | tf_op jit(solution)/shard_map/fqc,fkc->fqk/dot_general | solution.py:125
  59.7 1.7 %convolution_bitcast_fusion.1 = f32[1,512,768]{2,1,0:T(8,128)S(1)} fusion(bf16[1,768,384]{2,1,0:T(8,128)(2,1)} %collective-permute-done.10, bf16[1,256,384]{2,1,0:T(8,128)(2,1)S(1)} %get-tuple-element.26, bf16[1,256,384]{2,1,0:T(8,128)(2,1)S(1)} %get-tuple-element.25), kind=kOutput, calls=%fused_computation.10 | convolution fusion | flops 302776320 | bytes 2555904 | tf_op jit(solution)/shard_map/fqc,fkc->fqk/dot_general | solution.py:125
  62.8 0.8 copy-done.2
  64.2 1.3 %fusion.91 = f32[256,384]{1,0:T(8,128)S(1)} fusion(bf16[1,512,384]{2,1,0:T(8,128)(2,1)} %collective-permute-done.6, f32[256]{0:T(256)S(1)} %maximum_maximum_fusion, f32[1,512,512]{1,2,0:T(8,128)S(1)} %convolution_bitcast_fusion.4), kind=kOutput, calls=%fused_computation.107 | convolution fusion | flops 101187584 | bytes 1836032 | tf_op jit(solution)/shard_map/fqk,fkc->fqc/dot_general | solution.py:131
  65.8 1.2 %fusion.178 = f32[256,384]{1,0:T(8,128)S(1)} fusion(bf16[1,256,384]{2,1,0:T(8,128)(2,1)} %collective-permute-done.8, f32[256]{0:T(256)S(1)} %maximum_maximum_fusion, f32[1,512,256]{1,2,0:T(8,128)S(1)} %copy-done.4), kind=kOutput, calls=%fused_computation.241 | convolution fusion | flops 50593792 | bytes 1115136 | tf_op jit(solution)/shard_map/fqk,fkc->fqc/dot_general | solution.py:131
  67.0 1.2 %fusion.175 = f32[256,384]{1,0:T(8,128)S(1)} fusion(bf16[1,256,384]{2,1,0:T(8,128)(2,1)} %collective-permute-done.9, f32[256]{0:T(256)S(1)} %maximum_maximum_fusion, f32[1,512,256]{1,2,0:T(8,128)S(1)} %copy-done.6), kind=kOutput, calls=%fused_computation.238 | convolution fusion | flops 50593792 | bytes 1115136 | tf_op jit(solution)/shard_map/fqk,fkc->fqc/dot_general | solution.py:131
  68.2 1.5 %fusion.68 = f32[256,384]{1,0:T(8,128)S(1)} fusion(bf16[1,768,384]{2,1,0:T(8,128)(2,1)} %collective-permute-done.10, f32[256]{0:T(256)S(1)} %maximum_maximum_fusion, f32[1,512,768]{2,1,0:T(8,128)S(1)} %convolution_bitcast_fusion.1), kind=kOutput, calls=%fused_computation.76 | convolution fusion | flops 151781376 | bytes 2556928 | tf_op jit(solution)/shard_map/fqk,fkc->fqc/dot_general | solution.py:131
  69.8 1.6 %fusion.40 = f32[256,384]{1,0:T(8,128)S(1)} fusion(f32[256,384]{1,0:T(8,128)S(1)} %fusion.68, f32[256,384]{1,0:T(8,128)S(1)} %fusion.175, f32[256,384]{1,0:T(8,128)S(1)} %fusion.178, f32[256,384]{1,0:T(8,128)S(1)} %fusion.181, f32[256,384]{1,0:T(8,128)S(1)} %fusion.91, bf16[1,768,384]{2,1,0:T(8,128)(2,1)} %constant_dynamic-update-slice_fusion, ...), kind=kOutput, calls=%fused_computation.42 | convolution fusion | flops 152272896 | bytes 4523008 | tf_op jit(solution)/shard_map/fqk,fkc->fqc/dot_general | solution.py:131
  71.4 1.2 %fusion.172 = f32[256,384]{1,0:T(8,128)S(1)} fusion(bf16[1,256,384]{2,1,0:T(8,128)(2,1)} %collective-permute-done.12, f32[256]{0:T(256)S(1)} %maximum_maximum_fusion, f32[1,512,256]{1,2,0:T(8,128)S(1)} %convolution_bitcast_fusion.8), kind=kOutput, calls=%fused_computation.235 | convolution fusion | flops 50593792 | bytes 1115136 | tf_op jit(solution)/shard_map/fqk,fkc->fqc/dot_general | solution.py:131
  72.6 1.2 %fusion.169 = f32[256,384]{1,0:T(8,128)S(1)} fusion(bf16[1,256,384]{2,1,0:T(8,128)(2,1)} %collective-permute-done.13, f32[256]{0:T(256)S(1)} %maximum_maximum_fusion, f32[1,512,256]{1,2,0:T(8,128)S(1)} %convolution_bitcast_fusion.7), kind=kOutput, calls=%fused_computation.232 | convolution fusion | flops 50593792 | bytes 1115136 | tf_op jit(solution)/shard_map/fqk,fkc->fqc/dot_general | solution.py:131
  73.8 1.2 %fusion.166 = f32[256,384]{1,0:T(8,128)S(1)} fusion(bf16[1,256,384]{2,1,0:T(8,128)(2,1)} %collective-permute-done.14, f32[256]{0:T(256)S(1)} %maximum_maximum_fusion, f32[1,512,256]{1,2,0:T(8,128)S(1)} %convolution_bitcast_fusion.6), kind=kOutput, calls=%fused_computation.229 | convolution fusion | flops 50593792 | bytes 1115136 | tf_op jit(solution)/shard_map/fqk,fkc->fqc/dot_general | solution.py:131
  77.1 6.2 %collective-permute-start.15 = (bf16[1,2,128,384]{3,2,1,0:T(8,128)(2,1)S(1)}, bf16[1,2,128,384]{3,2,1,0:T(8,128)(2,1)S(1)}, u32[]{:S(2)}, u32[]{:S(2)}) collective-permute-start(bf16[1,2,128,384]{3,2,1,0:T(8,128)(2,1)S(1)} %bitcast.494), channel_id=1, source_target_pairs={{1,2},{3,4},{5,6},{7,8},{9,10},{11,12},{13,14},{2,1},{4,3},{6,5},{... | collective-permute-start | bytes 589832 | tf_op jit(solution)/shard_map/ppermute | solution.py:22
  83.4 4.8 %fusion.28 = f32[4,8,17,384]{3,1,2,0:T(8,128)} fusion(f32[4,8,17,384]{3,1,2,0:T(8,128)S(1)} %copy-done.23, bf16[3,3,3,384,384]{4,3,2,1,0:T(8,128)(2,1)} %param.18, bf16[6,1,7,2,384]{4,2,3,0,1:T(8,128)(2,1)S(1)} %slice.238, bf16[6,1,8,17,384]{4,2,3,0,1:T(8,128)(2,1)S(1)} %copy.39, pred[8,17]{0,1:T(8,128)(4,1)S(1)} %copy-done.22), kind=kOutput, calls=%fused_computation.25 | convolution fusion | flops 1446408192 | bytes 5016712 | tf_op jit(solution)/shard_map/conv_general_dilated | solution.py:59
  88.8 1.0 %copy-done.24 = f32[4,8,17,384]{3,1,2,0:T(8,128)S(1)} copy-done((f32[4,8,17,384]{3,1,2,0:T(8,128)S(1)}, f32[4,8,17,384]{3,1,2,0:T(8,128)}, u32[]{:S(2)}) %copy-start.24) | copy-done | bytes 835608
  89.8 3.9 %fusion.31 = bf16[4,8,17,384]{3,1,2,0:T(8,128)(2,1)S(1)} fusion(f32[4,8,17,384]{3,1,2,0:T(8,128)S(1)} %copy-done.24, bf16[3,3,3,384,384]{4,3,2,1,0:T(8,128)(2,1)} %param.18, bf16[6,1,7,2,384]{4,2,3,0,1:T(8,128)(2,1)S(1)} %slice.263, bf16[6,1,8,17,384]{4,2,3,0,1:T(8,128)(2,1)S(1)} %copy.41, pred[4]{0:T(512)(128)(4,1)S(1)} %or_and_fusion, ...), kind=kOutput, calls=%fused_computation.26 | convolution fusion | flops 1446825984 | bytes 4598924 | tf_op jit(solution)/shard_map/conv_general_dilated | solution.py:59
  94.1 1.5 %convolution_bitcast_fusion = f32[1,4,130,3,3,192]{5,2,4,3,1,0:T(8,128)S(1)} fusion(bf16[3,3,384,192]{2,3,1,0:T(8,128)(2,1)S(1)} %copy-done, bf16[1,4,128,384]{3,2,1,0:T(8,128)(2,1)S(1)} %bitcast.493), kind=kOutput, calls=%fused_computation.9 | convolution fusion | flops 690094080 | bytes 5314560 | tf_op jit(solution)/shard_map/frwc,ijco->frwijo/dot_general | solution.py:76
  97.1 1.3 %convert_element_type.171 = bf16[1,4,49152]{2,1,0:T(4,128)(2,1)} reshape(bf16[1,2,2,128,2,192]{5,4,3,2,1,0:T(2,128)(2,1)S(1)} %copy.69) | data formatting | bytes 786432 | tf_op jit(solution)/shard_map/convert_element_type | solution.py:93
  (119 shorter events, 11.8 us)
Async XLA Ops:
  0.0 94.1 %copy-start = (bf16[3,3,384,192]{2,3,1,0:T(8,128)(2,1)S(1)}, bf16[3,3,384,192]{2,3,1,0:T(8,128)(2,1)}, u32[]{:S(2)}) copy-start(bf16[3,3,384,192]{2,3,1,0:T(8,128)(2,1)} %param.19) | copy-start | bytes 3981316
  0.0 12.8 %copy-start.18 = (bf16[384,384]{1,0:T(8,128)(2,1)S(1)}, bf16[384,384]{1,0:T(8,128)(2,1)}, u32[]{:S(2)}) copy-start(bf16[384,384]{1,0:T(8,128)(2,1)} %param.12) | copy-start | bytes 884740
  0.0 12.8 %copy-start.17 = (bf16[384,384]{1,0:T(8,128)(2,1)S(1)}, bf16[384,384]{1,0:T(8,128)(2,1)}, u32[]{:S(2)}) copy-start(bf16[384,384]{1,0:T(8,128)(2,1)} %param.13) | copy-start | bytes 884740
  3.0 17.2 %copy-start.9 = (bf16[1,128,384]{2,1,0:T(8,128)(2,1)}, bf16[1,128,384]{2,1,0:T(8,128)(2,1)S(1)}, u32[]{:S(2)}) copy-start(bf16[1,128,384]{2,1,0:T(8,128)(2,1)S(1)} %get-tuple-element.27) | copy-start | bytes 294916
  3.0 10.5 %collective-permute-start.2 = (bf16[1,128,384]{2,1,0:T(8,128)(2,1)S(1)}, bf16[1,128,384]{2,1,0:T(8,128)(2,1)S(1)}, u32[]{:S(2)}, u32[]{:S(2)}) collective-permute-start(bf16[1,128,384]{2,1,0:T(8,128)(2,1)S(1)} %get-tuple-element.27), channel_id=1, source_target_pairs={{0,4},{1,5},{2,6},{3,7},{4,0},{5,1},{6,2},{7,3},{8,12},{9,13},{10,... | collective-permute-start | bytes 294920 | tf_op jit(solution)/shard_map/ppermute | solution.py:46
  4.4 11.2 %collective-permute-start.3 = (bf16[1,128,384]{2,1,0:T(8,128)(2,1)S(1)}, bf16[1,128,384]{2,1,0:T(8,128)(2,1)S(1)}, u32[]{:S(2)}, u32[]{:S(2)}) collective-permute-start(bf16[1,128,384]{2,1,0:T(8,128)(2,1)S(1)} %get-tuple-element.27), channel_id=1, source_target_pairs={{0,8},{1,9},{2,10},{3,11},{4,12},{5,13},{6,14},{7,15},{8,0},{9,1},... | collective-permute-start | bytes 294920 | tf_op jit(solution)/shard_map/ppermute | solution.py:46
  6.7 11.4 %collective-permute-start.4 = (bf16[1,128,384]{2,1,0:T(8,128)(2,1)S(1)}, bf16[1,128,384]{2,1,0:T(8,128)(2,1)S(1)}, u32[]{:S(2)}, u32[]{:S(2)}) collective-permute-start(bf16[1,128,384]{2,1,0:T(8,128)(2,1)S(1)} %get-tuple-element.27), channel_id=1, source_target_pairs={{0,12},{1,13},{2,14},{3,15},{4,8},{5,9},{6,10},{7,11},{8,4},{9,5},... | collective-permute-start | bytes 294920 | tf_op jit(solution)/shard_map/ppermute | solution.py:46
  6.7 6.7 %collective-permute-start.5 = (bf16[1,128,384]{2,1,0:T(8,128)(2,1)S(1)}, bf16[1,128,384]{2,1,0:T(8,128)(2,1)S(1)}, u32[]{:S(2)}, u32[]{:S(2)}) collective-permute-start(bf16[1,128,384]{2,1,0:T(8,128)(2,1)S(1)} %get-tuple-element.28), channel_id=1, source_target_pairs={{0,2},{1,3},{2,0},{3,1},{4,6},{5,7},{6,4},{7,5},{8,10},{9,11},{10,... | collective-permute-start | bytes 294920 | tf_op jit(solution)/shard_map/ppermute | solution.py:46
  6.9 29.0 %collective-permute-start = (bf16[2,2,128,384]{3,2,1,0:T(8,128)(2,1)}, bf16[2,2,128,384]{3,2,1,0:T(8,128)(2,1)}, u32[]{:S(2)}, u32[]{:S(2)}) collective-permute-start(bf16[2,2,128,384]{3,2,1,0:T(8,128)(2,1)} %param.16), channel_id=1, source_target_pairs={{1,2},{3,4},{5,6},{7,8},{9,10},{11,12},{13,14},{2,1},{4,3},{6,5},{... | collective-permute-start | bytes 1179656 | tf_op jit(solution)/shard_map/ppermute | solution.py:22
  13.4 23.2 %collective-permute-start.1 = (bf16[2,2,128,384]{3,2,1,0:T(8,128)(2,1)}, bf16[2,2,128,384]{3,2,1,0:T(8,128)(2,1)S(1)}, u32[]{:S(2)}, u32[]{:S(2)}) collective-permute-start(bf16[2,2,128,384]{3,2,1,0:T(8,128)(2,1)} %param.16), channel_id=1, source_target_pairs={{0,1},{1,0},{2,3},{3,2},{4,5},{5,4},{6,7},{7,6},{8,9},{9,8},{10,11... | collective-permute-start | bytes 1179656 | tf_op jit(solution)/shard_map/ppermute | solution.py:18
  13.5 6.7 %copy-start.11 = (bf16[1,128,384]{2,1,0:T(8,128)(2,1)}, bf16[1,128,384]{2,1,0:T(8,128)(2,1)S(1)}, u32[]{:S(2)}) copy-start(bf16[1,128,384]{2,1,0:T(8,128)(2,1)S(1)} %collective-permute-done.2) | copy-start | bytes 294916
  13.5 9.8 %collective-permute-start.7 = (bf16[1,256,384]{2,1,0:T(8,128)(2,1)S(1)}, bf16[1,256,384]{2,1,0:T(8,128)(2,1)S(1)}, u32[]{:S(2)}, u32[]{:S(2)}) collective-permute-start(bf16[1,256,384]{2,1,0:T(8,128)(2,1)S(1)} %pad_maximum_fusion.3), channel_id=1, source_target_pairs={{0,4},{1,5},{2,6},{3,7},{4,0},{5,1},{6,2},{7,3},{8,12},{9,13},{10,... | collective-permute-start | bytes 589832 | tf_op jit(solution)/shard_map/ppermute | solution.py:46
  15.5 4.7 %copy-start.13 = (bf16[1,128,384]{2,1,0:T(8,128)(2,1)}, bf16[1,128,384]{2,1,0:T(8,128)(2,1)S(1)}, u32[]{:S(2)}) copy-start(bf16[1,128,384]{2,1,0:T(8,128)(2,1)S(1)} %collective-permute-done.3) | copy-start | bytes 294916
  15.5 13.1 %collective-permute-start.8 = (bf16[1,256,384]{2,1,0:T(8,128)(2,1)S(1)}, bf16[1,256,384]{2,1,0:T(8,128)(2,1)}, u32[]{:S(2)}, u32[]{:S(2)}) collective-permute-start(bf16[1,256,384]{2,1,0:T(8,128)(2,1)S(1)} %pad_maximum_fusion.3), channel_id=1, source_target_pairs={{0,8},{1,9},{2,10},{3,11},{4,12},{5,13},{6,14},{7,15},{8,0},{9,1},... | collective-permute-start | bytes 589832 | tf_op jit(solution)/shard_map/ppermute | solution.py:46
  18.1 2.1 %copy-start.15 = (bf16[1,128,384]{2,1,0:T(8,128)(2,1)}, bf16[1,128,384]{2,1,0:T(8,128)(2,1)S(1)}, u32[]{:S(2)}) copy-start(bf16[1,128,384]{2,1,0:T(8,128)(2,1)S(1)} %collective-permute-done.4) | copy-start | bytes 294916
  19.4 40.2 %collective-permute-start.10 = (bf16[1,768,384]{2,1,0:T(8,128)(2,1)}, bf16[1,768,384]{2,1,0:T(8,128)(2,1)}, u32[]{:S(2)}, u32[]{:S(2)}) collective-permute-start(bf16[1,768,384]{2,1,0:T(8,128)(2,1)} %constant_dynamic-update-slice_fusion), channel_id=1, source_target_pairs={{0,1},{1,0},{2,3},{3,2},{4,5},{5,4},{6,7},{7,6},{8,9},{9,8},{10,11... | collective-permute-start | bytes 1769480 | tf_op jit(solution)/shard_map/ppermute | solution.py:46
  20.2 1.9 %copy-start.10 = (bf16[1,128,384]{2,1,0:T(8,128)(2,1)S(1)}, bf16[1,128,384]{2,1,0:T(8,128)(2,1)}, u32[]{:S(2)}) copy-start(bf16[1,128,384]{2,1,0:T(8,128)(2,1)} %copy-done.9) | copy-start | bytes 294916
  20.2 1.9 %copy-start.12 = (bf16[1,128,384]{2,1,0:T(8,128)(2,1)S(1)}, bf16[1,128,384]{2,1,0:T(8,128)(2,1)}, u32[]{:S(2)}) copy-start(bf16[1,128,384]{2,1,0:T(8,128)(2,1)} %copy-done.11) | copy-start | bytes 294916
  20.2 1.9 %copy-start.14 = (bf16[1,128,384]{2,1,0:T(8,128)(2,1)S(1)}, bf16[1,128,384]{2,1,0:T(8,128)(2,1)}, u32[]{:S(2)}) copy-start(bf16[1,128,384]{2,1,0:T(8,128)(2,1)} %copy-done.13) | copy-start | bytes 294916
  20.2 1.9 %copy-start.16 = (bf16[1,128,384]{2,1,0:T(8,128)(2,1)S(1)}, bf16[1,128,384]{2,1,0:T(8,128)(2,1)}, u32[]{:S(2)}) copy-start(bf16[1,128,384]{2,1,0:T(8,128)(2,1)} %copy-done.15) | copy-start | bytes 294916
  23.3 10.1 %collective-permute-start.9 = (bf16[1,256,384]{2,1,0:T(8,128)(2,1)S(1)}, bf16[1,256,384]{2,1,0:T(8,128)(2,1)}, u32[]{:S(2)}, u32[]{:S(2)}) collective-permute-start(bf16[1,256,384]{2,1,0:T(8,128)(2,1)S(1)} %pad_maximum_fusion.3), channel_id=1, source_target_pairs={{0,12},{1,13},{2,14},{3,15},{4,8},{5,9},{6,10},{7,11},{8,4},{9,5},... | collective-permute-start | bytes 589832 | tf_op jit(solution)/shard_map/ppermute | solution.py:46
  28.7 7.1 %copy-start.1 = (f32[1,512,256]{1,2,0:T(8,128)}, f32[1,512,256]{1,2,0:T(8,128)S(1)}, u32[]{:S(2)}) copy-start(f32[1,512,256]{1,2,0:T(8,128)S(1)} %convolution_bitcast_fusion.11) | copy-start | bytes 1572868
  28.7 28.0 %collective-permute-start.6 = (bf16[1,512,384]{2,1,0:T(8,128)(2,1)}, bf16[1,512,384]{2,1,0:T(8,128)(2,1)}, u32[]{:S(2)}, u32[]{:S(2)}) collective-permute-start(bf16[1,512,384]{2,1,0:T(8,128)(2,1)} %pad_maximum_fusion.2), channel_id=1, source_target_pairs={{0,2},{1,3},{2,0},{3,1},{4,6},{5,7},{6,4},{7,5},{8,10},{9,11},{10,... | collective-permute-start | bytes 1179656 | tf_op jit(solution)/shard_map/ppermute | solution.py:46
  30.1 5.7 %copy-start.3 = (f32[1,512,256]{1,2,0:T(8,128)}, f32[1,512,256]{1,2,0:T(8,128)S(1)}, u32[]{:S(2)}) copy-start(f32[1,512,256]{1,2,0:T(8,128)S(1)} %convolution_bitcast_fusion.10) | copy-start | bytes 1572868
  33.4 20.6 %collective-permute-start.12 = (bf16[1,256,384]{2,1,0:T(8,128)(2,1)S(1)}, bf16[1,256,384]{2,1,0:T(8,128)(2,1)}, u32[]{:S(2)}, u32[]{:S(2)}) collective-permute-start(bf16[1,256,384]{2,1,0:T(8,128)(2,1)S(1)} %collective-permute-done.7), channel_id=1, source_target_pairs={{0,1},{1,0},{2,3},{3,2},{4,5},{5,4},{6,7},{7,6},{8,9},{9,8},{10,11... | collective-permute-start | bytes 589832 | tf_op jit(solution)/shard_map/ppermute | solution.py:46
  35.8 0.8 copy-start.5
  36.6 18.8 %collective-permute-start.13 = (bf16[1,256,384]{2,1,0:T(8,128)(2,1)}, bf16[1,256,384]{2,1,0:T(8,128)(2,1)}, u32[]{:S(2)}, u32[]{:S(2)}) collective-permute-start(bf16[1,256,384]{2,1,0:T(8,128)(2,1)} %collective-permute-done.8), channel_id=1, source_target_pairs={{0,1},{1,0},{2,3},{3,2},{4,5},{5,4},{6,7},{7,6},{8,9},{9,8},{10,11... | collective-permute-start | bytes 589832 | tf_op jit(solution)/shard_map/ppermute | solution.py:46
  36.6 21.7 %collective-permute-start.14 = (bf16[1,256,384]{2,1,0:T(8,128)(2,1)}, bf16[1,256,384]{2,1,0:T(8,128)(2,1)}, u32[]{:S(2)}, u32[]{:S(2)}) collective-permute-start(bf16[1,256,384]{2,1,0:T(8,128)(2,1)} %collective-permute-done.9), channel_id=1, source_target_pairs={{0,1},{1,0},{2,3},{3,2},{4,5},{5,4},{6,7},{7,6},{8,9},{9,8},{10,11... | collective-permute-start | bytes 589832 | tf_op jit(solution)/shard_map/ppermute | solution.py:46
  41.3 3.5 %copy-start.22 = (pred[8,17]{0,1:T(8,128)(4,1)S(1)}, pred[8,17]{0,1:T(8,128)(4,1)}, u32[]{:S(2)}) copy-start(pred[8,17]{0,1:T(8,128)(4,1)} %constant.64) | copy-start | bytes 412
  44.8 4.9 %copy-start.7 = (bf16[6,1,128,384]{3,2,0,1:T(8,128)(2,1)S(1)}, bf16[6,1,128,384]{3,2,0,1:T(8,128)(2,1)}, u32[]{:S(2)}) copy-start(bf16[6,1,128,384]{3,2,0,1:T(8,128)(2,1)} %get-tuple-element.17) | copy-start | bytes 1769476
  56.7 4.8 %collective-permute-start.11 = (bf16[1,512,384]{2,1,0:T(8,128)(2,1)}, bf16[1,512,384]{2,1,0:T(8,128)(2,1)S(1)}, u32[]{:S(2)}, u32[]{:S(2)}) collective-permute-start(bf16[1,512,384]{2,1,0:T(8,128)(2,1)} %collective-permute-done.6), channel_id=1, source_target_pairs={{0,1},{1,0},{2,3},{3,2},{4,5},{5,4},{6,7},{7,6},{8,9},{9,8},{10,11... | collective-permute-start | bytes 1179656 | tf_op jit(solution)/shard_map/ppermute | solution.py:46
  62.5 1.0 %copy-start.2 = (f32[1,512,256]{1,2,0:T(8,128)S(1)}, f32[1,512,256]{1,2,0:T(8,128)}, u32[]{:S(2)}) copy-start(f32[1,512,256]{1,2,0:T(8,128)} %copy-done.1) | copy-start | bytes 1572868
  62.5 1.2 %copy-start.4 = (f32[1,512,256]{1,2,0:T(8,128)S(1)}, f32[1,512,256]{1,2,0:T(8,128)}, u32[]{:S(2)}) copy-start(f32[1,512,256]{1,2,0:T(8,128)} %copy-done.3) | copy-start | bytes 1572868
  62.5 1.3 %copy-start.6 = (f32[1,512,256]{1,2,0:T(8,128)S(1)}, f32[1,512,256]{1,2,0:T(8,128)}, u32[]{:S(2)}) copy-start(f32[1,512,256]{1,2,0:T(8,128)} %copy-done.5) | copy-start | bytes 1572868
  75.0 1.0 copy-start.19
  75.0 1.4 %copy-start.8 = (bf16[1,2,128,384]{3,2,1,0:T(8,128)(2,1)S(1)}, bf16[1,2,128,384]{3,2,1,0:T(8,128)(2,1)}, u32[]{:S(2)}) copy-start(bf16[1,2,128,384]{3,2,1,0:T(8,128)(2,1)} %param.10) | copy-start | bytes 589828
  75.0 1.4 %copy-start.21 = (bf16[384,384]{1,0:T(8,128)(2,1)S(1)}, bf16[384,384]{1,0:T(8,128)(2,1)}, u32[]{:S(2)}) copy-start(bf16[384,384]{1,0:T(8,128)(2,1)} %param.15) | copy-start | bytes 884740
  76.0 0.9 copy-start.20
  76.4 7.0 %copy-start.23 = (f32[4,8,17,384]{3,1,2,0:T(8,128)S(1)}, f32[4,8,17,384]{3,1,2,0:T(8,128)}, u32[]{:S(2)}) copy-start(f32[4,8,17,384]{3,1,2,0:T(8,128)} %fusion.13) | copy-start | bytes 2506756
  77.1 11.1 %collective-permute-start.15 = (bf16[1,2,128,384]{3,2,1,0:T(8,128)(2,1)S(1)}, bf16[1,2,128,384]{3,2,1,0:T(8,128)(2,1)S(1)}, u32[]{:S(2)}, u32[]{:S(2)}) collective-permute-start(bf16[1,2,128,384]{3,2,1,0:T(8,128)(2,1)S(1)} %bitcast.494), channel_id=1, source_target_pairs={{1,2},{3,4},{5,6},{7,8},{9,10},{11,12},{13,14},{2,1},{4,3},{6,5},{... | collective-permute-start | bytes 589832 | tf_op jit(solution)/shard_map/ppermute | solution.py:22
  83.3 4.9 %collective-permute-start.16 = (bf16[1,2,128,384]{3,2,1,0:T(8,128)(2,1)S(1)}, bf16[1,2,128,384]{3,2,1,0:T(8,128)(2,1)S(1)}, u32[]{:S(2)}, u32[]{:S(2)}) collective-permute-start(bf16[1,2,128,384]{3,2,1,0:T(8,128)(2,1)S(1)} %bitcast.495), channel_id=1, source_target_pairs={{0,1},{1,0},{2,3},{3,2},{4,5},{5,4},{6,7},{7,6},{8,9},{9,8},{10,11... | collective-permute-start | bytes 589832 | tf_op jit(solution)/shard_map/ppermute | solution.py:18
  88.7 1.2 %copy-start.24 = (f32[4,8,17,384]{3,1,2,0:T(8,128)S(1)}, f32[4,8,17,384]{3,1,2,0:T(8,128)}, u32[]{:S(2)}) copy-start(f32[4,8,17,384]{3,1,2,0:T(8,128)} %fusion.28) | copy-start | bytes 2506756

commit v13 on v10

--- a/solution.py
+++ b/solution.py
@@ -120,17 +120,30 @@
     q_keyed = jnp.einsum("fqc,dc->fqd", queries, w_key, preferred_element_type=jnp.float32)
     q_pair = split_pair(q_keyed, axis=1)
     count = queries.shape[1]
-    scores = []
-    for piece in pieces:
-        both = jnp.einsum("fqc,fkc->fqk", q_pair, piece, preferred_element_type=jnp.float32)
-        scores.append((both[:, :count] + both[:, count:]) * scale)
-    top = jnp.max(jnp.stack([jnp.max(s, axis=-1) for s in scores], axis=-1), axis=-1)[..., None]
-    expos = [jnp.exp(s - top) for s in scores]
-    denom = sum(jnp.sum(e, axis=-1, keepdims=True) for e in expos)
-    mixed_in = sum(
-        jnp.einsum("fqk,fkc->fqc", e.astype(jnp.bfloat16), p, preferred_element_type=jnp.float32)
-        for e, p in zip(expos, pieces)
-    )
+    groups = [[mine[0], pieces[len(mine)]], mine[1:], pieces[len(mine) + 1 :]]
+    top = denom = mixed_in = None
+    for group in groups:
+        scores = []
+        for piece in group:
+            both = jnp.einsum("fqc,fkc->fqk", q_pair, piece, preferred_element_type=jnp.float32)
+            scores.append((both[:, :count] + both[:, count:]) * scale)
+        peak = jnp.max(jnp.stack([jnp.max(s, axis=-1) for s in scores], axis=-1), axis=-1)
+        new_top = peak[..., None] if top is None else jnp.maximum(top, peak[..., None])
+        expos = [jnp.exp(s - new_top) for s in scores]
+        part_denom = sum(jnp.sum(e, axis=-1, keepdims=True) for e in expos)
+        part_mixed = sum(
+            jnp.einsum(
+                "fqk,fkc->fqc", e.astype(jnp.bfloat16), p, preferred_element_type=jnp.float32
+            )
+            for e, p in zip(expos, group)
+        )
+        if top is None:
+            denom, mixed_in = part_denom, part_mixed
+        else:
+            shrink = jnp.exp(top - new_top)
+            denom = denom * shrink + part_denom
+            mixed_in = mixed_in * shrink + part_mixed
+        top = new_top
     both = jnp.einsum(
         "fqc,cd->fqd", split_pair(mixed_in, axis=1), w_value, preferred_element_type=jnp.float32
     )

time: 69 us -> 68.9 us (level)
  no operation moved by 1% of the time
where the time goes in v13:
time: 68.9 us; the launch traced here: 68.7 us
  starting transfers between devices  22.9 us (33%)
  waiting for transfers between devices  17.7 us (26%)
  matrix products  14.8 us (21%)
  other arithmetic  8.44 us (12%)
  local copies, waits for them, and re-layouts  4.15 us (6%)
  between operations  0.77 us (1%)
    ppermute x13, starting transfers between devices, exchange(): lax.ppermute(values, ROWS, [(i, i ^ mask) for i in range(size)])  13.3 us
    ppermute x13, waiting for transfers between devices, exchange(): lax.ppermute(values, ROWS, [(i, i ^ mask) for i in range(size)])  10.4 us
    ppermute x3, starting transfers between devices, padded_2(): lax.ppermute(jnp.where(even, first, last), axis, pairs + [(j, i) for i, j...  9.38 us
    ppermute x3, waiting for transfers between devices, padded_2(): lax.ppermute(jnp.where(even, first, last), axis, pairs + [(j, i) for i, j...  7.23 us
    dot_general x10, matrix products, body(): jnp.einsum('fqc,fkc->fqk', q_pair, piece, preferred_element_type=jnp.floa...  4.07 us
    conv_general_dilated x3, matrix products, conv_rows(): lax.conv_general_dilated(haloed[tstep:tstep + 1], weight[tstep], window_s...  3.58 us
    dot_general x10, matrix products, body(): jnp.einsum('fqk,fkc->fqc', e.astype(jnp.bfloat16), p, preferred_element_t...  3.31 us
    select_n x3, other arithmetic, padded_2(): jnp.where(even, first, last)  1.79 us
  transfers between devices with their start and end apart: 19, of which 4 were waited for; matrix products, arithmetic and copies ran while one was open for 17% of the time, Pallas kernels for 0%

profile of v13, /device:TPU:5, one launch (start us, length us, event | category | flops | bytes accessed | tf_op | source)
XLA Modules:
  0.0 68.7 jit_solution(7712130734854603942)
XLA Ops:
  0.0 1.1 %multiply_reduce_fusion.1 = f32[2,128]{1,0:T(2,128)S(1)} fusion(bf16[1,2,128,384]{3,2,1,0:T(8,128)(2,1)} %param.10), kind=kLoop, calls=%fused_computation.133 | loop fusion | flops 294656 | bytes 197632 | tf_op jit(solution)/shard_map/reduce_sum | solution.py:32
  1.2 1.1 %constant_dynamic-update-slice_fusion.4 = (bf16[1,768,384]{2,1,0:T(8,128)(2,1)S(1)}, bf16[1,256,384]{2,1,0:T(8,128)(2,1)S(1)}) fusion(f32[384]{0:T(512)} %param.11, f32[256]{0:T(256)S(1)} %rsqrt_bitcast_fusion, bf16[1,2,128,384]{3,2,1,0:T(8,128)(2,1)} %param.10), kind=kLoop, calls=%fused_computation.292 | loop fusion | flops 393215 | bytes 592384
  2.3 3.4 %collective-permute-start.4 = (bf16[1,128,384]{2,1,0:T(8,128)(2,1)S(1)}, bf16[1,128,384]{2,1,0:T(8,128)(2,1)S(1)}, u32[]{:S(2)}, u32[]{:S(2)}) collective-permute-start(bf16[1,128,384]{2,1,0:T(8,128)(2,1)S(1)} %get-tuple-element.39), channel_id=1, source_target_pairs={{0,12},{1,13},{2,14},{3,15},{4,8},{5,9},{6,10},{7,11},{8,4},{9,5},... | collective-permute-start | bytes 294920 | tf_op jit(solution)/shard_map/ppermute | solution.py:46
  5.7 0.4 collective-permute-start.2
  6.2 1.7 %broadcast_select_fusion.3 = (bf16[2,1,128,384]{3,2,1,0:T(8,128)(2,1)}, bf16[2,1,128,384]{3,2,1,0:T(8,128)(2,1)S(1)}) fusion(pred[]{:T(512)S(6)} %eq.9, bf16[2,2,128,384]{3,2,1,0:T(8,128)(2,1)} %param.16), kind=kLoop, calls=%fused_computation.261 | loop fusion | flops 196608 | bytes 786433 | tf_op jit(solution)/shard_map/jit(_where)/select_n | solution.py:23
  8.0 5.4 %collective-permute-start = (bf16[2,1,128,384]{3,2,1,0:T(8,128)(2,1)}, bf16[2,1,128,384]{3,2,1,0:T(8,128)(2,1)S(1)}, u32[]{:S(2)}, u32[]{:S(2)}) collective-permute-start(bf16[2,1,128,384]{3,2,1,0:T(8,128)(2,1)} %get-tuple-element.25), channel_id=1, source_target_pairs={{1,2},{3,4},{5,6},{7,8},{9,10},{11,12},{13,14},{2,1},{4,3},{6,5},{... | collective-permute-start | bytes 589832 | tf_op jit(solution)/shard_map/ppermute | solution.py:22
  13.3 1.0 %fusion.107 = bf16[256,384]{1,0:T(8,128)(2,1)S(1)} fusion(bf16[1,2,128,384]{3,2,1,0:T(8,128)(2,1)} %param.10, f32[384]{0:T(512)} %param.11, f32[256]{0:T(256)S(1)} %rsqrt_bitcast_fusion), kind=kLoop, calls=%fused_computation.126 | loop fusion | flops 393216 | bytes 395776 | tf_op jit(solution)/shard_map/convert_element_type | solution.py:106
  14.4 1.6 %convert_bitcast_fusion.1 = (bf16[1,256,384]{2,1,0:T(8,128)(2,1)S(1)}, bf16[1,256,384]{2,1,0:T(8,128)(2,1)S(1)}) fusion(bf16[384,384]{1,0:T(8,128)(2,1)} %param.13, bf16[256,384]{1,0:T(8,128)(2,1)S(1)} %fusion.107, bf16[384,384]{1,0:T(8,128)(2,1)} %param.12), kind=kOutput, calls=%fused_computation.281 | convolution fusion | flops 151486464 | bytes 1179648 | tf_op jit(solution)/shard_map/fqc,dc->fqd/dot_general | solution.py:120
  16.1 1.6 %collective-permute-start.10 = (bf16[1,256,384]{2,1,0:T(8,128)(2,1)S(1)}, bf16[1,256,384]{2,1,0:T(8,128)(2,1)S(1)}, u32[]{:S(2)}, u32[]{:S(2)}) collective-permute-start(bf16[1,256,384]{2,1,0:T(8,128)(2,1)S(1)} %pad_maximum_fusion.3), channel_id=1, source_target_pairs={{0,12},{1,13},{2,14},{3,15},{4,8},{5,9},{6,10},{7,11},{8,4},{9,5},... | collective-permute-start | bytes 589832 | tf_op jit(solution)/shard_map/ppermute | solution.py:46
  17.7 1.2 %collective-permute-start.9 = (bf16[1,256,384]{2,1,0:T(8,128)(2,1)S(1)}, bf16[1,256,384]{2,1,0:T(8,128)(2,1)S(1)}, u32[]{:S(2)}, u32[]{:S(2)}) collective-permute-start(bf16[1,256,384]{2,1,0:T(8,128)(2,1)S(1)} %pad_maximum_fusion.3), channel_id=1, source_target_pairs={{0,8},{1,9},{2,10},{3,11},{4,12},{5,13},{6,14},{7,15},{8,0},{9,1},... | collective-permute-start | bytes 589832 | tf_op jit(solution)/shard_map/ppermute | solution.py:46
  18.9 1.0 %collective-permute-start.8 = (bf16[1,256,384]{2,1,0:T(8,128)(2,1)S(1)}, bf16[1,256,384]{2,1,0:T(8,128)(2,1)S(1)}, u32[]{:S(2)}, u32[]{:S(2)}) collective-permute-start(bf16[1,256,384]{2,1,0:T(8,128)(2,1)S(1)} %pad_maximum_fusion.3), channel_id=1, source_target_pairs={{0,4},{1,5},{2,6},{3,7},{4,0},{5,1},{6,2},{7,3},{8,12},{9,13},{10,... | collective-permute-start | bytes 589832 | tf_op jit(solution)/shard_map/ppermute | solution.py:46
  19.9 0.6 convolution_bitcast_fusion.2
  20.8 1.4 %collective-permute-start.6 = (bf16[1,768,384]{2,1,0:T(8,128)(2,1)S(1)}, bf16[1,768,384]{2,1,0:T(8,128)(2,1)S(1)}, u32[]{:S(2)}, u32[]{:S(2)}) collective-permute-start(bf16[1,768,384]{2,1,0:T(8,128)(2,1)S(1)} %constant_dynamic-update-slice_fusion), channel_id=1, source_target_pairs={{0,1},{1,0},{2,3},{3,2},{4,5},{5,4},{6,7},{7,6},{8,9},{9,8},{10,11... | collective-permute-start | bytes 1769480 | tf_op jit(solution)/shard_map/ppermute | solution.py:46
  22.4 0.3 copy.102
  23.0 1.0 %collective-permute-done.10 = bf16[1,256,384]{2,1,0:T(8,128)(2,1)S(1)} collective-permute-done((bf16[1,256,384]{2,1,0:T(8,128)(2,1)S(1)}, bf16[1,256,384]{2,1,0:T(8,128)(2,1)S(1)}, u32[]{:S(2)}, u32[]{:S(2)}) %collective-permute-start.10) | collective-permute-done | bytes 196640 | tf_op jit(solution)/shard_map/ppermute | solution.py:46
  24.0 0.3 convolution_bitcast_fusion.9
  24.4 2.5 %collective-permute-start.14 = (bf16[1,256,384]{2,1,0:T(8,128)(2,1)S(1)}, bf16[1,256,384]{2,1,0:T(8,128)(2,1)S(1)}, u32[]{:S(2)}, u32[]{:S(2)}) collective-permute-start(bf16[1,256,384]{2,1,0:T(8,128)(2,1)S(1)} %collective-permute-done.10), channel_id=1, source_target_pairs={{0,1},{1,0},{2,3},{3,2},{4,5},{5,4},{6,7},{7,6},{8,9},{9,8},{10,11... | collective-permute-start | bytes 589832 | tf_op jit(solution)/shard_map/ppermute | solution.py:46
  26.8 9.4 %collective-permute-done.9 = bf16[1,256,384]{2,1,0:T(8,128)(2,1)S(1)} collective-permute-done((bf16[1,256,384]{2,1,0:T(8,128)(2,1)S(1)}, bf16[1,256,384]{2,1,0:T(8,128)(2,1)S(1)}, u32[]{:S(2)}, u32[]{:S(2)}) %collective-permute-start.9) | collective-permute-done | bytes 196640 | tf_op jit(solution)/shard_map/ppermute | solution.py:46
  36.2 1.1 %collective-permute-start.13 = (bf16[1,256,384]{2,1,0:T(8,128)(2,1)S(1)}, bf16[1,256,384]{2,1,0:T(8,128)(2,1)S(1)}, u32[]{:S(2)}, u32[]{:S(2)}) collective-permute-start(bf16[1,256,384]{2,1,0:T(8,128)(2,1)S(1)} %collective-permute-done.9), channel_id=1, source_target_pairs={{0,1},{1,0},{2,3},{3,2},{4,5},{5,4},{6,7},{7,6},{8,9},{9,8},{10,11... | collective-permute-start | bytes 589832 | tf_op jit(solution)/shard_map/ppermute | solution.py:46
  37.3 0.3 convolution_bitcast_fusion.10
  37.7 0.3 convolution_bitcast_fusion.11
  38.2 0.3 convolution_bitcast_fusion.6
  38.6 0.3 convolution_bitcast_fusion.7
  39.0 0.6 collective-permute-start.11
  39.5 0.5 convolution_bitcast_fusion.4
  40.1 0.3 convolution_bitcast_fusion.8
  40.5 0.6 convolution_bitcast_fusion.1
  41.3 0.5 convolution_bitcast_fusion.3
  41.9 0.3 fusion.161
  42.4 0.4 fusion.47
  43.7 0.5 fusion.49
  44.2 0.4 fusion.11
  44.6 0.5 fusion.17
  45.9 0.4 convert_bitcast_fusion
  46.3 0.4 convolution_bitcast_fusion.5
  46.8 0.4 multiply_reduce_fusion
  47.4 2.1 %collective-permute-start.15 = (bf16[1,1,128,384]{3,2,1,0:T(8,128)(2,1)S(1)}, bf16[1,1,128,384]{3,2,1,0:T(8,128)(2,1)S(1)}, u32[]{:S(2)}, u32[]{:S(2)}) collective-permute-start(bf16[1,1,128,384]{3,2,1,0:T(8,128)(2,1)S(1)} %get-tuple-element.37), channel_id=1, source_target_pairs={{1,2},{3,4},{5,6},{7,8},{9,10},{11,12},{13,14},{2,1},{4,3},{6,5},{... | collective-permute-start | bytes 294920 | tf_op jit(solution)/shard_map/ppermute | solution.py:22
  49.7 1.2 %fusion.32 = f32[2,8,17,384]{3,1,2,0:T(8,128)S(1)} fusion(bf16[3,3,3,384,384]{4,3,2,1,0:T(8,128)(2,1)S(1)} %bitcast.489, bf16[4,1,7,2,384]{4,2,3,0,1:T(8,128)(2,1)S(1)} %slice.266, bf16[4,1,8,17,384]{4,2,3,0,1:T(8,128)(2,1)S(1)} %copy.41, pred[8,17]{0,1:T(8,128)(4,1)S(1)} %copy-done.6), kind=kOutput, calls=%fused_computation.43 | convolution fusion | flops 723449856 | bytes 3542016 | tf_op jit(solution)/shard_map/conv_general_dilated | solution.py:59
  50.9 0.3 copy.101
  51.4 2.9 %collective-permute-done.15 = bf16[1,1,128,384]{3,2,1,0:T(8,128)(2,1)S(1)} collective-permute-done((bf16[1,1,128,384]{3,2,1,0:T(8,128)(2,1)S(1)}, bf16[1,1,128,384]{3,2,1,0:T(8,128)(2,1)S(1)}, u32[]{:S(2)}, u32[]{:S(2)}) %collective-permute-start.15) | collective-permute-done | bytes 98336 | tf_op jit(solution)/shard_map/ppermute | solution.py:22
  54.9 1.2 %fusion.35 = f32[2,8,17,384]{3,1,2,0:T(8,128)S(1)} fusion(bf16[3,3,3,384,384]{4,3,2,1,0:T(8,128)(2,1)S(1)} %bitcast.489, bf16[4,1,7,2,384]{4,2,3,0,1:T(8,128)(2,1)S(1)} %slice.293, bf16[4,1,8,17,384]{4,2,3,0,1:T(8,128)(2,1)S(1)} %copy.44, pred[8,17]{0,1:T(8,128)(4,1)S(1)} %copy-done.6), kind=kOutput, calls=%fused_computation.44 | convolution fusion | flops 723449856 | bytes 3542016 | tf_op jit(solution)/shard_map/conv_general_dilated | solution.py:59
  56.1 1.2 %fusion.29 = bf16[2,8,17,384]{3,1,2,0:T(8,128)(2,1)S(1)} fusion(f32[2,8,17,384]{3,1,2,0:T(8,128)S(1)} %fusion.35, f32[2,8,17,384]{3,1,2,0:T(8,128)S(1)} %fusion.32, bf16[3,3,3,384,384]{4,3,2,1,0:T(8,128)(2,1)S(1)} %bitcast.489, bf16[4,1,7,2,384]{4,2,3,0,1:T(8,128)(2,1)S(1)} %slice.264, bf16[4,1,8,17,384]{4,2,3,0,1:T(8,128)(2,1)S(1)} %copy.38, ...), kind=kOutput, calls=%fused_computation.42 | convolution fusion | flops 723763200 | bytes 4168704 | tf_op jit(solution)/shard_map/conv_general_dilated | solution.py:59
  57.5 1.9 %collective-permute-start.17 = (bf16[1,1,128,384]{3,2,1,0:T(8,128)(2,1)S(1)}, bf16[1,1,128,384]{3,2,1,0:T(8,128)(2,1)S(1)}, u32[]{:S(2)}, u32[]{:S(2)}) collective-permute-start(bf16[1,1,128,384]{3,2,1,0:T(8,128)(2,1)S(1)} %slice.296), channel_id=1, source_target_pairs={{1,2},{3,4},{5,6},{7,8},{9,10},{11,12},{13,14},{2,1},{4,3},{6,5},{... | collective-permute-start | bytes 294920 | tf_op jit(solution)/shard_map/ppermute | solution.py:22
  59.9 4.4 %collective-permute-done.17 = bf16[1,1,128,384]{3,2,1,0:T(8,128)(2,1)S(1)} collective-permute-done((bf16[1,1,128,384]{3,2,1,0:T(8,128)(2,1)S(1)}, bf16[1,1,128,384]{3,2,1,0:T(8,128)(2,1)S(1)}, u32[]{:S(2)}, u32[]{:S(2)}) %collective-permute-start.17) | collective-permute-done | bytes 98336 | tf_op jit(solution)/shard_map/ppermute | solution.py:22
  64.4 1.5 %convolution_bitcast_fusion = f32[1,4,130,3,3,192]{5,2,4,3,1,0:T(8,128)S(1)} fusion(bf16[3,3,384,192]{2,3,1,0:T(8,128)(2,1)S(1)} %copy-done, bf16[1,1,128,384]{3,2,1,0:T(8,128)(2,1)S(1)} %get-tuple-element.34, bf16[1,2,128,384]{3,2,1,0:T(8,128)(2,1)S(1)} %bitcast.487, bf16[1,1,128,384]{3,2,1,0:T(8,128)(2,1)S(1)} %get-tuple-element.33), kind=kOutput, calls=%fused_computation.9 | convolution fusion | flops 692490240 | bytes 5314560 | tf_op jit(solution)/shard_map/frwc,ijco->frwijo/dot_general | solution.py:76
  66.3 0.4 fusion.214
  66.9 0.5 copy.74
  67.4 1.3 %convert_element_type.171 = bf16[1,4,49152]{2,1,0:T(4,128)(2,1)} reshape(bf16[1,2,2,128,2,192]{5,4,3,2,1,0:T(2,128)(2,1)S(1)} %copy.74) | data formatting | bytes 786432 | tf_op jit(solution)/shard_map/convert_element_type | solution.py:93
  (102 shorter events, 6.2 us)
Async XLA Ops:
  0.0 64.3 %copy-start = (bf16[3,3,384,192]{2,3,1,0:T(8,128)(2,1)S(1)}, bf16[3,3,384,192]{2,3,1,0:T(8,128)(2,1)}, u32[]{:S(2)}) copy-start(bf16[3,3,384,192]{2,3,1,0:T(8,128)(2,1)} %param.19) | copy-start | bytes 3981316
  2.3 16.7 %collective-permute-start.4 = (bf16[1,128,384]{2,1,0:T(8,128)(2,1)S(1)}, bf16[1,128,384]{2,1,0:T(8,128)(2,1)S(1)}, u32[]{:S(2)}, u32[]{:S(2)}) collective-permute-start(bf16[1,128,384]{2,1,0:T(8,128)(2,1)S(1)} %get-tuple-element.39), channel_id=1, source_target_pairs={{0,12},{1,13},{2,14},{3,15},{4,8},{5,9},{6,10},{7,11},{8,4},{9,5},... | collective-permute-start | bytes 294920 | tf_op jit(solution)/shard_map/ppermute | solution.py:46
  5.6 12.0 %collective-permute-start.3 = (bf16[1,128,384]{2,1,0:T(8,128)(2,1)S(1)}, bf16[1,128,384]{2,1,0:T(8,128)(2,1)S(1)}, u32[]{:S(2)}, u32[]{:S(2)}) collective-permute-start(bf16[1,128,384]{2,1,0:T(8,128)(2,1)S(1)} %get-tuple-element.39), channel_id=1, source_target_pairs={{0,8},{1,9},{2,10},{3,11},{4,12},{5,13},{6,14},{7,15},{8,0},{9,1},... | collective-permute-start | bytes 294920 | tf_op jit(solution)/shard_map/ppermute | solution.py:46
  5.7 10.4 %collective-permute-start.2 = (bf16[1,128,384]{2,1,0:T(8,128)(2,1)S(1)}, bf16[1,128,384]{2,1,0:T(8,128)(2,1)S(1)}, u32[]{:S(2)}, u32[]{:S(2)}) collective-permute-start(bf16[1,128,384]{2,1,0:T(8,128)(2,1)S(1)} %get-tuple-element.39), channel_id=1, source_target_pairs={{0,4},{1,5},{2,6},{3,7},{4,0},{5,1},{6,2},{7,3},{8,12},{9,13},{10,... | collective-permute-start | bytes 294920 | tf_op jit(solution)/shard_map/ppermute | solution.py:46
  6.0 9.9 %collective-permute-start.5 = (bf16[1,128,384]{2,1,0:T(8,128)(2,1)S(1)}, bf16[1,128,384]{2,1,0:T(8,128)(2,1)S(1)}, u32[]{:S(2)}, u32[]{:S(2)}) collective-permute-start(bf16[1,128,384]{2,1,0:T(8,128)(2,1)S(1)} %get-tuple-element.40), channel_id=1, source_target_pairs={{0,2},{1,3},{2,0},{3,1},{4,6},{5,7},{6,4},{7,5},{8,10},{9,11},{10,... | collective-permute-start | bytes 294920 | tf_op jit(solution)/shard_map/ppermute | solution.py:46
  8.0 12.8 %collective-permute-start = (bf16[2,1,128,384]{3,2,1,0:T(8,128)(2,1)}, bf16[2,1,128,384]{3,2,1,0:T(8,128)(2,1)S(1)}, u32[]{:S(2)}, u32[]{:S(2)}) collective-permute-start(bf16[2,1,128,384]{3,2,1,0:T(8,128)(2,1)} %get-tuple-element.25), channel_id=1, source_target_pairs={{1,2},{3,4},{5,6},{7,8},{9,10},{11,12},{13,14},{2,1},{4,3},{6,5},{... | collective-permute-start | bytes 589832 | tf_op jit(solution)/shard_map/ppermute | solution.py:22
  16.0 6.2 %collective-permute-start.1 = (bf16[2,1,128,384]{3,2,1,0:T(8,128)(2,1)S(1)}, bf16[2,1,128,384]{3,2,1,0:T(8,128)(2,1)S(1)}, u32[]{:S(2)}, u32[]{:S(2)}) collective-permute-start(bf16[2,1,128,384]{3,2,1,0:T(8,128)(2,1)S(1)} %get-tuple-element.26), channel_id=1, source_target_pairs={{0,1},{1,0},{2,3},{3,2},{4,5},{5,4},{6,7},{7,6},{8,9},{9,8},{10,11... | collective-permute-start | bytes 589832 | tf_op jit(solution)/shard_map/ppermute | solution.py:18
  16.1 7.9 %collective-permute-start.10 = (bf16[1,256,384]{2,1,0:T(8,128)(2,1)S(1)}, bf16[1,256,384]{2,1,0:T(8,128)(2,1)S(1)}, u32[]{:S(2)}, u32[]{:S(2)}) collective-permute-start(bf16[1,256,384]{2,1,0:T(8,128)(2,1)S(1)} %pad_maximum_fusion.3), channel_id=1, source_target_pairs={{0,12},{1,13},{2,14},{3,15},{4,8},{5,9},{6,10},{7,11},{8,4},{9,5},... | collective-permute-start | bytes 589832 | tf_op jit(solution)/shard_map/ppermute | solution.py:46
  17.7 18.5 %collective-permute-start.9 = (bf16[1,256,384]{2,1,0:T(8,128)(2,1)S(1)}, bf16[1,256,384]{2,1,0:T(8,128)(2,1)S(1)}, u32[]{:S(2)}, u32[]{:S(2)}) collective-permute-start(bf16[1,256,384]{2,1,0:T(8,128)(2,1)S(1)} %pad_maximum_fusion.3), channel_id=1, source_target_pairs={{0,8},{1,9},{2,10},{3,11},{4,12},{5,13},{6,14},{7,15},{8,0},{9,1},... | collective-permute-start | bytes 589832 | tf_op jit(solution)/shard_map/ppermute | solution.py:46
  18.9 18.7 %collective-permute-start.8 = (bf16[1,256,384]{2,1,0:T(8,128)(2,1)S(1)}, bf16[1,256,384]{2,1,0:T(8,128)(2,1)S(1)}, u32[]{:S(2)}, u32[]{:S(2)}) collective-permute-start(bf16[1,256,384]{2,1,0:T(8,128)(2,1)S(1)} %pad_maximum_fusion.3), channel_id=1, source_target_pairs={{0,4},{1,5},{2,6},{3,7},{4,0},{5,1},{6,2},{7,3},{8,12},{9,13},{10,... | collective-permute-start | bytes 589832 | tf_op jit(solution)/shard_map/ppermute | solution.py:46
  19.9 2.3 %copy-start.2 = (bf16[2,2,128,384]{3,2,1,0:T(8,128)(2,1)S(1)}, bf16[2,2,128,384]{3,2,1,0:T(8,128)(2,1)}, u32[]{:S(2)}) copy-start(bf16[2,2,128,384]{3,2,1,0:T(8,128)(2,1)} %param.16) | copy-start | bytes 1179652
  20.8 19.7 %collective-permute-start.6 = (bf16[1,768,384]{2,1,0:T(8,128)(2,1)S(1)}, bf16[1,768,384]{2,1,0:T(8,128)(2,1)S(1)}, u32[]{:S(2)}, u32[]{:S(2)}) collective-permute-start(bf16[1,768,384]{2,1,0:T(8,128)(2,1)S(1)} %constant_dynamic-update-slice_fusion), channel_id=1, source_target_pairs={{0,1},{1,0},{2,3},{3,2},{4,5},{5,4},{6,7},{7,6},{8,9},{9,8},{10,11... | collective-permute-start | bytes 1769480 | tf_op jit(solution)/shard_map/ppermute | solution.py:46
  22.2 16.8 %collective-permute-start.7 = (bf16[1,512,384]{2,1,0:T(8,128)(2,1)S(1)}, bf16[1,512,384]{2,1,0:T(8,128)(2,1)S(1)}, u32[]{:S(2)}, u32[]{:S(2)}) collective-permute-start(bf16[1,512,384]{2,1,0:T(8,128)(2,1)S(1)} %pad_maximum_fusion.2), channel_id=1, source_target_pairs={{0,2},{1,3},{2,0},{3,1},{4,6},{5,7},{6,4},{7,5},{8,10},{9,11},{10,... | collective-permute-start | bytes 1179656 | tf_op jit(solution)/shard_map/ppermute | solution.py:46
  24.4 13.8 %collective-permute-start.14 = (bf16[1,256,384]{2,1,0:T(8,128)(2,1)S(1)}, bf16[1,256,384]{2,1,0:T(8,128)(2,1)S(1)}, u32[]{:S(2)}, u32[]{:S(2)}) collective-permute-start(bf16[1,256,384]{2,1,0:T(8,128)(2,1)S(1)} %collective-permute-done.10), channel_id=1, source_target_pairs={{0,1},{1,0},{2,3},{3,2},{4,5},{5,4},{6,7},{7,6},{8,9},{9,8},{10,11... | collective-permute-start | bytes 589832 | tf_op jit(solution)/shard_map/ppermute | solution.py:46
  36.2 2.3 %collective-permute-start.13 = (bf16[1,256,384]{2,1,0:T(8,128)(2,1)S(1)}, bf16[1,256,384]{2,1,0:T(8,128)(2,1)S(1)}, u32[]{:S(2)}, u32[]{:S(2)}) collective-permute-start(bf16[1,256,384]{2,1,0:T(8,128)(2,1)S(1)} %collective-permute-done.9), channel_id=1, source_target_pairs={{0,1},{1,0},{2,3},{3,2},{4,5},{5,4},{6,7},{7,6},{8,9},{9,8},{10,11... | collective-permute-start | bytes 589832 | tf_op jit(solution)/shard_map/ppermute | solution.py:46
  37.6 2.5 %collective-permute-start.12 = (bf16[1,256,384]{2,1,0:T(8,128)(2,1)S(1)}, bf16[1,256,384]{2,1,0:T(8,128)(2,1)S(1)}, u32[]{:S(2)}, u32[]{:S(2)}) collective-permute-start(bf16[1,256,384]{2,1,0:T(8,128)(2,1)S(1)} %collective-permute-done.8), channel_id=1, source_target_pairs={{0,1},{1,0},{2,3},{3,2},{4,5},{5,4},{6,7},{7,6},{8,9},{9,8},{10,11... | collective-permute-start | bytes 589832 | tf_op jit(solution)/shard_map/ppermute | solution.py:46
  39.0 2.3 %collective-permute-start.11 = (bf16[1,512,384]{2,1,0:T(8,128)(2,1)S(1)}, bf16[1,512,384]{2,1,0:T(8,128)(2,1)S(1)}, u32[]{:S(2)}, u32[]{:S(2)}) collective-permute-start(bf16[1,512,384]{2,1,0:T(8,128)(2,1)S(1)} %collective-permute-done.7), channel_id=1, source_target_pairs={{0,1},{1,0},{2,3},{3,2},{4,5},{5,4},{6,7},{7,6},{8,9},{9,8},{10,11... | collective-permute-start | bytes 1179656 | tf_op jit(solution)/shard_map/ppermute | solution.py:46
  44.2 5.5 %slice-start = ((s8[7962624]{0:T(1024)(128)(4,1)}), s8[3768320]{0:T(1024)(128)(4,1)S(1)}, s32[]{:S(2)}) async-start(s8[7962624]{0:T(1024)(128)(4,1)} %bitcast.488), calls=%async_computation | async-start | bytes 7536640
  45.0 1.3 %copy-start.3 = (bf16[384,384]{1,0:T(8,128)(2,1)S(1)}, bf16[384,384]{1,0:T(8,128)(2,1)}, u32[]{:S(2)}) copy-start(bf16[384,384]{1,0:T(8,128)(2,1)} %param.14) | copy-start | bytes 884740
  45.6 1.1 %copy-start.1 = (bf16[1,2,128,384]{3,2,1,0:T(8,128)(2,1)S(1)}, bf16[1,2,128,384]{3,2,1,0:T(8,128)(2,1)}, u32[]{:S(2)}) copy-start(bf16[1,2,128,384]{3,2,1,0:T(8,128)(2,1)} %param.10) | copy-start | bytes 589828
  45.6 1.1 %copy-start.5 = (bf16[384,384]{1,0:T(8,128)(2,1)S(1)}, bf16[384,384]{1,0:T(8,128)(2,1)}, u32[]{:S(2)}) copy-start(bf16[384,384]{1,0:T(8,128)(2,1)} %param.15) | copy-start | bytes 884740
  45.9 1.3 %copy-start.4 = (f32[384]{0:T(512)S(1)}, f32[384]{0:T(512)}, u32[]{:S(2)}) copy-start(f32[384]{0:T(512)} %param.17) | copy-start | bytes 4612
  45.9 3.7 %slice-start.1 = ((s8[7962624]{0:T(1024)(128)(4,1)}), s8[4194304]{0:T(1024)(128)(4,1)S(1)}, s32[]{:S(2)}) async-start(s8[7962624]{0:T(1024)(128)(4,1)} %bitcast.488), calls=%async_computation.1 | async-start | bytes 8388608
  46.3 3.3 %copy-start.6 = (pred[8,17]{0,1:T(8,128)(4,1)S(1)}, pred[8,17]{0,1:T(8,128)(4,1)}, u32[]{:S(2)}) copy-start(pred[8,17]{0,1:T(8,128)(4,1)} %constant.61) | copy-start | bytes 412
  47.4 6.8 %collective-permute-start.15 = (bf16[1,1,128,384]{3,2,1,0:T(8,128)(2,1)S(1)}, bf16[1,1,128,384]{3,2,1,0:T(8,128)(2,1)S(1)}, u32[]{:S(2)}, u32[]{:S(2)}) collective-permute-start(bf16[1,1,128,384]{3,2,1,0:T(8,128)(2,1)S(1)} %get-tuple-element.37), channel_id=1, source_target_pairs={{1,2},{3,4},{5,6},{7,8},{9,10},{11,12},{13,14},{2,1},{4,3},{6,5},{... | collective-permute-start | bytes 294920 | tf_op jit(solution)/shard_map/ppermute | solution.py:22
  49.5 4.7 %collective-permute-start.16 = (bf16[1,1,128,384]{3,2,1,0:T(8,128)(2,1)S(1)}, bf16[1,1,128,384]{3,2,1,0:T(8,128)(2,1)S(1)}, u32[]{:S(2)}, u32[]{:S(2)}) collective-permute-start(bf16[1,1,128,384]{3,2,1,0:T(8,128)(2,1)S(1)} %get-tuple-element.38), channel_id=1, source_target_pairs={{0,1},{1,0},{2,3},{3,2},{4,5},{5,4},{6,7},{7,6},{8,9},{9,8},{10,11... | collective-permute-start | bytes 294920 | tf_op jit(solution)/shard_map/ppermute | solution.py:18
  57.5 6.8 %collective-permute-start.17 = (bf16[1,1,128,384]{3,2,1,0:T(8,128)(2,1)S(1)}, bf16[1,1,128,384]{3,2,1,0:T(8,128)(2,1)S(1)}, u32[]{:S(2)}, u32[]{:S(2)}) collective-permute-start(bf16[1,1,128,384]{3,2,1,0:T(8,128)(2,1)S(1)} %slice.296), channel_id=1, source_target_pairs={{1,2},{3,4},{5,6},{7,8},{9,10},{11,12},{13,14},{2,1},{4,3},{6,5},{... | collective-permute-start | bytes 294920 | tf_op jit(solution)/shard_map/ppermute | solution.py:22
  59.5 4.8 %collective-permute-start.18 = (bf16[1,1,128,384]{3,2,1,0:T(8,128)(2,1)S(1)}, bf16[1,1,128,384]{3,2,1,0:T(8,128)(2,1)S(1)}, u32[]{:S(2)}, u32[]{:S(2)}) collective-permute-start(bf16[1,1,128,384]{3,2,1,0:T(8,128)(2,1)S(1)} %slice.297), channel_id=1, source_target_pairs={{0,1},{1,0},{2,3},{3,2},{4,5},{5,4},{6,7},{7,6},{8,9},{9,8},{10,11... | collective-permute-start | bytes 294920 | tf_op jit(solution)/shard_map/ppermute | solution.py:18

commit v14 on v13

--- a/solution.py
+++ b/solution.py
@@ -2,6 +2,7 @@
 import jax.numpy as jnp
 from jax import lax
 from jax.sharding import PartitionSpec as P
+
 
 EPS = 1e-06
 
@@ -69,7 +70,7 @@
 
 
 def upsample_conv(extended, w_up):
-    nf, rp, ncols, chans = extended.shape
+    nf, rp, ncols, _ = extended.shape
     nrows = rp - 2
     outs = w_up.shape[-1]
     padded = jnp.pad(extended, ((0, 0), (0, 0), (1, 1), (0, 0)))
@@ -93,7 +94,7 @@
     return result.astype(jnp.bfloat16).reshape(nf, 2 * nrows, 2 * ncols * outs)
 
 
-def body(
+def layer(
     frames, norm_attn, w_query, w_key, w_value, w_out, cache_one, norm_conv, conv_weight, w_up
 ):
     nframes, nrows, ncols, chans = frames.shape
@@ -116,7 +117,9 @@
     first_out = exchange(jnp.concatenate([first] + first_in, axis=1), low, size)
     second_out = exchange(jnp.concatenate([second] + second_in, axis=1), high, size)
     mine = [gathered] + first_out + second_out
-    pieces = mine + [exchange(piece, [1], size)[0] for piece in mine]
+    mirrors = exchange(gathered, [1], size)
+    mirrors = mirrors + [exchange(piece, [1], size)[0] for piece in mine[1:]]
+    pieces = mine + mirrors
     q_keyed = jnp.einsum("fqc,dc->fqd", queries, w_key, preferred_element_type=jnp.float32)
     q_pair = split_pair(q_keyed, axis=1)
     count = queries.shape[1]
@@ -143,7 +146,7 @@
             shrink = jnp.exp(top - new_top)
             denom = denom * shrink + part_denom
             mixed_in = mixed_in * shrink + part_mixed
-        top = new_top
+        top, denom, mixed_in = lax.optimization_barrier((new_top, denom, mixed_in))
     both = jnp.einsum(
         "fqc,cd->fqd", split_pair(mixed_in, axis=1), w_value, preferred_element_type=jnp.float32
     )
@@ -180,5 +183,5 @@
         P(),
     )
     return jax.shard_map(
-        body, mesh=mesh, in_specs=placed, out_specs=P("clips", ROWS, None), check_vma=False
+        layer, mesh=mesh, in_specs=placed, out_specs=P("clips", ROWS, None), check_vma=False
     )

time: 68.9 us -> 69.2 us (level)
  the two profiles are of different devices: /device:TPU:5 before, /device:TPU:23 now
where the time goes in v14:
time: 69.2 us; the launch traced here: 69 us
  starting transfers between devices  24.7 us (36%)
  waiting for transfers between devices  15.7 us (23%)
  matrix products  14.8 us (21%)
  other arithmetic  8.6 us (12%)
  local copies, waits for them, and re-layouts  4.42 us (6%)
  between operations  0.76 us (1%)
    ppermute x13, starting transfers between devices, exchange(): lax.ppermute(values, ROWS, [(i, i ^ mask) for i in range(size)])  13.2 us
    ppermute x3, starting transfers between devices, padded_2(): lax.ppermute(jnp.where(even, first, last), axis, pairs + [(j, i) for i, j...  10.8 us
    ppermute x13, waiting for transfers between devices, exchange(): lax.ppermute(values, ROWS, [(i, i ^ mask) for i in range(size)])  8.95 us
    ppermute x3, waiting for transfers between devices, padded_2(): lax.ppermute(jnp.where(even, first, last), axis, pairs + [(j, i) for i, j...  6.73 us
    dot_general x10, matrix products, layer(): jnp.einsum('fqc,fkc->fqk', q_pair, piece, preferred_element_type=jnp.floa...  4.07 us
    conv_general_dilated x3, matrix products, conv_rows(): lax.conv_general_dilated(haloed[tstep:tstep + 1], weight[tstep], window_s...  3.62 us
    dot_general x10, matrix products, layer(): jnp.einsum('fqk,fkc->fqc', e.astype(jnp.bfloat16), p, preferred_element_t...  3.3 us
    select_n x3, other arithmetic, padded_2(): jnp.where(even, first, last)  1.79 us
  transfers between devices with their start and end apart: 19, of which 6 were waited for; matrix products, arithmetic and copies ran while one was open for 21% of the time, Pallas kernels for 0%

profile of v14, /device:TPU:23, one launch (start us, length us, event | category | flops | bytes accessed | tf_op | source)
XLA Modules:
  0.0 69.0 jit_solution(8547863840334854570)
XLA Ops:
  0.0 1.1 %multiply_reduce_fusion.1 = f32[2,128]{1,0:T(2,128)S(1)} fusion(bf16[1,2,128,384]{3,2,1,0:T(8,128)(2,1)} %param.10), kind=kLoop, calls=%fused_computation.134 | loop fusion | flops 294656 | bytes 197632 | tf_op jit(solution)/shard_map/reduce_sum | solution.py:33
  1.2 1.1 %constant_dynamic-update-slice_fusion.4 = (bf16[1,768,384]{2,1,0:T(8,128)(2,1)S(1)}, bf16[1,256,384]{2,1,0:T(8,128)(2,1)S(1)}) fusion(f32[384]{0:T(512)} %param.11, f32[256]{0:T(256)S(1)} %rsqrt_bitcast_fusion, bf16[1,2,128,384]{3,2,1,0:T(8,128)(2,1)} %param.10), kind=kLoop, calls=%fused_computation.291 | loop fusion | flops 393215 | bytes 592384
  2.3 1.4 %collective-permute-start.2 = (bf16[1,128,384]{2,1,0:T(8,128)(2,1)S(1)}, bf16[1,128,384]{2,1,0:T(8,128)(2,1)S(1)}, u32[]{:S(2)}, u32[]{:S(2)}) collective-permute-start(bf16[1,128,384]{2,1,0:T(8,128)(2,1)S(1)} %get-tuple-element.54), channel_id=1, source_target_pairs={{0,4},{1,5},{2,6},{3,7},{4,0},{5,1},{6,2},{7,3},{8,12},{9,13},{10,... | collective-permute-start | bytes 294920 | tf_op jit(solution)/shard_map/ppermute | solution.py:47
  3.7 1.3 %collective-permute-start.4 = (bf16[1,128,384]{2,1,0:T(8,128)(2,1)S(1)}, bf16[1,128,384]{2,1,0:T(8,128)(2,1)S(1)}, u32[]{:S(2)}, u32[]{:S(2)}) collective-permute-start(bf16[1,128,384]{2,1,0:T(8,128)(2,1)S(1)} %get-tuple-element.54), channel_id=1, source_target_pairs={{0,12},{1,13},{2,14},{3,15},{4,8},{5,9},{6,10},{7,11},{8,4},{9,5},... | collective-permute-start | bytes 294920 | tf_op jit(solution)/shard_map/ppermute | solution.py:47
  5.2 1.7 %broadcast_select_fusion.3 = (bf16[2,1,128,384]{3,2,1,0:T(8,128)(2,1)}, bf16[2,1,128,384]{3,2,1,0:T(8,128)(2,1)S(1)}) fusion(pred[]{:T(512)S(6)} %eq.9, bf16[2,2,128,384]{3,2,1,0:T(8,128)(2,1)} %param.16), kind=kLoop, calls=%fused_computation.261 | loop fusion | flops 196608 | bytes 786433 | tf_op jit(solution)/shard_map/jit(_where)/select_n | solution.py:24
  6.9 6.7 %collective-permute-start = (bf16[2,1,128,384]{3,2,1,0:T(8,128)(2,1)}, bf16[2,1,128,384]{3,2,1,0:T(8,128)(2,1)S(1)}, u32[]{:S(2)}, u32[]{:S(2)}) collective-permute-start(bf16[2,1,128,384]{3,2,1,0:T(8,128)(2,1)} %get-tuple-element.41), channel_id=1, source_target_pairs={{1,2},{3,4},{5,6},{7,8},{9,10},{11,12},{13,14},{2,1},{4,3},{6,5},{... | collective-permute-start | bytes 589832 | tf_op jit(solution)/shard_map/ppermute | solution.py:23
  13.7 1.0 %fusion.108 = bf16[256,384]{1,0:T(8,128)(2,1)S(1)} fusion(bf16[1,2,128,384]{3,2,1,0:T(8,128)(2,1)} %param.10, f32[384]{0:T(512)} %param.11, f32[256]{0:T(256)S(1)} %rsqrt_bitcast_fusion), kind=kLoop, calls=%fused_computation.127 | loop fusion | flops 393216 | bytes 395776 | tf_op jit(solution)/shard_map/convert_element_type | solution.py:107
  14.7 1.6 %convert_bitcast_fusion = (bf16[1,256,384]{2,1,0:T(8,128)(2,1)S(1)}, bf16[1,256,384]{2,1,0:T(8,128)(2,1)S(1)}) fusion(bf16[384,384]{1,0:T(8,128)(2,1)} %param.13, bf16[256,384]{1,0:T(8,128)(2,1)S(1)} %fusion.108, bf16[384,384]{1,0:T(8,128)(2,1)} %param.12), kind=kOutput, calls=%fused_computation.280 | convolution fusion | flops 151486464 | bytes 1179648 | tf_op jit(solution)/shard_map/fqc,dc->fqd/dot_general | solution.py:123
  16.5 0.5 collective-permute-start.9
  17.1 1.1 %collective-permute-start.6 = (bf16[1,768,384]{2,1,0:T(8,128)(2,1)S(1)}, bf16[1,768,384]{2,1,0:T(8,128)(2,1)S(1)}, u32[]{:S(2)}, u32[]{:S(2)}) collective-permute-start(bf16[1,768,384]{2,1,0:T(8,128)(2,1)S(1)} %constant_dynamic-update-slice_fusion), channel_id=1, source_target_pairs={{0,1},{1,0},{2,3},{3,2},{4,5},{5,4},{6,7},{7,6},{8,9},{9,8},{10,11... | collective-permute-start | bytes 1769480 | tf_op jit(solution)/shard_map/ppermute | solution.py:47
  18.2 0.6 convolution_bitcast_fusion.2
  19.0 2.3 %collective-permute-start.10 = (bf16[1,256,384]{2,1,0:T(8,128)(2,1)S(1)}, bf16[1,256,384]{2,1,0:T(8,128)(2,1)S(1)}, u32[]{:S(2)}, u32[]{:S(2)}) collective-permute-start(bf16[1,256,384]{2,1,0:T(8,128)(2,1)S(1)} %pad_maximum_fusion.3), channel_id=1, source_target_pairs={{0,12},{1,13},{2,14},{3,15},{4,8},{5,9},{6,10},{7,11},{8,4},{9,5},... | collective-permute-start | bytes 589832 | tf_op jit(solution)/shard_map/ppermute | solution.py:47
  21.6 0.3 copy.102
  22.1 0.3 collective-permute-done.8
  22.4 0.3 convolution_bitcast_fusion.11
  22.8 2.4 %collective-permute-start.12 = (bf16[1,256,384]{2,1,0:T(8,128)(2,1)S(1)}, bf16[1,256,384]{2,1,0:T(8,128)(2,1)S(1)}, u32[]{:S(2)}, u32[]{:S(2)}) collective-permute-start(bf16[1,256,384]{2,1,0:T(8,128)(2,1)S(1)} %collective-permute-done.8), channel_id=1, source_target_pairs={{0,1},{1,0},{2,3},{3,2},{4,5},{5,4},{6,7},{7,6},{8,9},{9,8},{10,11... | collective-permute-start | bytes 589832 | tf_op jit(solution)/shard_map/ppermute | solution.py:47
  25.2 0.5 collective-permute-done.9
  25.7 2.3 %collective-permute-start.13 = (bf16[1,256,384]{2,1,0:T(8,128)(2,1)S(1)}, bf16[1,256,384]{2,1,0:T(8,128)(2,1)S(1)}, u32[]{:S(2)}, u32[]{:S(2)}) collective-permute-start(bf16[1,256,384]{2,1,0:T(8,128)(2,1)S(1)} %collective-permute-done.9), channel_id=1, source_target_pairs={{0,1},{1,0},{2,3},{3,2},{4,5},{5,4},{6,7},{7,6},{8,9},{9,8},{10,11... | collective-permute-start | bytes 589832 | tf_op jit(solution)/shard_map/ppermute | solution.py:47
  27.9 0.3 convolution_bitcast_fusion.10
  28.3 8.0 %collective-permute-done.10 = bf16[1,256,384]{2,1,0:T(8,128)(2,1)S(1)} collective-permute-done((bf16[1,256,384]{2,1,0:T(8,128)(2,1)S(1)}, bf16[1,256,384]{2,1,0:T(8,128)(2,1)S(1)}, u32[]{:S(2)}, u32[]{:S(2)}) %collective-permute-start.10) | collective-permute-done | bytes 196640 | tf_op jit(solution)/shard_map/ppermute | solution.py:47
  36.3 0.3 convolution_bitcast_fusion.9
  36.7 1.5 %collective-permute-start.14 = (bf16[1,256,384]{2,1,0:T(8,128)(2,1)S(1)}, bf16[1,256,384]{2,1,0:T(8,128)(2,1)S(1)}, u32[]{:S(2)}, u32[]{:S(2)}) collective-permute-start(bf16[1,256,384]{2,1,0:T(8,128)(2,1)S(1)} %collective-permute-done.10), channel_id=1, source_target_pairs={{0,1},{1,0},{2,3},{3,2},{4,5},{5,4},{6,7},{7,6},{8,9},{9,8},{10,11... | collective-permute-start | bytes 589832 | tf_op jit(solution)/shard_map/ppermute | solution.py:47
  38.3 0.3 convolution_bitcast_fusion.8
  38.7 0.3 convolution_bitcast_fusion.7
  39.3 0.3 convolution_bitcast_fusion.6
  39.7 0.5 convolution_bitcast_fusion.4
  40.3 0.6 convolution_bitcast_fusion.1
  41.1 0.4 fusion.49
  41.5 0.5 fusion.50
  42.0 0.5 fusion.16
  43.6 0.4 fusion.18
  44.1 0.5 convolution_bitcast_fusion.3
  45.9 0.4 fusion.17
  46.6 0.4 convolution_bitcast_fusion.5
  47.0 0.4 multiply_reduce_fusion
  47.7 2.1 %collective-permute-start.15 = (bf16[1,1,128,384]{3,2,1,0:T(8,128)(2,1)S(1)}, bf16[1,1,128,384]{3,2,1,0:T(8,128)(2,1)S(1)}, u32[]{:S(2)}, u32[]{:S(2)}) collective-permute-start(bf16[1,1,128,384]{3,2,1,0:T(8,128)(2,1)S(1)} %get-tuple-element.51), channel_id=1, source_target_pairs={{1,2},{3,4},{5,6},{7,8},{9,10},{11,12},{13,14},{2,1},{4,3},{6,5},{... | collective-permute-start | bytes 294920 | tf_op jit(solution)/shard_map/ppermute | solution.py:23
  49.8 0.4 collective-permute-start.16
  50.2 1.2 %fusion.33 = f32[2,8,17,384]{3,1,2,0:T(8,128)S(1)} fusion(bf16[3,3,3,384,384]{4,3,2,1,0:T(8,128)(2,1)S(1)} %bitcast.524, bf16[4,1,7,2,384]{4,2,3,0,1:T(8,128)(2,1)S(1)} %slice.266, bf16[4,1,8,17,384]{4,2,3,0,1:T(8,128)(2,1)S(1)} %copy.41, pred[8,17]{0,1:T(8,128)(4,1)S(1)} %copy-done.6), kind=kOutput, calls=%fused_computation.44 | convolution fusion | flops 723449856 | bytes 3542016 | tf_op jit(solution)/shard_map/conv_general_dilated | solution.py:60
  52.0 2.5 %collective-permute-done.15 = bf16[1,1,128,384]{3,2,1,0:T(8,128)(2,1)S(1)} collective-permute-done((bf16[1,1,128,384]{3,2,1,0:T(8,128)(2,1)S(1)}, bf16[1,1,128,384]{3,2,1,0:T(8,128)(2,1)S(1)}, u32[]{:S(2)}, u32[]{:S(2)}) %collective-permute-start.15) | collective-permute-done | bytes 98336 | tf_op jit(solution)/shard_map/ppermute | solution.py:23
  54.6 0.3 copy.103
  55.2 1.2 %fusion.36 = f32[2,8,17,384]{3,1,2,0:T(8,128)S(1)} fusion(bf16[3,3,3,384,384]{4,3,2,1,0:T(8,128)(2,1)S(1)} %bitcast.524, bf16[4,1,7,2,384]{4,2,3,0,1:T(8,128)(2,1)S(1)} %slice.293, bf16[4,1,8,17,384]{4,2,3,0,1:T(8,128)(2,1)S(1)} %copy.44, pred[8,17]{0,1:T(8,128)(4,1)S(1)} %copy-done.6), kind=kOutput, calls=%fused_computation.45 | convolution fusion | flops 723449856 | bytes 3542016 | tf_op jit(solution)/shard_map/conv_general_dilated | solution.py:60
  56.4 1.2 %fusion.30 = bf16[2,8,17,384]{3,1,2,0:T(8,128)(2,1)S(1)} fusion(f32[2,8,17,384]{3,1,2,0:T(8,128)S(1)} %fusion.36, f32[2,8,17,384]{3,1,2,0:T(8,128)S(1)} %fusion.33, bf16[3,3,3,384,384]{4,3,2,1,0:T(8,128)(2,1)S(1)} %bitcast.524, bf16[4,1,7,2,384]{4,2,3,0,1:T(8,128)(2,1)S(1)} %slice.264, bf16[4,1,8,17,384]{4,2,3,0,1:T(8,128)(2,1)S(1)} %copy.38, ...), kind=kOutput, calls=%fused_computation.43 | convolution fusion | flops 723763200 | bytes 4168704 | tf_op jit(solution)/shard_map/conv_general_dilated | solution.py:60
  57.8 1.9 %collective-permute-start.17 = (bf16[1,1,128,384]{3,2,1,0:T(8,128)(2,1)S(1)}, bf16[1,1,128,384]{3,2,1,0:T(8,128)(2,1)S(1)}, u32[]{:S(2)}, u32[]{:S(2)}) collective-permute-start(bf16[1,1,128,384]{3,2,1,0:T(8,128)(2,1)S(1)} %slice.296), channel_id=1, source_target_pairs={{1,2},{3,4},{5,6},{7,8},{9,10},{11,12},{13,14},{2,1},{4,3},{6,5},{... | collective-permute-start | bytes 294920 | tf_op jit(solution)/shard_map/ppermute | solution.py:23
  60.4 4.2 %collective-permute-done.17 = bf16[1,1,128,384]{3,2,1,0:T(8,128)(2,1)S(1)} collective-permute-done((bf16[1,1,128,384]{3,2,1,0:T(8,128)(2,1)S(1)}, bf16[1,1,128,384]{3,2,1,0:T(8,128)(2,1)S(1)}, u32[]{:S(2)}, u32[]{:S(2)}) %collective-permute-start.17) | collective-permute-done | bytes 98336 | tf_op jit(solution)/shard_map/ppermute | solution.py:23
  64.6 1.5 %convolution_bitcast_fusion = f32[1,4,130,3,3,192]{5,2,4,3,1,0:T(8,128)S(1)} fusion(bf16[3,3,384,192]{2,3,1,0:T(8,128)(2,1)S(1)} %copy-done, bf16[1,1,128,384]{3,2,1,0:T(8,128)(2,1)S(1)} %get-tuple-element.48, bf16[1,2,128,384]{3,2,1,0:T(8,128)(2,1)S(1)} %bitcast.500, bf16[1,1,128,384]{3,2,1,0:T(8,128)(2,1)S(1)} %get-tuple-element.47), kind=kOutput, calls=%fused_computation.9 | convolution fusion | flops 692490240 | bytes 5314560 | tf_op jit(solution)/shard_map/frwc,ijco->frwijo/dot_general | solution.py:77
  66.1 0.4 fusion.214
  67.1 0.5 copy.74
  67.7 1.3 %convert_element_type.162 = bf16[1,4,49152]{2,1,0:T(4,128)(2,1)} reshape(bf16[1,2,2,128,2,192]{5,4,3,2,1,0:T(2,128)(2,1)S(1)} %copy.74) | data formatting | bytes 786432 | tf_op jit(solution)/shard_map/convert_element_type | solution.py:94
  (112 shorter events, 7.4 us)
Async XLA Ops:
  0.0 64.6 %copy-start = (bf16[3,3,384,192]{2,3,1,0:T(8,128)(2,1)S(1)}, bf16[3,3,384,192]{2,3,1,0:T(8,128)(2,1)}, u32[]{:S(2)}) copy-start(bf16[3,3,384,192]{2,3,1,0:T(8,128)(2,1)} %param.19) | copy-start | bytes 3981316
  2.3 14.1 %collective-permute-start.2 = (bf16[1,128,384]{2,1,0:T(8,128)(2,1)S(1)}, bf16[1,128,384]{2,1,0:T(8,128)(2,1)S(1)}, u32[]{:S(2)}, u32[]{:S(2)}) collective-permute-start(bf16[1,128,384]{2,1,0:T(8,128)(2,1)S(1)} %get-tuple-element.54), channel_id=1, source_target_pairs={{0,4},{1,5},{2,6},{3,7},{4,0},{5,1},{6,2},{7,3},{8,12},{9,13},{10,... | collective-permute-start | bytes 294920 | tf_op jit(solution)/shard_map/ppermute | solution.py:47
  3.6 12.9 %collective-permute-start.3 = (bf16[1,128,384]{2,1,0:T(8,128)(2,1)S(1)}, bf16[1,128,384]{2,1,0:T(8,128)(2,1)S(1)}, u32[]{:S(2)}, u32[]{:S(2)}) collective-permute-start(bf16[1,128,384]{2,1,0:T(8,128)(2,1)S(1)} %get-tuple-element.54), channel_id=1, source_target_pairs={{0,8},{1,9},{2,10},{3,11},{4,12},{5,13},{6,14},{7,15},{8,0},{9,1},... | collective-permute-start | bytes 294920 | tf_op jit(solution)/shard_map/ppermute | solution.py:47
  3.7 13.4 %collective-permute-start.4 = (bf16[1,128,384]{2,1,0:T(8,128)(2,1)S(1)}, bf16[1,128,384]{2,1,0:T(8,128)(2,1)S(1)}, u32[]{:S(2)}, u32[]{:S(2)}) collective-permute-start(bf16[1,128,384]{2,1,0:T(8,128)(2,1)S(1)} %get-tuple-element.54), channel_id=1, source_target_pairs={{0,12},{1,13},{2,14},{3,15},{4,8},{5,9},{6,10},{7,11},{8,4},{9,5},... | collective-permute-start | bytes 294920 | tf_op jit(solution)/shard_map/ppermute | solution.py:47
  5.0 11.3 %collective-permute-start.5 = (bf16[1,128,384]{2,1,0:T(8,128)(2,1)S(1)}, bf16[1,128,384]{2,1,0:T(8,128)(2,1)S(1)}, u32[]{:S(2)}, u32[]{:S(2)}) collective-permute-start(bf16[1,128,384]{2,1,0:T(8,128)(2,1)S(1)} %get-tuple-element.53), channel_id=1, source_target_pairs={{0,2},{1,3},{2,0},{3,1},{4,6},{5,7},{6,4},{7,5},{8,10},{9,11},{10,... | collective-permute-start | bytes 294920 | tf_op jit(solution)/shard_map/ppermute | solution.py:47
  6.9 12.1 %collective-permute-start = (bf16[2,1,128,384]{3,2,1,0:T(8,128)(2,1)}, bf16[2,1,128,384]{3,2,1,0:T(8,128)(2,1)S(1)}, u32[]{:S(2)}, u32[]{:S(2)}) collective-permute-start(bf16[2,1,128,384]{3,2,1,0:T(8,128)(2,1)} %get-tuple-element.41), channel_id=1, source_target_pairs={{1,2},{3,4},{5,6},{7,8},{9,10},{11,12},{13,14},{2,1},{4,3},{6,5},{... | collective-permute-start | bytes 589832 | tf_op jit(solution)/shard_map/ppermute | solution.py:23
  16.3 5.0 %collective-permute-start.1 = (bf16[2,1,128,384]{3,2,1,0:T(8,128)(2,1)S(1)}, bf16[2,1,128,384]{3,2,1,0:T(8,128)(2,1)S(1)}, u32[]{:S(2)}, u32[]{:S(2)}) collective-permute-start(bf16[2,1,128,384]{3,2,1,0:T(8,128)(2,1)S(1)} %get-tuple-element.42), channel_id=1, source_target_pairs={{0,1},{1,0},{2,3},{3,2},{4,5},{5,4},{6,7},{7,6},{8,9},{9,8},{10,11... | collective-permute-start | bytes 589832 | tf_op jit(solution)/shard_map/ppermute | solution.py:19
  16.4 6.0 %collective-permute-start.8 = (bf16[1,256,384]{2,1,0:T(8,128)(2,1)S(1)}, bf16[1,256,384]{2,1,0:T(8,128)(2,1)S(1)}, u32[]{:S(2)}, u32[]{:S(2)}) collective-permute-start(bf16[1,256,384]{2,1,0:T(8,128)(2,1)S(1)} %pad_maximum_fusion.3), channel_id=1, source_target_pairs={{0,4},{1,5},{2,6},{3,7},{4,0},{5,1},{6,2},{7,3},{8,12},{9,13},{10,... | collective-permute-start | bytes 589832 | tf_op jit(solution)/shard_map/ppermute | solution.py:47
  16.5 9.1 %collective-permute-start.9 = (bf16[1,256,384]{2,1,0:T(8,128)(2,1)S(1)}, bf16[1,256,384]{2,1,0:T(8,128)(2,1)S(1)}, u32[]{:S(2)}, u32[]{:S(2)}) collective-permute-start(bf16[1,256,384]{2,1,0:T(8,128)(2,1)S(1)} %pad_maximum_fusion.3), channel_id=1, source_target_pairs={{0,8},{1,9},{2,10},{3,11},{4,12},{5,13},{6,14},{7,15},{8,0},{9,1},... | collective-permute-start | bytes 589832 | tf_op jit(solution)/shard_map/ppermute | solution.py:47
  17.1 23.2 %collective-permute-start.6 = (bf16[1,768,384]{2,1,0:T(8,128)(2,1)S(1)}, bf16[1,768,384]{2,1,0:T(8,128)(2,1)S(1)}, u32[]{:S(2)}, u32[]{:S(2)}) collective-permute-start(bf16[1,768,384]{2,1,0:T(8,128)(2,1)S(1)} %constant_dynamic-update-slice_fusion), channel_id=1, source_target_pairs={{0,1},{1,0},{2,3},{3,2},{4,5},{5,4},{6,7},{7,6},{8,9},{9,8},{10,11... | collective-permute-start | bytes 1769480 | tf_op jit(solution)/shard_map/ppermute | solution.py:47
  18.2 3.1 %copy-start.2 = (bf16[2,2,128,384]{3,2,1,0:T(8,128)(2,1)S(1)}, bf16[2,2,128,384]{3,2,1,0:T(8,128)(2,1)}, u32[]{:S(2)}) copy-start(bf16[2,2,128,384]{3,2,1,0:T(8,128)(2,1)} %param.16) | copy-start | bytes 1179652
  19.0 17.2 %collective-permute-start.10 = (bf16[1,256,384]{2,1,0:T(8,128)(2,1)S(1)}, bf16[1,256,384]{2,1,0:T(8,128)(2,1)S(1)}, u32[]{:S(2)}, u32[]{:S(2)}) collective-permute-start(bf16[1,256,384]{2,1,0:T(8,128)(2,1)S(1)} %pad_maximum_fusion.3), channel_id=1, source_target_pairs={{0,12},{1,13},{2,14},{3,15},{4,8},{5,9},{6,10},{7,11},{8,4},{9,5},... | collective-permute-start | bytes 589832 | tf_op jit(solution)/shard_map/ppermute | solution.py:47
  21.3 16.9 %collective-permute-start.7 = (bf16[1,512,384]{2,1,0:T(8,128)(2,1)S(1)}, bf16[1,512,384]{2,1,0:T(8,128)(2,1)S(1)}, u32[]{:S(2)}, u32[]{:S(2)}) collective-permute-start(bf16[1,512,384]{2,1,0:T(8,128)(2,1)S(1)} %pad_maximum_fusion.2), channel_id=1, source_target_pairs={{0,2},{1,3},{2,0},{3,1},{4,6},{5,7},{6,4},{7,5},{8,10},{9,11},{10,... | collective-permute-start | bytes 1179656 | tf_op jit(solution)/shard_map/ppermute | solution.py:47
  22.8 15.5 %collective-permute-start.12 = (bf16[1,256,384]{2,1,0:T(8,128)(2,1)S(1)}, bf16[1,256,384]{2,1,0:T(8,128)(2,1)S(1)}, u32[]{:S(2)}, u32[]{:S(2)}) collective-permute-start(bf16[1,256,384]{2,1,0:T(8,128)(2,1)S(1)} %collective-permute-done.8), channel_id=1, source_target_pairs={{0,1},{1,0},{2,3},{3,2},{4,5},{5,4},{6,7},{7,6},{8,9},{9,8},{10,11... | collective-permute-start | bytes 589832 | tf_op jit(solution)/shard_map/ppermute | solution.py:47
  25.7 13.0 %collective-permute-start.13 = (bf16[1,256,384]{2,1,0:T(8,128)(2,1)S(1)}, bf16[1,256,384]{2,1,0:T(8,128)(2,1)S(1)}, u32[]{:S(2)}, u32[]{:S(2)}) collective-permute-start(bf16[1,256,384]{2,1,0:T(8,128)(2,1)S(1)} %collective-permute-done.9), channel_id=1, source_target_pairs={{0,1},{1,0},{2,3},{3,2},{4,5},{5,4},{6,7},{7,6},{8,9},{9,8},{10,11... | collective-permute-start | bytes 589832 | tf_op jit(solution)/shard_map/ppermute | solution.py:47
  36.7 2.6 %collective-permute-start.14 = (bf16[1,256,384]{2,1,0:T(8,128)(2,1)S(1)}, bf16[1,256,384]{2,1,0:T(8,128)(2,1)S(1)}, u32[]{:S(2)}, u32[]{:S(2)}) collective-permute-start(bf16[1,256,384]{2,1,0:T(8,128)(2,1)S(1)} %collective-permute-done.10), channel_id=1, source_target_pairs={{0,1},{1,0},{2,3},{3,2},{4,5},{5,4},{6,7},{7,6},{8,9},{9,8},{10,11... | collective-permute-start | bytes 589832 | tf_op jit(solution)/shard_map/ppermute | solution.py:47
  38.3 5.8 %collective-permute-start.11 = (bf16[1,512,384]{2,1,0:T(8,128)(2,1)S(1)}, bf16[1,512,384]{2,1,0:T(8,128)(2,1)S(1)}, u32[]{:S(2)}, u32[]{:S(2)}) collective-permute-start(bf16[1,512,384]{2,1,0:T(8,128)(2,1)S(1)} %collective-permute-done.7), channel_id=1, source_target_pairs={{0,1},{1,0},{2,3},{3,2},{4,5},{5,4},{6,7},{7,6},{8,9},{9,8},{10,11... | collective-permute-start | bytes 1179656 | tf_op jit(solution)/shard_map/ppermute | solution.py:47
  42.0 8.3 %slice-start = ((s8[7962624]{0:T(1024)(128)(4,1)}), s8[3768320]{0:T(1024)(128)(4,1)S(1)}, s32[]{:S(2)}) async-start(s8[7962624]{0:T(1024)(128)(4,1)} %bitcast.523), calls=%async_computation | async-start | bytes 7536640
  44.7 5.6 %slice-start.1 = ((s8[7962624]{0:T(1024)(128)(4,1)}), s8[4194304]{0:T(1024)(128)(4,1)S(1)}, s32[]{:S(2)}) async-start(s8[7962624]{0:T(1024)(128)(4,1)} %bitcast.523), calls=%async_computation.1 | async-start | bytes 8388608
  45.3 1.3 %copy-start.3 = (bf16[384,384]{1,0:T(8,128)(2,1)S(1)}, bf16[384,384]{1,0:T(8,128)(2,1)}, u32[]{:S(2)}) copy-start(bf16[384,384]{1,0:T(8,128)(2,1)} %param.14) | copy-start | bytes 884740
  45.8 1.1 %copy-start.1 = (bf16[1,2,128,384]{3,2,1,0:T(8,128)(2,1)S(1)}, bf16[1,2,128,384]{3,2,1,0:T(8,128)(2,1)}, u32[]{:S(2)}) copy-start(bf16[1,2,128,384]{3,2,1,0:T(8,128)(2,1)} %param.10) | copy-start | bytes 589828
  45.9 1.1 %copy-start.5 = (bf16[384,384]{1,0:T(8,128)(2,1)S(1)}, bf16[384,384]{1,0:T(8,128)(2,1)}, u32[]{:S(2)}) copy-start(bf16[384,384]{1,0:T(8,128)(2,1)} %param.15) | copy-start | bytes 884740
  46.2 1.2 %copy-start.4 = (f32[384]{0:T(512)S(1)}, f32[384]{0:T(512)}, u32[]{:S(2)}) copy-start(f32[384]{0:T(512)} %param.17) | copy-start | bytes 4612
  46.3 4.0 %copy-start.6 = (pred[8,17]{0,1:T(8,128)(4,1)S(1)}, pred[8,17]{0,1:T(8,128)(4,1)}, u32[]{:S(2)}) copy-start(pred[8,17]{0,1:T(8,128)(4,1)} %constant.61) | copy-start | bytes 412
  47.7 6.8 %collective-permute-start.15 = (bf16[1,1,128,384]{3,2,1,0:T(8,128)(2,1)S(1)}, bf16[1,1,128,384]{3,2,1,0:T(8,128)(2,1)S(1)}, u32[]{:S(2)}, u32[]{:S(2)}) collective-permute-start(bf16[1,1,128,384]{3,2,1,0:T(8,128)(2,1)S(1)} %get-tuple-element.51), channel_id=1, source_target_pairs={{1,2},{3,4},{5,6},{7,8},{9,10},{11,12},{13,14},{2,1},{4,3},{6,5},{... | collective-permute-start | bytes 294920 | tf_op jit(solution)/shard_map/ppermute | solution.py:23
  49.8 4.7 %collective-permute-start.16 = (bf16[1,1,128,384]{3,2,1,0:T(8,128)(2,1)S(1)}, bf16[1,1,128,384]{3,2,1,0:T(8,128)(2,1)S(1)}, u32[]{:S(2)}, u32[]{:S(2)}) collective-permute-start(bf16[1,1,128,384]{3,2,1,0:T(8,128)(2,1)S(1)} %get-tuple-element.52), channel_id=1, source_target_pairs={{0,1},{1,0},{2,3},{3,2},{4,5},{5,4},{6,7},{7,6},{8,9},{9,8},{10,11... | collective-permute-start | bytes 294920 | tf_op jit(solution)/shard_map/ppermute | solution.py:19
  57.8 6.8 %collective-permute-start.17 = (bf16[1,1,128,384]{3,2,1,0:T(8,128)(2,1)S(1)}, bf16[1,1,128,384]{3,2,1,0:T(8,128)(2,1)S(1)}, u32[]{:S(2)}, u32[]{:S(2)}) collective-permute-start(bf16[1,1,128,384]{3,2,1,0:T(8,128)(2,1)S(1)} %slice.296), channel_id=1, source_target_pairs={{1,2},{3,4},{5,6},{7,8},{9,10},{11,12},{13,14},{2,1},{4,3},{6,5},{... | collective-permute-start | bytes 294920 | tf_op jit(solution)/shard_map/ppermute | solution.py:23
  59.8 4.8 %collective-permute-start.18 = (bf16[1,1,128,384]{3,2,1,0:T(8,128)(2,1)S(1)}, bf16[1,1,128,384]{3,2,1,0:T(8,128)(2,1)S(1)}, u32[]{:S(2)}, u32[]{:S(2)}) collective-permute-start(bf16[1,1,128,384]{3,2,1,0:T(8,128)(2,1)S(1)} %slice.297), channel_id=1, source_target_pairs={{0,1},{1,0},{2,3},{3,2},{4,5},{5,4},{6,7},{7,6},{8,9},{9,8},{10,11... | collective-permute-start | bytes 294920 | tf_op jit(solution)/shard_map/ppermute | solution.py:19

commit v15 on v14

--- a/solution.py
+++ b/solution.py
@@ -46,6 +46,17 @@
     return [
         lax.ppermute(values, ROWS, [(i, i ^ mask) for i in range(size)]) for mask in masks[1:]
     ]
+
+
+def tap_row(rows, weight):
+    return lax.conv_general_dilated(
+        rows,
+        weight[None],
+        window_strides=(1, 1),
+        padding=((0, 0), (1, 1)),
+        dimension_numbers=("NHWC", "HWIO", "NHWC"),
+        preferred_element_type=jnp.float32,
+    )
 
 
 def split_pair(values, axis):
@@ -89,9 +100,10 @@
                     term = taps[:, ro : ro + nrows, co : co + ncols, dr, dc, :]
                     acc = term if acc is None else acc + term
             phases_b.append(acc)
-        phases_a.append(jnp.stack(phases_b, axis=3))
+        phase = jnp.concatenate(phases_b, axis=-1).astype(jnp.bfloat16)
+        phases_a.append(phase.reshape(nf, nrows, 2 * ncols * outs))
     result = jnp.stack(phases_a, axis=2)
-    return result.astype(jnp.bfloat16).reshape(nf, 2 * nrows, 2 * ncols * outs)
+    return result.reshape(nf, 2 * nrows, 2 * ncols * outs)
 
 
 def layer(
@@ -161,8 +173,12 @@
         .astype(jnp.bfloat16)
         .reshape(nframes, nrows, ncols, chans)
     )
+    centre = cache_part + tap_row(activ, conv_weight[2, 1])
     activ_haloed = padded_2(activ, ((ROWS, 1),), 1)
-    conv_out = (cache_part + conv_rows(activ_haloed, conv_weight[2:])).astype(jnp.bfloat16)
+    edges = tap_row(activ_haloed[:, :nrows], conv_weight[2, 0]) + tap_row(
+        activ_haloed[:, 2:], conv_weight[2, 2]
+    )
+    conv_out = (centre + edges).astype(jnp.bfloat16)
     extended = padded_2(conv_out, ((ROWS, 1),), 1)
     return upsample_conv(extended, w_up)
 

time: 69.2 us -> 68.9 us (level)
  the two profiles are of different devices: /device:TPU:23 before, /device:TPU:5 now
where the time goes in v15:
time: 68.9 us; the launch traced here: 68.6 us
  starting transfers between devices  19.9 us (29%)
  waiting for transfers between devices  17.3 us (25%)
  matrix products  17 us (25%)
  other arithmetic  9.19 us (13%)
  local copies, waits for them, and re-layouts  4.42 us (6%)
  between operations  0.85 us (1%)
    ppermute x13, starting transfers between devices, exchange(): lax.ppermute(values, ROWS, [(i, i ^ mask) for i in range(size)])  10.5 us
    ppermute x13, waiting for transfers between devices, exchange(): lax.ppermute(values, ROWS, [(i, i ^ mask) for i in range(size)])  10.2 us
    ppermute x3, starting transfers between devices, padded_2(): lax.ppermute(jnp.where(even, first, last), axis, pairs + [(j, i) for i, j...  9.07 us
    ppermute x3, waiting for transfers between devices, padded_2(): lax.ppermute(jnp.where(even, first, last), axis, pairs + [(j, i) for i, j...  7.07 us
    conv_general_dilated x2, matrix products, conv_rows(): lax.conv_general_dilated(haloed[tstep:tstep + 1], weight[tstep], window_s...  4.14 us
    dot_general x10, matrix products, layer(): jnp.einsum('fqc,fkc->fqk', q_pair, piece, preferred_element_type=jnp.floa...  4.07 us
    dot_general x10, matrix products, layer(): jnp.einsum('fqk,fkc->fqc', e.astype(jnp.bfloat16), p, preferred_element_t...  3.32 us
    select_n x3, other arithmetic, padded_2(): jnp.where(even, first, last)  1.79 us
  transfers between devices with their start and end apart: 19, of which 4 were waited for; matrix products, arithmetic and copies ran while one was open for 26% of the time, Pallas kernels for 0%

profile of v15, /device:TPU:5, one launch (start us, length us, event | category | flops | bytes accessed | tf_op | source)
XLA Modules:
  0.0 68.6 jit_solution(10653722156021736391)
XLA Ops:
  0.0 1.1 %multiply_reduce_fusion.1 = f32[2,128]{1,0:T(2,128)S(1)} fusion(bf16[1,2,128,384]{3,2,1,0:T(8,128)(2,1)} %param.10), kind=kLoop, calls=%fused_computation.140 | loop fusion | flops 294656 | bytes 197632 | tf_op jit(solution)/shard_map/reduce_sum | solution.py:33
  1.2 1.1 %constant_dynamic-update-slice_fusion.4 = (bf16[1,768,384]{2,1,0:T(8,128)(2,1)S(1)}, bf16[1,256,384]{2,1,0:T(8,128)(2,1)S(1)}) fusion(f32[384]{0:T(512)} %param.11, f32[256]{0:T(256)S(1)} %rsqrt_bitcast_fusion, bf16[1,2,128,384]{3,2,1,0:T(8,128)(2,1)} %param.10), kind=kLoop, calls=%fused_computation.302 | loop fusion | flops 393215 | bytes 592384
  2.3 1.4 %collective-permute-start.2 = (bf16[1,128,384]{2,1,0:T(8,128)(2,1)S(1)}, bf16[1,128,384]{2,1,0:T(8,128)(2,1)S(1)}, u32[]{:S(2)}, u32[]{:S(2)}) collective-permute-start(bf16[1,128,384]{2,1,0:T(8,128)(2,1)S(1)} %get-tuple-element.54), channel_id=1, source_target_pairs={{0,4},{1,5},{2,6},{3,7},{4,0},{5,1},{6,2},{7,3},{8,12},{9,13},{10,... | collective-permute-start | bytes 294920 | tf_op jit(solution)/shard_map/ppermute | solution.py:47
  3.6 2.3 %collective-permute-start.3 = (bf16[1,128,384]{2,1,0:T(8,128)(2,1)S(1)}, bf16[1,128,384]{2,1,0:T(8,128)(2,1)S(1)}, u32[]{:S(2)}, u32[]{:S(2)}) collective-permute-start(bf16[1,128,384]{2,1,0:T(8,128)(2,1)S(1)} %get-tuple-element.54), channel_id=1, source_target_pairs={{0,8},{1,9},{2,10},{3,11},{4,12},{5,13},{6,14},{7,15},{8,0},{9,1},... | collective-permute-start | bytes 294920 | tf_op jit(solution)/shard_map/ppermute | solution.py:47
  6.2 1.7 %broadcast_select_fusion.3 = (bf16[2,1,128,384]{3,2,1,0:T(8,128)(2,1)}, bf16[2,1,128,384]{3,2,1,0:T(8,128)(2,1)S(1)}) fusion(pred[]{:T(512)S(6)} %eq.9, bf16[2,2,128,384]{3,2,1,0:T(8,128)(2,1)} %param.16), kind=kLoop, calls=%fused_computation.271 | loop fusion | flops 196608 | bytes 786433 | tf_op jit(solution)/shard_map/jit(_where)/select_n | solution.py:24
  7.9 4.9 %collective-permute-start = (bf16[2,1,128,384]{3,2,1,0:T(8,128)(2,1)}, bf16[2,1,128,384]{3,2,1,0:T(8,128)(2,1)S(1)}, u32[]{:S(2)}, u32[]{:S(2)}) collective-permute-start(bf16[2,1,128,384]{3,2,1,0:T(8,128)(2,1)} %get-tuple-element.41), channel_id=1, source_target_pairs={{1,2},{3,4},{5,6},{7,8},{9,10},{11,12},{13,14},{2,1},{4,3},{6,5},{... | collective-permute-start | bytes 589832 | tf_op jit(solution)/shard_map/ppermute | solution.py:23
  12.8 1.0 %fusion.103 = bf16[256,384]{1,0:T(8,128)(2,1)S(1)} fusion(bf16[1,2,128,384]{3,2,1,0:T(8,128)(2,1)} %param.10, f32[384]{0:T(512)} %param.11, f32[256]{0:T(256)S(1)} %rsqrt_bitcast_fusion), kind=kLoop, calls=%fused_computation.133 | loop fusion | flops 393216 | bytes 395776 | tf_op jit(solution)/shard_map/convert_element_type | solution.py:119
  13.8 1.6 %convert_bitcast_fusion = (bf16[1,256,384]{2,1,0:T(8,128)(2,1)S(1)}, bf16[1,256,384]{2,1,0:T(8,128)(2,1)S(1)}) fusion(bf16[384,384]{1,0:T(8,128)(2,1)} %param.13, bf16[256,384]{1,0:T(8,128)(2,1)S(1)} %fusion.103, bf16[384,384]{1,0:T(8,128)(2,1)} %param.12), kind=kOutput, calls=%fused_computation.291 | convolution fusion | flops 151486464 | bytes 1179648 | tf_op jit(solution)/shard_map/fqc,dc->fqd/dot_general | solution.py:135
  15.5 2.1 %collective-permute-start.10 = (bf16[1,256,384]{2,1,0:T(8,128)(2,1)S(1)}, bf16[1,256,384]{2,1,0:T(8,128)(2,1)S(1)}, u32[]{:S(2)}, u32[]{:S(2)}) collective-permute-start(bf16[1,256,384]{2,1,0:T(8,128)(2,1)S(1)} %pad_maximum_fusion.3), channel_id=1, source_target_pairs={{0,12},{1,13},{2,14},{3,15},{4,8},{5,9},{6,10},{7,11},{8,4},{9,5},... | collective-permute-start | bytes 589832 | tf_op jit(solution)/shard_map/ppermute | solution.py:47
  17.7 1.2 %collective-permute-start.9 = (bf16[1,256,384]{2,1,0:T(8,128)(2,1)S(1)}, bf16[1,256,384]{2,1,0:T(8,128)(2,1)S(1)}, u32[]{:S(2)}, u32[]{:S(2)}) collective-permute-start(bf16[1,256,384]{2,1,0:T(8,128)(2,1)S(1)} %pad_maximum_fusion.3), channel_id=1, source_target_pairs={{0,8},{1,9},{2,10},{3,11},{4,12},{5,13},{6,14},{7,15},{8,0},{9,1},... | collective-permute-start | bytes 589832 | tf_op jit(solution)/shard_map/ppermute | solution.py:47
  19.0 0.8 %collective-permute-start.6 = (bf16[1,768,384]{2,1,0:T(8,128)(2,1)S(1)}, bf16[1,768,384]{2,1,0:T(8,128)(2,1)S(1)}, u32[]{:S(2)}, u32[]{:S(2)}) collective-permute-start(bf16[1,768,384]{2,1,0:T(8,128)(2,1)S(1)} %constant_dynamic-update-slice_fusion), channel_id=1, source_target_pairs={{0,1},{1,0},{2,3},{3,2},{4,5},{5,4},{6,7},{7,6},{8,9},{9,8},{10,11... | collective-permute-start | bytes 1769480 | tf_op jit(solution)/shard_map/ppermute | solution.py:47
  19.8 0.6 convolution_bitcast_fusion.2
  20.6 0.7 collective-permute-start.8
  21.6 0.3 copy.106
  22.7 2.9 %fusion.28 = f32[2,8,17,384]{3,1,2,0:T(8,128)S(1)} fusion(bf16[3,3,3,384,384]{4,3,2,1,0:T(8,128)(2,1)} %param.18, bf16[4,1,7,2,384]{4,2,3,0,1:T(8,128)(2,1)S(1)} %slice.278, bf16[4,1,8,17,384]{4,2,3,0,1:T(8,128)(2,1)S(1)} %copy.42, pred[8,17]{0,1:T(8,128)(4,1)S(1)} %copy-done.6), kind=kOutput, calls=%fused_computation.46 | convolution fusion | flops 723449856 | bytes 3532936 | tf_op jit(solution)/shard_map/conv_general_dilated | solution.py:71
  25.7 0.3 convolution_bitcast_fusion.9
  26.1 0.5 collective-permute-start.14
  26.6 10.1 %collective-permute-done.9 = bf16[1,256,384]{2,1,0:T(8,128)(2,1)S(1)} collective-permute-done((bf16[1,256,384]{2,1,0:T(8,128)(2,1)S(1)}, bf16[1,256,384]{2,1,0:T(8,128)(2,1)S(1)}, u32[]{:S(2)}, u32[]{:S(2)}) %collective-permute-start.9) | collective-permute-done | bytes 196640 | tf_op jit(solution)/shard_map/ppermute | solution.py:47
  36.7 0.5 collective-permute-start.13
  37.3 0.3 convolution_bitcast_fusion.10
  37.6 0.3 convolution_bitcast_fusion.11
  38.2 0.3 convolution_bitcast_fusion.6
  38.5 0.3 convolution_bitcast_fusion.7
  38.9 0.6 collective-permute-start.11
  39.6 0.3 convolution_bitcast_fusion.8
  40.0 0.5 convolution_bitcast_fusion.4
  40.6 0.6 convolution_bitcast_fusion.1
  41.3 0.4 fusion.47
  41.8 0.5 fusion.48
  42.2 0.5 fusion.16
  43.9 0.4 fusion.19
  44.3 0.5 convolution_bitcast_fusion.3
  46.2 0.4 fusion.18
  46.8 0.4 convolution_bitcast_fusion.5
  47.3 0.4 multiply_reduce_fusion
  48.0 2.1 %collective-permute-start.15 = (bf16[1,1,128,384]{3,2,1,0:T(8,128)(2,1)S(1)}, bf16[1,1,128,384]{3,2,1,0:T(8,128)(2,1)S(1)}, u32[]{:S(2)}, u32[]{:S(2)}) collective-permute-start(bf16[1,1,128,384]{3,2,1,0:T(8,128)(2,1)S(1)} %get-tuple-element.51), channel_id=1, source_target_pairs={{1,2},{3,4},{5,6},{7,8},{9,10},{11,12},{13,14},{2,1},{4,3},{6,5},{... | collective-permute-start | bytes 294920 | tf_op jit(solution)/shard_map/ppermute | solution.py:23
  50.3 1.2 %fusion.25 = f32[2,8,17,384]{3,1,2,0:T(8,128)S(1)} fusion(f32[2,8,17,384]{3,1,2,0:T(8,128)S(1)} %fusion.28, bf16[3,3,3,384,384]{4,3,2,1,0:T(8,128)(2,1)S(1)} %bitcast.532, bf16[4,1,7,2,384]{4,2,3,0,1:T(8,128)(2,1)S(1)} %slice.276, bf16[4,1,8,17,384]{4,2,3,0,1:T(8,128)(2,1)S(1)} %copy.39, pred[8,17]{0,1:T(8,128)(4,1)S(1)} %copy-done.6), kind=kOutput, calls=%fused_computation.45 | convolution fusion | flops 723554304 | bytes 3959808 | tf_op jit(solution)/shard_map/conv_general_dilated | solution.py:71
  51.9 2.9 %collective-permute-done.15 = bf16[1,1,128,384]{3,2,1,0:T(8,128)(2,1)S(1)} collective-permute-done((bf16[1,1,128,384]{3,2,1,0:T(8,128)(2,1)S(1)}, bf16[1,1,128,384]{3,2,1,0:T(8,128)(2,1)S(1)}, u32[]{:S(2)}, u32[]{:S(2)}) %collective-permute-start.15) | collective-permute-done | bytes 98336 | tf_op jit(solution)/shard_map/ppermute | solution.py:23
  55.5 0.5 convolution_select_fusion
  56.0 0.5 fusion.9
  56.6 0.6 fusion.17
  57.3 2.1 %collective-permute-start.17 = (bf16[1,1,128,384]{3,2,1,0:T(8,128)(2,1)S(1)}, bf16[1,1,128,384]{3,2,1,0:T(8,128)(2,1)S(1)}, u32[]{:S(2)}, u32[]{:S(2)}) collective-permute-start(bf16[1,1,128,384]{3,2,1,0:T(8,128)(2,1)S(1)} %slice.309), channel_id=1, source_target_pairs={{1,2},{3,4},{5,6},{7,8},{9,10},{11,12},{13,14},{2,1},{4,3},{6,5},{... | collective-permute-start | bytes 294920 | tf_op jit(solution)/shard_map/ppermute | solution.py:23
  59.9 4.2 %collective-permute-done.17 = bf16[1,1,128,384]{3,2,1,0:T(8,128)(2,1)S(1)} collective-permute-done((bf16[1,1,128,384]{3,2,1,0:T(8,128)(2,1)S(1)}, bf16[1,1,128,384]{3,2,1,0:T(8,128)(2,1)S(1)}, u32[]{:S(2)}, u32[]{:S(2)}) %collective-permute-start.17) | collective-permute-done | bytes 98336 | tf_op jit(solution)/shard_map/ppermute | solution.py:23
  64.1 1.5 %convolution_bitcast_fusion = f32[1,4,130,3,3,192]{5,2,4,3,1,0:T(8,128)S(1)} fusion(bf16[3,3,384,192]{2,3,1,0:T(8,128)(2,1)S(1)} %copy-done, bf16[1,1,128,384]{3,2,1,0:T(8,128)(2,1)S(1)} %get-tuple-element.48, bf16[1,2,128,384]{3,2,1,0:T(8,128)(2,1)S(1)} %bitcast.508, bf16[1,1,128,384]{3,2,1,0:T(8,128)(2,1)S(1)} %get-tuple-element.47), kind=kOutput, calls=%fused_computation.6 | convolution fusion | flops 692490240 | bytes 5314560 | tf_op jit(solution)/shard_map/frwc,ijco->frwijo/dot_general | solution.py:88
  66.1 0.4 fusion.216
  66.8 0.6 pad_maximum_fusion.2
  67.3 0.4 copy.78
  67.7 0.9 %reshape.982 = bf16[1,4,49152]{2,1,0:T(4,128)(2,1)} reshape(bf16[1,2,2,49152]{3,2,1,0:T(2,128)(2,1)S(1)} %copy.78) | data formatting | bytes 786432 | tf_op jit(solution)/shard_map/reshape | solution.py:106
  (121 shorter events, 8.0 us)
Async XLA Ops:
  0.0 64.1 %copy-start = (bf16[3,3,384,192]{2,3,1,0:T(8,128)(2,1)S(1)}, bf16[3,3,384,192]{2,3,1,0:T(8,128)(2,1)}, u32[]{:S(2)}) copy-start(bf16[3,3,384,192]{2,3,1,0:T(8,128)(2,1)} %param.19) | copy-start | bytes 3981316
  2.3 13.2 %collective-permute-start.2 = (bf16[1,128,384]{2,1,0:T(8,128)(2,1)S(1)}, bf16[1,128,384]{2,1,0:T(8,128)(2,1)S(1)}, u32[]{:S(2)}, u32[]{:S(2)}) collective-permute-start(bf16[1,128,384]{2,1,0:T(8,128)(2,1)S(1)} %get-tuple-element.54), channel_id=1, source_target_pairs={{0,4},{1,5},{2,6},{3,7},{4,0},{5,1},{6,2},{7,3},{8,12},{9,13},{10,... | collective-permute-start | bytes 294920 | tf_op jit(solution)/shard_map/ppermute | solution.py:47
  3.6 14.1 %collective-permute-start.3 = (bf16[1,128,384]{2,1,0:T(8,128)(2,1)S(1)}, bf16[1,128,384]{2,1,0:T(8,128)(2,1)S(1)}, u32[]{:S(2)}, u32[]{:S(2)}) collective-permute-start(bf16[1,128,384]{2,1,0:T(8,128)(2,1)S(1)} %get-tuple-element.54), channel_id=1, source_target_pairs={{0,8},{1,9},{2,10},{3,11},{4,12},{5,13},{6,14},{7,15},{8,0},{9,1},... | collective-permute-start | bytes 294920 | tf_op jit(solution)/shard_map/ppermute | solution.py:47
  5.9 13.0 %collective-permute-start.4 = (bf16[1,128,384]{2,1,0:T(8,128)(2,1)S(1)}, bf16[1,128,384]{2,1,0:T(8,128)(2,1)S(1)}, u32[]{:S(2)}, u32[]{:S(2)}) collective-permute-start(bf16[1,128,384]{2,1,0:T(8,128)(2,1)S(1)} %get-tuple-element.54), channel_id=1, source_target_pairs={{0,12},{1,13},{2,14},{3,15},{4,8},{5,9},{6,10},{7,11},{8,4},{9,5},... | collective-permute-start | bytes 294920 | tf_op jit(solution)/shard_map/ppermute | solution.py:47
  5.9 9.5 %collective-permute-start.5 = (bf16[1,128,384]{2,1,0:T(8,128)(2,1)S(1)}, bf16[1,128,384]{2,1,0:T(8,128)(2,1)S(1)}, u32[]{:S(2)}, u32[]{:S(2)}) collective-permute-start(bf16[1,128,384]{2,1,0:T(8,128)(2,1)S(1)} %get-tuple-element.53), channel_id=1, source_target_pairs={{0,2},{1,3},{2,0},{3,1},{4,6},{5,7},{6,4},{7,5},{8,10},{9,11},{10,... | collective-permute-start | bytes 294920 | tf_op jit(solution)/shard_map/ppermute | solution.py:47
  7.9 12.7 %collective-permute-start = (bf16[2,1,128,384]{3,2,1,0:T(8,128)(2,1)}, bf16[2,1,128,384]{3,2,1,0:T(8,128)(2,1)S(1)}, u32[]{:S(2)}, u32[]{:S(2)}) collective-permute-start(bf16[2,1,128,384]{3,2,1,0:T(8,128)(2,1)} %get-tuple-element.41), channel_id=1, source_target_pairs={{1,2},{3,4},{5,6},{7,8},{9,10},{11,12},{13,14},{2,1},{4,3},{6,5},{... | collective-permute-start | bytes 589832 | tf_op jit(solution)/shard_map/ppermute | solution.py:23
  15.4 5.9 %collective-permute-start.1 = (bf16[2,1,128,384]{3,2,1,0:T(8,128)(2,1)S(1)}, bf16[2,1,128,384]{3,2,1,0:T(8,128)(2,1)S(1)}, u32[]{:S(2)}, u32[]{:S(2)}) collective-permute-start(bf16[2,1,128,384]{3,2,1,0:T(8,128)(2,1)S(1)} %get-tuple-element.42), channel_id=1, source_target_pairs={{0,1},{1,0},{2,3},{3,2},{4,5},{5,4},{6,7},{7,6},{8,9},{9,8},{10,11... | collective-permute-start | bytes 589832 | tf_op jit(solution)/shard_map/ppermute | solution.py:19
  15.5 10.2 %collective-permute-start.10 = (bf16[1,256,384]{2,1,0:T(8,128)(2,1)S(1)}, bf16[1,256,384]{2,1,0:T(8,128)(2,1)S(1)}, u32[]{:S(2)}, u32[]{:S(2)}) collective-permute-start(bf16[1,256,384]{2,1,0:T(8,128)(2,1)S(1)} %pad_maximum_fusion.3), channel_id=1, source_target_pairs={{0,12},{1,13},{2,14},{3,15},{4,8},{5,9},{6,10},{7,11},{8,4},{9,5},... | collective-permute-start | bytes 589832 | tf_op jit(solution)/shard_map/ppermute | solution.py:47
  17.7 19.0 %collective-permute-start.9 = (bf16[1,256,384]{2,1,0:T(8,128)(2,1)S(1)}, bf16[1,256,384]{2,1,0:T(8,128)(2,1)S(1)}, u32[]{:S(2)}, u32[]{:S(2)}) collective-permute-start(bf16[1,256,384]{2,1,0:T(8,128)(2,1)S(1)} %pad_maximum_fusion.3), channel_id=1, source_target_pairs={{0,8},{1,9},{2,10},{3,11},{4,12},{5,13},{6,14},{7,15},{8,0},{9,1},... | collective-permute-start | bytes 589832 | tf_op jit(solution)/shard_map/ppermute | solution.py:47
  19.0 21.6 %collective-permute-start.6 = (bf16[1,768,384]{2,1,0:T(8,128)(2,1)S(1)}, bf16[1,768,384]{2,1,0:T(8,128)(2,1)S(1)}, u32[]{:S(2)}, u32[]{:S(2)}) collective-permute-start(bf16[1,768,384]{2,1,0:T(8,128)(2,1)S(1)} %constant_dynamic-update-slice_fusion), channel_id=1, source_target_pairs={{0,1},{1,0},{2,3},{3,2},{4,5},{5,4},{6,7},{7,6},{8,9},{9,8},{10,11... | collective-permute-start | bytes 1769480 | tf_op jit(solution)/shard_map/ppermute | solution.py:47
  19.8 1.5 %copy-start.2 = (bf16[2,2,128,384]{3,2,1,0:T(8,128)(2,1)S(1)}, bf16[2,2,128,384]{3,2,1,0:T(8,128)(2,1)}, u32[]{:S(2)}) copy-start(bf16[2,2,128,384]{3,2,1,0:T(8,128)(2,1)} %param.16) | copy-start | bytes 1179652
  20.6 17.0 %collective-permute-start.8 = (bf16[1,256,384]{2,1,0:T(8,128)(2,1)S(1)}, bf16[1,256,384]{2,1,0:T(8,128)(2,1)S(1)}, u32[]{:S(2)}, u32[]{:S(2)}) collective-permute-start(bf16[1,256,384]{2,1,0:T(8,128)(2,1)S(1)} %pad_maximum_fusion.3), channel_id=1, source_target_pairs={{0,4},{1,5},{2,6},{3,7},{4,0},{5,1},{6,2},{7,3},{8,12},{9,13},{10,... | collective-permute-start | bytes 589832 | tf_op jit(solution)/shard_map/ppermute | solution.py:47
  21.3 17.5 %collective-permute-start.7 = (bf16[1,512,384]{2,1,0:T(8,128)(2,1)S(1)}, bf16[1,512,384]{2,1,0:T(8,128)(2,1)S(1)}, u32[]{:S(2)}, u32[]{:S(2)}) collective-permute-start(bf16[1,512,384]{2,1,0:T(8,128)(2,1)S(1)} %pad_maximum_fusion.1), channel_id=1, source_target_pairs={{0,2},{1,3},{2,0},{3,1},{4,6},{5,7},{6,4},{7,5},{8,10},{9,11},{10,... | collective-permute-start | bytes 1179656 | tf_op jit(solution)/shard_map/ppermute | solution.py:47
  21.6 1.1 %copy-start.6 = (pred[8,17]{0,1:T(8,128)(4,1)S(1)}, pred[8,17]{0,1:T(8,128)(4,1)}, u32[]{:S(2)}) copy-start(pred[8,17]{0,1:T(8,128)(4,1)} %constant.69) | copy-start | bytes 412
  26.1 12.1 %collective-permute-start.14 = (bf16[1,256,384]{2,1,0:T(8,128)(2,1)S(1)}, bf16[1,256,384]{2,1,0:T(8,128)(2,1)S(1)}, u32[]{:S(2)}, u32[]{:S(2)}) collective-permute-start(bf16[1,256,384]{2,1,0:T(8,128)(2,1)S(1)} %collective-permute-done.10), channel_id=1, source_target_pairs={{0,1},{1,0},{2,3},{3,2},{4,5},{5,4},{6,7},{7,6},{8,9},{9,8},{10,11... | collective-permute-start | bytes 589832 | tf_op jit(solution)/shard_map/ppermute | solution.py:47
  36.7 1.8 %collective-permute-start.13 = (bf16[1,256,384]{2,1,0:T(8,128)(2,1)S(1)}, bf16[1,256,384]{2,1,0:T(8,128)(2,1)S(1)}, u32[]{:S(2)}, u32[]{:S(2)}) collective-permute-start(bf16[1,256,384]{2,1,0:T(8,128)(2,1)S(1)} %collective-permute-done.9), channel_id=1, source_target_pairs={{0,1},{1,0},{2,3},{3,2},{4,5},{5,4},{6,7},{7,6},{8,9},{9,8},{10,11... | collective-permute-start | bytes 589832 | tf_op jit(solution)/shard_map/ppermute | solution.py:47
  38.1 1.5 %collective-permute-start.12 = (bf16[1,256,384]{2,1,0:T(8,128)(2,1)S(1)}, bf16[1,256,384]{2,1,0:T(8,128)(2,1)S(1)}, u32[]{:S(2)}, u32[]{:S(2)}) collective-permute-start(bf16[1,256,384]{2,1,0:T(8,128)(2,1)S(1)} %collective-permute-done.8), channel_id=1, source_target_pairs={{0,1},{1,0},{2,3},{3,2},{4,5},{5,4},{6,7},{7,6},{8,9},{9,8},{10,11... | collective-permute-start | bytes 589832 | tf_op jit(solution)/shard_map/ppermute | solution.py:47
  38.9 5.5 %collective-permute-start.11 = (bf16[1,512,384]{2,1,0:T(8,128)(2,1)S(1)}, bf16[1,512,384]{2,1,0:T(8,128)(2,1)S(1)}, u32[]{:S(2)}, u32[]{:S(2)}) collective-permute-start(bf16[1,512,384]{2,1,0:T(8,128)(2,1)S(1)} %collective-permute-done.7), channel_id=1, source_target_pairs={{0,1},{1,0},{2,3},{3,2},{4,5},{5,4},{6,7},{7,6},{8,9},{9,8},{10,11... | collective-permute-start | bytes 1179656 | tf_op jit(solution)/shard_map/ppermute | solution.py:47
  42.7 7.6 %slice-start = ((s8[7962624]{0:T(1024)(128)(4,1)}), s8[3768320]{0:T(1024)(128)(4,1)S(1)}, s32[]{:S(2)}) async-start(s8[7962624]{0:T(1024)(128)(4,1)} %bitcast.531), calls=%async_computation | async-start | bytes 7536640
  44.9 5.4 %slice-start.1 = ((s8[7962624]{0:T(1024)(128)(4,1)}), s8[4194304]{0:T(1024)(128)(4,1)S(1)}, s32[]{:S(2)}) async-start(s8[7962624]{0:T(1024)(128)(4,1)} %bitcast.531), calls=%async_computation.1 | async-start | bytes 8388608
  45.6 1.3 %copy-start.3 = (bf16[384,384]{1,0:T(8,128)(2,1)S(1)}, bf16[384,384]{1,0:T(8,128)(2,1)}, u32[]{:S(2)}) copy-start(bf16[384,384]{1,0:T(8,128)(2,1)} %param.14) | copy-start | bytes 884740
  46.1 1.1 %copy-start.1 = (bf16[1,2,128,384]{3,2,1,0:T(8,128)(2,1)S(1)}, bf16[1,2,128,384]{3,2,1,0:T(8,128)(2,1)}, u32[]{:S(2)}) copy-start(bf16[1,2,128,384]{3,2,1,0:T(8,128)(2,1)} %param.10) | copy-start | bytes 589828
  46.1 1.2 %copy-start.5 = (bf16[384,384]{1,0:T(8,128)(2,1)S(1)}, bf16[384,384]{1,0:T(8,128)(2,1)}, u32[]{:S(2)}) copy-start(bf16[384,384]{1,0:T(8,128)(2,1)} %param.15) | copy-start | bytes 884740
  46.5 1.2 %copy-start.4 = (f32[384]{0:T(512)S(1)}, f32[384]{0:T(512)}, u32[]{:S(2)}) copy-start(f32[384]{0:T(512)} %param.17) | copy-start | bytes 4612
  48.0 6.8 %collective-permute-start.15 = (bf16[1,1,128,384]{3,2,1,0:T(8,128)(2,1)S(1)}, bf16[1,1,128,384]{3,2,1,0:T(8,128)(2,1)S(1)}, u32[]{:S(2)}, u32[]{:S(2)}) collective-permute-start(bf16[1,1,128,384]{3,2,1,0:T(8,128)(2,1)S(1)} %get-tuple-element.51), channel_id=1, source_target_pairs={{1,2},{3,4},{5,6},{7,8},{9,10},{11,12},{13,14},{2,1},{4,3},{6,5},{... | collective-permute-start | bytes 294920 | tf_op jit(solution)/shard_map/ppermute | solution.py:23
  50.1 4.7 %collective-permute-start.16 = (bf16[1,1,128,384]{3,2,1,0:T(8,128)(2,1)S(1)}, bf16[1,1,128,384]{3,2,1,0:T(8,128)(2,1)S(1)}, u32[]{:S(2)}, u32[]{:S(2)}) collective-permute-start(bf16[1,1,128,384]{3,2,1,0:T(8,128)(2,1)S(1)} %get-tuple-element.52), channel_id=1, source_target_pairs={{0,1},{1,0},{2,3},{3,2},{4,5},{5,4},{6,7},{7,6},{8,9},{9,8},{10,11... | collective-permute-start | bytes 294920 | tf_op jit(solution)/shard_map/ppermute | solution.py:19
  57.3 6.8 %collective-permute-start.17 = (bf16[1,1,128,384]{3,2,1,0:T(8,128)(2,1)S(1)}, bf16[1,1,128,384]{3,2,1,0:T(8,128)(2,1)S(1)}, u32[]{:S(2)}, u32[]{:S(2)}) collective-permute-start(bf16[1,1,128,384]{3,2,1,0:T(8,128)(2,1)S(1)} %slice.309), channel_id=1, source_target_pairs={{1,2},{3,4},{5,6},{7,8},{9,10},{11,12},{13,14},{2,1},{4,3},{6,5},{... | collective-permute-start | bytes 294920 | tf_op jit(solution)/shard_map/ppermute | solution.py:23
  59.5 4.6 %collective-permute-start.18 = (bf16[1,1,128,384]{3,2,1,0:T(8,128)(2,1)S(1)}, bf16[1,1,128,384]{3,2,1,0:T(8,128)(2,1)S(1)}, u32[]{:S(2)}, u32[]{:S(2)}) collective-permute-start(bf16[1,1,128,384]{3,2,1,0:T(8,128)(2,1)S(1)} %slice.310), channel_id=1, source_target_pairs={{0,1},{1,0},{2,3},{3,2},{4,5},{5,4},{6,7},{7,6},{8,9},{9,8},{10,11... | collective-permute-start | bytes 294920 | tf_op jit(solution)/shard_map/ppermute | solution.py:19

commit v16 on v15

--- a/solution.py
+++ b/solution.py
@@ -16,12 +16,12 @@
         even = (lax.axis_index(axis) % 2) == 0
         first = lax.slice_in_dim(array, 0, width, axis=dim)
         last = lax.slice_in_dim(array, array.shape[dim] - width, array.shape[dim], axis=dim)
-        on_chip = lax.ppermute(
-            jnp.where(even, last, first), axis, [(i, i ^ 1) for i in range(size)]
-        )
         pairs = [(i, i + 1) for i in range(1, size - 1, 2)]
         across = lax.ppermute(
             jnp.where(even, first, last), axis, pairs + [(j, i) for i, j in pairs]
+        )
+        on_chip = lax.ppermute(
+            jnp.where(even, last, first), axis, [(i, i ^ 1) for i in range(size)]
         )
         before = jnp.where(even, across, on_chip)
         after = jnp.where(even, on_chip, across)
@@ -100,10 +100,9 @@
                     term = taps[:, ro : ro + nrows, co : co + ncols, dr, dc, :]
                     acc = term if acc is None else acc + term
             phases_b.append(acc)
-        phase = jnp.concatenate(phases_b, axis=-1).astype(jnp.bfloat16)
-        phases_a.append(phase.reshape(nf, nrows, 2 * ncols * outs))
+        phases_a.append(jnp.concatenate(phases_b, axis=-1))
     result = jnp.stack(phases_a, axis=2)
-    return result.reshape(nf, 2 * nrows, 2 * ncols * outs)
+    return result.astype(jnp.bfloat16).reshape(nf, 2 * nrows, 2 * ncols * outs)
 
 
 def layer(
@@ -137,11 +136,20 @@
     count = queries.shape[1]
     groups = [[mine[0], pieces[len(mine)]], mine[1:], pieces[len(mine) + 1 :]]
     top = denom = mixed_in = None
-    for group in groups:
+    for number, group in enumerate(groups):
         scores = []
         for piece in group:
-            both = jnp.einsum("fqc,fkc->fqk", q_pair, piece, preferred_element_type=jnp.float32)
-            scores.append((both[:, :count] + both[:, count:]) * scale)
+            if number + 1 < len(groups):
+                both = jnp.einsum("fqc,fkc->fqk", q_pair, piece, preferred_element_type=jnp.float32)
+                scores.append((both[:, :count] + both[:, count:]) * scale)
+            else:
+                scores.append(
+                    jnp.einsum(
+                        "fqc,fkc->fqk", q_pair[:, :count], piece,
+                        preferred_element_type=jnp.float32,
+                    )
+                    * scale
+                )
         peak = jnp.max(jnp.stack([jnp.max(s, axis=-1) for s in scores], axis=-1), axis=-1)
         new_top = peak[..., None] if top is None else jnp.maximum(top, peak[..., None])
         expos = [jnp.exp(s - new_top) for s in scores]

time: 68.9 us -> 67.2 us (0.975)
  other arithmetic: 9.19 us -> 8.37 us
    dot_general x10 -> x6, matrix products: 4.07 us -> 2.63 us  [layer(): jnp.einsum('fqc,fkc->fqk', q_pair, piece, preferred_element_type=jnp.floa...]
    dot_general x0 -> x4, matrix products: none -> 1.22 us  [layer(): jnp.einsum('fqc,fkc->fqk', q_pair[:, :count], piece, preferred_element_ty...]
    reshape x1 -> x0, local copies, waits for them, and re-layouts: 0.9 us -> none  [upsample_conv(): return result.reshape(nf, 2 * nrows, 2 * ncols * outs)]
    convert_element_type x2 -> x1, local copies, waits for them, and re-layouts: 0.11 us -> 0.89 us  [upsample_conv(): return result.astype(jnp.bfloat16).reshape(nf, 2 * nrows, 2 * ncols * outs)]
  transfers between devices with their start and end apart: 19 -> 19, of which waited for: 4 -> 3; matrix products, arithmetic and copies ran while one was open for 26% -> 26% of each run, Pallas kernels for 0% -> 0%
where the time goes in v16:
time: 67.2 us; the launch traced here: 66.9 us
  starting transfers between devices  19.6 us (29%)
  waiting for transfers between devices  17.5 us (26%)
  matrix products  16.8 us (25%)
  other arithmetic  8.37 us (12%)
  local copies, waits for them, and re-layouts  3.84 us (6%)
  between operations  0.85 us (1%)
    ppermute x13, starting transfers between devices, exchange(): lax.ppermute(values, ROWS, [(i, i ^ mask) for i in range(size)])  10.5 us
    ppermute x13, waiting for transfers between devices, exchange(): lax.ppermute(values, ROWS, [(i, i ^ mask) for i in range(size)])  10.1 us
    ppermute x3, starting transfers between devices, padded_2(): lax.ppermute(jnp.where(even, first, last), axis, pairs + [(j, i) for i, j...  8.89 us
    ppermute x3, waiting for transfers between devices, padded_2(): lax.ppermute(jnp.where(even, first, last), axis, pairs + [(j, i) for i, j...  7.37 us
    conv_general_dilated x2, matrix products, conv_rows(): lax.conv_general_dilated(haloed[tstep:tstep + 1], weight[tstep], window_s...  4.13 us
    dot_general x10, matrix products, layer(): jnp.einsum('fqk,fkc->fqc', e.astype(jnp.bfloat16), p, preferred_element_t...  3.3 us
    dot_general x6, matrix products, layer(): jnp.einsum('fqc,fkc->fqk', q_pair, piece, preferred_element_type=jnp.floa...  2.63 us
    select_n x3, other arithmetic, padded_2(): jnp.where(even, first, last)  1.79 us
  transfers between devices with their start and end apart: 19, of which 3 were waited for; matrix products, arithmetic and copies ran while one was open for 26% of the time, Pallas kernels for 0%

profile of v16, /device:TPU:5, one launch (start us, length us, event | category | flops | bytes accessed | tf_op | source)
XLA Modules:
  0.0 66.9 jit_solution(2862322383235883303)
XLA Ops:
  0.0 1.1 %multiply_reduce_fusion.1 = f32[2,128]{1,0:T(2,128)S(1)} fusion(bf16[1,2,128,384]{3,2,1,0:T(8,128)(2,1)} %param.10), kind=kLoop, calls=%fused_computation.138 | loop fusion | flops 294656 | bytes 197632 | tf_op jit(solution)/shard_map/reduce_sum | solution.py:33
  1.2 1.1 %constant_dynamic-update-slice_fusion.4 = (bf16[1,768,384]{2,1,0:T(8,128)(2,1)S(1)}, bf16[1,256,384]{2,1,0:T(8,128)(2,1)S(1)}) fusion(f32[384]{0:T(512)} %param.11, f32[256]{0:T(256)S(1)} %rsqrt_bitcast_fusion, bf16[1,2,128,384]{3,2,1,0:T(8,128)(2,1)} %param.10), kind=kLoop, calls=%fused_computation.289 | loop fusion | flops 393215 | bytes 592384
  2.3 1.4 %collective-permute-start.2 = (bf16[1,128,384]{2,1,0:T(8,128)(2,1)S(1)}, bf16[1,128,384]{2,1,0:T(8,128)(2,1)S(1)}, u32[]{:S(2)}, u32[]{:S(2)}) collective-permute-start(bf16[1,128,384]{2,1,0:T(8,128)(2,1)S(1)} %get-tuple-element.54), channel_id=1, source_target_pairs={{0,4},{1,5},{2,6},{3,7},{4,0},{5,1},{6,2},{7,3},{8,12},{9,13},{10,... | collective-permute-start | bytes 294920 | tf_op jit(solution)/shard_map/ppermute | solution.py:47
  3.6 2.3 %collective-permute-start.3 = (bf16[1,128,384]{2,1,0:T(8,128)(2,1)S(1)}, bf16[1,128,384]{2,1,0:T(8,128)(2,1)S(1)}, u32[]{:S(2)}, u32[]{:S(2)}) collective-permute-start(bf16[1,128,384]{2,1,0:T(8,128)(2,1)S(1)} %get-tuple-element.54), channel_id=1, source_target_pairs={{0,8},{1,9},{2,10},{3,11},{4,12},{5,13},{6,14},{7,15},{8,0},{9,1},... | collective-permute-start | bytes 294920 | tf_op jit(solution)/shard_map/ppermute | solution.py:47
  6.2 1.7 %broadcast_select_fusion.3 = (bf16[2,1,128,384]{3,2,1,0:T(8,128)(2,1)}, bf16[2,1,128,384]{3,2,1,0:T(8,128)(2,1)S(1)}) fusion(pred[]{:T(512)S(6)} %eq.9, bf16[2,2,128,384]{3,2,1,0:T(8,128)(2,1)} %param.16), kind=kLoop, calls=%fused_computation.262 | loop fusion | flops 196608 | bytes 786433 | tf_op jit(solution)/shard_map/jit(_where)/select_n | solution.py:21
  7.9 4.9 %collective-permute-start = (bf16[2,1,128,384]{3,2,1,0:T(8,128)(2,1)}, bf16[2,1,128,384]{3,2,1,0:T(8,128)(2,1)S(1)}, u32[]{:S(2)}, u32[]{:S(2)}) collective-permute-start(bf16[2,1,128,384]{3,2,1,0:T(8,128)(2,1)} %get-tuple-element.43), channel_id=1, source_target_pairs={{1,2},{3,4},{5,6},{7,8},{9,10},{11,12},{13,14},{2,1},{4,3},{6,5},{... | collective-permute-start | bytes 589832 | tf_op jit(solution)/shard_map/ppermute | solution.py:20
  12.8 1.0 %fusion.102 = bf16[256,384]{1,0:T(8,128)(2,1)S(1)} fusion(bf16[1,2,128,384]{3,2,1,0:T(8,128)(2,1)} %param.10, f32[384]{0:T(512)} %param.11, f32[256]{0:T(256)S(1)} %rsqrt_bitcast_fusion), kind=kLoop, calls=%fused_computation.131 | loop fusion | flops 393216 | bytes 395776 | tf_op jit(solution)/shard_map/convert_element_type | solution.py:118
  13.8 1.6 %fusion.170 = (bf16[1,256,384]{2,1,0:T(8,128)(2,1)S(1)}, bf16[256,384]{1,0:T(8,128)(2,1)S(1)}) fusion(bf16[384,384]{1,0:T(8,128)(2,1)} %param.13, bf16[256,384]{1,0:T(8,128)(2,1)S(1)} %fusion.102, bf16[384,384]{1,0:T(8,128)(2,1)} %param.12), kind=kOutput, calls=%fused_computation.235 | convolution fusion | flops 151486464 | bytes 1179648 | tf_op jit(solution)/shard_map/fqc,dc->fqd/dot_general | solution.py:134
  15.5 2.1 %collective-permute-start.10 = (bf16[1,256,384]{2,1,0:T(8,128)(2,1)S(1)}, bf16[1,256,384]{2,1,0:T(8,128)(2,1)S(1)}, u32[]{:S(2)}, u32[]{:S(2)}) collective-permute-start(bf16[1,256,384]{2,1,0:T(8,128)(2,1)S(1)} %pad_maximum_fusion.3), channel_id=1, source_target_pairs={{0,12},{1,13},{2,14},{3,15},{4,8},{5,9},{6,10},{7,11},{8,4},{9,5},... | collective-permute-start | bytes 589832 | tf_op jit(solution)/shard_map/ppermute | solution.py:47
  17.7 1.2 %collective-permute-start.9 = (bf16[1,256,384]{2,1,0:T(8,128)(2,1)S(1)}, bf16[1,256,384]{2,1,0:T(8,128)(2,1)S(1)}, u32[]{:S(2)}, u32[]{:S(2)}) collective-permute-start(bf16[1,256,384]{2,1,0:T(8,128)(2,1)S(1)} %pad_maximum_fusion.3), channel_id=1, source_target_pairs={{0,8},{1,9},{2,10},{3,11},{4,12},{5,13},{6,14},{7,15},{8,0},{9,1},... | collective-permute-start | bytes 589832 | tf_op jit(solution)/shard_map/ppermute | solution.py:47
  19.0 0.8 %collective-permute-start.6 = (bf16[1,768,384]{2,1,0:T(8,128)(2,1)S(1)}, bf16[1,768,384]{2,1,0:T(8,128)(2,1)S(1)}, u32[]{:S(2)}, u32[]{:S(2)}) collective-permute-start(bf16[1,768,384]{2,1,0:T(8,128)(2,1)S(1)} %constant_dynamic-update-slice_fusion), channel_id=1, source_target_pairs={{0,1},{1,0},{2,3},{3,2},{4,5},{5,4},{6,7},{7,6},{8,9},{9,8},{10,11... | collective-permute-start | bytes 1769480 | tf_op jit(solution)/shard_map/ppermute | solution.py:47
  19.8 0.6 convolution_bitcast_fusion.2
  20.6 0.7 collective-permute-start.8
  21.6 0.3 copy.105
  22.2 0.3 copy.104
  22.7 2.9 %fusion.28 = f32[2,8,17,384]{3,1,2,0:T(8,128)S(1)} fusion(bf16[3,3,3,384,384]{4,3,2,1,0:T(8,128)(2,1)} %param.18, bf16[4,1,7,2,384]{4,2,3,0,1:T(8,128)(2,1)S(1)} %slice.246, bf16[4,1,8,17,384]{4,2,3,0,1:T(8,128)(2,1)S(1)} %copy.41, pred[8,17]{0,1:T(8,128)(4,1)S(1)} %copy-done.6), kind=kOutput, calls=%fused_computation.46 | convolution fusion | flops 723449856 | bytes 3532936 | tf_op jit(solution)/shard_map/conv_general_dilated | solution.py:71
  25.7 0.3 convolution_bitcast_fusion.5
  26.1 0.5 collective-permute-start.14
  26.6 10.1 %collective-permute-done.9 = bf16[1,256,384]{2,1,0:T(8,128)(2,1)S(1)} collective-permute-done((bf16[1,256,384]{2,1,0:T(8,128)(2,1)S(1)}, bf16[1,256,384]{2,1,0:T(8,128)(2,1)S(1)}, u32[]{:S(2)}, u32[]{:S(2)}) %collective-permute-start.9) | collective-permute-done | bytes 196640 | tf_op jit(solution)/shard_map/ppermute | solution.py:47
  36.7 0.5 collective-permute-start.13
  37.3 0.3 convolution_bitcast_fusion.6
  37.6 0.3 convolution_bitcast_fusion.7
  38.2 0.3 fusion.246
  38.4 0.6 collective-permute-start.11
  39.0 0.5 convolution_bitcast_fusion.3
  40.2 0.6 convolution_bitcast_fusion.1
  40.9 0.4 fusion.47
  41.4 0.5 fusion.48
  41.8 0.5 fusion.16
  42.9 0.3 fusion.184
  43.2 0.3 fusion.187
  43.5 0.4 fusion.19
  43.9 0.4 fusion.248
  45.6 0.4 fusion.18
  46.1 0.4 convolution_bitcast_fusion.4
  46.7 0.4 multiply_reduce_fusion
  47.3 2.1 %collective-permute-start.15 = (bf16[1,1,128,384]{3,2,1,0:T(8,128)(2,1)S(1)}, bf16[1,1,128,384]{3,2,1,0:T(8,128)(2,1)S(1)}, u32[]{:S(2)}, u32[]{:S(2)}) collective-permute-start(bf16[1,1,128,384]{3,2,1,0:T(8,128)(2,1)S(1)} %get-tuple-element.51), channel_id=1, source_target_pairs={{1,2},{3,4},{5,6},{7,8},{9,10},{11,12},{13,14},{2,1},{4,3},{6,5},{... | collective-permute-start | bytes 294920 | tf_op jit(solution)/shard_map/ppermute | solution.py:20
  49.6 1.2 %fusion.25 = f32[2,8,17,384]{3,1,2,0:T(8,128)S(1)} fusion(f32[2,8,17,384]{3,1,2,0:T(8,128)S(1)} %fusion.28, bf16[3,3,3,384,384]{4,3,2,1,0:T(8,128)(2,1)S(1)} %bitcast.527, bf16[4,1,7,2,384]{4,2,3,0,1:T(8,128)(2,1)S(1)} %slice.244, bf16[4,1,8,17,384]{4,2,3,0,1:T(8,128)(2,1)S(1)} %copy.38, pred[8,17]{0,1:T(8,128)(4,1)S(1)} %copy-done.6), kind=kOutput, calls=%fused_computation.45 | convolution fusion | flops 723554304 | bytes 3959808 | tf_op jit(solution)/shard_map/conv_general_dilated | solution.py:71
  51.2 3.0 %collective-permute-done.15 = bf16[1,1,128,384]{3,2,1,0:T(8,128)(2,1)S(1)} collective-permute-done((bf16[1,1,128,384]{3,2,1,0:T(8,128)(2,1)S(1)}, bf16[1,1,128,384]{3,2,1,0:T(8,128)(2,1)S(1)}, u32[]{:S(2)}, u32[]{:S(2)}) %collective-permute-start.15) | collective-permute-done | bytes 98336 | tf_op jit(solution)/shard_map/ppermute | solution.py:20
  54.3 0.3 copy.106
  54.8 0.5 convolution_select_fusion
  55.4 0.5 fusion.9
  55.9 0.5 fusion.17
  56.6 1.9 %collective-permute-start.17 = (bf16[1,1,128,384]{3,2,1,0:T(8,128)(2,1)S(1)}, bf16[1,1,128,384]{3,2,1,0:T(8,128)(2,1)S(1)}, u32[]{:S(2)}, u32[]{:S(2)}) collective-permute-start(bf16[1,1,128,384]{3,2,1,0:T(8,128)(2,1)S(1)} %slice.269), channel_id=1, source_target_pairs={{1,2},{3,4},{5,6},{7,8},{9,10},{11,12},{13,14},{2,1},{4,3},{6,5},{... | collective-permute-start | bytes 294920 | tf_op jit(solution)/shard_map/ppermute | solution.py:20
  59.1 4.4 %collective-permute-done.17 = bf16[1,1,128,384]{3,2,1,0:T(8,128)(2,1)S(1)} collective-permute-done((bf16[1,1,128,384]{3,2,1,0:T(8,128)(2,1)S(1)}, bf16[1,1,128,384]{3,2,1,0:T(8,128)(2,1)S(1)}, u32[]{:S(2)}, u32[]{:S(2)}) %collective-permute-start.17) | collective-permute-done | bytes 98336 | tf_op jit(solution)/shard_map/ppermute | solution.py:20
  63.5 1.5 %convolution_bitcast_fusion = f32[1,4,130,3,3,192]{5,2,4,3,1,0:T(8,128)S(1)} fusion(bf16[3,3,384,192]{2,3,1,0:T(8,128)(2,1)S(1)} %copy-done, bf16[1,1,128,384]{3,2,1,0:T(8,128)(2,1)S(1)} %get-tuple-element.48, bf16[1,2,128,384]{3,2,1,0:T(8,128)(2,1)S(1)} %bitcast.503, bf16[1,1,128,384]{3,2,1,0:T(8,128)(2,1)S(1)} %get-tuple-element.47), kind=kOutput, calls=%fused_computation.6 | convolution fusion | flops 692490240 | bytes 5314560 | tf_op jit(solution)/shard_map/frwc,ijco->frwijo/dot_general | solution.py:88
  65.0 0.4 fusion.208
  66.0 0.9 %convert_element_type.166 = bf16[1,4,49152]{2,1,0:T(4,128)(2,1)} reshape(bf16[1,2,2,128,384]{4,3,2,1,0:T(8,128)(2,1)S(1)} %copy.77) | data formatting | bytes 786432 | tf_op jit(solution)/shard_map/convert_element_type | solution.py:105
  (114 shorter events, 6.8 us)
Async XLA Ops:
  0.0 63.5 %copy-start = (bf16[3,3,384,192]{2,3,1,0:T(8,128)(2,1)S(1)}, bf16[3,3,384,192]{2,3,1,0:T(8,128)(2,1)}, u32[]{:S(2)}) copy-start(bf16[3,3,384,192]{2,3,1,0:T(8,128)(2,1)} %param.19) | copy-start | bytes 3981316
  2.3 13.2 %collective-permute-start.2 = (bf16[1,128,384]{2,1,0:T(8,128)(2,1)S(1)}, bf16[1,128,384]{2,1,0:T(8,128)(2,1)S(1)}, u32[]{:S(2)}, u32[]{:S(2)}) collective-permute-start(bf16[1,128,384]{2,1,0:T(8,128)(2,1)S(1)} %get-tuple-element.54), channel_id=1, source_target_pairs={{0,4},{1,5},{2,6},{3,7},{4,0},{5,1},{6,2},{7,3},{8,12},{9,13},{10,... | collective-permute-start | bytes 294920 | tf_op jit(solution)/shard_map/ppermute | solution.py:47
  3.6 14.1 %collective-permute-start.3 = (bf16[1,128,384]{2,1,0:T(8,128)(2,1)S(1)}, bf16[1,128,384]{2,1,0:T(8,128)(2,1)S(1)}, u32[]{:S(2)}, u32[]{:S(2)}) collective-permute-start(bf16[1,128,384]{2,1,0:T(8,128)(2,1)S(1)} %get-tuple-element.54), channel_id=1, source_target_pairs={{0,8},{1,9},{2,10},{3,11},{4,12},{5,13},{6,14},{7,15},{8,0},{9,1},... | collective-permute-start | bytes 294920 | tf_op jit(solution)/shard_map/ppermute | solution.py:47
  5.9 13.0 %collective-permute-start.4 = (bf16[1,128,384]{2,1,0:T(8,128)(2,1)S(1)}, bf16[1,128,384]{2,1,0:T(8,128)(2,1)S(1)}, u32[]{:S(2)}, u32[]{:S(2)}) collective-permute-start(bf16[1,128,384]{2,1,0:T(8,128)(2,1)S(1)} %get-tuple-element.54), channel_id=1, source_target_pairs={{0,12},{1,13},{2,14},{3,15},{4,8},{5,9},{6,10},{7,11},{8,4},{9,5},... | collective-permute-start | bytes 294920 | tf_op jit(solution)/shard_map/ppermute | solution.py:47
  5.9 9.5 %collective-permute-start.5 = (bf16[1,128,384]{2,1,0:T(8,128)(2,1)S(1)}, bf16[1,128,384]{2,1,0:T(8,128)(2,1)S(1)}, u32[]{:S(2)}, u32[]{:S(2)}) collective-permute-start(bf16[1,128,384]{2,1,0:T(8,128)(2,1)S(1)} %get-tuple-element.53), channel_id=1, source_target_pairs={{0,2},{1,3},{2,0},{3,1},{4,6},{5,7},{6,4},{7,5},{8,10},{9,11},{10,... | collective-permute-start | bytes 294920 | tf_op jit(solution)/shard_map/ppermute | solution.py:47
  7.9 12.7 %collective-permute-start = (bf16[2,1,128,384]{3,2,1,0:T(8,128)(2,1)}, bf16[2,1,128,384]{3,2,1,0:T(8,128)(2,1)S(1)}, u32[]{:S(2)}, u32[]{:S(2)}) collective-permute-start(bf16[2,1,128,384]{3,2,1,0:T(8,128)(2,1)} %get-tuple-element.43), channel_id=1, source_target_pairs={{1,2},{3,4},{5,6},{7,8},{9,10},{11,12},{13,14},{2,1},{4,3},{6,5},{... | collective-permute-start | bytes 589832 | tf_op jit(solution)/shard_map/ppermute | solution.py:20
  15.4 5.9 %collective-permute-start.1 = (bf16[2,1,128,384]{3,2,1,0:T(8,128)(2,1)S(1)}, bf16[2,1,128,384]{3,2,1,0:T(8,128)(2,1)S(1)}, u32[]{:S(2)}, u32[]{:S(2)}) collective-permute-start(bf16[2,1,128,384]{3,2,1,0:T(8,128)(2,1)S(1)} %get-tuple-element.44), channel_id=1, source_target_pairs={{0,1},{1,0},{2,3},{3,2},{4,5},{5,4},{6,7},{7,6},{8,9},{9,8},{10,11... | collective-permute-start | bytes 589832 | tf_op jit(solution)/shard_map/ppermute | solution.py:23
  15.5 10.2 %collective-permute-start.10 = (bf16[1,256,384]{2,1,0:T(8,128)(2,1)S(1)}, bf16[1,256,384]{2,1,0:T(8,128)(2,1)S(1)}, u32[]{:S(2)}, u32[]{:S(2)}) collective-permute-start(bf16[1,256,384]{2,1,0:T(8,128)(2,1)S(1)} %pad_maximum_fusion.3), channel_id=1, source_target_pairs={{0,12},{1,13},{2,14},{3,15},{4,8},{5,9},{6,10},{7,11},{8,4},{9,5},... | collective-permute-start | bytes 589832 | tf_op jit(solution)/shard_map/ppermute | solution.py:47
  17.7 19.0 %collective-permute-start.9 = (bf16[1,256,384]{2,1,0:T(8,128)(2,1)S(1)}, bf16[1,256,384]{2,1,0:T(8,128)(2,1)S(1)}, u32[]{:S(2)}, u32[]{:S(2)}) collective-permute-start(bf16[1,256,384]{2,1,0:T(8,128)(2,1)S(1)} %pad_maximum_fusion.3), channel_id=1, source_target_pairs={{0,8},{1,9},{2,10},{3,11},{4,12},{5,13},{6,14},{7,15},{8,0},{9,1},... | collective-permute-start | bytes 589832 | tf_op jit(solution)/shard_map/ppermute | solution.py:47
  19.0 21.2 %collective-permute-start.6 = (bf16[1,768,384]{2,1,0:T(8,128)(2,1)S(1)}, bf16[1,768,384]{2,1,0:T(8,128)(2,1)S(1)}, u32[]{:S(2)}, u32[]{:S(2)}) collective-permute-start(bf16[1,768,384]{2,1,0:T(8,128)(2,1)S(1)} %constant_dynamic-update-slice_fusion), channel_id=1, source_target_pairs={{0,1},{1,0},{2,3},{3,2},{4,5},{5,4},{6,7},{7,6},{8,9},{9,8},{10,11... | collective-permute-start | bytes 1769480 | tf_op jit(solution)/shard_map/ppermute | solution.py:47
  19.8 1.5 %copy-start.2 = (bf16[2,2,128,384]{3,2,1,0:T(8,128)(2,1)S(1)}, bf16[2,2,128,384]{3,2,1,0:T(8,128)(2,1)}, u32[]{:S(2)}) copy-start(bf16[2,2,128,384]{3,2,1,0:T(8,128)(2,1)} %param.16) | copy-start | bytes 1179652
  20.6 17.0 %collective-permute-start.8 = (bf16[1,256,384]{2,1,0:T(8,128)(2,1)S(1)}, bf16[1,256,384]{2,1,0:T(8,128)(2,1)S(1)}, u32[]{:S(2)}, u32[]{:S(2)}) collective-permute-start(bf16[1,256,384]{2,1,0:T(8,128)(2,1)S(1)} %pad_maximum_fusion.3), channel_id=1, source_target_pairs={{0,4},{1,5},{2,6},{3,7},{4,0},{5,1},{6,2},{7,3},{8,12},{9,13},{10,... | collective-permute-start | bytes 589832 | tf_op jit(solution)/shard_map/ppermute | solution.py:47
  21.3 17.1 %collective-permute-start.7 = (bf16[1,512,384]{2,1,0:T(8,128)(2,1)S(1)}, bf16[1,512,384]{2,1,0:T(8,128)(2,1)S(1)}, u32[]{:S(2)}, u32[]{:S(2)}) collective-permute-start(bf16[1,512,384]{2,1,0:T(8,128)(2,1)S(1)} %pad_maximum_fusion.1), channel_id=1, source_target_pairs={{0,2},{1,3},{2,0},{3,1},{4,6},{5,7},{6,4},{7,5},{8,10},{9,11},{10,... | collective-permute-start | bytes 1179656 | tf_op jit(solution)/shard_map/ppermute | solution.py:47
  21.6 1.1 %copy-start.6 = (pred[8,17]{0,1:T(8,128)(4,1)S(1)}, pred[8,17]{0,1:T(8,128)(4,1)}, u32[]{:S(2)}) copy-start(pred[8,17]{0,1:T(8,128)(4,1)} %constant.69) | copy-start | bytes 412
  26.1 12.1 %collective-permute-start.14 = (bf16[1,256,384]{2,1,0:T(8,128)(2,1)S(1)}, bf16[1,256,384]{2,1,0:T(8,128)(2,1)S(1)}, u32[]{:S(2)}, u32[]{:S(2)}) collective-permute-start(bf16[1,256,384]{2,1,0:T(8,128)(2,1)S(1)} %collective-permute-done.10), channel_id=1, source_target_pairs={{0,1},{1,0},{2,3},{3,2},{4,5},{5,4},{6,7},{7,6},{8,9},{9,8},{10,11... | collective-permute-start | bytes 589832 | tf_op jit(solution)/shard_map/ppermute | solution.py:47
  36.7 2.7 %collective-permute-start.13 = (bf16[1,256,384]{2,1,0:T(8,128)(2,1)S(1)}, bf16[1,256,384]{2,1,0:T(8,128)(2,1)S(1)}, u32[]{:S(2)}, u32[]{:S(2)}) collective-permute-start(bf16[1,256,384]{2,1,0:T(8,128)(2,1)S(1)} %collective-permute-done.9), channel_id=1, source_target_pairs={{0,1},{1,0},{2,3},{3,2},{4,5},{5,4},{6,7},{7,6},{8,9},{9,8},{10,11... | collective-permute-start | bytes 589832 | tf_op jit(solution)/shard_map/ppermute | solution.py:47
  38.0 1.8 %collective-permute-start.12 = (bf16[1,256,384]{2,1,0:T(8,128)(2,1)S(1)}, bf16[1,256,384]{2,1,0:T(8,128)(2,1)S(1)}, u32[]{:S(2)}, u32[]{:S(2)}) collective-permute-start(bf16[1,256,384]{2,1,0:T(8,128)(2,1)S(1)} %collective-permute-done.8), channel_id=1, source_target_pairs={{0,1},{1,0},{2,3},{3,2},{4,5},{5,4},{6,7},{7,6},{8,9},{9,8},{10,11... | collective-permute-start | bytes 589832 | tf_op jit(solution)/shard_map/ppermute | solution.py:47
  38.4 5.5 %collective-permute-start.11 = (bf16[1,512,384]{2,1,0:T(8,128)(2,1)S(1)}, bf16[1,512,384]{2,1,0:T(8,128)(2,1)S(1)}, u32[]{:S(2)}, u32[]{:S(2)}) collective-permute-start(bf16[1,512,384]{2,1,0:T(8,128)(2,1)S(1)} %collective-permute-done.7), channel_id=1, source_target_pairs={{0,1},{1,0},{2,3},{3,2},{4,5},{5,4},{6,7},{7,6},{8,9},{9,8},{10,11... | collective-permute-start | bytes 1179656 | tf_op jit(solution)/shard_map/ppermute | solution.py:47
  41.4 8.2 %slice-start = ((s8[7962624]{0:T(1024)(128)(4,1)}), s8[3768320]{0:T(1024)(128)(4,1)S(1)}, s32[]{:S(2)}) async-start(s8[7962624]{0:T(1024)(128)(4,1)} %bitcast.526), calls=%async_computation | async-start | bytes 7536640
  43.9 5.6 %slice-start.1 = ((s8[7962624]{0:T(1024)(128)(4,1)}), s8[4194304]{0:T(1024)(128)(4,1)S(1)}, s32[]{:S(2)}) async-start(s8[7962624]{0:T(1024)(128)(4,1)} %bitcast.526), calls=%async_computation.1 | async-start | bytes 8388608
  45.0 1.1 %copy-start.3 = (bf16[384,384]{1,0:T(8,128)(2,1)S(1)}, bf16[384,384]{1,0:T(8,128)(2,1)}, u32[]{:S(2)}) copy-start(bf16[384,384]{1,0:T(8,128)(2,1)} %param.14) | copy-start | bytes 884740
  45.6 1.0 %copy-start.1 = (bf16[1,2,128,384]{3,2,1,0:T(8,128)(2,1)S(1)}, bf16[1,2,128,384]{3,2,1,0:T(8,128)(2,1)}, u32[]{:S(2)}) copy-start(bf16[1,2,128,384]{3,2,1,0:T(8,128)(2,1)} %param.10) | copy-start | bytes 589828
  45.6 1.1 %copy-start.5 = (bf16[384,384]{1,0:T(8,128)(2,1)S(1)}, bf16[384,384]{1,0:T(8,128)(2,1)}, u32[]{:S(2)}) copy-start(bf16[384,384]{1,0:T(8,128)(2,1)} %param.15) | copy-start | bytes 884740
  46.0 1.1 %copy-start.4 = (f32[384]{0:T(512)S(1)}, f32[384]{0:T(512)}, u32[]{:S(2)}) copy-start(f32[384]{0:T(512)} %param.17) | copy-start | bytes 4612
  47.3 6.8 %collective-permute-start.15 = (bf16[1,1,128,384]{3,2,1,0:T(8,128)(2,1)S(1)}, bf16[1,1,128,384]{3,2,1,0:T(8,128)(2,1)S(1)}, u32[]{:S(2)}, u32[]{:S(2)}) collective-permute-start(bf16[1,1,128,384]{3,2,1,0:T(8,128)(2,1)S(1)} %get-tuple-element.51), channel_id=1, source_target_pairs={{1,2},{3,4},{5,6},{7,8},{9,10},{11,12},{13,14},{2,1},{4,3},{6,5},{... | collective-permute-start | bytes 294920 | tf_op jit(solution)/shard_map/ppermute | solution.py:20
  49.4 4.7 %collective-permute-start.16 = (bf16[1,1,128,384]{3,2,1,0:T(8,128)(2,1)S(1)}, bf16[1,1,128,384]{3,2,1,0:T(8,128)(2,1)S(1)}, u32[]{:S(2)}, u32[]{:S(2)}) collective-permute-start(bf16[1,1,128,384]{3,2,1,0:T(8,128)(2,1)S(1)} %get-tuple-element.52), channel_id=1, source_target_pairs={{0,1},{1,0},{2,3},{3,2},{4,5},{5,4},{6,7},{7,6},{8,9},{9,8},{10,11... | collective-permute-start | bytes 294920 | tf_op jit(solution)/shard_map/ppermute | solution.py:23
  56.6 6.8 %collective-permute-start.17 = (bf16[1,1,128,384]{3,2,1,0:T(8,128)(2,1)S(1)}, bf16[1,1,128,384]{3,2,1,0:T(8,128)(2,1)S(1)}, u32[]{:S(2)}, u32[]{:S(2)}) collective-permute-start(bf16[1,1,128,384]{3,2,1,0:T(8,128)(2,1)S(1)} %slice.269), channel_id=1, source_target_pairs={{1,2},{3,4},{5,6},{7,8},{9,10},{11,12},{13,14},{2,1},{4,3},{6,5},{... | collective-permute-start | bytes 294920 | tf_op jit(solution)/shard_map/ppermute | solution.py:20
  58.6 4.8 %collective-permute-start.18 = (bf16[1,1,128,384]{3,2,1,0:T(8,128)(2,1)S(1)}, bf16[1,1,128,384]{3,2,1,0:T(8,128)(2,1)S(1)}, u32[]{:S(2)}, u32[]{:S(2)}) collective-permute-start(bf16[1,1,128,384]{3,2,1,0:T(8,128)(2,1)S(1)} %slice.270), channel_id=1, source_target_pairs={{0,1},{1,0},{2,3},{3,2},{4,5},{5,4},{6,7},{7,6},{8,9},{9,8},{10,11... | collective-permute-start | bytes 294920 | tf_op jit(solution)/shard_map/ppermute | solution.py:23

commit v17 on v15

--- a/solution.py
+++ b/solution.py
@@ -16,12 +16,12 @@
         even = (lax.axis_index(axis) % 2) == 0
         first = lax.slice_in_dim(array, 0, width, axis=dim)
         last = lax.slice_in_dim(array, array.shape[dim] - width, array.shape[dim], axis=dim)
-        on_chip = lax.ppermute(
-            jnp.where(even, last, first), axis, [(i, i ^ 1) for i in range(size)]
-        )
         pairs = [(i, i + 1) for i in range(1, size - 1, 2)]
         across = lax.ppermute(
             jnp.where(even, first, last), axis, pairs + [(j, i) for i, j in pairs]
+        )
+        on_chip = lax.ppermute(
+            jnp.where(even, last, first), axis, [(i, i ^ 1) for i in range(size)]
         )
         before = jnp.where(even, across, on_chip)
         after = jnp.where(even, on_chip, across)
@@ -100,10 +100,9 @@
                     term = taps[:, ro : ro + nrows, co : co + ncols, dr, dc, :]
                     acc = term if acc is None else acc + term
             phases_b.append(acc)
-        phase = jnp.concatenate(phases_b, axis=-1).astype(jnp.bfloat16)
-        phases_a.append(phase.reshape(nf, nrows, 2 * ncols * outs))
+        phases_a.append(jnp.concatenate(phases_b, axis=-1))
     result = jnp.stack(phases_a, axis=2)
-    return result.reshape(nf, 2 * nrows, 2 * ncols * outs)
+    return result.astype(jnp.bfloat16).reshape(nf, 2 * nrows, 2 * ncols * outs)
 
 
 def layer(
@@ -130,7 +129,7 @@
     second_out = exchange(jnp.concatenate([second] + second_in, axis=1), high, size)
     mine = [gathered] + first_out + second_out
     mirrors = exchange(gathered, [1], size)
-    mirrors = mirrors + [exchange(piece, [1], size)[0] for piece in mine[1:]]
+    mirrors = mirrors + exchange(jnp.concatenate(mine[1:], axis=1), [1], size)
     pieces = mine + mirrors
     q_keyed = jnp.einsum("fqc,dc->fqd", queries, w_key, preferred_element_type=jnp.float32)
     q_pair = split_pair(q_keyed, axis=1)

time: 68.9 us -> 65.7 us (0.954)
  starting transfers between devices: 19.9 us -> 18.5 us
  other arithmetic: 9.19 us -> 7.85 us
  matrix products: 17 us -> 15.9 us
  waiting for transfers between devices: 17.3 us -> 18 us
    ppermute x13 -> x10, starting transfers between devices: 10.5 us -> 9.37 us  [exchange(): lax.ppermute(values, ROWS, [(i, i ^ mask) for i in range(size)])]
    convert_element_type x1, other arithmetic: 1.04 us -> 0.11 us  [layer(): normed = rms_gain(flat.astype(jnp.float32), norm_attn).astype(jnp.bfloat16)]
    reshape x1 -> x0, local copies, waits for them, and re-layouts: 0.9 us -> none  [upsample_conv(): return result.reshape(nf, 2 * nrows, 2 * ncols * outs)]
    convert_element_type x2 -> x1, local copies, waits for them, and re-layouts: 0.11 us -> 0.89 us  [upsample_conv(): return result.astype(jnp.bfloat16).reshape(nf, 2 * nrows, 2 * ncols * outs)]
    dot_general x10 -> x7, matrix products: 3.32 us -> 2.73 us  [layer(): jnp.einsum('fqk,fkc->fqc', e.astype(jnp.bfloat16), p, preferred_element_t...]
    dot_general x10 -> x7, matrix products: 4.07 us -> 3.49 us  [layer(): jnp.einsum('fqc,fkc->fqk', q_pair, piece, preferred_element_type=jnp.floa...]
    unnamed x25 -> x27, local copies, waits for them, and re-layouts: 1.34 us -> 1.81 us
    ppermute x13 -> x10, waiting for transfers between devices: 10.2 us -> 10.6 us  [exchange(): lax.ppermute(values, ROWS, [(i, i ^ mask) for i in range(size)])]
  transfers between devices with their start and end apart: 19 -> 16, of which waited for: 4 -> 3; matrix products, arithmetic and copies ran while one was open for 26% -> 25% of each run, Pallas kernels for 0% -> 0%
where the time goes in v17:
time: 65.7 us; the launch traced here: 65.3 us
  starting transfers between devices  18.5 us (28%)
  waiting for transfers between devices  18 us (27%)
  matrix products  15.9 us (24%)
  other arithmetic  7.85 us (12%)
  local copies, waits for them, and re-layouts  4.41 us (7%)
  between operations  0.76 us (1%)
    ppermute x10, waiting for transfers between devices, exchange(): lax.ppermute(values, ROWS, [(i, i ^ mask) for i in range(size)])  10.6 us
    ppermute x10, starting transfers between devices, exchange(): lax.ppermute(values, ROWS, [(i, i ^ mask) for i in range(size)])  9.37 us
    ppermute x3, starting transfers between devices, padded_2(): lax.ppermute(jnp.where(even, first, last), axis, pairs + [(j, i) for i, j...  8.89 us
    ppermute x3, waiting for transfers between devices, padded_2(): lax.ppermute(jnp.where(even, first, last), axis, pairs + [(j, i) for i, j...  7.36 us
    conv_general_dilated x2, matrix products, conv_rows(): lax.conv_general_dilated(haloed[tstep:tstep + 1], weight[tstep], window_s...  4.14 us
    dot_general x7, matrix products, layer(): jnp.einsum('fqc,fkc->fqk', q_pair, piece, preferred_element_type=jnp.floa...  3.49 us
    dot_general x7, matrix products, layer(): jnp.einsum('fqk,fkc->fqc', e.astype(jnp.bfloat16), p, preferred_element_t...  2.73 us
    select_n x3, other arithmetic, padded_2(): jnp.where(even, first, last)  1.85 us
  transfers between devices with their start and end apart: 16, of which 3 were waited for; matrix products, arithmetic and copies ran while one was open for 25% of the time, Pallas kernels for 0%

profile of v17, /device:TPU:5, one launch (start us, length us, event | category | flops | bytes accessed | tf_op | source)
XLA Modules:
  0.0 65.3 jit_solution(2968872431539206874)
XLA Ops:
  0.0 1.2 %multiply_reduce_fusion.1 = f32[2,128]{1,0:T(2,128)S(1)} fusion(bf16[1,2,128,384]{3,2,1,0:T(8,128)(2,1)} %param.10), kind=kLoop, calls=%fused_computation.137 | loop fusion | flops 294656 | bytes 197632 | tf_op jit(solution)/shard_map/reduce_sum | solution.py:33
  1.2 1.1 %constant_dynamic-update-slice_fusion.4 = (bf16[1,768,384]{2,1,0:T(8,128)(2,1)S(1)}, bf16[1,256,384]{2,1,0:T(8,128)(2,1)S(1)}) fusion(f32[384]{0:T(512)} %param.11, f32[256]{0:T(256)S(1)} %rsqrt_bitcast_fusion, bf16[1,2,128,384]{3,2,1,0:T(8,128)(2,1)} %param.10), kind=kLoop, calls=%fused_computation.267 | loop fusion | flops 393215 | bytes 592384
  2.3 1.4 %collective-permute-start.2 = (bf16[1,128,384]{2,1,0:T(8,128)(2,1)S(1)}, bf16[1,128,384]{2,1,0:T(8,128)(2,1)S(1)}, u32[]{:S(2)}, u32[]{:S(2)}) collective-permute-start(bf16[1,128,384]{2,1,0:T(8,128)(2,1)S(1)} %get-tuple-element.51), channel_id=1, source_target_pairs={{0,4},{1,5},{2,6},{3,7},{4,0},{5,1},{6,2},{7,3},{8,12},{9,13},{10,... | collective-permute-start | bytes 294920 | tf_op jit(solution)/shard_map/ppermute | solution.py:47
  3.6 2.3 %collective-permute-start.3 = (bf16[1,128,384]{2,1,0:T(8,128)(2,1)S(1)}, bf16[1,128,384]{2,1,0:T(8,128)(2,1)S(1)}, u32[]{:S(2)}, u32[]{:S(2)}) collective-permute-start(bf16[1,128,384]{2,1,0:T(8,128)(2,1)S(1)} %get-tuple-element.51), channel_id=1, source_target_pairs={{0,8},{1,9},{2,10},{3,11},{4,12},{5,13},{6,14},{7,15},{8,0},{9,1},... | collective-permute-start | bytes 294920 | tf_op jit(solution)/shard_map/ppermute | solution.py:47
  6.2 1.8 %broadcast_select_fusion.3 = (bf16[2,1,128,384]{3,2,1,0:T(8,128)(2,1)}, bf16[2,1,128,384]{3,2,1,0:T(8,128)(2,1)}) fusion(pred[]{:T(512)S(6)} %eq.9, bf16[2,2,128,384]{3,2,1,0:T(8,128)(2,1)} %param.16), kind=kLoop, calls=%fused_computation.242 | loop fusion | flops 196608 | bytes 786433 | tf_op jit(solution)/shard_map/jit(_where)/select_n | solution.py:21
  8.0 4.9 %collective-permute-start = (bf16[2,1,128,384]{3,2,1,0:T(8,128)(2,1)}, bf16[2,1,128,384]{3,2,1,0:T(8,128)(2,1)S(1)}, u32[]{:S(2)}, u32[]{:S(2)}) collective-permute-start(bf16[2,1,128,384]{3,2,1,0:T(8,128)(2,1)} %get-tuple-element.38), channel_id=1, source_target_pairs={{1,2},{3,4},{5,6},{7,8},{9,10},{11,12},{13,14},{2,1},{4,3},{6,5},{... | collective-permute-start | bytes 589832 | tf_op jit(solution)/shard_map/ppermute | solution.py:20
  13.0 1.6 %convert_bitcast_fusion = (bf16[1,256,384]{2,1,0:T(8,128)(2,1)S(1)}, bf16[1,256,384]{2,1,0:T(8,128)(2,1)S(1)}) fusion(bf16[384,384]{1,0:T(8,128)(2,1)} %param.13, bf16[256,384]{1,0:T(8,128)(2,1)S(1)} %fusion.103, bf16[384,384]{1,0:T(8,128)(2,1)} %param.12), kind=kOutput, calls=%fused_computation.256 | convolution fusion | flops 151486464 | bytes 1179648 | tf_op jit(solution)/shard_map/fqc,dc->fqd/dot_general | solution.py:134
  14.7 2.1 %collective-permute-start.10 = (bf16[1,256,384]{2,1,0:T(8,128)(2,1)S(1)}, bf16[1,256,384]{2,1,0:T(8,128)(2,1)S(1)}, u32[]{:S(2)}, u32[]{:S(2)}) collective-permute-start(bf16[1,256,384]{2,1,0:T(8,128)(2,1)S(1)} %pad_maximum_fusion.4), channel_id=1, source_target_pairs={{0,12},{1,13},{2,14},{3,15},{4,8},{5,9},{6,10},{7,11},{8,4},{9,5},... | collective-permute-start | bytes 589832 | tf_op jit(solution)/shard_map/ppermute | solution.py:47
  16.9 1.2 %collective-permute-start.9 = (bf16[1,256,384]{2,1,0:T(8,128)(2,1)S(1)}, bf16[1,256,384]{2,1,0:T(8,128)(2,1)S(1)}, u32[]{:S(2)}, u32[]{:S(2)}) collective-permute-start(bf16[1,256,384]{2,1,0:T(8,128)(2,1)S(1)} %pad_maximum_fusion.4), channel_id=1, source_target_pairs={{0,8},{1,9},{2,10},{3,11},{4,12},{5,13},{6,14},{7,15},{8,0},{9,1},... | collective-permute-start | bytes 589832 | tf_op jit(solution)/shard_map/ppermute | solution.py:47
  18.2 0.8 %collective-permute-start.6 = (bf16[1,768,384]{2,1,0:T(8,128)(2,1)S(1)}, bf16[1,768,384]{2,1,0:T(8,128)(2,1)S(1)}, u32[]{:S(2)}, u32[]{:S(2)}) collective-permute-start(bf16[1,768,384]{2,1,0:T(8,128)(2,1)S(1)} %constant_dynamic-update-slice_fusion), channel_id=1, source_target_pairs={{0,1},{1,0},{2,3},{3,2},{4,5},{5,4},{6,7},{7,6},{8,9},{9,8},{10,11... | collective-permute-start | bytes 1769480 | tf_op jit(solution)/shard_map/ppermute | solution.py:47
  19.0 0.6 convolution_bitcast_fusion.3
  19.8 0.7 %collective-permute-start.8 = (bf16[1,256,384]{2,1,0:T(8,128)(2,1)S(1)}, bf16[1,256,384]{2,1,0:T(8,128)(2,1)S(1)}, u32[]{:S(2)}, u32[]{:S(2)}) collective-permute-start(bf16[1,256,384]{2,1,0:T(8,128)(2,1)S(1)} %pad_maximum_fusion.4), channel_id=1, source_target_pairs={{0,4},{1,5},{2,6},{3,7},{4,0},{5,1},{6,2},{7,3},{8,12},{9,13},{10,... | collective-permute-start | bytes 589832 | tf_op jit(solution)/shard_map/ppermute | solution.py:47
  20.8 0.3 copy.105
  21.5 2.9 %fusion.26 = f32[2,8,17,384]{3,1,2,0:T(8,128)S(1)} fusion(bf16[3,3,3,384,384]{4,3,2,1,0:T(8,128)(2,1)} %param.18, bf16[4,1,7,2,384]{4,2,3,0,1:T(8,128)(2,1)S(1)} %slice.254, bf16[4,1,8,17,384]{4,2,3,0,1:T(8,128)(2,1)S(1)} %copy.41, pred[8,17]{0,1:T(8,128)(4,1)S(1)} %copy-done.7), kind=kOutput, calls=%fused_computation.43 | convolution fusion | flops 723449856 | bytes 3532936 | tf_op jit(solution)/shard_map/conv_general_dilated | solution.py:71
  24.4 0.3 copy.104
  25.0 0.3 convolution_bitcast_fusion.6
  25.3 10.6 %collective-permute-done.9 = bf16[1,256,384]{2,1,0:T(8,128)(2,1)S(1)} collective-permute-done((bf16[1,256,384]{2,1,0:T(8,128)(2,1)S(1)}, bf16[1,256,384]{2,1,0:T(8,128)(2,1)S(1)}, u32[]{:S(2)}, u32[]{:S(2)}) %collective-permute-start.9) | collective-permute-done | bytes 196640 | tf_op jit(solution)/shard_map/ppermute | solution.py:47
  35.9 0.3 convolution_bitcast_fusion.7
  36.4 0.3 convolution_bitcast_fusion.8
  36.9 0.6 collective-permute-start.11
  37.5 0.5 convolution_bitcast_fusion.4
  38.1 0.6 convolution_bitcast_fusion.2
  38.8 0.4 fusion.49
  39.3 0.5 fusion.53
  39.7 0.5 fusion.14
  40.6 0.3 fusion.165
  40.9 0.3 fusion.168
  41.1 0.3 fusion.171
  41.4 0.4 fusion.16
  41.8 0.9 %convolution_bitcast_fusion = f32[1,512,1280]{2,1,0:T(8,128)S(1)} fusion(bf16[1,1280,384]{2,1,0:T(8,128)(2,1)S(1)} %collective-permute-done.11, bf16[1,256,384]{2,1,0:T(8,128)(2,1)S(1)} %get-tuple-element.41, bf16[1,256,384]{2,1,0:T(8,128)(2,1)S(1)} %get-tuple-element.40), kind=kOutput, calls=%fused_computation | convolution fusion | flops 504102912 | bytes 3997696 | tf_op jit(solution)/shard_map/fqc,fkc->fqk/dot_general | solution.py:142
  42.9 0.4 fusion.30
  43.4 0.6 fusion.17
  44.0 0.6 copy-done.3
  44.6 0.4 convolution_bitcast_fusion.5
  45.0 0.4 multiply_reduce_fusion
  45.7 2.1 %collective-permute-start.12 = (bf16[1,1,128,384]{3,2,1,0:T(8,128)(2,1)S(1)}, bf16[1,1,128,384]{3,2,1,0:T(8,128)(2,1)S(1)}, u32[]{:S(2)}, u32[]{:S(2)}) collective-permute-start(bf16[1,1,128,384]{3,2,1,0:T(8,128)(2,1)S(1)} %get-tuple-element.48), channel_id=1, source_target_pairs={{1,2},{3,4},{5,6},{7,8},{9,10},{11,12},{13,14},{2,1},{4,3},{6,5},{... | collective-permute-start | bytes 294920 | tf_op jit(solution)/shard_map/ppermute | solution.py:20
  47.9 1.2 %fusion.23 = f32[2,8,17,384]{3,1,2,0:T(8,128)S(1)} fusion(f32[2,8,17,384]{3,1,2,0:T(8,128)S(1)} %fusion.26, bf16[3,3,3,384,384]{4,3,2,1,0:T(8,128)(2,1)S(1)} %bitcast.497, bf16[4,1,7,2,384]{4,2,3,0,1:T(8,128)(2,1)S(1)} %slice.252, bf16[4,1,8,17,384]{4,2,3,0,1:T(8,128)(2,1)S(1)} %copy.38, pred[8,17]{0,1:T(8,128)(4,1)S(1)} %copy-done.7), kind=kOutput, calls=%fused_computation.42 | convolution fusion | flops 723554304 | bytes 3959808 | tf_op jit(solution)/shard_map/conv_general_dilated | solution.py:71
  49.6 3.0 %collective-permute-done.12 = bf16[1,1,128,384]{3,2,1,0:T(8,128)(2,1)S(1)} collective-permute-done((bf16[1,1,128,384]{3,2,1,0:T(8,128)(2,1)S(1)}, bf16[1,1,128,384]{3,2,1,0:T(8,128)(2,1)S(1)}, u32[]{:S(2)}, u32[]{:S(2)}) %collective-permute-start.12) | collective-permute-done | bytes 98336 | tf_op jit(solution)/shard_map/ppermute | solution.py:20
  52.7 0.3 copy.106
  53.2 0.5 convolution_select_fusion
  53.8 0.5 fusion.10
  54.3 0.6 fusion.15
  55.0 1.9 %collective-permute-start.14 = (bf16[1,1,128,384]{3,2,1,0:T(8,128)(2,1)S(1)}, bf16[1,1,128,384]{3,2,1,0:T(8,128)(2,1)S(1)}, u32[]{:S(2)}, u32[]{:S(2)}) collective-permute-start(bf16[1,1,128,384]{3,2,1,0:T(8,128)(2,1)S(1)} %slice.279), channel_id=1, source_target_pairs={{1,2},{3,4},{5,6},{7,8},{9,10},{11,12},{13,14},{2,1},{4,3},{6,5},{... | collective-permute-start | bytes 294920 | tf_op jit(solution)/shard_map/ppermute | solution.py:20
  57.5 4.4 %collective-permute-done.14 = bf16[1,1,128,384]{3,2,1,0:T(8,128)(2,1)S(1)} collective-permute-done((bf16[1,1,128,384]{3,2,1,0:T(8,128)(2,1)S(1)}, bf16[1,1,128,384]{3,2,1,0:T(8,128)(2,1)S(1)}, u32[]{:S(2)}, u32[]{:S(2)}) %collective-permute-start.14) | collective-permute-done | bytes 98336 | tf_op jit(solution)/shard_map/ppermute | solution.py:20
  61.9 1.5 %convolution_bitcast_fusion.1 = f32[1,4,130,3,3,192]{5,2,4,3,1,0:T(8,128)S(1)} fusion(bf16[3,3,384,192]{2,3,1,0:T(8,128)(2,1)S(1)} %copy-done, bf16[1,1,128,384]{3,2,1,0:T(8,128)(2,1)S(1)} %get-tuple-element.45, bf16[1,2,128,384]{3,2,1,0:T(8,128)(2,1)S(1)} %bitcast.477, bf16[1,1,128,384]{3,2,1,0:T(8,128)(2,1)S(1)} %get-tuple-element.44), kind=kOutput, calls=%fused_computation.7 | convolution fusion | flops 692490240 | bytes 5314560 | tf_op jit(solution)/shard_map/frwc,ijco->frwijo/dot_general | solution.py:88
  63.4 0.4 fusion.186
  63.8 0.2 fusion.189
  64.5 0.9 %convert_element_type.150 = bf16[1,4,49152]{2,1,0:T(4,128)(2,1)} reshape(bf16[1,2,2,128,384]{4,3,2,1,0:T(8,128)(2,1)S(1)} %copy.77) | data formatting | bytes 786432 | tf_op jit(solution)/shard_map/convert_element_type | solution.py:105
  (103 shorter events, 4.9 us)
Async XLA Ops:
  0.0 61.9 %copy-start = (bf16[3,3,384,192]{2,3,1,0:T(8,128)(2,1)S(1)}, bf16[3,3,384,192]{2,3,1,0:T(8,128)(2,1)}, u32[]{:S(2)}) copy-start(bf16[3,3,384,192]{2,3,1,0:T(8,128)(2,1)} %param.19) | copy-start | bytes 3981316
  0.0 12.9 %copy-start.1 = (bf16[1,2,128,384]{3,2,1,0:T(8,128)(2,1)S(1)}, bf16[1,2,128,384]{3,2,1,0:T(8,128)(2,1)}, u32[]{:S(2)}) copy-start(bf16[1,2,128,384]{3,2,1,0:T(8,128)(2,1)} %param.10) | copy-start | bytes 589828
  0.0 12.9 %copy-start.4 = (f32[384]{0:T(512)S(1)}, f32[384]{0:T(512)}, u32[]{:S(2)}) copy-start(f32[384]{0:T(512)} %param.11) | copy-start | bytes 4612
  2.3 12.4 %collective-permute-start.2 = (bf16[1,128,384]{2,1,0:T(8,128)(2,1)S(1)}, bf16[1,128,384]{2,1,0:T(8,128)(2,1)S(1)}, u32[]{:S(2)}, u32[]{:S(2)}) collective-permute-start(bf16[1,128,384]{2,1,0:T(8,128)(2,1)S(1)} %get-tuple-element.51), channel_id=1, source_target_pairs={{0,4},{1,5},{2,6},{3,7},{4,0},{5,1},{6,2},{7,3},{8,12},{9,13},{10,... | collective-permute-start | bytes 294920 | tf_op jit(solution)/shard_map/ppermute | solution.py:47
  3.6 13.2 %collective-permute-start.3 = (bf16[1,128,384]{2,1,0:T(8,128)(2,1)S(1)}, bf16[1,128,384]{2,1,0:T(8,128)(2,1)S(1)}, u32[]{:S(2)}, u32[]{:S(2)}) collective-permute-start(bf16[1,128,384]{2,1,0:T(8,128)(2,1)S(1)} %get-tuple-element.51), channel_id=1, source_target_pairs={{0,8},{1,9},{2,10},{3,11},{4,12},{5,13},{6,14},{7,15},{8,0},{9,1},... | collective-permute-start | bytes 294920 | tf_op jit(solution)/shard_map/ppermute | solution.py:47
  6.0 12.1 %collective-permute-start.4 = (bf16[1,128,384]{2,1,0:T(8,128)(2,1)S(1)}, bf16[1,128,384]{2,1,0:T(8,128)(2,1)S(1)}, u32[]{:S(2)}, u32[]{:S(2)}) collective-permute-start(bf16[1,128,384]{2,1,0:T(8,128)(2,1)S(1)} %get-tuple-element.51), channel_id=1, source_target_pairs={{0,12},{1,13},{2,14},{3,15},{4,8},{5,9},{6,10},{7,11},{8,4},{9,5},... | collective-permute-start | bytes 294920 | tf_op jit(solution)/shard_map/ppermute | solution.py:47
  6.0 8.6 %collective-permute-start.5 = (bf16[1,128,384]{2,1,0:T(8,128)(2,1)S(1)}, bf16[1,128,384]{2,1,0:T(8,128)(2,1)S(1)}, u32[]{:S(2)}, u32[]{:S(2)}) collective-permute-start(bf16[1,128,384]{2,1,0:T(8,128)(2,1)S(1)} %get-tuple-element.50), channel_id=1, source_target_pairs={{0,2},{1,3},{2,0},{3,1},{4,6},{5,7},{6,4},{7,5},{8,10},{9,11},{10,... | collective-permute-start | bytes 294920 | tf_op jit(solution)/shard_map/ppermute | solution.py:47
  8.0 11.8 %collective-permute-start = (bf16[2,1,128,384]{3,2,1,0:T(8,128)(2,1)}, bf16[2,1,128,384]{3,2,1,0:T(8,128)(2,1)S(1)}, u32[]{:S(2)}, u32[]{:S(2)}) collective-permute-start(bf16[2,1,128,384]{3,2,1,0:T(8,128)(2,1)} %get-tuple-element.38), channel_id=1, source_target_pairs={{1,2},{3,4},{5,6},{7,8},{9,10},{11,12},{13,14},{2,1},{4,3},{6,5},{... | collective-permute-start | bytes 589832 | tf_op jit(solution)/shard_map/ppermute | solution.py:20
  14.6 5.9 %collective-permute-start.1 = (bf16[2,1,128,384]{3,2,1,0:T(8,128)(2,1)}, bf16[2,1,128,384]{3,2,1,0:T(8,128)(2,1)S(1)}, u32[]{:S(2)}, u32[]{:S(2)}) collective-permute-start(bf16[2,1,128,384]{3,2,1,0:T(8,128)(2,1)} %get-tuple-element.39), channel_id=1, source_target_pairs={{0,1},{1,0},{2,3},{3,2},{4,5},{5,4},{6,7},{7,6},{8,9},{9,8},{10,11... | collective-permute-start | bytes 589832 | tf_op jit(solution)/shard_map/ppermute | solution.py:23
  14.7 10.3 %collective-permute-start.10 = (bf16[1,256,384]{2,1,0:T(8,128)(2,1)S(1)}, bf16[1,256,384]{2,1,0:T(8,128)(2,1)S(1)}, u32[]{:S(2)}, u32[]{:S(2)}) collective-permute-start(bf16[1,256,384]{2,1,0:T(8,128)(2,1)S(1)} %pad_maximum_fusion.4), channel_id=1, source_target_pairs={{0,12},{1,13},{2,14},{3,15},{4,8},{5,9},{6,10},{7,11},{8,4},{9,5},... | collective-permute-start | bytes 589832 | tf_op jit(solution)/shard_map/ppermute | solution.py:47
  16.9 19.1 %collective-permute-start.9 = (bf16[1,256,384]{2,1,0:T(8,128)(2,1)S(1)}, bf16[1,256,384]{2,1,0:T(8,128)(2,1)S(1)}, u32[]{:S(2)}, u32[]{:S(2)}) collective-permute-start(bf16[1,256,384]{2,1,0:T(8,128)(2,1)S(1)} %pad_maximum_fusion.4), channel_id=1, source_target_pairs={{0,8},{1,9},{2,10},{3,11},{4,12},{5,13},{6,14},{7,15},{8,0},{9,1},... | collective-permute-start | bytes 589832 | tf_op jit(solution)/shard_map/ppermute | solution.py:47
  18.2 19.9 %collective-permute-start.6 = (bf16[1,768,384]{2,1,0:T(8,128)(2,1)S(1)}, bf16[1,768,384]{2,1,0:T(8,128)(2,1)S(1)}, u32[]{:S(2)}, u32[]{:S(2)}) collective-permute-start(bf16[1,768,384]{2,1,0:T(8,128)(2,1)S(1)} %constant_dynamic-update-slice_fusion), channel_id=1, source_target_pairs={{0,1},{1,0},{2,3},{3,2},{4,5},{5,4},{6,7},{7,6},{8,9},{9,8},{10,11... | collective-permute-start | bytes 1769480 | tf_op jit(solution)/shard_map/ppermute | solution.py:47
  19.6 1.0 %copy-start.2 = (bf16[2,2,128,384]{3,2,1,0:T(8,128)(2,1)S(1)}, bf16[2,2,128,384]{3,2,1,0:T(8,128)(2,1)}, u32[]{:S(2)}) copy-start(bf16[2,2,128,384]{3,2,1,0:T(8,128)(2,1)} %param.16) | copy-start | bytes 1179652
  19.8 16.5 %collective-permute-start.8 = (bf16[1,256,384]{2,1,0:T(8,128)(2,1)S(1)}, bf16[1,256,384]{2,1,0:T(8,128)(2,1)S(1)}, u32[]{:S(2)}, u32[]{:S(2)}) collective-permute-start(bf16[1,256,384]{2,1,0:T(8,128)(2,1)S(1)} %pad_maximum_fusion.4), channel_id=1, source_target_pairs={{0,4},{1,5},{2,6},{3,7},{4,0},{5,1},{6,2},{7,3},{8,12},{9,13},{10,... | collective-permute-start | bytes 589832 | tf_op jit(solution)/shard_map/ppermute | solution.py:47
  20.5 16.3 %collective-permute-start.7 = (bf16[1,512,384]{2,1,0:T(8,128)(2,1)S(1)}, bf16[1,512,384]{2,1,0:T(8,128)(2,1)S(1)}, u32[]{:S(2)}, u32[]{:S(2)}) collective-permute-start(bf16[1,512,384]{2,1,0:T(8,128)(2,1)S(1)} %pad_maximum_fusion.2), channel_id=1, source_target_pairs={{0,2},{1,3},{2,0},{3,1},{4,6},{5,7},{6,4},{7,5},{8,10},{9,11},{10,... | collective-permute-start | bytes 1179656 | tf_op jit(solution)/shard_map/ppermute | solution.py:47
  20.8 0.7 %copy-start.7 = (pred[8,17]{0,1:T(8,128)(4,1)S(1)}, pred[8,17]{0,1:T(8,128)(4,1)}, u32[]{:S(2)}) copy-start(pred[8,17]{0,1:T(8,128)(4,1)} %constant.70) | copy-start | bytes 412
  36.9 5.0 %collective-permute-start.11 = (bf16[1,1280,384]{2,1,0:T(8,128)(2,1)S(1)}, bf16[1,1280,384]{2,1,0:T(8,128)(2,1)S(1)}, u32[]{:S(2)}, u32[]{:S(2)}) collective-permute-start(bf16[1,1280,384]{2,1,0:T(8,128)(2,1)S(1)} %pad_maximum_fusion), channel_id=1, source_target_pairs={{0,1},{1,0},{2,3},{3,2},{4,5},{5,4},{6,7},{7,6},{8,9},{9,8},{10,11... | collective-permute-start | bytes 2949128 | tf_op jit(solution)/shard_map/ppermute | solution.py:47
  40.6 7.4 %slice-start = ((s8[7962624]{0:T(1024)(128)(4,1)}), s8[3768320]{0:T(1024)(128)(4,1)S(1)}, s32[]{:S(2)}) async-start(s8[7962624]{0:T(1024)(128)(4,1)} %bitcast.496), calls=%async_computation | async-start | bytes 7536640
  42.7 5.2 %slice-start.1 = ((s8[7962624]{0:T(1024)(128)(4,1)}), s8[4194304]{0:T(1024)(128)(4,1)S(1)}, s32[]{:S(2)}) async-start(s8[7962624]{0:T(1024)(128)(4,1)} %bitcast.496), calls=%async_computation.1 | async-start | bytes 8388608
  43.4 1.3 %copy-start.3 = (bf16[384,384]{1,0:T(8,128)(2,1)S(1)}, bf16[384,384]{1,0:T(8,128)(2,1)}, u32[]{:S(2)}) copy-start(bf16[384,384]{1,0:T(8,128)(2,1)} %param.14) | copy-start | bytes 884740
  44.0 1.1 %copy-start.6 = (bf16[384,384]{1,0:T(8,128)(2,1)S(1)}, bf16[384,384]{1,0:T(8,128)(2,1)}, u32[]{:S(2)}) copy-start(bf16[384,384]{1,0:T(8,128)(2,1)} %param.15) | copy-start | bytes 884740
  44.6 0.9 %copy-start.5 = (f32[384]{0:T(512)S(1)}, f32[384]{0:T(512)}, u32[]{:S(2)}) copy-start(f32[384]{0:T(512)} %param.17) | copy-start | bytes 4612
  45.7 6.8 %collective-permute-start.12 = (bf16[1,1,128,384]{3,2,1,0:T(8,128)(2,1)S(1)}, bf16[1,1,128,384]{3,2,1,0:T(8,128)(2,1)S(1)}, u32[]{:S(2)}, u32[]{:S(2)}) collective-permute-start(bf16[1,1,128,384]{3,2,1,0:T(8,128)(2,1)S(1)} %get-tuple-element.48), channel_id=1, source_target_pairs={{1,2},{3,4},{5,6},{7,8},{9,10},{11,12},{13,14},{2,1},{4,3},{6,5},{... | collective-permute-start | bytes 294920 | tf_op jit(solution)/shard_map/ppermute | solution.py:20
  47.8 4.7 %collective-permute-start.13 = (bf16[1,1,128,384]{3,2,1,0:T(8,128)(2,1)S(1)}, bf16[1,1,128,384]{3,2,1,0:T(8,128)(2,1)S(1)}, u32[]{:S(2)}, u32[]{:S(2)}) collective-permute-start(bf16[1,1,128,384]{3,2,1,0:T(8,128)(2,1)S(1)} %get-tuple-element.49), channel_id=1, source_target_pairs={{0,1},{1,0},{2,3},{3,2},{4,5},{5,4},{6,7},{7,6},{8,9},{9,8},{10,11... | collective-permute-start | bytes 294920 | tf_op jit(solution)/shard_map/ppermute | solution.py:23
  55.0 6.8 %collective-permute-start.14 = (bf16[1,1,128,384]{3,2,1,0:T(8,128)(2,1)S(1)}, bf16[1,1,128,384]{3,2,1,0:T(8,128)(2,1)S(1)}, u32[]{:S(2)}, u32[]{:S(2)}) collective-permute-start(bf16[1,1,128,384]{3,2,1,0:T(8,128)(2,1)S(1)} %slice.279), channel_id=1, source_target_pairs={{1,2},{3,4},{5,6},{7,8},{9,10},{11,12},{13,14},{2,1},{4,3},{6,5},{... | collective-permute-start | bytes 294920 | tf_op jit(solution)/shard_map/ppermute | solution.py:20
  57.1 4.8 %collective-permute-start.15 = (bf16[1,1,128,384]{3,2,1,0:T(8,128)(2,1)S(1)}, bf16[1,1,128,384]{3,2,1,0:T(8,128)(2,1)S(1)}, u32[]{:S(2)}, u32[]{:S(2)}) collective-permute-start(bf16[1,1,128,384]{3,2,1,0:T(8,128)(2,1)S(1)} %slice.280), channel_id=1, source_target_pairs={{0,1},{1,0},{2,3},{3,2},{4,5},{5,4},{6,7},{7,6},{8,9},{9,8},{10,11... | collective-permute-start | bytes 294920 | tf_op jit(solution)/shard_map/ppermute | solution.py:23
